TPU v7x, 32 devices: a whole 2x2x4 slice. The times are simulated.
32 devices in a mesh: seq: 8 (over y, x, core), head: 4 (over z).
Axes of the slice: x: 2, y: 2, z: 4, core: 2. Of those that a mesh axis runs over, the one named last changes fastest.
Arguments:
- queries: bfloat16 [4096, 4096], P('seq', 'head'), may hold values from -6 to 6
- keys: bfloat16 [4096, 4096], P('seq', 'head'), may hold values from -6 to 6
- values: bfloat16 [4096, 4096], P('seq', 'head'), may hold values from -48 to 48
- gate_logits: bfloat16 [4096, 4096], P('seq', 'head'), may hold values from -8 to 8
- out_weight: bfloat16 [4096, 6144], P('head'), may hold values from -0.125 to 0.125
Outputs:
- layer_out: bfloat16 [4096, 6144], P('seq', 'head')
All inputs are finite; a program needn't handle non-finite values.
Results may differ from a plain program's by a relative error of at most 0.02.
Values may be sent and summed in bfloat16 or wider, within the bound.
No kernel may reach another device: no remote copies, remote signals or barrier semaphores. Data moves between devices by JAX's collectives and lax.ppermute only.
A program may use at most 64 MiB of HBM per device.

v0:
```python
import jax
import jax.numpy as jnp
from jax import lax
from jax.sharding import PartitionSpec as P

HEADS = 32
HEAD_DIM = 128


def activate(raw_input):
    return jax.nn.silu(raw_input.astype(jnp.float32)).astype(jnp.bfloat16)


def body(queries, keys, values, gate_logits, out_weight):
    tokens_here = queries.shape[0]
    feature_count = queries.shape[1]
    heads_here = feature_count // HEAD_DIM
    block_rows = min(512, tokens_here)
    block_count = tokens_here // block_rows
    shape_blocks = (block_count, block_rows, heads_here, HEAD_DIM)
    active_q = activate(queries).reshape(shape_blocks)
    active_k = activate(keys).reshape(shape_blocks)
    active_v = activate(values).reshape(shape_blocks)
    block_states = jnp.einsum(
        "nshd,nshe->nhde", active_k, active_v, preferred_element_type=jnp.float32
    )
    span_total = jnp.sum(block_states, axis=0)
    earlier_local = jnp.cumsum(block_states, axis=0) - block_states
    my_index = lax.axis_index("seq")
    shards = lax.all_gather(
        span_total[None].astype(jnp.bfloat16), "seq", axis=0, tiled=True
    ).astype(jnp.float32)
    positions = jnp.arange(shards.shape[0], dtype=jnp.int32)
    weights = (positions < my_index).astype(jnp.float32)
    prefix = jnp.zeros_like(span_total) + jnp.sum(shards * weights[:, None, None, None], axis=0)
    before = (prefix[None] + earlier_local).astype(jnp.bfloat16)
    causal_mask = jnp.tril(jnp.ones((block_rows, block_rows), jnp.float32))
    scores = jnp.einsum("nthd,nshd->nhts", active_q, active_k, preferred_element_type=jnp.float32)
    scores = (scores * causal_mask).astype(jnp.bfloat16)
    within_block = jnp.einsum(
        "nhts,nshd->nthd", scores, active_v, preferred_element_type=jnp.float32
    )
    from_state = jnp.einsum("nthd,nhde->nthe", active_q, before, preferred_element_type=jnp.float32)
    attended = (within_block + from_state).reshape(tokens_here, feature_count)
    square_sums = lax.psum(jnp.sum(attended * attended, axis=-1), "head")
    scaling = lax.rsqrt(square_sums / (HEADS * HEAD_DIM) + 1e-06)
    gate = jax.nn.sigmoid(gate_logits.astype(jnp.float32))
    normed = (attended * scaling[:, None] * gate).astype(jnp.bfloat16)
    reduced = lax.psum_scatter(
        lax.dot_general(
            out_weight, normed, (((0,), (1,)), ((), ())), preferred_element_type=jnp.float32
        ).astype(jnp.bfloat16),
        "head",
        scatter_dimension=0,
        tiled=True,
    ).astype(jnp.float32)
    return reduced.T.astype(jnp.bfloat16)


def solution(mesh):
    return jax.shard_map(
        body,
        mesh=mesh,
        in_specs=(
            P("seq", "head"),
            P("seq", "head"),
            P("seq", "head"),
            P("seq", "head"),
            P("head", None),
        ),
        out_specs=P("seq", "head"),
        check_vma=False,
    )
```

profile of v0, /device:TPU:0, one launch (start us, length us, event | category | flops | bytes accessed | tf_op | source)
XLA Modules:
  0.0 192.8 jit_solution(12036253391915671986)
XLA Ops:
  6.5 0.0 copy-start
  6.5 0.0 all-gather.3.cloned.1.call-start
  6.5 1.9 fusion.17
  8.5 0.5 copy.19
  9.0 0.0 copy-done
  9.0 1.8 fusion.38
  10.8 0.0 copy-start.1
  10.8 0.0 copy-start.2
  10.8 0.0 all-gather.3.cloned.1.call-update
  10.8 0.0 reduce-scatter.2.cloned.1.call-start
  10.9 1.1 fusion.31
  12.0 29.5 %all-gather.3.cloned.1.call-done = bf16[64,128,128]{2,1,0:T(8,128)(2,1)} async-done(((bf16[8,128,128]{2,1,0:T(8,128)(2,1)}), bf16[64,128,128]{2,1,0:T(8,128)(2,1)}) %all-gather.3.cloned.1.call-update) | async-done | bytes 2097168 | tf_op jit(solution)/shard_map/all_gather | solution.py:30
  41.5 2.1 %fusion.2 = f32[8,128,128]{2,1,0:T(8,128)S(1)} fusion(bf16[8,8,128,128]{3,2,1,0:T(8,128)(2,1)} %bitcast.47, f32[8]{0:T(128)S(1)} %compare_convert_fusion), kind=kLoop, calls=%fused_computation.5 | loop fusion | flops 3014656 | bytes 2621472 | tf_op jit(solution)/shard_map/reduce_sum | solution.py:35
  43.6 0.0 copy-done.1
  43.6 0.0 copy-done.2
  43.6 2.2 %fusion.24 = f32[8,128,512]{2,1,0:T(8,128)} fusion(f32[8,128,128]{2,1,0:T(8,128)S(1)} %fusion.2, f32[8,128,128]{2,1,0:T(8,128)S(1)} %copy-done.2, bf16[512,1024]{1,0:T(8,128)(2,1)S(1)} %copy-done.1), kind=kOutput, calls=%fused_computation.33 | convolution fusion | flops 137756672 | bytes 4194304 | tf_op jit(solution)/shard_map/nthd,nhde->nthe/dot_general | solution.py:43
  45.8 5.3 %fusion.18 = (f32[512]{0:T(512)S(1)}, f32[8,128,512]{2,1,0:T(8,128)S(1)}) fusion(f32[8,128,512]{2,1,0:T(8,128)} %fusion.24, f32[512,512]{1,0:T(8,128)} %fusion.31, bf16[512,8,128]{0,2,1:T(8,128)(2,1)S(1)} %bitcast.50, bf16[512,1024]{1,0:T(8,128)(2,1)} %param.7, bf16[512,1024]{1,0:T(8,128)(2,1)} %param.5), kind=kOutput, calls=%fused_computation.27 | convolution fusion | flops 1085799936 | bytes 8390656 | tf_op jit(solution)/shard_map/nhts,nshd->nthd/dot_general | solution.py:40
  51.1 11.7 %psum.7 = f32[512]{0:T(512)S(1)} all-reduce(f32[512]{0:T(512)S(1)} %get-tuple-element.7), channel_id=1, replica_groups=mesh['seq'=8,'head'=4] {'head'}, use_global_device_ids=true, to_apply=%region_2.3 | all-reduce | flops 512 | bytes 4096 | tf_op jit(solution)/shard_map/psum | solution.py:45
  62.8 1.8 copy.17
  64.6 13.1 %fusion = bf16[6144,512]{0,1:T(8,128)(2,1)} fusion(bf16[1024,6144]{1,0:T(8,128)(2,1)} %param.9, bf16[512,1024]{1,0:T(8,128)(2,1)} %param.8, f32[512,1024]{1,0:T(8,128)} %copy.17, f32[512]{0:T(512)S(1)} %add_rsqrt_fusion), kind=kOutput, calls=%fused_computation.2 | convolution fusion | flops 6449266688 | bytes 22022144 | tf_op jit(solution)/shard_map/dot_general | solution.py:50
  77.8 0.0 reduce-scatter.2.cloned.1.call-update
  77.8 108.2 %reduce-scatter.2.cloned.1.call-done = bf16[1536,512]{0,1:T(8,128)(2,1)} async-done(((bf16[6144,512]{0,1:T(8,128)(2,1)}), bf16[1536,512]{0,1:T(8,128)(2,1)}) %reduce-scatter.2.cloned.1.call-update) | async-done | bytes 1572880 | tf_op jit(solution)/shard_map/reduce_scatter | solution.py:49
  (2 shorter events, 0.0 us)
Async XLA Ops:
  6.5 2.5 %copy-start = (bf16[512,1024]{1,0:T(8,128)(2,1)S(1)}, bf16[512,1024]{1,0:T(8,128)(2,1)}, u32[]{:S(2)}) copy-start(bf16[512,1024]{1,0:T(8,128)(2,1)} %param.7) | copy-start | bytes 3145732
  6.5 34.9 %all-gather.3.cloned.1.call-start = ((), (), s32[]{:S(2)}) async-start(), calls=%async_computation.2 | async-start | bytes 2359296 | tf_op jit(solution)/shard_map/all_gather | solution.py:30
  10.8 32.8 %copy-start.1 = (bf16[512,1024]{1,0:T(8,128)(2,1)S(1)}, bf16[512,1024]{1,0:T(8,128)(2,1)}, u32[]{:S(2)}) copy-start(bf16[512,1024]{1,0:T(8,128)(2,1)} %param.5) | copy-start | bytes 3145732
  10.8 32.8 %copy-start.2 = (f32[8,128,128]{2,1,0:T(8,128)S(1)}, f32[8,128,128]{2,1,0:T(8,128)}, u32[]{:S(2)}) copy-start(f32[8,128,128]{2,1,0:T(8,128)} %get-tuple-element.6) | copy-start | bytes 1572868
  10.8 175.1 %reduce-scatter.2.cloned.1.call-start = ((), (), s32[]{:S(2)}) async-start(), calls=%async_computation.1 | async-start | bytes 7864320 | tf_op jit(solution)/shard_map/reduce_scatter | solution.py:49
Sparse Core Ops, SparseCore 0:
  10.9 30.4 all-gather.2
  77.9 107.9 reduce-scatter.1
where the time goes:
time: 193 us
  waiting for transfers between devices  138 us (72%)
  matrix products  22.3 us (12%)
  between operations  13.5 us (7%)
  blocking collectives  11.7 us (6%)
  other arithmetic  5.15 us (3%)
  local copies, waits for them, and re-layouts  2.39 us (1%)
    reduce_scatter x1, waiting for transfers between devices, body(): lax.psum_scatter(lax.dot_general(out_weight, normed, (((0,), (1,)), ((),...  108 us
    all_gather x1, waiting for transfers between devices, body(): lax.all_gather(span_total[None].astype(jnp.bfloat16), 'seq', axis=0, tile...  29.5 us
    dot_general x1, matrix products, body(): lax.dot_general(out_weight, normed, (((0,), (1,)), ((), ())), preferred_e...  13.1 us
    psum x1, blocking collectives, body(): square_sums = lax.psum(jnp.sum(attended * attended, axis=-1), 'head')  11.7 us
    dot_general x1, matrix products, body(): jnp.einsum('nhts,nshd->nthd', scores, active_v, preferred_element_type=jn...  5.26 us
  transfers between devices with their start and end apart: 2, of which 2 were waited for; matrix products, arithmetic and copies ran while one was open for 1% of the time, Pallas kernels for 0%

commit v1 on v0

--- a/solution.py
+++ b/solution.py
@@ -5,10 +5,25 @@
 
 HEADS = 32
 HEAD_DIM = 128
+OUT_CHUNKS = 4
 
 
 def activate(raw_input):
     return jax.nn.silu(raw_input.astype(jnp.float32)).astype(jnp.bfloat16)
+
+
+def exclusive_prefix(span_total, axis_name):
+    count = lax.axis_size(axis_name)
+    running = span_total
+    earlier = jnp.zeros_like(span_total)
+    shift = 1
+    while shift < count:
+        pairs = [(i, i + shift) for i in range(count - shift)]
+        arrived = lax.ppermute(running.astype(jnp.bfloat16), axis_name, pairs).astype(jnp.float32)
+        earlier = earlier + arrived
+        running = running + arrived
+        shift *= 2
+    return earlier
 
 
 def body(queries, keys, values, gate_logits, out_weight):
@@ -26,13 +41,7 @@
     )
     span_total = jnp.sum(block_states, axis=0)
     earlier_local = jnp.cumsum(block_states, axis=0) - block_states
-    my_index = lax.axis_index("seq")
-    shards = lax.all_gather(
-        span_total[None].astype(jnp.bfloat16), "seq", axis=0, tiled=True
-    ).astype(jnp.float32)
-    positions = jnp.arange(shards.shape[0], dtype=jnp.int32)
-    weights = (positions < my_index).astype(jnp.float32)
-    prefix = jnp.zeros_like(span_total) + jnp.sum(shards * weights[:, None, None, None], axis=0)
+    prefix = exclusive_prefix(span_total, "seq")
     before = (prefix[None] + earlier_local).astype(jnp.bfloat16)
     causal_mask = jnp.tril(jnp.ones((block_rows, block_rows), jnp.float32))
     scores = jnp.einsum("nthd,nshd->nhts", active_q, active_k, preferred_element_type=jnp.float32)
@@ -42,19 +51,22 @@
     )
     from_state = jnp.einsum("nthd,nhde->nthe", active_q, before, preferred_element_type=jnp.float32)
     attended = (within_block + from_state).reshape(tokens_here, feature_count)
-    square_sums = lax.psum(jnp.sum(attended * attended, axis=-1), "head")
-    scaling = lax.rsqrt(square_sums / (HEADS * HEAD_DIM) + 1e-06)
+    square_sums = jnp.sum(attended * attended, axis=-1)
     gate = jax.nn.sigmoid(gate_logits.astype(jnp.float32))
-    normed = (attended * scaling[:, None] * gate).astype(jnp.bfloat16)
-    reduced = lax.psum_scatter(
-        lax.dot_general(
-            out_weight, normed, (((0,), (1,)), ((), ())), preferred_element_type=jnp.float32
-        ).astype(jnp.bfloat16),
-        "head",
-        scatter_dimension=0,
-        tiled=True,
-    ).astype(jnp.float32)
-    return reduced.T.astype(jnp.bfloat16)
+    gated = (attended * gate).astype(jnp.bfloat16)
+    chunks = OUT_CHUNKS if tokens_here % (OUT_CHUNKS * 8) == 0 else 1
+    chunk_rows = tokens_here // chunks
+    pieces = []
+    for c in range(chunks):
+        part = gated[c * chunk_rows:(c + 1) * chunk_rows]
+        product = lax.dot_general(
+            out_weight, part, (((0,), (1,)), ((), ())), preferred_element_type=jnp.float32
+        ).astype(jnp.bfloat16)
+        pieces.append(lax.psum_scatter(product, "head", scatter_dimension=0, tiled=True))
+    reduced = jnp.concatenate(pieces, axis=1).astype(jnp.float32)
+    total_squares = lax.psum(square_sums, "head")
+    scaling = lax.rsqrt(total_squares / (HEADS * HEAD_DIM) + 1e-06)
+    return (reduced.T * scaling[:, None]).astype(jnp.bfloat16)
 
 
 def solution(mesh):

time: 193 us -> 210 us (1.088)
  waiting for transfers between devices: 138 us -> 115 us
  matrix products: 22.3 us -> 41 us
  starting transfers between devices: 0.04 us -> 17.8 us
    all_gather x1 -> x0, waiting for transfers between devices: 29.5 us -> none  [body(): lax.all_gather(span_total[None].astype(jnp.bfloat16), 'seq', axis=0, tile...]
    ppermute x0 -> x3, starting transfers between devices: none -> 17.5 us  [exclusive_prefix(): lax.ppermute(running.astype(jnp.bfloat16), axis_name, pairs)]
    dot_general x1 -> x4, matrix products: 13.1 us -> 30.3 us  [body(): lax.dot_general(out_weight, part, (((0,), (1,)), ((), ())), preferred_ele...]
    ppermute x0 -> x3, waiting for transfers between devices: none -> 5.83 us  [exclusive_prefix(): lax.ppermute(running.astype(jnp.bfloat16), axis_name, pairs)]
    convert_element_type x1 -> x4, other arithmetic: 0.01 us -> 4.74 us  [the longest x1 2.82 us: body(): return (reduced.T * scaling[:, None]).astype(jnp.bfloat16)]
    reduce_sum x1 -> x0, other arithmetic: 2.13 us -> none  [body(): jnp.sum(shards * weights[:, None, None, None], axis=0)]
    dot_general x1, matrix products: 2.2 us -> 4.32 us  [body(): jnp.einsum('nthd,nhde->nthe', active_q, before, preferred_element_type=jn...]
    reduce_scatter x1 -> x4, waiting for transfers between devices: 108 us -> 110 us  [body(): lax.psum_scatter(product, 'head', scatter_dimension=0, tiled=True)]
  transfers between devices with their start and end apart: 2 -> 7, of which waited for: 2 -> 5; matrix products, arithmetic and copies ran while one was open for 1% -> 14% of each run, Pallas kernels for 0% -> 0%
where the time goes in v1:
time: 210 us; the launch traced here: 209 us
  waiting for transfers between devices  115 us (55%)
  matrix products  41 us (20%)
  starting transfers between devices  17.8 us (8%)
  between operations  13.2 us (6%)
  blocking collectives  12.3 us (6%)
  other arithmetic  6.78 us (3%)
  local copies, waits for them, and re-layouts  2.47 us (1%)
    reduce_scatter x4, waiting for transfers between devices, body(): lax.psum_scatter(product, 'head', scatter_dimension=0, tiled=True)  110 us
    dot_general x4, matrix products, body(): lax.dot_general(out_weight, part, (((0,), (1,)), ((), ())), preferred_ele...  30.3 us
    ppermute x3, starting transfers between devices, exclusive_prefix(): lax.ppermute(running.astype(jnp.bfloat16), axis_name, pairs)  17.5 us
    psum x1, blocking collectives, body(): total_squares = lax.psum(square_sums, 'head')  12.3 us
    ppermute x3, waiting for transfers between devices, exclusive_prefix(): lax.ppermute(running.astype(jnp.bfloat16), axis_name, pairs)  5.83 us
    dot_general x1, matrix products, body(): jnp.einsum('nhts,nshd->nthd', scores, active_v, preferred_element_type=jn...  5.61 us
    dot_general x1, matrix products, body(): jnp.einsum('nthd,nhde->nthe', active_q, before, preferred_element_type=jn...  4.32 us
  transfers between devices with their start and end apart: 7, of which 5 were waited for; matrix products, arithmetic and copies ran while one was open for 14% of the time, Pallas kernels for 0%

profile of v1, /device:TPU:0, one launch (start us, length us, event | category | flops | bytes accessed | tf_op | source)
XLA Modules:
  0.0 209.0 jit_solution(13171815827879283072)
XLA Ops:
  6.5 1.9 fusion.19
  8.5 0.5 copy.13
  9.0 0.8 fusion.46
  9.9 2.4 %collective-permute-start = (bf16[8,128,128]{2,1,0:T(8,128)(2,1)S(1)}, bf16[8,128,128]{2,1,0:T(8,128)(2,1)S(1)}, u32[]{:S(2)}, u32[]{:S(2)}) collective-permute-start(bf16[8,128,128]{2,1,0:T(8,128)(2,1)S(1)} %get-tuple-element.5), channel_id=1, source_target_pairs={{0,4},{4,8},{8,12},{12,16},{16,20},{20,24},{24,28},{1,5},{5,9},{9,... | collective-permute-start | bytes 786440 | tf_op jit(solution)/shard_map/ppermute | solution.py:22
  12.3 1.1 collective-permute-done
  13.4 0.1 fusion.40
  13.5 9.0 %collective-permute-start.1 = (bf16[8,128,128]{2,1,0:T(8,128)(2,1)S(1)}, bf16[8,128,128]{2,1,0:T(8,128)(2,1)S(1)}, u32[]{:S(2)}, u32[]{:S(2)}) collective-permute-start(bf16[8,128,128]{2,1,0:T(8,128)(2,1)S(1)} %fusion.40), channel_id=1, source_target_pairs={{0,8},{4,12},{8,16},{12,20},{16,24},{20,28},{1,9},{5,13},{9,17},{1... | collective-permute-start | bytes 786440 | tf_op jit(solution)/shard_map/ppermute | solution.py:22
  22.5 0.1 fusion.30
  22.6 4.7 %collective-permute-done.1 = bf16[8,128,128]{2,1,0:T(8,128)(2,1)S(1)} collective-permute-done((bf16[8,128,128]{2,1,0:T(8,128)(2,1)S(1)}, bf16[8,128,128]{2,1,0:T(8,128)(2,1)S(1)}, u32[]{:S(2)}, u32[]{:S(2)}) %collective-permute-start.1) | collective-permute-done | bytes 262176 | tf_op jit(solution)/shard_map/ppermute | solution.py:22
  27.3 0.1 fusion.39
  27.4 6.1 %collective-permute-start.2 = (bf16[8,128,128]{2,1,0:T(8,128)(2,1)S(1)}, bf16[8,128,128]{2,1,0:T(8,128)(2,1)}, u32[]{:S(2)}, u32[]{:S(2)}) collective-permute-start(bf16[8,128,128]{2,1,0:T(8,128)(2,1)S(1)} %fusion.39), channel_id=1, source_target_pairs={{0,16},{4,20},{8,24},{12,28},{1,17},{5,21},{9,25},{13,29},{2,18},{... | collective-permute-start | bytes 786440 | tf_op jit(solution)/shard_map/ppermute | solution.py:22
  33.5 5.6 %fusion.4 = f32[8,128,512]{2,1,0:T(8,128)} fusion(f32[512,512]{1,0:T(8,128)S(1)} %fusion.30, bf16[512,8,128]{0,2,1:T(8,128)(2,1)S(1)} %bitcast.55, bf16[512,1024]{1,0:T(8,128)(2,1)} %param.7, bf16[512,1024]{1,0:T(8,128)(2,1)} %param.5), kind=kOutput, calls=%fused_computation.9 | convolution fusion | flops 1084227584 | bytes 6291456 | tf_op jit(solution)/shard_map/nhts,nshd->nthd/dot_general | solution.py:49
  39.1 4.3 %fusion.20 = (f32[512]{0:T(512)S(1)}, f32[8,128,512]{2,1,0:T(8,128)}) fusion(f32[8,128,512]{2,1,0:T(8,128)} %fusion.4, bf16[8,128,128]{2,1,0:T(8,128)(2,1)S(1)} %collective-permute-done.1, bf16[8,128,128]{2,1,0:T(8,128)(2,1)S(1)} %collective-permute-done, f32[8,128,128]{2,1,0:T(8,128)S(1)} %get-tuple-element.6, ...), kind=kOutput, calls=%fused_computation.32 | convolution fusion | flops 139984384 | bytes 6555648 | tf_op jit(solution)/shard_map/nthd,nhde->nthe/dot_general | solution.py:52
  43.4 1.9 copy.11
  45.4 1.8 multiply_convert_fusion.3
  47.2 7.5 %fusion.3 = bf16[6144,128]{0,1:T(8,128)(2,1)} fusion(bf16[1024,6144]{1,0:T(8,128)(2,1)} %param.9, bf16[512,1024]{1,0:T(8,128)(2,1)S(1)} %multiply_convert_fusion.3), kind=kOutput, calls=%fused_computation.8 | convolution fusion | flops 1611399168 | bytes 14417920 | tf_op jit(solution)/shard_map/dot_general | solution.py:62
  54.7 0.0 reduce-scatter.11.cloned.1.call-update
  54.7 0.0 reduce-scatter.9.cloned.1.call-start
  54.8 7.5 %fusion.2 = bf16[6144,128]{0,1:T(8,128)(2,1)} fusion(bf16[1024,6144]{1,0:T(8,128)(2,1)} %param.9, bf16[512,1024]{1,0:T(8,128)(2,1)S(1)} %multiply_convert_fusion.3), kind=kOutput, calls=%fused_computation.7 | convolution fusion | flops 1611399168 | bytes 14417920 | tf_op jit(solution)/shard_map/dot_general | solution.py:62
  62.3 0.0 reduce-scatter.9.cloned.1.call-update
  62.3 0.2 reduce-scatter.7.cloned.1.call-start
  62.6 7.6 %fusion.1 = bf16[6144,128]{0,1:T(8,128)(2,1)} fusion(bf16[1024,6144]{1,0:T(8,128)(2,1)} %param.9, bf16[512,1024]{1,0:T(8,128)(2,1)S(1)} %multiply_convert_fusion.3), kind=kOutput, calls=%fused_computation.6 | convolution fusion | flops 1611399168 | bytes 14417920 | tf_op jit(solution)/shard_map/dot_general | solution.py:62
  70.1 0.0 reduce-scatter.7.cloned.1.call-update
  70.1 0.0 reduce-scatter.5.cloned.1.call-start
  70.2 7.6 %fusion = bf16[6144,128]{0,1:T(8,128)(2,1)} fusion(bf16[1024,6144]{1,0:T(8,128)(2,1)} %param.9, bf16[512,1024]{1,0:T(8,128)(2,1)S(1)} %multiply_convert_fusion.3), kind=kOutput, calls=%fused_computation.5 | convolution fusion | flops 1611399168 | bytes 14417920 | tf_op jit(solution)/shard_map/dot_general | solution.py:62
  77.8 0.0 reduce-scatter.5.cloned.1.call-update
  77.8 12.3 %psum.7 = f32[512]{0:T(512)S(1)} all-reduce(f32[512]{0:T(512)S(1)} %get-tuple-element.7), channel_id=1, replica_groups=mesh['seq'=8,'head'=4] {'head'}, use_global_device_ids=true, to_apply=%region_5.6 | all-reduce | flops 512 | bytes 4096 | tf_op jit(solution)/shard_map/psum | solution.py:67
  90.2 0.0 reduce-scatter.11.cloned.1.call-done
  90.2 36.4 %reduce-scatter.9.cloned.1.call-done = bf16[1536,128]{0,1:T(8,128)(2,1)} async-done(((bf16[6144,128]{0,1:T(8,128)(2,1)}), bf16[1536,128]{0,1:T(8,128)(2,1)}) %reduce-scatter.9.cloned.1.call-update) | async-done | bytes 393232 | tf_op jit(solution)/shard_map/reduce_scatter | solution.py:65
  126.6 36.6 %reduce-scatter.7.cloned.1.call-done = bf16[1536,128]{0,1:T(8,128)(2,1)} async-done(((bf16[6144,128]{0,1:T(8,128)(2,1)}), bf16[1536,128]{0,1:T(8,128)(2,1)}) %reduce-scatter.7.cloned.1.call-update) | async-done | bytes 393232 | tf_op jit(solution)/shard_map/reduce_scatter | solution.py:65
  163.2 36.5 %reduce-scatter.5.cloned.1.call-done = bf16[1536,128]{0,1:T(8,128)(2,1)} async-done(((bf16[6144,128]{0,1:T(8,128)(2,1)}), bf16[1536,128]{0,1:T(8,128)(2,1)}) %reduce-scatter.5.cloned.1.call-update) | async-done | bytes 393232 | tf_op jit(solution)/shard_map/reduce_scatter | solution.py:65
  199.7 2.8 %fusion.21 = bf16[512,1536]{1,0:T(8,128)(2,1)} fusion(bf16[1536,128]{0,1:T(8,128)(2,1)} %reduce-scatter.11.cloned.1.call-done, bf16[1536,128]{0,1:T(8,128)(2,1)} %reduce-scatter.9.cloned.1.call-done, bf16[1536,128]{0,1:T(8,128)(2,1)} %reduce-scatter.7.cloned.1.call-done, bf16[1536,128]{0,1:T(8,128)(2,1)} %reduce-scatter.5.cloned.1.call-done, ...), kind=kLoop, calls=%fused_computation.35 | loop fusion | flops 7864320 | bytes 3147776 | tf_op jit(solution)/shard_map/convert_element_type | solution.py:69
  (5 shorter events, 0.0 us)
Async XLA Ops:
  6.5 2.5 %copy-start = (bf16[512,1024]{1,0:T(8,128)(2,1)S(1)}, bf16[512,1024]{1,0:T(8,128)(2,1)}, u32[]{:S(2)}) copy-start(bf16[512,1024]{1,0:T(8,128)(2,1)} %param.7) | copy-start | bytes 3145732
  6.5 83.6 %reduce-scatter.11.cloned.1.call-start = ((), (), s32[]{:S(2)}) async-start(), calls=%async_computation.7 | async-start | bytes 1966080 | tf_op jit(solution)/shard_map/reduce_scatter | solution.py:65
  9.9 3.5 %collective-permute-start = (bf16[8,128,128]{2,1,0:T(8,128)(2,1)S(1)}, bf16[8,128,128]{2,1,0:T(8,128)(2,1)S(1)}, u32[]{:S(2)}, u32[]{:S(2)}) collective-permute-start(bf16[8,128,128]{2,1,0:T(8,128)(2,1)S(1)} %get-tuple-element.5), channel_id=1, source_target_pairs={{0,4},{4,8},{8,12},{12,16},{16,20},{20,24},{24,28},{1,5},{5,9},{9,... | collective-permute-start | bytes 786440 | tf_op jit(solution)/shard_map/ppermute | solution.py:22
  13.5 13.9 %collective-permute-start.1 = (bf16[8,128,128]{2,1,0:T(8,128)(2,1)S(1)}, bf16[8,128,128]{2,1,0:T(8,128)(2,1)S(1)}, u32[]{:S(2)}, u32[]{:S(2)}) collective-permute-start(bf16[8,128,128]{2,1,0:T(8,128)(2,1)S(1)} %fusion.40), channel_id=1, source_target_pairs={{0,8},{4,12},{8,16},{12,20},{16,24},{20,28},{1,9},{5,13},{9,17},{1... | collective-permute-start | bytes 786440 | tf_op jit(solution)/shard_map/ppermute | solution.py:22
  27.4 11.7 %collective-permute-start.2 = (bf16[8,128,128]{2,1,0:T(8,128)(2,1)S(1)}, bf16[8,128,128]{2,1,0:T(8,128)(2,1)}, u32[]{:S(2)}, u32[]{:S(2)}) collective-permute-start(bf16[8,128,128]{2,1,0:T(8,128)(2,1)S(1)} %fusion.39), channel_id=1, source_target_pairs={{0,16},{4,20},{8,24},{12,28},{1,17},{5,21},{9,25},{13,29},{2,18},{... | collective-permute-start | bytes 786440 | tf_op jit(solution)/shard_map/ppermute | solution.py:22
  54.7 71.9 %reduce-scatter.9.cloned.1.call-start = ((), (), s32[]{:S(2)}) async-start(), calls=%async_computation.6 | async-start | bytes 1966080 | tf_op jit(solution)/shard_map/reduce_scatter | solution.py:65
  62.3 100.9 %reduce-scatter.7.cloned.1.call-start = ((), (), s32[]{:S(2)}) async-start(), calls=%async_computation.5 | async-start | bytes 1966080 | tf_op jit(solution)/shard_map/reduce_scatter | solution.py:65
  70.1 129.5 %reduce-scatter.5.cloned.1.call-start = ((), (), s32[]{:S(2)}) async-start(), calls=%async_computation.4 | async-start | bytes 1966080 | tf_op jit(solution)/shard_map/reduce_scatter | solution.py:65
Sparse Core Ops, SparseCore 0:
  54.8 34.9 reduce-scatter.10
  92.2 34.3 reduce-scatter.8
  128.9 34.2 reduce-scatter.6
  165.4 34.2 reduce-scatter.4

commit v2 on v1

--- a/solution.py
+++ b/solution.py
@@ -5,25 +5,11 @@
 
 HEADS = 32
 HEAD_DIM = 128
-OUT_CHUNKS = 4
+OUT_CHUNKS = 1
 
 
 def activate(raw_input):
     return jax.nn.silu(raw_input.astype(jnp.float32)).astype(jnp.bfloat16)
-
-
-def exclusive_prefix(span_total, axis_name):
-    count = lax.axis_size(axis_name)
-    running = span_total
-    earlier = jnp.zeros_like(span_total)
-    shift = 1
-    while shift < count:
-        pairs = [(i, i + shift) for i in range(count - shift)]
-        arrived = lax.ppermute(running.astype(jnp.bfloat16), axis_name, pairs).astype(jnp.float32)
-        earlier = earlier + arrived
-        running = running + arrived
-        shift *= 2
-    return earlier
 
 
 def body(queries, keys, values, gate_logits, out_weight):
@@ -41,14 +27,21 @@
     )
     span_total = jnp.sum(block_states, axis=0)
     earlier_local = jnp.cumsum(block_states, axis=0) - block_states
-    prefix = exclusive_prefix(span_total, "seq")
-    before = (prefix[None] + earlier_local).astype(jnp.bfloat16)
+    my_index = lax.axis_index("seq")
+    shards = lax.all_gather(
+        span_total[None].astype(jnp.bfloat16), "seq", axis=0, tiled=True
+    ).astype(jnp.float32)
+    positions = jnp.arange(shards.shape[0], dtype=jnp.int32)
+    weights = (positions < my_index).astype(jnp.float32)
+    prefix = jnp.sum(shards * weights[:, None, None, None], axis=0)
     causal_mask = jnp.tril(jnp.ones((block_rows, block_rows), jnp.float32))
     scores = jnp.einsum("nthd,nshd->nhts", active_q, active_k, preferred_element_type=jnp.float32)
     scores = (scores * causal_mask).astype(jnp.bfloat16)
     within_block = jnp.einsum(
         "nhts,nshd->nthd", scores, active_v, preferred_element_type=jnp.float32
     )
+    within_block, prefix = lax.optimization_barrier((within_block, prefix))
+    before = (prefix[None] + earlier_local).astype(jnp.bfloat16)
     from_state = jnp.einsum("nthd,nhde->nthe", active_q, before, preferred_element_type=jnp.float32)
     attended = (within_block + from_state).reshape(tokens_here, feature_count)
     square_sums = jnp.sum(attended * attended, axis=-1)

time: 210 us -> 181 us (0.86)
  matrix products: 41 us -> 21.7 us
  starting transfers between devices: 17.8 us -> 0.04 us
  waiting for transfers between devices: 115 us -> 124 us
    all_gather x0 -> x1, waiting for transfers between devices: none -> 25.1 us  [body(): lax.all_gather(span_total[None].astype(jnp.bfloat16), 'seq', axis=0, tile...]
    dot_general x4 -> x1, matrix products: 30.3 us -> 12.1 us  [body(): lax.dot_general(out_weight, part, (((0,), (1,)), ((), ())), preferred_ele...]
    ppermute x3 -> x0, starting transfers between devices: 17.5 us -> none  [exclusive_prefix(): lax.ppermute(running.astype(jnp.bfloat16), axis_name, pairs)]
    reduce_scatter x4 -> x1, waiting for transfers between devices: 110 us -> 99.1 us  [body(): lax.psum_scatter(product, 'head', scatter_dimension=0, tiled=True)]
    ppermute x3 -> x0, waiting for transfers between devices: 5.83 us -> none  [exclusive_prefix(): lax.ppermute(running.astype(jnp.bfloat16), axis_name, pairs)]
    reduce_sum x0 -> x1, other arithmetic: none -> 2.18 us  [body(): prefix = jnp.sum(shards * weights[:, None, None, None], axis=0)]
  transfers between devices with their start and end apart: 7 -> 2, of which waited for: 5 -> 2; matrix products, arithmetic and copies ran while one was open for 14% -> 3% of each run, Pallas kernels for 0% -> 0%
where the time goes in v2:
time: 181 us
  waiting for transfers between devices  124 us (69%)
  matrix products  21.7 us (12%)
  between operations  13.5 us (7%)
  blocking collectives  11.9 us (7%)
  other arithmetic  7.1 us (4%)
  local copies, waits for them, and re-layouts  2.4 us (1%)
    reduce_scatter x1, waiting for transfers between devices, body(): lax.psum_scatter(product, 'head', scatter_dimension=0, tiled=True)  99.1 us
    all_gather x1, waiting for transfers between devices, body(): lax.all_gather(span_total[None].astype(jnp.bfloat16), 'seq', axis=0, tile...  25.1 us
    dot_general x1, matrix products, body(): lax.dot_general(out_weight, part, (((0,), (1,)), ((), ())), preferred_ele...  12.1 us
    psum x1, blocking collectives, body(): total_squares = lax.psum(square_sums, 'head')  11.9 us
    dot_general x1, matrix products, body(): jnp.einsum('nhts,nshd->nthd', scores, active_v, preferred_element_type=jn...  5.4 us
  transfers between devices with their start and end apart: 2, of which 2 were waited for; matrix products, arithmetic and copies ran while one was open for 3% of the time, Pallas kernels for 0%

profile of v2, /device:TPU:0, one launch (start us, length us, event | category | flops | bytes accessed | tf_op | source)
XLA Modules:
  0.0 180.9 jit_solution(12256609530185934179)
XLA Ops:
  6.5 0.0 copy-start
  6.5 0.0 all-gather.3.cloned.1.call-start
  6.5 1.9 %fusion.17 = bf16[512,1024]{1,0:T(8,128)(2,1)S(1)} fusion(bf16[512,1024]{1,0:T(8,128)(2,1)} %param.6), kind=kLoop, calls=%fused_computation.26 | loop fusion | flops 3145728 | bytes 2097152 | tf_op jit(solution)/shard_map/convert_element_type | solution.py:12
  8.5 0.5 copy.19
  9.0 0.0 copy-done
  9.0 1.7 fusion.36
  10.7 0.0 all-gather.3.cloned.1.call-update
  10.8 0.0 reduce-scatter.2.cloned.1.call-start
  10.8 0.1 fusion.29
  10.9 5.4 %fusion.18 = f32[1,512,8,128]{1,3,2,0:T(8,128)} fusion(f32[512,512]{1,0:T(8,128)S(1)} %fusion.29, bf16[512,8,128]{0,2,1:T(8,128)(2,1)S(1)} %bitcast.50, bf16[512,1024]{1,0:T(8,128)(2,1)S(1)} %copy-done, bf16[512,1024]{1,0:T(8,128)(2,1)} %param.5), kind=kOutput, calls=%fused_computation.30 | convolution fusion | flops 1084227584 | bytes 6291456 | tf_op jit(solution)/shard_map/nhts,nshd->nthd/dot_general | solution.py:40
  16.3 0.0 copy-start.1
  16.3 25.1 %all-gather.3.cloned.1.call-done = bf16[64,128,128]{2,1,0:T(8,128)(2,1)} async-done(((bf16[8,128,128]{2,1,0:T(8,128)(2,1)}), bf16[64,128,128]{2,1,0:T(8,128)(2,1)}) %all-gather.3.cloned.1.call-update) | async-done | bytes 2097168 | tf_op jit(solution)/shard_map/all_gather | solution.py:31
  41.4 0.0 copy-start.3
  41.4 2.2 %fusion.2 = f32[8,128,128]{2,1,0:T(8,128)S(1)} fusion(bf16[8,8,128,128]{3,2,1,0:T(8,128)(2,1)} %bitcast.47, f32[8]{0:T(128)S(1)} %compare_convert_fusion), kind=kLoop, calls=%fused_computation.5 | loop fusion | flops 3014656 | bytes 2621472 | tf_op jit(solution)/shard_map/reduce_sum | solution.py:36
  43.6 0.0 copy-done.1
  43.6 0.0 copy-done.3
  43.6 2.5 %multiply_reduce_fusion = (f32[512]{0:T(512)S(1)}, f32[1,512,8,128]{1,3,2,0:T(8,128)S(1)}) fusion(f32[1,512,8,128]{1,3,2,0:T(8,128)} %fusion.18, f32[8,128,128]{2,1,0:T(8,128)S(1)} %fusion.2, f32[8,128,128]{2,1,0:T(8,128)S(1)} %copy-done.3, bf16[512,1024]{1,0:T(8,128)(2,1)S(1)} %copy-done.1), kind=kOutput, calls=%fused_computation.28 | convolution fusion | flops 139329024 | bytes 6293504 | tf_op jit(solution)/shard_map/nthd,nhde->nthe/dot_general | solution.py:45
  46.2 0.0 copy-start.2
  46.2 1.8 %copy.17 = f32[512,1024]{1,0:T(8,128)} copy(f32[512,1024]{0,1:T(8,128)S(1)} %bitcast.48) | data formatting | bytes 4194304 | tf_op jit(solution)/shard_map/reshape | solution.py:46
  48.0 0.0 copy-done.2
  48.0 12.1 %fusion = bf16[6144,512]{0,1:T(8,128)(2,1)} fusion(bf16[1024,6144]{1,0:T(8,128)(2,1)} %param.9, f32[512,1024]{1,0:T(8,128)} %copy.17, bf16[512,1024]{1,0:T(8,128)(2,1)S(1)} %copy-done.2), kind=kOutput, calls=%fused_computation.2 | convolution fusion | flops 6448742400 | bytes 22020096 | tf_op jit(solution)/shard_map/dot_general | solution.py:55
  60.1 0.0 reduce-scatter.2.cloned.1.call-update
  60.1 11.9 %psum.7 = f32[512]{0:T(512)S(1)} all-reduce(f32[512]{0:T(512)S(1)} %get-tuple-element.11), channel_id=1, replica_groups=mesh['seq'=8,'head'=4] {'head'}, use_global_device_ids=true, to_apply=%region_3.4 | all-reduce | flops 512 | bytes 4096 | tf_op jit(solution)/shard_map/psum | solution.py:60
  72.0 99.1 %reduce-scatter.2.cloned.1.call-done = bf16[1536,512]{0,1:T(8,128)(2,1)} async-done(((bf16[6144,512]{0,1:T(8,128)(2,1)}), bf16[1536,512]{0,1:T(8,128)(2,1)}) %reduce-scatter.2.cloned.1.call-update) | async-done | bytes 1572880 | tf_op jit(solution)/shard_map/reduce_scatter | solution.py:58
  171.1 2.9 %fusion.19 = bf16[512,1536]{1,0:T(8,128)(2,1)} fusion(bf16[1536,512]{0,1:T(8,128)(2,1)} %reduce-scatter.2.cloned.1.call-done, f32[512]{0:T(512)S(1)} %add_rsqrt_fusion), kind=kLoop, calls=%fused_computation.31 | loop fusion | flops 2359296 | bytes 3147776 | tf_op jit(solution)/shard_map/convert_element_type | solution.py:62
  (2 shorter events, 0.0 us)
Async XLA Ops:
  6.5 2.5 %copy-start = (bf16[512,1024]{1,0:T(8,128)(2,1)S(1)}, bf16[512,1024]{1,0:T(8,128)(2,1)}, u32[]{:S(2)}) copy-start(bf16[512,1024]{1,0:T(8,128)(2,1)} %param.7) | copy-start | bytes 3145732
  6.5 34.9 %all-gather.3.cloned.1.call-start = ((), (), s32[]{:S(2)}) async-start(), calls=%async_computation.2 | async-start | bytes 2359296 | tf_op jit(solution)/shard_map/all_gather | solution.py:31
  10.8 160.4 %reduce-scatter.2.cloned.1.call-start = ((), (), s32[]{:S(2)}) async-start(), calls=%async_computation.1 | async-start | bytes 7864320 | tf_op jit(solution)/shard_map/reduce_scatter | solution.py:58
  16.3 27.3 %copy-start.1 = (bf16[512,1024]{1,0:T(8,128)(2,1)S(1)}, bf16[512,1024]{1,0:T(8,128)(2,1)}, u32[]{:S(2)}) copy-start(bf16[512,1024]{1,0:T(8,128)(2,1)} %param.5) | copy-start | bytes 3145732
  41.4 2.2 %copy-start.3 = (f32[8,128,128]{2,1,0:T(8,128)S(1)}, f32[8,128,128]{2,1,0:T(8,128)}, u32[]{:S(2)}) copy-start(f32[8,128,128]{2,1,0:T(8,128)} %get-tuple-element.10) | copy-start | bytes 1572868
  46.2 1.9 %copy-start.2 = (bf16[512,1024]{1,0:T(8,128)(2,1)S(1)}, bf16[512,1024]{1,0:T(8,128)(2,1)}, u32[]{:S(2)}) copy-start(bf16[512,1024]{1,0:T(8,128)(2,1)} %param.8) | copy-start | bytes 3145732
Sparse Core Ops, SparseCore 0:
  10.9 30.4 all-gather.2
  60.3 110.8 reduce-scatter.1

commit v3 on v2

--- a/solution.py
+++ b/solution.py
@@ -27,13 +27,18 @@
     )
     span_total = jnp.sum(block_states, axis=0)
     earlier_local = jnp.cumsum(block_states, axis=0) - block_states
-    my_index = lax.axis_index("seq")
+    partner = lax.ppermute(span_total.astype(jnp.bfloat16), "core", [(0, 1), (1, 0)])
+    partner = partner.astype(jnp.float32)
+    chip_total = span_total + partner
+    chip_index = lax.axis_index("chip")
+    core_index = lax.axis_index("core")
     shards = lax.all_gather(
-        span_total[None].astype(jnp.bfloat16), "seq", axis=0, tiled=True
+        chip_total[None].astype(jnp.bfloat16), "chip", axis=0, tiled=True
     ).astype(jnp.float32)
     positions = jnp.arange(shards.shape[0], dtype=jnp.int32)
-    weights = (positions < my_index).astype(jnp.float32)
+    weights = (positions < chip_index).astype(jnp.float32)
     prefix = jnp.sum(shards * weights[:, None, None, None], axis=0)
+    prefix = prefix + partner * (core_index == 1).astype(jnp.float32)
     causal_mask = jnp.tril(jnp.ones((block_rows, block_rows), jnp.float32))
     scores = jnp.einsum("nthd,nshd->nhts", active_q, active_k, preferred_element_type=jnp.float32)
     scores = (scores * causal_mask).astype(jnp.bfloat16)
@@ -63,16 +68,22 @@
 
 
 def solution(mesh):
+    seq_size = mesh.shape["seq"]
+    head_size = mesh.shape["head"]
+    split = jax.sharding.Mesh(
+        mesh.devices.reshape(seq_size // 2, 2, head_size), ("chip", "core", "head")
+    )
+    rows = ("chip", "core")
     return jax.shard_map(
         body,
-        mesh=mesh,
+        mesh=split,
         in_specs=(
-            P("seq", "head"),
-            P("seq", "head"),
-            P("seq", "head"),
-            P("seq", "head"),
+            P(rows, "head"),
+            P(rows, "head"),
+            P(rows, "head"),
+            P(rows, "head"),
             P("head", None),
         ),
-        out_specs=P("seq", "head"),
+        out_specs=P(rows, "head"),
         check_vma=False,
     )

time: 181 us -> 184 us (1.017)
  matrix products: 21.7 us -> 24 us
  transfers between devices with their start and end apart: 2 -> 3, of which waited for: 2 -> 3; matrix products, arithmetic and copies ran while one was open for 3% -> 3% of each run, Pallas kernels for 0% -> 0%
where the time goes in v3:
time: 184 us; the launch traced here: 183 us
  waiting for transfers between devices  124 us (67%)
  matrix products  24 us (13%)
  between operations  13.5 us (7%)
  blocking collectives  11.8 us (6%)
  other arithmetic  7.27 us (4%)
  local copies, waits for them, and re-layouts  2.39 us (1%)
    reduce_scatter x1, waiting for transfers between devices, body(): lax.psum_scatter(product, 'head', scatter_dimension=0, tiled=True)  99.2 us
    all_gather x1, waiting for transfers between devices, body(): lax.all_gather(chip_total[None].astype(jnp.bfloat16), 'chip', axis=0, til...  23.3 us
    dot_general x1, matrix products, body(): lax.dot_general(out_weight, part, (((0,), (1,)), ((), ())), preferred_ele...  13.7 us
    psum x1, blocking collectives, body(): total_squares = lax.psum(square_sums, 'head')  11.8 us
    dot_general x1, matrix products, body(): jnp.einsum('nhts,nshd->nthd', scores, active_v, preferred_element_type=jn...  5.75 us
  transfers between devices with their start and end apart: 3, of which 3 were waited for; matrix products, arithmetic and copies ran while one was open for 3% of the time, Pallas kernels for 0%

profile of v3, /device:TPU:0, one launch (start us, length us, event | category | flops | bytes accessed | tf_op | source)
XLA Modules:
  0.0 183.3 jit_solution(2613811406257446908)
XLA Ops:
  6.5 0.0 all-gather.3.cloned.1.call-start
  6.5 1.8 %fusion.16 = bf16[512,1024]{1,0:T(8,128)(2,1)S(1)} fusion(bf16[512,1024]{1,0:T(8,128)(2,1)} %param.6), kind=kLoop, calls=%fused_computation.24 | loop fusion | flops 3145728 | bytes 2097152 | tf_op jit(solution)/shard_map/convert_element_type | solution.py:12
  8.4 0.5 copy.19
  8.9 2.1 %fusion.38 = (bf16[8,128,128]{2,1,0:T(8,128)(2,1)S(1)}, f32[8,128,128]{2,1,0:T(8,128)S(1)}) fusion(bf16[512,8,128]{0,2,1:T(8,128)(2,1)S(1)} %bitcast.48, bf16[512,1024]{1,0:T(8,128)(2,1)} %param.7), kind=kOutput, calls=%fused_computation.54 | convolution fusion | flops 137494528 | bytes 2883584 | tf_op jit(solution)/shard_map/nshd,nshe->nhde/dot_general | solution.py:25
  11.0 0.6 collective-permute-start
  11.6 1.2 collective-permute-done
  12.7 0.8 fusion.35
  13.5 0.0 all-gather.3.cloned.1.call-update
  13.5 0.0 reduce-scatter.2.cloned.1.call-start
  13.6 0.1 fusion.29
  13.7 5.7 %fusion.18 = f32[1,512,8,128]{1,3,2,0:T(8,128)} fusion(f32[512,512]{1,0:T(8,128)S(1)} %fusion.29, bf16[512,8,128]{0,2,1:T(8,128)(2,1)S(1)} %bitcast.49, bf16[512,1024]{1,0:T(8,128)(2,1)} %param.7, bf16[512,1024]{1,0:T(8,128)(2,1)} %param.5), kind=kOutput, calls=%fused_computation.30 | convolution fusion | flops 1084227584 | bytes 6291456 | tf_op jit(solution)/shard_map/nhts,nshd->nthd/dot_general | solution.py:45
  19.4 23.3 %all-gather.3.cloned.1.call-done = bf16[32,128,128]{2,1,0:T(8,128)(2,1)} async-done(((bf16[8,128,128]{2,1,0:T(8,128)(2,1)}), bf16[32,128,128]{2,1,0:T(8,128)(2,1)}) %all-gather.3.cloned.1.call-update) | async-done | bytes 1048592 | tf_op jit(solution)/shard_map/all_gather | solution.py:35
  42.8 0.0 copy-start
  42.8 1.6 fusion.17
  44.4 0.1 fusion.36
  44.5 0.0 copy-done
  44.5 2.5 %multiply_reduce_fusion = (f32[512]{0:T(512)S(1)}, f32[1,512,8,128]{1,3,2,0:T(8,128)S(1)}) fusion(f32[1,512,8,128]{1,3,2,0:T(8,128)} %fusion.18, f32[8,128,128]{2,1,0:T(8,128)S(1)} %fusion.36, f32[8,128,128]{2,1,0:T(8,128)S(1)} %get-tuple-element.10, bf16[512,1024]{1,0:T(8,128)(2,1)S(1)} %copy-done), kind=kOutput, calls=%fused_computation.28 | convolution fusion | flops 139329024 | bytes 6293504 | tf_op jit(solution)/shard_map/nthd,nhde->nthe/dot_general | solution.py:50
  47.0 1.8 %copy.17 = f32[512,1024]{1,0:T(8,128)} copy(f32[512,1024]{0,1:T(8,128)S(1)} %bitcast.47) | data formatting | bytes 4194304 | tf_op jit(solution)/shard_map/reshape | solution.py:51
  48.9 13.7 %fusion = bf16[6144,512]{0,1:T(8,128)(2,1)} fusion(bf16[1024,6144]{1,0:T(8,128)(2,1)} %param.9, f32[512,1024]{1,0:T(8,128)} %copy.17, bf16[512,1024]{1,0:T(8,128)(2,1)} %param.8), kind=kOutput, calls=%fused_computation.2 | convolution fusion | flops 6448742400 | bytes 22020096 | tf_op jit(solution)/shard_map/dot_general | solution.py:60
  62.5 0.0 reduce-scatter.2.cloned.1.call-update
  62.6 11.8 %psum.7 = f32[512]{0:T(512)S(1)} all-reduce(f32[512]{0:T(512)S(1)} %get-tuple-element.11), channel_id=1, replica_groups=mesh['chip'=4,'core'=2,'head'=4] {'head'}, use_global_device_ids=true, to_apply=%region_3.4 | all-reduce | flops 512 | bytes 4096 | tf_op jit(solution)/shard_map/psum | solution.py:65
  74.4 99.2 %reduce-scatter.2.cloned.1.call-done = bf16[1536,512]{0,1:T(8,128)(2,1)} async-done(((bf16[6144,512]{0,1:T(8,128)(2,1)}), bf16[1536,512]{0,1:T(8,128)(2,1)}) %reduce-scatter.2.cloned.1.call-update) | async-done | bytes 1572880 | tf_op jit(solution)/shard_map/reduce_scatter | solution.py:63
  173.6 2.9 %fusion.19 = bf16[512,1536]{1,0:T(8,128)(2,1)} fusion(bf16[1536,512]{0,1:T(8,128)(2,1)} %reduce-scatter.2.cloned.1.call-done, f32[512]{0:T(512)S(1)} %add_rsqrt_fusion), kind=kLoop, calls=%fused_computation.31 | loop fusion | flops 2359296 | bytes 3147776 | tf_op jit(solution)/shard_map/convert_element_type | solution.py:67
  (2 shorter events, 0.0 us)
Async XLA Ops:
  6.5 36.2 %all-gather.3.cloned.1.call-start = ((), (), s32[]{:S(2)}) async-start(), calls=%async_computation.2 | async-start | bytes 1310720 | tf_op jit(solution)/shard_map/all_gather | solution.py:35
  11.0 1.7 collective-permute-start
  13.5 160.1 %reduce-scatter.2.cloned.1.call-start = ((), (), s32[]{:S(2)}) async-start(), calls=%async_computation.1 | async-start | bytes 7864320 | tf_op jit(solution)/shard_map/reduce_scatter | solution.py:63
  42.8 1.7 copy-start
Sparse Core Ops, SparseCore 0:
  13.6 29.0 all-gather.2
  62.7 110.8 reduce-scatter.1

commit v4 on v2

--- a/solution.py
+++ b/solution.py
@@ -10,6 +10,30 @@
 
 def activate(raw_input):
     return jax.nn.silu(raw_input.astype(jnp.float32)).astype(jnp.bfloat16)
+
+
+def exclusive_prefix(span_total, axis_name):
+    count = lax.axis_size(axis_name)
+    my_index = lax.axis_index(axis_name)
+    if count & (count - 1):
+        shards = lax.all_gather(
+            span_total[None].astype(jnp.bfloat16), axis_name, axis=0, tiled=True
+        ).astype(jnp.float32)
+        positions = jnp.arange(count, dtype=jnp.int32)
+        weights = (positions < my_index).astype(jnp.float32)
+        return jnp.sum(shards * weights[:, None, None, None], axis=0)
+    group_total = span_total
+    prefix = jnp.zeros_like(span_total)
+    bit = 1
+    while bit < count:
+        pairs = [(i, i ^ bit) for i in range(count)]
+        arrived = lax.ppermute(group_total.astype(jnp.bfloat16), axis_name, pairs)
+        arrived = arrived.astype(jnp.float32)
+        upper = ((my_index // bit) % 2).astype(jnp.float32)
+        prefix = prefix + upper * arrived
+        group_total = group_total + arrived
+        bit *= 2
+    return prefix
 
 
 def body(queries, keys, values, gate_logits, out_weight):
@@ -27,13 +51,7 @@
     )
     span_total = jnp.sum(block_states, axis=0)
     earlier_local = jnp.cumsum(block_states, axis=0) - block_states
-    my_index = lax.axis_index("seq")
-    shards = lax.all_gather(
-        span_total[None].astype(jnp.bfloat16), "seq", axis=0, tiled=True
-    ).astype(jnp.float32)
-    positions = jnp.arange(shards.shape[0], dtype=jnp.int32)
-    weights = (positions < my_index).astype(jnp.float32)
-    prefix = jnp.sum(shards * weights[:, None, None, None], axis=0)
+    prefix = exclusive_prefix(span_total, "seq")
     causal_mask = jnp.tril(jnp.ones((block_rows, block_rows), jnp.float32))
     scores = jnp.einsum("nthd,nshd->nhts", active_q, active_k, preferred_element_type=jnp.float32)
     scores = (scores * causal_mask).astype(jnp.bfloat16)

time: 181 us -> 171 us (0.945)
  waiting for transfers between devices: 124 us -> 108 us
  starting transfers between devices: 0.04 us -> 5.31 us
    all_gather x1 -> x0, waiting for transfers between devices: 25.1 us -> none  [body(): lax.all_gather(span_total[None].astype(jnp.bfloat16), 'seq', axis=0, tile...]
    ppermute x0 -> x3, waiting for transfers between devices: none -> 8.15 us  [exclusive_prefix(): arrived = lax.ppermute(group_total.astype(jnp.bfloat16), axis_name, pairs)]
    ppermute x0 -> x3, starting transfers between devices: none -> 5.31 us  [exclusive_prefix(): arrived = lax.ppermute(group_total.astype(jnp.bfloat16), axis_name, pairs)]
    reduce_sum x1 -> x0, other arithmetic: 2.18 us -> none  [body(): prefix = jnp.sum(shards * weights[:, None, None, None], axis=0)]
  transfers between devices with their start and end apart: 2 -> 4, of which waited for: 2 -> 4; matrix products, arithmetic and copies ran while one was open for 3% -> 3% of each run, Pallas kernels for 0% -> 0%
where the time goes in v4:
time: 171 us
  waiting for transfers between devices  108 us (63%)
  matrix products  23 us (13%)
  between operations  13.4 us (8%)
  blocking collectives  12 us (7%)
  other arithmetic  6.15 us (4%)
  starting transfers between devices  5.31 us (3%)
  local copies, waits for them, and re-layouts  2.38 us (1%)
    reduce_scatter x1, waiting for transfers between devices, body(): lax.psum_scatter(product, 'head', scatter_dimension=0, tiled=True)  100 us
    dot_general x1, matrix products, body(): lax.dot_general(out_weight, part, (((0,), (1,)), ((), ())), preferred_ele...  13.7 us
    psum x1, blocking collectives, body(): total_squares = lax.psum(square_sums, 'head')  12 us
    ppermute x3, waiting for transfers between devices, exclusive_prefix(): arrived = lax.ppermute(group_total.astype(jnp.bfloat16), axis_name, pairs)  8.15 us
    dot_general x1, matrix products, body(): jnp.einsum('nhts,nshd->nthd', scores, active_v, preferred_element_type=jn...  5.61 us
    ppermute x3, starting transfers between devices, exclusive_prefix(): arrived = lax.ppermute(group_total.astype(jnp.bfloat16), axis_name, pairs)  5.31 us
  transfers between devices with their start and end apart: 4, of which 4 were waited for; matrix products, arithmetic and copies ran while one was open for 3% of the time, Pallas kernels for 0%

profile of v4, /device:TPU:0, one launch (start us, length us, event | category | flops | bytes accessed | tf_op | source)
XLA Modules:
  0.0 170.6 jit_solution(12037850568352222770)
XLA Ops:
  6.5 0.0 copy-start
  6.5 0.0 reduce-scatter.2.cloned.1.call-start
  6.5 1.9 %fusion.16 = bf16[512,1024]{1,0:T(8,128)(2,1)S(1)} fusion(bf16[512,1024]{1,0:T(8,128)(2,1)} %param.6), kind=kLoop, calls=%fused_computation.24 | loop fusion | flops 3145728 | bytes 2097152 | tf_op jit(solution)/shard_map/convert_element_type | solution.py:12
  8.5 0.5 copy.13
  9.0 0.0 copy-done
  9.0 0.8 fusion.39
  9.9 0.6 collective-permute-start
  10.4 1.2 collective-permute-done
  11.6 0.1 fusion.37
  11.7 2.9 %collective-permute-start.1 = (bf16[8,128,128]{2,1,0:T(8,128)(2,1)S(1)}, bf16[8,128,128]{2,1,0:T(8,128)(2,1)S(1)}, u32[]{:S(2)}, u32[]{:S(2)}) collective-permute-start(bf16[8,128,128]{2,1,0:T(8,128)(2,1)S(1)} %fusion.37), channel_id=1, source_target_pairs={{0,8},{4,12},{8,0},{12,4},{16,24},{20,28},{24,16},{28,20},{1,9},{5... | collective-permute-start | bytes 786440 | tf_op jit(solution)/shard_map/ppermute | solution.py:30
  14.6 0.1 fusion.28
  14.7 6.5 %collective-permute-done.1 = bf16[8,128,128]{2,1,0:T(8,128)(2,1)S(1)} collective-permute-done((bf16[8,128,128]{2,1,0:T(8,128)(2,1)S(1)}, bf16[8,128,128]{2,1,0:T(8,128)(2,1)S(1)}, u32[]{:S(2)}, u32[]{:S(2)}) %collective-permute-start.1) | collective-permute-done | bytes 262176 | tf_op jit(solution)/shard_map/ppermute | solution.py:30
  21.2 0.1 fusion.36
  21.3 1.8 %collective-permute-start.2 = (bf16[8,128,128]{2,1,0:T(8,128)(2,1)S(1)}, bf16[8,128,128]{2,1,0:T(8,128)(2,1)}, u32[]{:S(2)}, u32[]{:S(2)}) collective-permute-start(bf16[8,128,128]{2,1,0:T(8,128)(2,1)S(1)} %fusion.36), channel_id=1, source_target_pairs={{0,16},{4,20},{8,24},{12,28},{16,0},{20,4},{24,8},{28,12},{1,17},{... | collective-permute-start | bytes 786440 | tf_op jit(solution)/shard_map/ppermute | solution.py:30
  23.1 5.6 %fusion.17 = f32[1,512,8,128]{1,3,2,0:T(8,128)} fusion(f32[512,512]{1,0:T(8,128)S(1)} %fusion.28, bf16[512,8,128]{0,2,1:T(8,128)(2,1)S(1)} %bitcast.47, bf16[512,1024]{1,0:T(8,128)(2,1)} %param.7, bf16[512,1024]{1,0:T(8,128)(2,1)} %param.5), kind=kOutput, calls=%fused_computation.28 | convolution fusion | flops 1084227584 | bytes 6291456 | tf_op jit(solution)/shard_map/nhts,nshd->nthd/dot_general | solution.py:58
  28.7 0.5 collective-permute-done.2
  29.2 1.1 fusion.35
  30.3 2.9 %multiply_reduce_fusion = (f32[512]{0:T(512)S(1)}, f32[1,512,8,128]{1,3,2,0:T(8,128)S(1)}) fusion(f32[1,512,8,128]{1,3,2,0:T(8,128)} %fusion.17, f32[8,128,128]{2,1,0:T(8,128)S(1)} %fusion.35, f32[8,128,128]{2,1,0:T(8,128)S(1)} %get-tuple-element.10, bf16[512,1024]{1,0:T(8,128)(2,1)} %param.5), kind=kOutput, calls=%fused_computation.26 | convolution fusion | flops 139329024 | bytes 6293504 | tf_op jit(solution)/shard_map/nthd,nhde->nthe/dot_general | solution.py:63
  33.2 1.8 %copy.11 = f32[512,1024]{1,0:T(8,128)} copy(f32[512,1024]{0,1:T(8,128)S(1)} %bitcast.45) | data formatting | bytes 4194304 | tf_op jit(solution)/shard_map/reshape | solution.py:64
  35.0 13.7 %fusion = bf16[6144,512]{0,1:T(8,128)(2,1)} fusion(bf16[1024,6144]{1,0:T(8,128)(2,1)} %param.9, f32[512,1024]{1,0:T(8,128)} %copy.11, bf16[512,1024]{1,0:T(8,128)(2,1)} %param.8), kind=kOutput, calls=%fused_computation.2 | convolution fusion | flops 6448742400 | bytes 22020096 | tf_op jit(solution)/shard_map/dot_general | solution.py:73
  48.7 0.0 reduce-scatter.2.cloned.1.call-update
  48.7 12.0 %psum.7 = f32[512]{0:T(512)S(1)} all-reduce(f32[512]{0:T(512)S(1)} %get-tuple-element.11), channel_id=1, replica_groups=mesh['seq'=8,'head'=4] {'head'}, use_global_device_ids=true, to_apply=%region_2.3 | all-reduce | flops 512 | bytes 4096 | tf_op jit(solution)/shard_map/psum | solution.py:78
  60.8 100.1 %reduce-scatter.2.cloned.1.call-done = bf16[1536,512]{0,1:T(8,128)(2,1)} async-done(((bf16[6144,512]{0,1:T(8,128)(2,1)}), bf16[1536,512]{0,1:T(8,128)(2,1)}) %reduce-scatter.2.cloned.1.call-update) | async-done | bytes 1572880 | tf_op jit(solution)/shard_map/reduce_scatter | solution.py:76
  160.9 2.9 %fusion.18 = bf16[512,1536]{1,0:T(8,128)(2,1)} fusion(bf16[1536,512]{0,1:T(8,128)(2,1)} %reduce-scatter.2.cloned.1.call-done, f32[512]{0:T(512)S(1)} %add_rsqrt_fusion), kind=kLoop, calls=%fused_computation.29 | loop fusion | flops 2359296 | bytes 3147776 | tf_op jit(solution)/shard_map/convert_element_type | solution.py:80
  (1 shorter events, 0.0 us)
Async XLA Ops:
  6.5 2.5 %copy-start = (bf16[512,1024]{1,0:T(8,128)(2,1)S(1)}, bf16[512,1024]{1,0:T(8,128)(2,1)}, u32[]{:S(2)}) copy-start(bf16[512,1024]{1,0:T(8,128)(2,1)} %param.7) | copy-start | bytes 3145732
  6.5 154.4 %reduce-scatter.2.cloned.1.call-start = ((), (), s32[]{:S(2)}) async-start(), calls=%async_computation.1 | async-start | bytes 7864320 | tf_op jit(solution)/shard_map/reduce_scatter | solution.py:76
  9.9 1.7 %collective-permute-start = (bf16[8,128,128]{2,1,0:T(8,128)(2,1)S(1)}, bf16[8,128,128]{2,1,0:T(8,128)(2,1)S(1)}, u32[]{:S(2)}, u32[]{:S(2)}) collective-permute-start(bf16[8,128,128]{2,1,0:T(8,128)(2,1)S(1)} %get-tuple-element.9), channel_id=1, source_target_pairs={{0,4},{4,0},{8,12},{12,8},{16,20},{20,16},{24,28},{28,24},{1,5},{5... | collective-permute-start | bytes 786440 | tf_op jit(solution)/shard_map/ppermute | solution.py:30
  11.7 9.5 %collective-permute-start.1 = (bf16[8,128,128]{2,1,0:T(8,128)(2,1)S(1)}, bf16[8,128,128]{2,1,0:T(8,128)(2,1)S(1)}, u32[]{:S(2)}, u32[]{:S(2)}) collective-permute-start(bf16[8,128,128]{2,1,0:T(8,128)(2,1)S(1)} %fusion.37), channel_id=1, source_target_pairs={{0,8},{4,12},{8,0},{12,4},{16,24},{20,28},{24,16},{28,20},{1,9},{5... | collective-permute-start | bytes 786440 | tf_op jit(solution)/shard_map/ppermute | solution.py:30
  21.3 7.9 %collective-permute-start.2 = (bf16[8,128,128]{2,1,0:T(8,128)(2,1)S(1)}, bf16[8,128,128]{2,1,0:T(8,128)(2,1)}, u32[]{:S(2)}, u32[]{:S(2)}) collective-permute-start(bf16[8,128,128]{2,1,0:T(8,128)(2,1)S(1)} %fusion.36), channel_id=1, source_target_pairs={{0,16},{4,20},{8,24},{12,28},{16,0},{20,4},{24,8},{28,12},{1,17},{... | collective-permute-start | bytes 786440 | tf_op jit(solution)/shard_map/ppermute | solution.py:30
Sparse Core Ops, SparseCore 0:
  48.8 112.0 reduce-scatter.1

commit v5 on v4

--- a/solution.py
+++ b/solution.py
@@ -5,7 +5,6 @@
 
 HEADS = 32
 HEAD_DIM = 128
-OUT_CHUNKS = 1
 
 
 def activate(raw_input):
@@ -34,6 +33,38 @@
         group_total = group_total + arrived
         bit *= 2
     return prefix
+
+
+def shard_product(gated, out_weight, shard, width):
+    columns = lax.dynamic_slice_in_dim(out_weight, shard * width, width, axis=1)
+    return jnp.dot(gated, columns, preferred_element_type=jnp.float32)
+
+
+def line_reduce_scatter(gated, out_weight, axis_name):
+    count = lax.axis_size(axis_name)
+    here = lax.axis_index(axis_name)
+    width = out_weight.shape[1] // count
+    from_left = None
+    from_right = None
+    for step in range(1, count):
+        right_shard = jnp.clip(here + count - step, 0, count - 1)
+        left_shard = jnp.clip(here - count + step, 0, count - 1)
+        to_right = shard_product(gated, out_weight, right_shard, width)
+        to_left = shard_product(gated, out_weight, left_shard, width)
+        to_right, to_left = lax.optimization_barrier((to_right, to_left))
+        if from_left is not None:
+            to_right = to_right + from_left
+            to_left = to_left + from_right
+        right_pairs = [(i, i + 1) for i in range(step) if i + 1 < count]
+        left_pairs = [(i, i - 1) for i in range(count - step, count) if i >= 1]
+        from_left = lax.ppermute(to_right.astype(jnp.bfloat16), axis_name, right_pairs)
+        from_right = lax.ppermute(to_left.astype(jnp.bfloat16), axis_name, left_pairs)
+        from_left = from_left.astype(jnp.float32)
+        from_right = from_right.astype(jnp.float32)
+    own = shard_product(gated, out_weight, here, width)
+    if from_left is None:
+        return own
+    return own + from_left + from_right
 
 
 def body(queries, keys, values, gate_logits, out_weight):
@@ -65,19 +96,10 @@
     square_sums = jnp.sum(attended * attended, axis=-1)
     gate = jax.nn.sigmoid(gate_logits.astype(jnp.float32))
     gated = (attended * gate).astype(jnp.bfloat16)
-    chunks = OUT_CHUNKS if tokens_here % (OUT_CHUNKS * 8) == 0 else 1
-    chunk_rows = tokens_here // chunks
-    pieces = []
-    for c in range(chunks):
-        part = gated[c * chunk_rows:(c + 1) * chunk_rows]
-        product = lax.dot_general(
-            out_weight, part, (((0,), (1,)), ((), ())), preferred_element_type=jnp.float32
-        ).astype(jnp.bfloat16)
-        pieces.append(lax.psum_scatter(product, "head", scatter_dimension=0, tiled=True))
-    reduced = jnp.concatenate(pieces, axis=1).astype(jnp.float32)
     total_squares = lax.psum(square_sums, "head")
     scaling = lax.rsqrt(total_squares / (HEADS * HEAD_DIM) + 1e-06)
-    return (reduced.T * scaling[:, None]).astype(jnp.bfloat16)
+    reduced = line_reduce_scatter(gated, out_weight, "head")
+    return (reduced * scaling[:, None]).astype(jnp.bfloat16)
 
 
 def solution(mesh):

time: 171 us -> 168 us (0.982)
  waiting for transfers between devices: 108 us -> 47.5 us
  blocking collectives: 12 us -> 36.3 us
  starting transfers between devices: 5.31 us -> 27.4 us
  matrix products: 23 us -> 39.1 us
  between operations: 13.4 us -> 0.19 us
  other arithmetic: 6.15 us -> 14.7 us
    reduce_scatter x1 -> x0, waiting for transfers between devices: 100 us -> none  [body(): lax.psum_scatter(product, 'head', scatter_dimension=0, tiled=True)]
    ppermute x0 -> x6, waiting for transfers between devices: none -> 39.4 us  [the longest x3 39.4 us: line_reduce_scatter(): lax.ppermute(to_right.astype(jnp.bfloat16), axis_name, right_pairs)]
    psum x1, blocking collectives: 12 us -> 36.3 us  [body(): total_squares = lax.psum(square_sums, 'head')]
    ppermute x0 -> x6, starting transfers between devices: none -> 22.1 us  [the longest x3 18.2 us: line_reduce_scatter(): lax.ppermute(to_right.astype(jnp.bfloat16), axis_name, right_pairs)]
    dot_general x1 -> x7, matrix products: 13.7 us -> 28.4 us  [shard_product(): return jnp.dot(gated, columns, preferred_element_type=jnp.float32)]
    convert_element_type x1 -> x6, other arithmetic: 2.87 us -> 11.4 us  [the longest x2 3.97 us: line_reduce_scatter(): to_right.astype(jnp.bfloat16)]
  transfers between devices with their start and end apart: 4 -> 9, of which waited for: 4 -> 5; matrix products, arithmetic and copies ran while one was open for 3% -> 20% of each run, Pallas kernels for 0% -> 0%
where the time goes in v5:
time: 168 us
  waiting for transfers between devices  47.5 us (28%)
  matrix products  39.1 us (23%)
  blocking collectives  36.3 us (22%)
  starting transfers between devices  27.4 us (16%)
  other arithmetic  14.7 us (9%)
  local copies, waits for them, and re-layouts  2.57 us (2%)
    ppermute x3, waiting for transfers between devices, line_reduce_scatter(): lax.ppermute(to_right.astype(jnp.bfloat16), axis_name, right_pairs)  39.4 us
    psum x1, blocking collectives, body(): total_squares = lax.psum(square_sums, 'head')  36.3 us
    dot_general x7, matrix products, shard_product(): return jnp.dot(gated, columns, preferred_element_type=jnp.float32)  28.4 us
    ppermute x3, starting transfers between devices, line_reduce_scatter(): lax.ppermute(to_right.astype(jnp.bfloat16), axis_name, right_pairs)  18.2 us
    ppermute x3, waiting for transfers between devices, exclusive_prefix(): arrived = lax.ppermute(group_total.astype(jnp.bfloat16), axis_name, pairs)  8.16 us
    dot_general x1, matrix products, body(): jnp.einsum('nhts,nshd->nthd', scores, active_v, preferred_element_type=jn...  5.6 us
    ppermute x3, starting transfers between devices, exclusive_prefix(): arrived = lax.ppermute(group_total.astype(jnp.bfloat16), axis_name, pairs)  5.3 us
    dot_general x1, matrix products, body(): jnp.einsum('nthd,nhde->nthe', active_q, before, preferred_element_type=jn...  4.19 us
  transfers between devices with their start and end apart: 9, of which 5 were waited for; matrix products, arithmetic and copies ran while one was open for 20% of the time, Pallas kernels for 0%

profile of v5, /device:TPU:0, one launch (start us, length us, event | category | flops | bytes accessed | tf_op | source)
XLA Modules:
  0.0 167.7 jit_solution(7312044664210870520)
XLA Ops:
  0.0 1.9 %fusion.29 = bf16[512,1024]{1,0:T(8,128)(2,1)S(1)} fusion(bf16[512,1024]{1,0:T(8,128)(2,1)} %param.6), kind=kLoop, calls=%fused_computation.40 | loop fusion | flops 3145728 | bytes 2097152 | tf_op jit(solution)/shard_map/convert_element_type | solution.py:11
  2.5 0.8 fusion.56
  3.9 1.2 collective-permute-done
  5.1 2.9 %collective-permute-start.1 = (bf16[8,128,128]{2,1,0:T(8,128)(2,1)S(1)}, bf16[8,128,128]{2,1,0:T(8,128)(2,1)S(1)}, u32[]{:S(2)}, u32[]{:S(2)}) collective-permute-start(bf16[8,128,128]{2,1,0:T(8,128)(2,1)S(1)} %fusion.48), channel_id=1, source_target_pairs={{0,8},{4,12},{8,0},{12,4},{16,24},{20,28},{24,16},{28,20},{1,9},{5... | collective-permute-start | bytes 786440 | tf_op jit(solution)/shard_map/ppermute | solution.py:29
  8.2 6.5 %collective-permute-done.1 = bf16[8,128,128]{2,1,0:T(8,128)(2,1)S(1)} collective-permute-done((bf16[8,128,128]{2,1,0:T(8,128)(2,1)S(1)}, bf16[8,128,128]{2,1,0:T(8,128)(2,1)S(1)}, u32[]{:S(2)}, u32[]{:S(2)}) %collective-permute-start.1) | collective-permute-done | bytes 262176 | tf_op jit(solution)/shard_map/ppermute | solution.py:29
  14.7 1.8 %collective-permute-start.2 = (bf16[8,128,128]{2,1,0:T(8,128)(2,1)S(1)}, bf16[8,128,128]{2,1,0:T(8,128)(2,1)}, u32[]{:S(2)}, u32[]{:S(2)}) collective-permute-start(bf16[8,128,128]{2,1,0:T(8,128)(2,1)S(1)} %fusion.47), channel_id=1, source_target_pairs={{0,16},{4,20},{8,24},{12,28},{16,0},{20,4},{24,8},{28,12},{1,17},{... | collective-permute-start | bytes 786440 | tf_op jit(solution)/shard_map/ppermute | solution.py:29
  16.6 5.6 %fusion.30 = f32[1,512,8,128]{1,3,2,0:T(8,128)} fusion(f32[512,512]{1,0:T(8,128)S(1)} %fusion.39, bf16[512,8,128]{0,2,1:T(8,128)(2,1)S(1)} %bitcast.49, bf16[512,1024]{1,0:T(8,128)(2,1)} %param.7, bf16[512,1024]{1,0:T(8,128)(2,1)} %param.5), kind=kOutput, calls=%fused_computation.44 | convolution fusion | flops 1084227584 | bytes 6291456 | tf_op jit(solution)/shard_map/nhts,nshd->nthd/dot_general | solution.py:89
  22.7 1.1 fusion.46
  23.8 4.2 %multiply_reduce_fusion = (f32[512]{0:T(512)S(1)}, f32[1,512,8,128]{1,3,2,0:T(8,128)}) fusion(f32[1,512,8,128]{1,3,2,0:T(8,128)} %fusion.30, f32[8,128,128]{2,1,0:T(8,128)S(1)} %fusion.46, f32[8,128,128]{2,1,0:T(8,128)S(1)} %get-tuple-element.22, bf16[512,1024]{1,0:T(8,128)(2,1)} %param.5), kind=kOutput, calls=%fused_computation.42 | convolution fusion | flops 139329024 | bytes 6293504 | tf_op jit(solution)/shard_map/nthd,nhde->nthe/dot_general | solution.py:94
  28.0 2.0 %copy.11 = f32[512,1024]{1,0:T(8,128)S(1)} copy(f32[512,1024]{0,1:T(8,128)} %bitcast.47) | data formatting | bytes 4194304 | tf_op jit(solution)/shard_map/reshape | solution.py:95
  30.0 0.6 multiply_convert_fusion.3
  30.6 4.1 %fusion.4 = bf16[512,1536]{1,0:T(8,128)(2,1)S(1)} fusion(bf16[512,1024]{1,0:T(8,128)(2,1)S(1)} %multiply_convert_fusion.3, bf16[1024,6144]{1,0:T(8,128)(2,1)} %param.9, s32[]{:T(128)S(6)} %select_n.64), kind=kOutput, calls=%fused_computation.9 | convolution fusion | flops 1610612736 | bytes 5767172 | tf_op jit(solution)/shard_map/dot_general | solution.py:40
  34.6 4.8 %fusion.6 = bf16[512,1536]{1,0:T(8,128)(2,1)} fusion(bf16[512,1024]{1,0:T(8,128)(2,1)S(1)} %multiply_convert_fusion.3, bf16[1024,6144]{1,0:T(8,128)(2,1)} %param.9, s32[]{:T(128)S(6)} %select_n.63), kind=kOutput, calls=%fused_computation.11 | convolution fusion | flops 1610612736 | bytes 5767172 | tf_op jit(solution)/shard_map/dot_general | solution.py:40
  39.5 0.8 collective-permute-start.6
  40.2 4.6 %collective-permute-start.3 = (bf16[512,1536]{1,0:T(8,128)(2,1)}, bf16[512,1536]{1,0:T(8,128)(2,1)}, u32[]{:S(2)}, u32[]{:S(2)}) collective-permute-start(bf16[512,1536]{1,0:T(8,128)(2,1)} %fusion.6), channel_id=1, source_target_pairs={{0,1},{4,5},{8,9},{12,13},{16,17},{20,21},{24,25},{28,29}} | collective-permute-start | bytes 4718600 | tf_op jit(solution)/shard_map/ppermute | solution.py:60
  44.9 4.1 %fusion.8 = f32[512,1536]{1,0:T(8,128)S(1)} fusion(bf16[512,1024]{1,0:T(8,128)(2,1)} %copy-done.1, bf16[1024,6144]{1,0:T(8,128)(2,1)} %param.9, s32[]{:T(128)S(6)} %select_n.62), kind=kOutput, calls=%fused_computation.13 | convolution fusion | flops 1610612736 | bytes 7340036 | tf_op jit(solution)/shard_map/dot_general | solution.py:40
  48.9 3.7 %fusion.10 = f32[512,1536]{1,0:T(8,128)S(1)} fusion(bf16[512,1024]{1,0:T(8,128)(2,1)S(1)} %copy-done.2, bf16[1024,6144]{1,0:T(8,128)(2,1)} %param.9, s32[]{:T(128)S(6)} %select_n.61), kind=kOutput, calls=%fused_computation.15 | convolution fusion | flops 1610612736 | bytes 7340036 | tf_op jit(solution)/shard_map/dot_general | solution.py:40
  52.6 0.6 add_convert_fusion.1
  53.2 1.8 %collective-permute-start.7 = (bf16[512,1536]{1,0:T(8,128)(2,1)S(1)}, bf16[512,1536]{1,0:T(8,128)(2,1)}, u32[]{:S(2)}, u32[]{:S(2)}) collective-permute-start(bf16[512,1536]{1,0:T(8,128)(2,1)S(1)} %add_convert_fusion.1), channel_id=1, source_target_pairs={{2,1},{3,2},{6,5},{7,6},{10,9},{11,10},{14,13},{15,14},{18,17},{19... | collective-permute-start | bytes 4718600 | tf_op jit(solution)/shard_map/ppermute | solution.py:61
  55.1 21.3 %collective-permute-done.3 = bf16[512,1536]{1,0:T(8,128)(2,1)} collective-permute-done((bf16[512,1536]{1,0:T(8,128)(2,1)}, bf16[512,1536]{1,0:T(8,128)(2,1)}, u32[]{:S(2)}, u32[]{:S(2)}) %collective-permute-start.3) | collective-permute-done | bytes 1572896 | tf_op jit(solution)/shard_map/ppermute | solution.py:60
  76.3 2.0 %add_convert_fusion.3 = bf16[512,1536]{1,0:T(8,128)(2,1)S(1)} fusion(f32[512,1536]{1,0:T(8,128)S(1)} %fusion.10, bf16[512,1536]{1,0:T(8,128)(2,1)} %collective-permute-done.3), kind=kLoop, calls=%fused_computation.8 | loop fusion | flops 2359296 | bytes 6291456 | tf_op jit(solution)/shard_map/convert_element_type | solution.py:60
  78.3 5.6 %collective-permute-start.4 = (bf16[512,1536]{1,0:T(8,128)(2,1)S(1)}, bf16[512,1536]{1,0:T(8,128)(2,1)}, u32[]{:S(2)}, u32[]{:S(2)}) collective-permute-start(bf16[512,1536]{1,0:T(8,128)(2,1)S(1)} %add_convert_fusion.3), channel_id=1, source_target_pairs={{0,1},{1,2},{4,5},{5,6},{8,9},{9,10},{12,13},{13,14},{16,17},{17,1... | collective-permute-start | bytes 4718600 | tf_op jit(solution)/shard_map/ppermute | solution.py:60
  83.9 4.1 %fusion.12 = f32[512,1536]{1,0:T(8,128)S(1)} fusion(bf16[512,1024]{1,0:T(8,128)(2,1)} %copy-done.1, bf16[1024,6144]{1,0:T(8,128)(2,1)} %param.9, s32[]{:T(128)S(6)} %select_n.60), kind=kOutput, calls=%fused_computation.17 | convolution fusion | flops 1610612736 | bytes 7340036 | tf_op jit(solution)/shard_map/dot_general | solution.py:40
  88.0 3.7 %fusion.14 = f32[512,1536]{1,0:T(8,128)S(1)} fusion(bf16[512,1024]{1,0:T(8,128)(2,1)S(1)} %copy-done.3, bf16[1024,6144]{1,0:T(8,128)(2,1)} %param.9, s32[]{:T(128)S(6)} %select_n.59), kind=kOutput, calls=%fused_computation.19 | convolution fusion | flops 1610612736 | bytes 7340036 | tf_op jit(solution)/shard_map/dot_general | solution.py:40
  91.7 3.1 %add_convert_fusion = bf16[512,1536]{1,0:T(8,128)(2,1)} fusion(f32[512,1536]{1,0:T(8,128)S(1)} %fusion.12, bf16[512,1536]{1,0:T(8,128)(2,1)} %collective-permute-done.7), kind=kLoop, calls=%fused_computation.5 | loop fusion | flops 2359296 | bytes 6291456 | tf_op jit(solution)/shard_map/convert_element_type | solution.py:61
  94.8 1.3 collective-permute-start.8
  96.1 18.1 %collective-permute-done.4 = bf16[512,1536]{1,0:T(8,128)(2,1)} collective-permute-done((bf16[512,1536]{1,0:T(8,128)(2,1)S(1)}, bf16[512,1536]{1,0:T(8,128)(2,1)}, u32[]{:S(2)}, u32[]{:S(2)}) %collective-permute-start.4) | collective-permute-done | bytes 1572896 | tf_op jit(solution)/shard_map/ppermute | solution.py:60
  114.2 2.0 %add_convert_fusion.2 = bf16[512,1536]{1,0:T(8,128)(2,1)S(1)} fusion(f32[512,1536]{1,0:T(8,128)S(1)} %fusion.14, bf16[512,1536]{1,0:T(8,128)(2,1)} %collective-permute-done.4), kind=kLoop, calls=%fused_computation.7 | loop fusion | flops 2359296 | bytes 6291456 | tf_op jit(solution)/shard_map/convert_element_type | solution.py:60
  116.2 8.0 %collective-permute-start.5 = (bf16[512,1536]{1,0:T(8,128)(2,1)S(1)}, bf16[512,1536]{1,0:T(8,128)(2,1)}, u32[]{:S(2)}, u32[]{:S(2)}) collective-permute-start(bf16[512,1536]{1,0:T(8,128)(2,1)S(1)} %add_convert_fusion.2), channel_id=1, source_target_pairs={{0,1},{1,2},{2,3},{4,5},{5,6},{6,7},{8,9},{9,10},{10,11},{12,13},{... | collective-permute-start | bytes 4718600 | tf_op jit(solution)/shard_map/ppermute | solution.py:60
  124.2 36.3 %psum.7 = f32[512]{0:T(512)S(1)} all-reduce(f32[512]{0:T(512)S(1)} %get-tuple-element.23), channel_id=1, replica_groups=mesh['seq'=8,'head'=4] {'head'}, use_global_device_ids=true, to_apply=%region_1.2 | all-reduce | flops 512 | bytes 4096 | tf_op jit(solution)/shard_map/psum | solution.py:99
  160.5 4.0 %fusion.16 = f32[512,1536]{1,0:T(8,128)S(1)} fusion(bf16[512,1024]{1,0:T(8,128)(2,1)} %copy-done.1, bf16[1024,6144]{1,0:T(8,128)(2,1)} %param.9, s32[]{:T(128)S(6)} %select_n.58), kind=kOutput, calls=%fused_computation.21 | convolution fusion | flops 1610612736 | bytes 7340036 | tf_op jit(solution)/shard_map/dot_general | solution.py:40
  164.5 3.2 %multiply_convert_fusion.2 = bf16[512,1536]{1,0:T(8,128)(2,1)} fusion(bf16[512,1536]{1,0:T(8,128)(2,1)S(1)} %collective-permute-done.8, f32[512,1536]{1,0:T(8,128)S(1)} %fusion.16, bf16[512,1536]{1,0:T(8,128)(2,1)} %collective-permute-done.5, f32[512]{0:T(512)S(1)} %add_rsqrt_fusion), kind=kLoop, calls=%fused_computation.4 | loop fusion | flops 4718592 | bytes 7866368 | tf_op jit(solution)/shard_map/convert_element_type | solution.py:102
  (21 shorter events, 1.9 us)
Async XLA Ops:
  0.0 2.5 %copy-start.4 = (bf16[512,1024]{1,0:T(8,128)(2,1)S(1)}, bf16[512,1024]{1,0:T(8,128)(2,1)}, u32[]{:S(2)}) copy-start(bf16[512,1024]{1,0:T(8,128)(2,1)} %param.7) | copy-start | bytes 3145732
  3.3 1.7 %collective-permute-start = (bf16[8,128,128]{2,1,0:T(8,128)(2,1)S(1)}, bf16[8,128,128]{2,1,0:T(8,128)(2,1)S(1)}, u32[]{:S(2)}, u32[]{:S(2)}) collective-permute-start(bf16[8,128,128]{2,1,0:T(8,128)(2,1)S(1)} %get-tuple-element.21), channel_id=1, source_target_pairs={{0,4},{4,0},{8,12},{12,8},{16,20},{20,16},{24,28},{28,24},{1,5},{5... | collective-permute-start | bytes 786440 | tf_op jit(solution)/shard_map/ppermute | solution.py:29
  5.1 9.5 %collective-permute-start.1 = (bf16[8,128,128]{2,1,0:T(8,128)(2,1)S(1)}, bf16[8,128,128]{2,1,0:T(8,128)(2,1)S(1)}, u32[]{:S(2)}, u32[]{:S(2)}) collective-permute-start(bf16[8,128,128]{2,1,0:T(8,128)(2,1)S(1)} %fusion.48), channel_id=1, source_target_pairs={{0,8},{4,12},{8,0},{12,4},{16,24},{20,28},{24,16},{28,20},{1,9},{5... | collective-permute-start | bytes 786440 | tf_op jit(solution)/shard_map/ppermute | solution.py:29
  14.7 7.9 %collective-permute-start.2 = (bf16[8,128,128]{2,1,0:T(8,128)(2,1)S(1)}, bf16[8,128,128]{2,1,0:T(8,128)(2,1)}, u32[]{:S(2)}, u32[]{:S(2)}) collective-permute-start(bf16[8,128,128]{2,1,0:T(8,128)(2,1)S(1)} %fusion.47), channel_id=1, source_target_pairs={{0,16},{4,20},{8,24},{12,28},{16,0},{20,4},{24,8},{28,12},{1,17},{... | collective-permute-start | bytes 786440 | tf_op jit(solution)/shard_map/ppermute | solution.py:29
  28.0 2.0 %copy-start = (bf16[512,1024]{1,0:T(8,128)(2,1)S(1)}, bf16[512,1024]{1,0:T(8,128)(2,1)}, u32[]{:S(2)}) copy-start(bf16[512,1024]{1,0:T(8,128)(2,1)} %param.8) | copy-start | bytes 3145732
  30.6 8.9 %copy-start.1 = (bf16[512,1024]{1,0:T(8,128)(2,1)}, bf16[512,1024]{1,0:T(8,128)(2,1)S(1)}, u32[]{:S(2)}) copy-start(bf16[512,1024]{1,0:T(8,128)(2,1)S(1)} %multiply_convert_fusion.3) | copy-start | bytes 3145732
  39.5 13.2 %collective-permute-start.6 = (bf16[512,1536]{1,0:T(8,128)(2,1)S(1)}, bf16[512,1536]{1,0:T(8,128)(2,1)S(1)}, u32[]{:S(2)}, u32[]{:S(2)}) collective-permute-start(bf16[512,1536]{1,0:T(8,128)(2,1)S(1)} %fusion.4), channel_id=1, source_target_pairs={{3,2},{7,6},{11,10},{15,14},{19,18},{23,22},{27,26},{31,30}} | collective-permute-start | bytes 4718600 | tf_op jit(solution)/shard_map/ppermute | solution.py:61
  40.2 36.1 %collective-permute-start.3 = (bf16[512,1536]{1,0:T(8,128)(2,1)}, bf16[512,1536]{1,0:T(8,128)(2,1)}, u32[]{:S(2)}, u32[]{:S(2)}) collective-permute-start(bf16[512,1536]{1,0:T(8,128)(2,1)} %fusion.6), channel_id=1, source_target_pairs={{0,1},{4,5},{8,9},{12,13},{16,17},{20,21},{24,25},{28,29}} | collective-permute-start | bytes 4718600 | tf_op jit(solution)/shard_map/ppermute | solution.py:60
  44.9 4.1 %copy-start.2 = (bf16[512,1024]{1,0:T(8,128)(2,1)S(1)}, bf16[512,1024]{1,0:T(8,128)(2,1)}, u32[]{:S(2)}) copy-start(bf16[512,1024]{1,0:T(8,128)(2,1)} %copy-done.1) | copy-start | bytes 3145732
  53.2 38.4 %collective-permute-start.7 = (bf16[512,1536]{1,0:T(8,128)(2,1)S(1)}, bf16[512,1536]{1,0:T(8,128)(2,1)}, u32[]{:S(2)}, u32[]{:S(2)}) collective-permute-start(bf16[512,1536]{1,0:T(8,128)(2,1)S(1)} %add_convert_fusion.1), channel_id=1, source_target_pairs={{2,1},{3,2},{6,5},{7,6},{10,9},{11,10},{14,13},{15,14},{18,17},{19... | collective-permute-start | bytes 4718600 | tf_op jit(solution)/shard_map/ppermute | solution.py:61
  78.3 35.9 %collective-permute-start.4 = (bf16[512,1536]{1,0:T(8,128)(2,1)S(1)}, bf16[512,1536]{1,0:T(8,128)(2,1)}, u32[]{:S(2)}, u32[]{:S(2)}) collective-permute-start(bf16[512,1536]{1,0:T(8,128)(2,1)S(1)} %add_convert_fusion.3), channel_id=1, source_target_pairs={{0,1},{1,2},{4,5},{5,6},{8,9},{9,10},{12,13},{13,14},{16,17},{17,1... | collective-permute-start | bytes 4718600 | tf_op jit(solution)/shard_map/ppermute | solution.py:60
  83.9 4.1 %copy-start.3 = (bf16[512,1024]{1,0:T(8,128)(2,1)S(1)}, bf16[512,1024]{1,0:T(8,128)(2,1)}, u32[]{:S(2)}) copy-start(bf16[512,1024]{1,0:T(8,128)(2,1)} %copy-done.1) | copy-start | bytes 3145732
  94.8 69.7 %collective-permute-start.8 = (bf16[512,1536]{1,0:T(8,128)(2,1)}, bf16[512,1536]{1,0:T(8,128)(2,1)S(1)}, u32[]{:S(2)}, u32[]{:S(2)}) collective-permute-start(bf16[512,1536]{1,0:T(8,128)(2,1)} %add_convert_fusion), channel_id=1, source_target_pairs={{1,0},{2,1},{3,2},{5,4},{6,5},{7,6},{9,8},{10,9},{11,10},{13,12},{... | collective-permute-start | bytes 4718600 | tf_op jit(solution)/shard_map/ppermute | solution.py:61
  116.2 48.3 %collective-permute-start.5 = (bf16[512,1536]{1,0:T(8,128)(2,1)S(1)}, bf16[512,1536]{1,0:T(8,128)(2,1)}, u32[]{:S(2)}, u32[]{:S(2)}) collective-permute-start(bf16[512,1536]{1,0:T(8,128)(2,1)S(1)} %add_convert_fusion.2), channel_id=1, source_target_pairs={{0,1},{1,2},{2,3},{4,5},{5,6},{6,7},{8,9},{9,10},{10,11},{12,13},{... | collective-permute-start | bytes 4718600 | tf_op jit(solution)/shard_map/ppermute | solution.py:60

commit v6 on v5

--- a/solution.py
+++ b/solution.py
@@ -40,7 +40,7 @@
     return jnp.dot(gated, columns, preferred_element_type=jnp.float32)
 
 
-def line_reduce_scatter(gated, out_weight, axis_name):
+def line_reduce_scatter(gated, out_weight, axis_name, square_sums):
     count = lax.axis_size(axis_name)
     here = lax.axis_index(axis_name)
     width = out_weight.shape[1] // count
@@ -49,9 +49,14 @@
     for step in range(1, count):
         right_shard = jnp.clip(here + count - step, 0, count - 1)
         left_shard = jnp.clip(here - count + step, 0, count - 1)
-        to_right = shard_product(gated, out_weight, right_shard, width)
-        to_left = shard_product(gated, out_weight, left_shard, width)
-        to_right, to_left = lax.optimization_barrier((to_right, to_left))
+        if 2 * step <= count:
+            shard = jnp.where(here < step, right_shard, left_shard)
+            to_right = lax.optimization_barrier(shard_product(gated, out_weight, shard, width))
+            to_left = to_right
+        else:
+            to_right = shard_product(gated, out_weight, right_shard, width)
+            to_left = shard_product(gated, out_weight, left_shard, width)
+            to_right, to_left = lax.optimization_barrier((to_right, to_left))
         if from_left is not None:
             to_right = to_right + from_left
             to_left = to_left + from_right
@@ -62,9 +67,12 @@
         from_left = from_left.astype(jnp.float32)
         from_right = from_right.astype(jnp.float32)
     own = shard_product(gated, out_weight, here, width)
-    if from_left is None:
-        return own
-    return own + from_left + from_right
+    own, square_sums = lax.optimization_barrier((own, square_sums))
+    total_squares = lax.psum(square_sums, axis_name)
+    scaling = lax.rsqrt(total_squares / (HEADS * HEAD_DIM) + 1e-06)
+    if from_left is not None:
+        own = own + from_left + from_right
+    return own * scaling[:, None]
 
 
 def body(queries, keys, values, gate_logits, out_weight):
@@ -96,10 +104,8 @@
     square_sums = jnp.sum(attended * attended, axis=-1)
     gate = jax.nn.sigmoid(gate_logits.astype(jnp.float32))
     gated = (attended * gate).astype(jnp.bfloat16)
-    total_squares = lax.psum(square_sums, "head")
-    scaling = lax.rsqrt(total_squares / (HEADS * HEAD_DIM) + 1e-06)
-    reduced = line_reduce_scatter(gated, out_weight, "head")
-    return (reduced * scaling[:, None]).astype(jnp.bfloat16)
+    reduced = line_reduce_scatter(gated, out_weight, "head", square_sums)
+    return reduced.astype(jnp.bfloat16)
 
 
 def solution(mesh):

time: 168 us -> 167 us (level)
  matrix products: 39.1 us -> 30.1 us
  waiting for transfers between devices: 47.5 us -> 51.6 us
  starting transfers between devices: 27.4 us -> 31 us
  blocking collectives: 36.3 us -> 33.5 us
  other arithmetic: 14.7 us -> 16.5 us
    dot_general x7 -> x5, matrix products: 28.4 us -> 19.4 us  [shard_product(): return jnp.dot(gated, columns, preferred_element_type=jnp.float32)]
    ppermute x3, waiting for transfers between devices: 39.4 us -> 43.5 us  [line_reduce_scatter(): lax.ppermute(to_right.astype(jnp.bfloat16), axis_name, right_pairs)]
    psum x1, blocking collectives: 36.3 us -> 33.5 us  [line_reduce_scatter(): total_squares = lax.psum(square_sums, axis_name)]
    ppermute x3, starting transfers between devices: 18.2 us -> 20.8 us  [line_reduce_scatter(): lax.ppermute(to_right.astype(jnp.bfloat16), axis_name, right_pairs)]
    convert_element_type x2, other arithmetic: 3.97 us -> 5.9 us  [line_reduce_scatter(): to_right.astype(jnp.bfloat16)]
    convert_element_type x2 -> x1, other arithmetic: 3.71 us -> 3.13 us  [line_reduce_scatter(): to_left.astype(jnp.bfloat16)]
  transfers between devices with their start and end apart: 9 -> 9, of which waited for: 5 -> 5; matrix products, arithmetic and copies ran while one was open for 20% -> 17% of each run, Pallas kernels for 0% -> 0%
where the time goes in v6:
time: 167 us; the launch traced here: 166 us
  waiting for transfers between devices  51.6 us (31%)
  blocking collectives  33.5 us (20%)
  starting transfers between devices  31 us (19%)
  matrix products  30.1 us (18%)
  other arithmetic  16.5 us (10%)
  local copies, waits for them, and re-layouts  3.57 us (2%)
    ppermute x3, waiting for transfers between devices, line_reduce_scatter(): lax.ppermute(to_right.astype(jnp.bfloat16), axis_name, right_pairs)  43.5 us
    psum x1, blocking collectives, line_reduce_scatter(): total_squares = lax.psum(square_sums, axis_name)  33.5 us
    ppermute x3, starting transfers between devices, line_reduce_scatter(): lax.ppermute(to_right.astype(jnp.bfloat16), axis_name, right_pairs)  20.8 us
    dot_general x5, matrix products, shard_product(): return jnp.dot(gated, columns, preferred_element_type=jnp.float32)  19.4 us
    ppermute x3, waiting for transfers between devices, exclusive_prefix(): arrived = lax.ppermute(group_total.astype(jnp.bfloat16), axis_name, pairs)  8.16 us
    convert_element_type x2, other arithmetic, line_reduce_scatter(): to_right.astype(jnp.bfloat16)  5.9 us
    dot_general x1, matrix products, body(): jnp.einsum('nhts,nshd->nthd', scores, active_v, preferred_element_type=jn...  5.6 us
    ppermute x3, starting transfers between devices, exclusive_prefix(): arrived = lax.ppermute(group_total.astype(jnp.bfloat16), axis_name, pairs)  5.3 us
  transfers between devices with their start and end apart: 9, of which 5 were waited for; matrix products, arithmetic and copies ran while one was open for 17% of the time, Pallas kernels for 0%

profile of v6, /device:TPU:0, one launch (start us, length us, event | category | flops | bytes accessed | tf_op | source)
XLA Modules:
  0.0 166.4 jit_solution(4640472732793913898)
XLA Ops:
  0.0 1.9 %fusion.25 = bf16[512,1024]{1,0:T(8,128)(2,1)S(1)} fusion(bf16[512,1024]{1,0:T(8,128)(2,1)} %param.6), kind=kLoop, calls=%fused_computation.36 | loop fusion | flops 3145728 | bytes 2097152 | tf_op jit(solution)/shard_map/convert_element_type | solution.py:11
  1.9 0.5 copy.13
  2.5 0.8 fusion.50
  3.3 0.6 collective-permute-start
  3.9 1.2 collective-permute-done
  5.1 2.9 %collective-permute-start.1 = (bf16[8,128,128]{2,1,0:T(8,128)(2,1)S(1)}, bf16[8,128,128]{2,1,0:T(8,128)(2,1)S(1)}, u32[]{:S(2)}, u32[]{:S(2)}) collective-permute-start(bf16[8,128,128]{2,1,0:T(8,128)(2,1)S(1)} %fusion.44), channel_id=1, source_target_pairs={{0,8},{4,12},{8,0},{12,4},{16,24},{20,28},{24,16},{28,20},{1,9},{5... | collective-permute-start | bytes 786440 | tf_op jit(solution)/shard_map/ppermute | solution.py:29
  8.2 6.5 %collective-permute-done.1 = bf16[8,128,128]{2,1,0:T(8,128)(2,1)S(1)} collective-permute-done((bf16[8,128,128]{2,1,0:T(8,128)(2,1)S(1)}, bf16[8,128,128]{2,1,0:T(8,128)(2,1)S(1)}, u32[]{:S(2)}, u32[]{:S(2)}) %collective-permute-start.1) | collective-permute-done | bytes 262176 | tf_op jit(solution)/shard_map/ppermute | solution.py:29
  14.7 1.8 %collective-permute-start.2 = (bf16[8,128,128]{2,1,0:T(8,128)(2,1)S(1)}, bf16[8,128,128]{2,1,0:T(8,128)(2,1)}, u32[]{:S(2)}, u32[]{:S(2)}) collective-permute-start(bf16[8,128,128]{2,1,0:T(8,128)(2,1)S(1)} %fusion.43), channel_id=1, source_target_pairs={{0,16},{4,20},{8,24},{12,28},{16,0},{20,4},{24,8},{28,12},{1,17},{... | collective-permute-start | bytes 786440 | tf_op jit(solution)/shard_map/ppermute | solution.py:29
  16.6 5.6 %fusion.26 = f32[1,512,8,128]{1,3,2,0:T(8,128)} fusion(f32[512,512]{1,0:T(8,128)S(1)} %fusion.35, bf16[512,8,128]{0,2,1:T(8,128)(2,1)S(1)} %bitcast.47, bf16[512,1024]{1,0:T(8,128)(2,1)} %param.7, bf16[512,1024]{1,0:T(8,128)(2,1)} %param.5), kind=kOutput, calls=%fused_computation.40 | convolution fusion | flops 1084227584 | bytes 6291456 | tf_op jit(solution)/shard_map/nhts,nshd->nthd/dot_general | solution.py:97
  22.7 1.1 fusion.42
  23.8 4.2 %multiply_reduce_fusion = (f32[512]{0:T(512)S(1)}, f32[1,512,8,128]{1,3,2,0:T(8,128)}) fusion(f32[1,512,8,128]{1,3,2,0:T(8,128)} %fusion.26, f32[8,128,128]{2,1,0:T(8,128)S(1)} %fusion.42, f32[8,128,128]{2,1,0:T(8,128)S(1)} %get-tuple-element.20, bf16[512,1024]{1,0:T(8,128)(2,1)} %param.5), kind=kOutput, calls=%fused_computation.38 | convolution fusion | flops 139329024 | bytes 6293504 | tf_op jit(solution)/shard_map/nthd,nhde->nthe/dot_general | solution.py:102
  28.0 2.0 %copy.11 = f32[512,1024]{1,0:T(8,128)S(1)} copy(f32[512,1024]{0,1:T(8,128)} %bitcast.45) | data formatting | bytes 4194304 | tf_op jit(solution)/shard_map/reshape | solution.py:103
  30.0 0.6 multiply_convert_fusion.3
  30.6 1.0 copy-done.1
  31.6 3.7 %fusion.4 = bf16[512,1536]{1,0:T(8,128)(2,1)S(1)} fusion(bf16[512,1024]{1,0:T(8,128)(2,1)S(1)} %multiply_convert_fusion.3, bf16[1024,6144]{1,0:T(8,128)(2,1)} %param.9, s32[]{:T(128)S(6)} %select_n.64), kind=kOutput, calls=%fused_computation.9 | convolution fusion | flops 1610612736 | bytes 5767172 | tf_op jit(solution)/shard_map/dot_general | solution.py:40
  35.3 4.6 %collective-permute-start.3 = (bf16[512,1536]{1,0:T(8,128)(2,1)S(1)}, bf16[512,1536]{1,0:T(8,128)(2,1)}, u32[]{:S(2)}, u32[]{:S(2)}) collective-permute-start(bf16[512,1536]{1,0:T(8,128)(2,1)S(1)} %fusion.4), channel_id=1, source_target_pairs={{0,1},{4,5},{8,9},{12,13},{16,17},{20,21},{24,25},{28,29}} | collective-permute-start | bytes 4718600 | tf_op jit(solution)/shard_map/ppermute | solution.py:65
  39.9 1.8 %collective-permute-start.6 = (bf16[512,1536]{1,0:T(8,128)(2,1)S(1)}, bf16[512,1536]{1,0:T(8,128)(2,1)}, u32[]{:S(2)}, u32[]{:S(2)}) collective-permute-start(bf16[512,1536]{1,0:T(8,128)(2,1)S(1)} %fusion.4), channel_id=1, source_target_pairs={{3,2},{7,6},{11,10},{15,14},{19,18},{23,22},{27,26},{31,30}} | collective-permute-start | bytes 4718600 | tf_op jit(solution)/shard_map/ppermute | solution.py:66
  41.7 4.0 %fusion.6 = f32[512,1536]{1,0:T(8,128)S(1)} fusion(bf16[512,1024]{1,0:T(8,128)(2,1)} %copy-done.1, bf16[1024,6144]{1,0:T(8,128)(2,1)} %param.9, s32[]{:T(128)S(6)} %select_n.62), kind=kOutput, calls=%fused_computation.11 | convolution fusion | flops 1610612736 | bytes 7340036 | tf_op jit(solution)/shard_map/dot_general | solution.py:40
  45.7 25.4 %collective-permute-done.3 = bf16[512,1536]{1,0:T(8,128)(2,1)} collective-permute-done((bf16[512,1536]{1,0:T(8,128)(2,1)S(1)}, bf16[512,1536]{1,0:T(8,128)(2,1)}, u32[]{:S(2)}, u32[]{:S(2)}) %collective-permute-start.3) | collective-permute-done | bytes 1572896 | tf_op jit(solution)/shard_map/ppermute | solution.py:65
  71.0 2.8 %add_convert_fusion.3 = (bf16[512,1536]{1,0:T(8,128)(2,1)S(1)}, bf16[512,1536]{1,0:T(8,128)(2,1)S(1)}) fusion(f32[512,1536]{1,0:T(8,128)S(1)} %fusion.6, bf16[512,1536]{1,0:T(8,128)(2,1)} %collective-permute-done.3, bf16[512,1536]{1,0:T(8,128)(2,1)} %collective-permute-done.6), kind=kLoop, calls=%fused_computation.8 | loop fusion | flops 4718592 | bytes 9437184 | tf_op jit(solution)/shard_map/convert_element_type | solution.py:65
  73.8 1.8 %collective-permute-start.7 = (bf16[512,1536]{1,0:T(8,128)(2,1)S(1)}, bf16[512,1536]{1,0:T(8,128)(2,1)}, u32[]{:S(2)}, u32[]{:S(2)}) collective-permute-start(bf16[512,1536]{1,0:T(8,128)(2,1)S(1)} %get-tuple-element.18), channel_id=1, source_target_pairs={{2,1},{3,2},{6,5},{7,6},{10,9},{11,10},{14,13},{15,14},{18,17},{19... | collective-permute-start | bytes 4718600 | tf_op jit(solution)/shard_map/ppermute | solution.py:66
  75.6 5.1 %collective-permute-start.4 = (bf16[512,1536]{1,0:T(8,128)(2,1)S(1)}, bf16[512,1536]{1,0:T(8,128)(2,1)}, u32[]{:S(2)}, u32[]{:S(2)}) collective-permute-start(bf16[512,1536]{1,0:T(8,128)(2,1)S(1)} %get-tuple-element.17), channel_id=1, source_target_pairs={{0,1},{1,2},{4,5},{5,6},{8,9},{9,10},{12,13},{13,14},{16,17},{17,1... | collective-permute-start | bytes 4718600 | tf_op jit(solution)/shard_map/ppermute | solution.py:65
  80.8 4.1 %fusion.8 = f32[512,1536]{1,0:T(8,128)S(1)} fusion(bf16[512,1024]{1,0:T(8,128)(2,1)} %copy-done.1, bf16[1024,6144]{1,0:T(8,128)(2,1)} %param.9, s32[]{:T(128)S(6)} %select_n.60), kind=kOutput, calls=%fused_computation.13 | convolution fusion | flops 1610612736 | bytes 7340036 | tf_op jit(solution)/shard_map/dot_general | solution.py:40
  84.9 3.7 %fusion.10 = f32[512,1536]{1,0:T(8,128)S(1)} fusion(bf16[512,1024]{1,0:T(8,128)(2,1)S(1)} %copy-done.2, bf16[1024,6144]{1,0:T(8,128)(2,1)} %param.9, s32[]{:T(128)S(6)} %select_n.59), kind=kOutput, calls=%fused_computation.15 | convolution fusion | flops 1610612736 | bytes 7340036 | tf_op jit(solution)/shard_map/dot_general | solution.py:40
  88.6 3.1 %add_convert_fusion = bf16[512,1536]{1,0:T(8,128)(2,1)} fusion(f32[512,1536]{1,0:T(8,128)S(1)} %fusion.8, bf16[512,1536]{1,0:T(8,128)(2,1)} %collective-permute-done.7), kind=kLoop, calls=%fused_computation.5 | loop fusion | flops 2359296 | bytes 6291456 | tf_op jit(solution)/shard_map/convert_element_type | solution.py:66
  91.7 1.3 collective-permute-start.8
  93.0 18.1 %collective-permute-done.4 = bf16[512,1536]{1,0:T(8,128)(2,1)} collective-permute-done((bf16[512,1536]{1,0:T(8,128)(2,1)S(1)}, bf16[512,1536]{1,0:T(8,128)(2,1)}, u32[]{:S(2)}, u32[]{:S(2)}) %collective-permute-start.4) | collective-permute-done | bytes 1572896 | tf_op jit(solution)/shard_map/ppermute | solution.py:65
  111.1 3.1 %add_convert_fusion.2 = bf16[512,1536]{1,0:T(8,128)(2,1)} fusion(f32[512,1536]{1,0:T(8,128)S(1)} %fusion.10, bf16[512,1536]{1,0:T(8,128)(2,1)} %collective-permute-done.4), kind=kLoop, calls=%fused_computation.7 | loop fusion | flops 2359296 | bytes 6291456 | tf_op jit(solution)/shard_map/convert_element_type | solution.py:65
  114.2 11.0 %collective-permute-start.5 = (bf16[512,1536]{1,0:T(8,128)(2,1)}, bf16[512,1536]{1,0:T(8,128)(2,1)}, u32[]{:S(2)}, u32[]{:S(2)}) collective-permute-start(bf16[512,1536]{1,0:T(8,128)(2,1)} %add_convert_fusion.2), channel_id=1, source_target_pairs={{0,1},{1,2},{2,3},{4,5},{5,6},{6,7},{8,9},{9,10},{10,11},{12,13},{... | collective-permute-start | bytes 4718600 | tf_op jit(solution)/shard_map/ppermute | solution.py:65
  125.3 4.0 %fusion.12 = f32[512,1536]{1,0:T(8,128)S(1)} fusion(bf16[512,1024]{1,0:T(8,128)(2,1)} %copy-done.1, bf16[1024,6144]{1,0:T(8,128)(2,1)} %param.9, s32[]{:T(128)S(6)} %select_n.58), kind=kOutput, calls=%fused_computation.17 | convolution fusion | flops 1610612736 | bytes 7340036 | tf_op jit(solution)/shard_map/dot_general | solution.py:40
  129.3 33.5 %psum.7 = f32[512]{0:T(512)S(1)} all-reduce(f32[512]{0:T(512)S(1)} %get-tuple-element.16), channel_id=1, replica_groups=mesh['seq'=8,'head'=4] {'head'}, use_global_device_ids=true, to_apply=%region_1.2 | all-reduce | flops 512 | bytes 4096 | tf_op jit(solution)/shard_map/psum | solution.py:71
  162.8 3.6 %multiply_convert_fusion.2 = bf16[512,1536]{1,0:T(8,128)(2,1)} fusion(bf16[512,1536]{1,0:T(8,128)(2,1)} %collective-permute-done.8, f32[512,1536]{1,0:T(8,128)S(1)} %fusion.12, bf16[512,1536]{1,0:T(8,128)(2,1)} %collective-permute-done.5, f32[512]{0:T(512)S(1)} %add_rsqrt_fusion), kind=kLoop, calls=%fused_computation.4 | loop fusion | flops 4718592 | bytes 7866368 | tf_op jit(solution)/shard_map/convert_element_type | solution.py:108
  (16 shorter events, 0.8 us)
Async XLA Ops:
  0.0 2.5 %copy-start.3 = (bf16[512,1024]{1,0:T(8,128)(2,1)S(1)}, bf16[512,1024]{1,0:T(8,128)(2,1)}, u32[]{:S(2)}) copy-start(bf16[512,1024]{1,0:T(8,128)(2,1)} %param.7) | copy-start | bytes 3145732
  3.3 1.7 %collective-permute-start = (bf16[8,128,128]{2,1,0:T(8,128)(2,1)S(1)}, bf16[8,128,128]{2,1,0:T(8,128)(2,1)S(1)}, u32[]{:S(2)}, u32[]{:S(2)}) collective-permute-start(bf16[8,128,128]{2,1,0:T(8,128)(2,1)S(1)} %get-tuple-element.19), channel_id=1, source_target_pairs={{0,4},{4,0},{8,12},{12,8},{16,20},{20,16},{24,28},{28,24},{1,5},{5... | collective-permute-start | bytes 786440 | tf_op jit(solution)/shard_map/ppermute | solution.py:29
  5.1 9.5 %collective-permute-start.1 = (bf16[8,128,128]{2,1,0:T(8,128)(2,1)S(1)}, bf16[8,128,128]{2,1,0:T(8,128)(2,1)S(1)}, u32[]{:S(2)}, u32[]{:S(2)}) collective-permute-start(bf16[8,128,128]{2,1,0:T(8,128)(2,1)S(1)} %fusion.44), channel_id=1, source_target_pairs={{0,8},{4,12},{8,0},{12,4},{16,24},{20,28},{24,16},{28,20},{1,9},{5... | collective-permute-start | bytes 786440 | tf_op jit(solution)/shard_map/ppermute | solution.py:29
  14.7 7.9 %collective-permute-start.2 = (bf16[8,128,128]{2,1,0:T(8,128)(2,1)S(1)}, bf16[8,128,128]{2,1,0:T(8,128)(2,1)}, u32[]{:S(2)}, u32[]{:S(2)}) collective-permute-start(bf16[8,128,128]{2,1,0:T(8,128)(2,1)S(1)} %fusion.43), channel_id=1, source_target_pairs={{0,16},{4,20},{8,24},{12,28},{16,0},{20,4},{24,8},{28,12},{1,17},{... | collective-permute-start | bytes 786440 | tf_op jit(solution)/shard_map/ppermute | solution.py:29
  28.0 2.0 %copy-start = (bf16[512,1024]{1,0:T(8,128)(2,1)S(1)}, bf16[512,1024]{1,0:T(8,128)(2,1)}, u32[]{:S(2)}) copy-start(bf16[512,1024]{1,0:T(8,128)(2,1)} %param.8) | copy-start | bytes 3145732
  30.6 1.0 copy-start.1
  35.3 35.8 %collective-permute-start.3 = (bf16[512,1536]{1,0:T(8,128)(2,1)S(1)}, bf16[512,1536]{1,0:T(8,128)(2,1)}, u32[]{:S(2)}, u32[]{:S(2)}) collective-permute-start(bf16[512,1536]{1,0:T(8,128)(2,1)S(1)} %fusion.4), channel_id=1, source_target_pairs={{0,1},{4,5},{8,9},{12,13},{16,17},{20,21},{24,25},{28,29}} | collective-permute-start | bytes 4718600 | tf_op jit(solution)/shard_map/ppermute | solution.py:65
  39.9 31.2 %collective-permute-start.6 = (bf16[512,1536]{1,0:T(8,128)(2,1)S(1)}, bf16[512,1536]{1,0:T(8,128)(2,1)}, u32[]{:S(2)}, u32[]{:S(2)}) collective-permute-start(bf16[512,1536]{1,0:T(8,128)(2,1)S(1)} %fusion.4), channel_id=1, source_target_pairs={{3,2},{7,6},{11,10},{15,14},{19,18},{23,22},{27,26},{31,30}} | collective-permute-start | bytes 4718600 | tf_op jit(solution)/shard_map/ppermute | solution.py:66
  73.8 14.7 %collective-permute-start.7 = (bf16[512,1536]{1,0:T(8,128)(2,1)S(1)}, bf16[512,1536]{1,0:T(8,128)(2,1)}, u32[]{:S(2)}, u32[]{:S(2)}) collective-permute-start(bf16[512,1536]{1,0:T(8,128)(2,1)S(1)} %get-tuple-element.18), channel_id=1, source_target_pairs={{2,1},{3,2},{6,5},{7,6},{10,9},{11,10},{14,13},{15,14},{18,17},{19... | collective-permute-start | bytes 4718600 | tf_op jit(solution)/shard_map/ppermute | solution.py:66
  75.6 35.4 %collective-permute-start.4 = (bf16[512,1536]{1,0:T(8,128)(2,1)S(1)}, bf16[512,1536]{1,0:T(8,128)(2,1)}, u32[]{:S(2)}, u32[]{:S(2)}) collective-permute-start(bf16[512,1536]{1,0:T(8,128)(2,1)S(1)} %get-tuple-element.17), channel_id=1, source_target_pairs={{0,1},{1,2},{4,5},{5,6},{8,9},{9,10},{12,13},{13,14},{16,17},{17,1... | collective-permute-start | bytes 4718600 | tf_op jit(solution)/shard_map/ppermute | solution.py:65
  80.8 4.1 %copy-start.2 = (bf16[512,1024]{1,0:T(8,128)(2,1)S(1)}, bf16[512,1024]{1,0:T(8,128)(2,1)}, u32[]{:S(2)}) copy-start(bf16[512,1024]{1,0:T(8,128)(2,1)} %copy-done.1) | copy-start | bytes 3145732
  91.7 71.1 %collective-permute-start.8 = (bf16[512,1536]{1,0:T(8,128)(2,1)}, bf16[512,1536]{1,0:T(8,128)(2,1)}, u32[]{:S(2)}, u32[]{:S(2)}) collective-permute-start(bf16[512,1536]{1,0:T(8,128)(2,1)} %add_convert_fusion), channel_id=1, source_target_pairs={{1,0},{2,1},{3,2},{5,4},{6,5},{7,6},{9,8},{10,9},{11,10},{13,12},{... | collective-permute-start | bytes 4718600 | tf_op jit(solution)/shard_map/ppermute | solution.py:66
  114.2 48.6 %collective-permute-start.5 = (bf16[512,1536]{1,0:T(8,128)(2,1)}, bf16[512,1536]{1,0:T(8,128)(2,1)}, u32[]{:S(2)}, u32[]{:S(2)}) collective-permute-start(bf16[512,1536]{1,0:T(8,128)(2,1)} %add_convert_fusion.2), channel_id=1, source_target_pairs={{0,1},{1,2},{2,3},{4,5},{5,6},{6,7},{8,9},{9,10},{10,11},{12,13},{... | collective-permute-start | bytes 4718600 | tf_op jit(solution)/shard_map/ppermute | solution.py:65

commit v7 on v6

--- a/solution.py
+++ b/solution.py
@@ -40,7 +40,18 @@
     return jnp.dot(gated, columns, preferred_element_type=jnp.float32)
 
 
-def line_reduce_scatter(gated, out_weight, axis_name, square_sums):
+def butterfly_sum(values, axis_name):
+    count = lax.axis_size(axis_name)
+    if count & (count - 1):
+        return lax.psum(values, axis_name)
+    bit = 1
+    while bit < count:
+        values = values + lax.ppermute(values, axis_name, [(i, i ^ bit) for i in range(count)])
+        bit *= 2
+    return values
+
+
+def line_reduce_scatter(gated, out_weight, axis_name, total_squares):
     count = lax.axis_size(axis_name)
     here = lax.axis_index(axis_name)
     width = out_weight.shape[1] // count
@@ -51,12 +62,21 @@
         left_shard = jnp.clip(here - count + step, 0, count - 1)
         if 2 * step <= count:
             shard = jnp.where(here < step, right_shard, left_shard)
-            to_right = lax.optimization_barrier(shard_product(gated, out_weight, shard, width))
+            to_right = shard_product(gated, out_weight, shard, width)
+            if step == min(2, count - 1):
+                to_right, total_squares = lax.optimization_barrier((to_right, total_squares))
+            else:
+                to_right = lax.optimization_barrier(to_right)
             to_left = to_right
         else:
             to_right = shard_product(gated, out_weight, right_shard, width)
             to_left = shard_product(gated, out_weight, left_shard, width)
-            to_right, to_left = lax.optimization_barrier((to_right, to_left))
+            if step == min(2, count - 1):
+                to_right, to_left, total_squares = lax.optimization_barrier(
+                    (to_right, to_left, total_squares)
+                )
+            else:
+                to_right, to_left = lax.optimization_barrier((to_right, to_left))
         if from_left is not None:
             to_right = to_right + from_left
             to_left = to_left + from_right
@@ -67,8 +87,6 @@
         from_left = from_left.astype(jnp.float32)
         from_right = from_right.astype(jnp.float32)
     own = shard_product(gated, out_weight, here, width)
-    own, square_sums = lax.optimization_barrier((own, square_sums))
-    total_squares = lax.psum(square_sums, axis_name)
     scaling = lax.rsqrt(total_squares / (HEADS * HEAD_DIM) + 1e-06)
     if from_left is not None:
         own = own + from_left + from_right
@@ -104,7 +122,8 @@
     square_sums = jnp.sum(attended * attended, axis=-1)
     gate = jax.nn.sigmoid(gate_logits.astype(jnp.float32))
     gated = (attended * gate).astype(jnp.bfloat16)
-    reduced = line_reduce_scatter(gated, out_weight, "head", square_sums)
+    total_squares = butterfly_sum(square_sums, "head")
+    reduced = line_reduce_scatter(gated, out_weight, "head", total_squares)
     return reduced.astype(jnp.bfloat16)
 
 

time: 167 us -> 158 us (0.946)
  waiting for transfers between devices: 51.6 us -> 86.7 us
  blocking collectives: 33.5 us -> 0 us
  starting transfers between devices: 31 us -> 25 us
  other arithmetic: 16.5 us -> 11.7 us
    psum x1 -> x0, blocking collectives: 33.5 us -> none  [line_reduce_scatter(): total_squares = lax.psum(square_sums, axis_name)]
    ppermute x0 -> x2, waiting for transfers between devices: none -> 31.7 us  [butterfly_sum(): lax.ppermute(values, axis_name, [(i, i ^ bit) for i in range(count)])]
    ppermute x3, waiting for transfers between devices: 0.01 us -> 23.5 us  [line_reduce_scatter(): lax.ppermute(to_left.astype(jnp.bfloat16), axis_name, left_pairs)]
    ppermute x3, waiting for transfers between devices: 43.5 us -> 23.3 us  [line_reduce_scatter(): lax.ppermute(to_right.astype(jnp.bfloat16), axis_name, right_pairs)]
    ppermute x3, starting transfers between devices: 20.8 us -> 12.6 us  [line_reduce_scatter(): lax.ppermute(to_right.astype(jnp.bfloat16), axis_name, right_pairs)]
    ppermute x0 -> x2, starting transfers between devices: none -> 4.27 us  [butterfly_sum(): lax.ppermute(values, axis_name, [(i, i ^ bit) for i in range(count)])]
    ppermute x3, starting transfers between devices: 4.92 us -> 2.79 us  [line_reduce_scatter(): lax.ppermute(to_left.astype(jnp.bfloat16), axis_name, left_pairs)]
    convert_element_type x1, other arithmetic: 3.59 us -> 1.78 us  [body(): return reduced.astype(jnp.bfloat16)]
  transfers between devices with their start and end apart: 9 -> 11, of which waited for: 5 -> 7; matrix products, arithmetic and copies ran while one was open for 17% -> 16% of each run, Pallas kernels for 0% -> 0%
where the time goes in v7:
time: 158 us
  waiting for transfers between devices  86.7 us (55%)
  matrix products  31.6 us (20%)
  starting transfers between devices  25 us (16%)
  other arithmetic  11.7 us (7%)
  local copies, waits for them, and re-layouts  2.57 us (2%)
    ppermute x2, waiting for transfers between devices, butterfly_sum(): lax.ppermute(values, axis_name, [(i, i ^ bit) for i in range(count)])  31.7 us
    ppermute x3, waiting for transfers between devices, line_reduce_scatter(): lax.ppermute(to_left.astype(jnp.bfloat16), axis_name, left_pairs)  23.5 us
    ppermute x3, waiting for transfers between devices, line_reduce_scatter(): lax.ppermute(to_right.astype(jnp.bfloat16), axis_name, right_pairs)  23.3 us
    dot_general x5, matrix products, shard_product(): return jnp.dot(gated, columns, preferred_element_type=jnp.float32)  21 us
    ppermute x3, starting transfers between devices, line_reduce_scatter(): lax.ppermute(to_right.astype(jnp.bfloat16), axis_name, right_pairs)  12.6 us
    ppermute x3, waiting for transfers between devices, exclusive_prefix(): arrived = lax.ppermute(group_total.astype(jnp.bfloat16), axis_name, pairs)  8.16 us
    dot_general x1, matrix products, body(): jnp.einsum('nhts,nshd->nthd', scores, active_v, preferred_element_type=jn...  5.6 us
    ppermute x3, starting transfers between devices, exclusive_prefix(): arrived = lax.ppermute(group_total.astype(jnp.bfloat16), axis_name, pairs)  5.3 us
  transfers between devices with their start and end apart: 11, of which 7 were waited for; matrix products, arithmetic and copies ran while one was open for 16% of the time, Pallas kernels for 0%

profile of v7, /device:TPU:0, one launch (start us, length us, event | category | flops | bytes accessed | tf_op | source)
XLA Modules:
  0.0 157.7 jit_solution(3786608212759299639)
XLA Ops:
  0.0 1.9 %fusion.25 = bf16[512,1024]{1,0:T(8,128)(2,1)S(1)} fusion(bf16[512,1024]{1,0:T(8,128)(2,1)} %param.6), kind=kLoop, calls=%fused_computation.36 | loop fusion | flops 3145728 | bytes 2097152 | tf_op jit(solution)/shard_map/convert_element_type | solution.py:11
  2.5 0.8 fusion.50
  3.3 0.6 collective-permute-start
  3.9 1.2 collective-permute-done
  5.1 2.9 %collective-permute-start.1 = (bf16[8,128,128]{2,1,0:T(8,128)(2,1)S(1)}, bf16[8,128,128]{2,1,0:T(8,128)(2,1)S(1)}, u32[]{:S(2)}, u32[]{:S(2)}) collective-permute-start(bf16[8,128,128]{2,1,0:T(8,128)(2,1)S(1)} %fusion.44), channel_id=1, source_target_pairs={{0,8},{4,12},{8,0},{12,4},{16,24},{20,28},{24,16},{28,20},{1,9},{5... | collective-permute-start | bytes 786440 | tf_op jit(solution)/shard_map/ppermute | solution.py:29
  8.2 6.5 %collective-permute-done.1 = bf16[8,128,128]{2,1,0:T(8,128)(2,1)S(1)} collective-permute-done((bf16[8,128,128]{2,1,0:T(8,128)(2,1)S(1)}, bf16[8,128,128]{2,1,0:T(8,128)(2,1)S(1)}, u32[]{:S(2)}, u32[]{:S(2)}) %collective-permute-start.1) | collective-permute-done | bytes 262176 | tf_op jit(solution)/shard_map/ppermute | solution.py:29
  14.7 1.8 %collective-permute-start.2 = (bf16[8,128,128]{2,1,0:T(8,128)(2,1)S(1)}, bf16[8,128,128]{2,1,0:T(8,128)(2,1)}, u32[]{:S(2)}, u32[]{:S(2)}) collective-permute-start(bf16[8,128,128]{2,1,0:T(8,128)(2,1)S(1)} %fusion.43), channel_id=1, source_target_pairs={{0,16},{4,20},{8,24},{12,28},{16,0},{20,4},{24,8},{28,12},{1,17},{... | collective-permute-start | bytes 786440 | tf_op jit(solution)/shard_map/ppermute | solution.py:29
  16.6 5.6 %fusion.26 = f32[1,512,8,128]{1,3,2,0:T(8,128)} fusion(f32[512,512]{1,0:T(8,128)S(1)} %fusion.35, bf16[512,8,128]{0,2,1:T(8,128)(2,1)S(1)} %bitcast.47, bf16[512,1024]{1,0:T(8,128)(2,1)} %param.7, bf16[512,1024]{1,0:T(8,128)(2,1)} %param.5), kind=kOutput, calls=%fused_computation.40 | convolution fusion | flops 1084227584 | bytes 6291456 | tf_op jit(solution)/shard_map/nhts,nshd->nthd/dot_general | solution.py:115
  22.7 1.1 fusion.42
  23.8 4.2 %multiply_reduce_fusion = (f32[512]{0:T(512)S(1)}, f32[1,512,8,128]{1,3,2,0:T(8,128)}) fusion(f32[1,512,8,128]{1,3,2,0:T(8,128)} %fusion.26, f32[8,128,128]{2,1,0:T(8,128)S(1)} %fusion.42, f32[8,128,128]{2,1,0:T(8,128)S(1)} %get-tuple-element.20, bf16[512,1024]{1,0:T(8,128)(2,1)} %param.5), kind=kOutput, calls=%fused_computation.38 | convolution fusion | flops 139329024 | bytes 6293504 | tf_op jit(solution)/shard_map/nthd,nhde->nthe/dot_general | solution.py:120
  28.0 2.0 %copy.11 = f32[512,1024]{1,0:T(8,128)S(1)} copy(f32[512,1024]{0,1:T(8,128)} %bitcast.45) | data formatting | bytes 4194304 | tf_op jit(solution)/shard_map/reshape | solution.py:121
  30.0 0.6 multiply_convert_fusion.3
  30.6 5.2 %fusion.4 = bf16[512,1536]{1,0:T(8,128)(2,1)} fusion(bf16[512,1024]{1,0:T(8,128)(2,1)S(1)} %multiply_convert_fusion.3, bf16[1024,6144]{1,0:T(8,128)(2,1)} %param.9, s32[]{:T(128)S(6)} %select_n.64), kind=kOutput, calls=%fused_computation.9 | convolution fusion | flops 1610612736 | bytes 5767172 | tf_op jit(solution)/shard_map/dot_general | solution.py:40
  35.8 3.5 %collective-permute-start.5 = (bf16[512,1536]{1,0:T(8,128)(2,1)}, bf16[512,1536]{1,0:T(8,128)(2,1)S(1)}, u32[]{:S(2)}, u32[]{:S(2)}) collective-permute-start(bf16[512,1536]{1,0:T(8,128)(2,1)} %fusion.4), channel_id=1, source_target_pairs={{0,1},{4,5},{8,9},{12,13},{16,17},{20,21},{24,25},{28,29}} | collective-permute-start | bytes 4718600 | tf_op jit(solution)/shard_map/ppermute | solution.py:85
  39.3 0.8 collective-permute-start.8
  40.2 31.7 %collective-permute-done.3 = f32[512]{0:T(512)S(1)} collective-permute-done((f32[512]{0:T(512)S(1)}, f32[512]{0:T(512)S(1)}, u32[]{:S(2)}, u32[]{:S(2)}) %collective-permute-start.3) | collective-permute-done | bytes 2080 | tf_op jit(solution)/shard_map/ppermute | solution.py:49
  71.9 4.2 %collective-permute-start.4 = (f32[512]{0:T(512)S(1)}, f32[512]{0:T(512)S(1)}, u32[]{:S(2)}, u32[]{:S(2)}) collective-permute-start(f32[512]{0:T(512)S(1)} %add.139), channel_id=1, source_target_pairs={{0,2},{1,3},{2,0},{3,1},{4,6},{5,7},{6,4},{7,5},{8,10},{9,11},{10,... | collective-permute-start | bytes 6152 | tf_op jit(solution)/shard_map/ppermute | solution.py:49
  76.1 4.0 %fusion.6 = f32[512,1536]{1,0:T(8,128)S(1)} fusion(bf16[512,1024]{1,0:T(8,128)(2,1)} %copy-done.1, bf16[1024,6144]{1,0:T(8,128)(2,1)} %param.9, s32[]{:T(128)S(6)} %select_n.62), kind=kOutput, calls=%fused_computation.11 | convolution fusion | flops 1610612736 | bytes 7340036 | tf_op jit(solution)/shard_map/dot_general | solution.py:40
  80.1 2.6 %add_convert_fusion.3 = (bf16[512,1536]{1,0:T(8,128)(2,1)}, bf16[512,1536]{1,0:T(8,128)(2,1)}) fusion(f32[512,1536]{1,0:T(8,128)S(1)} %fusion.6, bf16[512,1536]{1,0:T(8,128)(2,1)S(1)} %collective-permute-done.5, bf16[512,1536]{1,0:T(8,128)(2,1)S(1)} %collective-permute-done.8), kind=kLoop, calls=%fused_computation.8 | loop fusion | flops 4718592 | bytes 9437184 | tf_op jit(solution)/shard_map/convert_element_type | solution.py:85
  82.7 0.7 collective-permute-start.9
  83.5 2.3 %collective-permute-start.6 = (bf16[512,1536]{1,0:T(8,128)(2,1)}, bf16[512,1536]{1,0:T(8,128)(2,1)S(1)}, u32[]{:S(2)}, u32[]{:S(2)}) collective-permute-start(bf16[512,1536]{1,0:T(8,128)(2,1)} %get-tuple-element.17), channel_id=1, source_target_pairs={{0,1},{1,2},{4,5},{5,6},{8,9},{9,10},{12,13},{13,14},{16,17},{17,1... | collective-permute-start | bytes 4718600 | tf_op jit(solution)/shard_map/ppermute | solution.py:85
  85.8 4.1 %fusion.8 = f32[512,1536]{1,0:T(8,128)S(1)} fusion(bf16[512,1024]{1,0:T(8,128)(2,1)} %copy-done.1, bf16[1024,6144]{1,0:T(8,128)(2,1)} %param.9, s32[]{:T(128)S(6)} %select_n.60), kind=kOutput, calls=%fused_computation.13 | convolution fusion | flops 1610612736 | bytes 7340036 | tf_op jit(solution)/shard_map/dot_general | solution.py:40
  89.9 3.7 %fusion.10 = f32[512,1536]{1,0:T(8,128)S(1)} fusion(bf16[512,1024]{1,0:T(8,128)(2,1)S(1)} %copy-done.2, bf16[1024,6144]{1,0:T(8,128)(2,1)} %param.9, s32[]{:T(128)S(6)} %select_n.59), kind=kOutput, calls=%fused_computation.15 | convolution fusion | flops 1610612736 | bytes 7340036 | tf_op jit(solution)/shard_map/dot_general | solution.py:40
  93.6 1.7 %add_convert_fusion = bf16[512,1536]{1,0:T(8,128)(2,1)} fusion(f32[512,1536]{1,0:T(8,128)S(1)} %fusion.8, bf16[512,1536]{1,0:T(8,128)(2,1)S(1)} %collective-permute-done.9), kind=kLoop, calls=%fused_computation.5 | loop fusion | flops 2359296 | bytes 6291456 | tf_op jit(solution)/shard_map/convert_element_type | solution.py:86
  95.4 1.3 collective-permute-start.10
  96.7 20.3 %collective-permute-done.6 = bf16[512,1536]{1,0:T(8,128)(2,1)S(1)} collective-permute-done((bf16[512,1536]{1,0:T(8,128)(2,1)}, bf16[512,1536]{1,0:T(8,128)(2,1)S(1)}, u32[]{:S(2)}, u32[]{:S(2)}) %collective-permute-start.6) | collective-permute-done | bytes 1572896 | tf_op jit(solution)/shard_map/ppermute | solution.py:85
  117.0 1.7 %add_convert_fusion.2 = bf16[512,1536]{1,0:T(8,128)(2,1)} fusion(f32[512,1536]{1,0:T(8,128)S(1)} %fusion.10, bf16[512,1536]{1,0:T(8,128)(2,1)S(1)} %collective-permute-done.6), kind=kLoop, calls=%fused_computation.7 | loop fusion | flops 2359296 | bytes 6291456 | tf_op jit(solution)/shard_map/convert_element_type | solution.py:85
  118.7 6.7 %collective-permute-start.7 = (bf16[512,1536]{1,0:T(8,128)(2,1)}, bf16[512,1536]{1,0:T(8,128)(2,1)S(1)}, u32[]{:S(2)}, u32[]{:S(2)}) collective-permute-start(bf16[512,1536]{1,0:T(8,128)(2,1)} %add_convert_fusion.2), channel_id=1, source_target_pairs={{0,1},{1,2},{2,3},{4,5},{5,6},{6,7},{8,9},{9,10},{10,11},{12,13},{... | collective-permute-start | bytes 4718600 | tf_op jit(solution)/shard_map/ppermute | solution.py:85
  125.5 4.0 %fusion.12 = f32[512,1536]{1,0:T(8,128)S(1)} fusion(bf16[512,1024]{1,0:T(8,128)(2,1)} %copy-done.1, bf16[1024,6144]{1,0:T(8,128)(2,1)} %param.9, s32[]{:T(128)S(6)} %select_n.58), kind=kOutput, calls=%fused_computation.17 | convolution fusion | flops 1610612736 | bytes 7340036 | tf_op jit(solution)/shard_map/dot_general | solution.py:40
  129.5 23.5 %collective-permute-done.10 = bf16[512,1536]{1,0:T(8,128)(2,1)S(1)} collective-permute-done((bf16[512,1536]{1,0:T(8,128)(2,1)}, bf16[512,1536]{1,0:T(8,128)(2,1)S(1)}, u32[]{:S(2)}, u32[]{:S(2)}) %collective-permute-start.10) | collective-permute-done | bytes 1572896 | tf_op jit(solution)/shard_map/ppermute | solution.py:86
  152.9 3.0 %collective-permute-done.7 = bf16[512,1536]{1,0:T(8,128)(2,1)S(1)} collective-permute-done((bf16[512,1536]{1,0:T(8,128)(2,1)}, bf16[512,1536]{1,0:T(8,128)(2,1)S(1)}, u32[]{:S(2)}, u32[]{:S(2)}) %collective-permute-start.7) | collective-permute-done | bytes 1572896 | tf_op jit(solution)/shard_map/ppermute | solution.py:85
  156.0 1.8 %multiply_convert_fusion.2 = bf16[512,1536]{1,0:T(8,128)(2,1)} fusion(bf16[512,1536]{1,0:T(8,128)(2,1)S(1)} %collective-permute-done.10, f32[512,1536]{1,0:T(8,128)S(1)} %fusion.12, bf16[512,1536]{1,0:T(8,128)(2,1)S(1)} %collective-permute-done.7, f32[512]{0:T(512)S(1)} %add_rsqrt_fusion), kind=kLoop, calls=%fused_computation.4 | loop fusion | flops 4718592 | bytes 7866368 | tf_op jit(solution)/shard_map/convert_element_type | solution.py:127
  (21 shorter events, 1.4 us)
Async XLA Ops:
  0.0 2.5 %copy-start.3 = (bf16[512,1024]{1,0:T(8,128)(2,1)S(1)}, bf16[512,1024]{1,0:T(8,128)(2,1)}, u32[]{:S(2)}) copy-start(bf16[512,1024]{1,0:T(8,128)(2,1)} %param.7) | copy-start | bytes 3145732
  3.3 1.7 %collective-permute-start = (bf16[8,128,128]{2,1,0:T(8,128)(2,1)S(1)}, bf16[8,128,128]{2,1,0:T(8,128)(2,1)S(1)}, u32[]{:S(2)}, u32[]{:S(2)}) collective-permute-start(bf16[8,128,128]{2,1,0:T(8,128)(2,1)S(1)} %get-tuple-element.19), channel_id=1, source_target_pairs={{0,4},{4,0},{8,12},{12,8},{16,20},{20,16},{24,28},{28,24},{1,5},{5... | collective-permute-start | bytes 786440 | tf_op jit(solution)/shard_map/ppermute | solution.py:29
  5.1 9.5 %collective-permute-start.1 = (bf16[8,128,128]{2,1,0:T(8,128)(2,1)S(1)}, bf16[8,128,128]{2,1,0:T(8,128)(2,1)S(1)}, u32[]{:S(2)}, u32[]{:S(2)}) collective-permute-start(bf16[8,128,128]{2,1,0:T(8,128)(2,1)S(1)} %fusion.44), channel_id=1, source_target_pairs={{0,8},{4,12},{8,0},{12,4},{16,24},{20,28},{24,16},{28,20},{1,9},{5... | collective-permute-start | bytes 786440 | tf_op jit(solution)/shard_map/ppermute | solution.py:29
  14.7 7.9 %collective-permute-start.2 = (bf16[8,128,128]{2,1,0:T(8,128)(2,1)S(1)}, bf16[8,128,128]{2,1,0:T(8,128)(2,1)}, u32[]{:S(2)}, u32[]{:S(2)}) collective-permute-start(bf16[8,128,128]{2,1,0:T(8,128)(2,1)S(1)} %fusion.43), channel_id=1, source_target_pairs={{0,16},{4,20},{8,24},{12,28},{16,0},{20,4},{24,8},{28,12},{1,17},{... | collective-permute-start | bytes 786440 | tf_op jit(solution)/shard_map/ppermute | solution.py:29
  28.0 2.0 %copy-start = (bf16[512,1024]{1,0:T(8,128)(2,1)S(1)}, bf16[512,1024]{1,0:T(8,128)(2,1)}, u32[]{:S(2)}) copy-start(bf16[512,1024]{1,0:T(8,128)(2,1)} %param.8) | copy-start | bytes 3145732
  30.6 5.2 %copy-start.1 = (bf16[512,1024]{1,0:T(8,128)(2,1)}, bf16[512,1024]{1,0:T(8,128)(2,1)S(1)}, u32[]{:S(2)}) copy-start(bf16[512,1024]{1,0:T(8,128)(2,1)S(1)} %multiply_convert_fusion.3) | copy-start | bytes 3145732
  35.8 44.3 %collective-permute-start.5 = (bf16[512,1536]{1,0:T(8,128)(2,1)}, bf16[512,1536]{1,0:T(8,128)(2,1)S(1)}, u32[]{:S(2)}, u32[]{:S(2)}) collective-permute-start(bf16[512,1536]{1,0:T(8,128)(2,1)} %fusion.4), channel_id=1, source_target_pairs={{0,1},{4,5},{8,9},{12,13},{16,17},{20,21},{24,25},{28,29}} | collective-permute-start | bytes 4718600 | tf_op jit(solution)/shard_map/ppermute | solution.py:85
  39.3 40.8 %collective-permute-start.8 = (bf16[512,1536]{1,0:T(8,128)(2,1)}, bf16[512,1536]{1,0:T(8,128)(2,1)S(1)}, u32[]{:S(2)}, u32[]{:S(2)}) collective-permute-start(bf16[512,1536]{1,0:T(8,128)(2,1)} %fusion.4), channel_id=1, source_target_pairs={{3,2},{7,6},{11,10},{15,14},{19,18},{23,22},{27,26},{31,30}} | collective-permute-start | bytes 4718600 | tf_op jit(solution)/shard_map/ppermute | solution.py:86
  40.1 31.8 %collective-permute-start.3 = (f32[512]{0:T(512)S(1)}, f32[512]{0:T(512)S(1)}, u32[]{:S(2)}, u32[]{:S(2)}) collective-permute-start(f32[512]{0:T(512)S(1)} %get-tuple-element.21), channel_id=1, source_target_pairs={{0,1},{1,0},{2,3},{3,2},{4,5},{5,4},{6,7},{7,6},{8,9},{9,8},{10,11... | collective-permute-start | bytes 6152 | tf_op jit(solution)/shard_map/ppermute | solution.py:49
  71.9 8.2 %collective-permute-start.4 = (f32[512]{0:T(512)S(1)}, f32[512]{0:T(512)S(1)}, u32[]{:S(2)}, u32[]{:S(2)}) collective-permute-start(f32[512]{0:T(512)S(1)} %add.139), channel_id=1, source_target_pairs={{0,2},{1,3},{2,0},{3,1},{4,6},{5,7},{6,4},{7,5},{8,10},{9,11},{10,... | collective-permute-start | bytes 6152 | tf_op jit(solution)/shard_map/ppermute | solution.py:49
  82.7 10.9 %collective-permute-start.9 = (bf16[512,1536]{1,0:T(8,128)(2,1)}, bf16[512,1536]{1,0:T(8,128)(2,1)S(1)}, u32[]{:S(2)}, u32[]{:S(2)}) collective-permute-start(bf16[512,1536]{1,0:T(8,128)(2,1)} %get-tuple-element.18), channel_id=1, source_target_pairs={{2,1},{3,2},{6,5},{7,6},{10,9},{11,10},{14,13},{15,14},{18,17},{19... | collective-permute-start | bytes 4718600 | tf_op jit(solution)/shard_map/ppermute | solution.py:86
  83.5 33.5 %collective-permute-start.6 = (bf16[512,1536]{1,0:T(8,128)(2,1)}, bf16[512,1536]{1,0:T(8,128)(2,1)S(1)}, u32[]{:S(2)}, u32[]{:S(2)}) collective-permute-start(bf16[512,1536]{1,0:T(8,128)(2,1)} %get-tuple-element.17), channel_id=1, source_target_pairs={{0,1},{1,2},{4,5},{5,6},{8,9},{9,10},{12,13},{13,14},{16,17},{17,1... | collective-permute-start | bytes 4718600 | tf_op jit(solution)/shard_map/ppermute | solution.py:85
  85.8 4.1 %copy-start.2 = (bf16[512,1024]{1,0:T(8,128)(2,1)S(1)}, bf16[512,1024]{1,0:T(8,128)(2,1)}, u32[]{:S(2)}) copy-start(bf16[512,1024]{1,0:T(8,128)(2,1)} %copy-done.1) | copy-start | bytes 3145732
  95.4 57.6 %collective-permute-start.10 = (bf16[512,1536]{1,0:T(8,128)(2,1)}, bf16[512,1536]{1,0:T(8,128)(2,1)S(1)}, u32[]{:S(2)}, u32[]{:S(2)}) collective-permute-start(bf16[512,1536]{1,0:T(8,128)(2,1)} %add_convert_fusion), channel_id=1, source_target_pairs={{1,0},{2,1},{3,2},{5,4},{6,5},{7,6},{9,8},{10,9},{11,10},{13,12},{... | collective-permute-start | bytes 4718600 | tf_op jit(solution)/shard_map/ppermute | solution.py:86
  118.7 37.2 %collective-permute-start.7 = (bf16[512,1536]{1,0:T(8,128)(2,1)}, bf16[512,1536]{1,0:T(8,128)(2,1)S(1)}, u32[]{:S(2)}, u32[]{:S(2)}) collective-permute-start(bf16[512,1536]{1,0:T(8,128)(2,1)} %add_convert_fusion.2), channel_id=1, source_target_pairs={{0,1},{1,2},{2,3},{4,5},{5,6},{6,7},{8,9},{9,10},{10,11},{12,13},{... | collective-permute-start | bytes 4718600 | tf_op jit(solution)/shard_map/ppermute | solution.py:85

commit v8 on v7

--- a/solution.py
+++ b/solution.py
@@ -63,7 +63,7 @@
         if 2 * step <= count:
             shard = jnp.where(here < step, right_shard, left_shard)
             to_right = shard_product(gated, out_weight, shard, width)
-            if step == min(2, count - 1):
+            if step == 1:
                 to_right, total_squares = lax.optimization_barrier((to_right, total_squares))
             else:
                 to_right = lax.optimization_barrier(to_right)
@@ -71,7 +71,7 @@
         else:
             to_right = shard_product(gated, out_weight, right_shard, width)
             to_left = shard_product(gated, out_weight, left_shard, width)
-            if step == min(2, count - 1):
+            if step == 1:
                 to_right, to_left, total_squares = lax.optimization_barrier(
                     (to_right, to_left, total_squares)
                 )

time: 158 us -> 156 us (0.987)
  waiting for transfers between devices: 86.7 us -> 74.2 us
  starting transfers between devices: 25 us -> 33.6 us
  other arithmetic: 11.7 us -> 14.9 us
    ppermute x2, waiting for transfers between devices: 31.7 us -> 1.47 us  [butterfly_sum(): lax.ppermute(values, axis_name, [(i, i ^ bit) for i in range(count)])]
    ppermute x3, waiting for transfers between devices: 23.3 us -> 43.6 us  [line_reduce_scatter(): lax.ppermute(to_right.astype(jnp.bfloat16), axis_name, right_pairs)]
    ppermute x3, starting transfers between devices: 12.6 us -> 19.2 us  [line_reduce_scatter(): lax.ppermute(to_right.astype(jnp.bfloat16), axis_name, right_pairs)]
    ppermute x3, waiting for transfers between devices: 23.5 us -> 21 us  [line_reduce_scatter(): lax.ppermute(to_left.astype(jnp.bfloat16), axis_name, left_pairs)]
    ppermute x3, starting transfers between devices: 2.79 us -> 4.91 us  [line_reduce_scatter(): lax.ppermute(to_left.astype(jnp.bfloat16), axis_name, left_pairs)]
  transfers between devices with their start and end apart: 11 -> 11, of which waited for: 7 -> 8; matrix products, arithmetic and copies ran while one was open for 16% -> 20% of each run, Pallas kernels for 0% -> 0%
where the time goes in v8:
time: 156 us
  waiting for transfers between devices  74.2 us (48%)
  starting transfers between devices  33.6 us (22%)
  matrix products  30.1 us (19%)
  other arithmetic  14.9 us (10%)
  local copies, waits for them, and re-layouts  2.57 us (2%)
    ppermute x3, waiting for transfers between devices, line_reduce_scatter(): lax.ppermute(to_right.astype(jnp.bfloat16), axis_name, right_pairs)  43.6 us
    ppermute x3, waiting for transfers between devices, line_reduce_scatter(): lax.ppermute(to_left.astype(jnp.bfloat16), axis_name, left_pairs)  21 us
    dot_general x5, matrix products, shard_product(): return jnp.dot(gated, columns, preferred_element_type=jnp.float32)  19.4 us
    ppermute x3, starting transfers between devices, line_reduce_scatter(): lax.ppermute(to_right.astype(jnp.bfloat16), axis_name, right_pairs)  19.2 us
    ppermute x3, waiting for transfers between devices, exclusive_prefix(): arrived = lax.ppermute(group_total.astype(jnp.bfloat16), axis_name, pairs)  8.16 us
    dot_general x1, matrix products, body(): jnp.einsum('nhts,nshd->nthd', scores, active_v, preferred_element_type=jn...  5.6 us
    ppermute x3, starting transfers between devices, exclusive_prefix(): arrived = lax.ppermute(group_total.astype(jnp.bfloat16), axis_name, pairs)  5.3 us
    ppermute x3, starting transfers between devices, line_reduce_scatter(): lax.ppermute(to_left.astype(jnp.bfloat16), axis_name, left_pairs)  4.91 us
  transfers between devices with their start and end apart: 11, of which 8 were waited for; matrix products, arithmetic and copies ran while one was open for 20% of the time, Pallas kernels for 0%

profile of v8, /device:TPU:0, one launch (start us, length us, event | category | flops | bytes accessed | tf_op | source)
XLA Modules:
  0.0 155.5 jit_solution(4130874770035742472)
XLA Ops:
  0.0 1.9 %fusion.25 = bf16[512,1024]{1,0:T(8,128)(2,1)S(1)} fusion(bf16[512,1024]{1,0:T(8,128)(2,1)} %param.6), kind=kLoop, calls=%fused_computation.36 | loop fusion | flops 3145728 | bytes 2097152 | tf_op jit(solution)/shard_map/convert_element_type | solution.py:11
  2.5 0.8 fusion.50
  3.9 1.2 collective-permute-done
  5.1 2.9 %collective-permute-start.1 = (bf16[8,128,128]{2,1,0:T(8,128)(2,1)S(1)}, bf16[8,128,128]{2,1,0:T(8,128)(2,1)S(1)}, u32[]{:S(2)}, u32[]{:S(2)}) collective-permute-start(bf16[8,128,128]{2,1,0:T(8,128)(2,1)S(1)} %fusion.44), channel_id=1, source_target_pairs={{0,8},{4,12},{8,0},{12,4},{16,24},{20,28},{24,16},{28,20},{1,9},{5... | collective-permute-start | bytes 786440 | tf_op jit(solution)/shard_map/ppermute | solution.py:29
  8.2 6.5 %collective-permute-done.1 = bf16[8,128,128]{2,1,0:T(8,128)(2,1)S(1)} collective-permute-done((bf16[8,128,128]{2,1,0:T(8,128)(2,1)S(1)}, bf16[8,128,128]{2,1,0:T(8,128)(2,1)S(1)}, u32[]{:S(2)}, u32[]{:S(2)}) %collective-permute-start.1) | collective-permute-done | bytes 262176 | tf_op jit(solution)/shard_map/ppermute | solution.py:29
  14.7 1.8 %collective-permute-start.2 = (bf16[8,128,128]{2,1,0:T(8,128)(2,1)S(1)}, bf16[8,128,128]{2,1,0:T(8,128)(2,1)}, u32[]{:S(2)}, u32[]{:S(2)}) collective-permute-start(bf16[8,128,128]{2,1,0:T(8,128)(2,1)S(1)} %fusion.43), channel_id=1, source_target_pairs={{0,16},{4,20},{8,24},{12,28},{16,0},{20,4},{24,8},{28,12},{1,17},{... | collective-permute-start | bytes 786440 | tf_op jit(solution)/shard_map/ppermute | solution.py:29
  16.6 5.6 %fusion.26 = f32[1,512,8,128]{1,3,2,0:T(8,128)} fusion(f32[512,512]{1,0:T(8,128)S(1)} %fusion.35, bf16[512,8,128]{0,2,1:T(8,128)(2,1)S(1)} %bitcast.47, bf16[512,1024]{1,0:T(8,128)(2,1)} %param.7, bf16[512,1024]{1,0:T(8,128)(2,1)} %param.5), kind=kOutput, calls=%fused_computation.40 | convolution fusion | flops 1084227584 | bytes 6291456 | tf_op jit(solution)/shard_map/nhts,nshd->nthd/dot_general | solution.py:115
  22.7 1.1 fusion.42
  23.8 4.2 %multiply_reduce_fusion = (f32[512]{0:T(512)S(1)}, f32[1,512,8,128]{1,3,2,0:T(8,128)}) fusion(f32[1,512,8,128]{1,3,2,0:T(8,128)} %fusion.26, f32[8,128,128]{2,1,0:T(8,128)S(1)} %fusion.42, f32[8,128,128]{2,1,0:T(8,128)S(1)} %get-tuple-element.20, bf16[512,1024]{1,0:T(8,128)(2,1)} %param.5), kind=kOutput, calls=%fused_computation.38 | convolution fusion | flops 139329024 | bytes 6293504 | tf_op jit(solution)/shard_map/nthd,nhde->nthe/dot_general | solution.py:120
  28.0 2.0 %copy.11 = f32[512,1024]{1,0:T(8,128)S(1)} copy(f32[512,1024]{0,1:T(8,128)} %bitcast.45) | data formatting | bytes 4194304 | tf_op jit(solution)/shard_map/reshape | solution.py:121
  30.0 1.6 %collective-permute-start.3 = (f32[512]{0:T(512)S(1)}, f32[512]{0:T(512)S(1)}, u32[]{:S(2)}, u32[]{:S(2)}) collective-permute-start(f32[512]{0:T(512)S(1)} %get-tuple-element.21), channel_id=1, source_target_pairs={{0,1},{1,0},{2,3},{3,2},{4,5},{5,4},{6,7},{7,6},{8,9},{9,8},{10,11... | collective-permute-start | bytes 6152 | tf_op jit(solution)/shard_map/ppermute | solution.py:49
  32.2 1.5 collective-permute-done.3
  33.6 2.6 %collective-permute-start.4 = (f32[512]{0:T(512)S(1)}, f32[512]{0:T(512)S(1)}, u32[]{:S(2)}, u32[]{:S(2)}) collective-permute-start(f32[512]{0:T(512)S(1)} %add.141), channel_id=1, source_target_pairs={{0,2},{1,3},{2,0},{3,1},{4,6},{5,7},{6,4},{7,5},{8,10},{9,11},{10,... | collective-permute-start | bytes 6152 | tf_op jit(solution)/shard_map/ppermute | solution.py:49
  36.2 3.7 %fusion.4 = bf16[512,1536]{1,0:T(8,128)(2,1)S(1)} fusion(bf16[512,1024]{1,0:T(8,128)(2,1)S(1)} %multiply_convert_fusion.3, bf16[1024,6144]{1,0:T(8,128)(2,1)} %param.9, s32[]{:T(128)S(6)} %select_n.64), kind=kOutput, calls=%fused_computation.9 | convolution fusion | flops 1610612736 | bytes 5767172 | tf_op jit(solution)/shard_map/dot_general | solution.py:40
  39.9 4.7 %collective-permute-start.5 = (bf16[512,1536]{1,0:T(8,128)(2,1)S(1)}, bf16[512,1536]{1,0:T(8,128)(2,1)}, u32[]{:S(2)}, u32[]{:S(2)}) collective-permute-start(bf16[512,1536]{1,0:T(8,128)(2,1)S(1)} %fusion.4), channel_id=1, source_target_pairs={{0,1},{4,5},{8,9},{12,13},{16,17},{20,21},{24,25},{28,29}} | collective-permute-start | bytes 4718600 | tf_op jit(solution)/shard_map/ppermute | solution.py:85
  44.6 1.8 %collective-permute-start.8 = (bf16[512,1536]{1,0:T(8,128)(2,1)S(1)}, bf16[512,1536]{1,0:T(8,128)(2,1)}, u32[]{:S(2)}, u32[]{:S(2)}) collective-permute-start(bf16[512,1536]{1,0:T(8,128)(2,1)S(1)} %fusion.4), channel_id=1, source_target_pairs={{3,2},{7,6},{11,10},{15,14},{19,18},{23,22},{27,26},{31,30}} | collective-permute-start | bytes 4718600 | tf_op jit(solution)/shard_map/ppermute | solution.py:86
  46.4 4.0 %fusion.6 = f32[512,1536]{1,0:T(8,128)S(1)} fusion(bf16[512,1024]{1,0:T(8,128)(2,1)} %copy-done.1, bf16[1024,6144]{1,0:T(8,128)(2,1)} %param.9, s32[]{:T(128)S(6)} %select_n.62), kind=kOutput, calls=%fused_computation.11 | convolution fusion | flops 1610612736 | bytes 7340036 | tf_op jit(solution)/shard_map/dot_general | solution.py:40
  50.4 23.9 %collective-permute-done.5 = bf16[512,1536]{1,0:T(8,128)(2,1)} collective-permute-done((bf16[512,1536]{1,0:T(8,128)(2,1)S(1)}, bf16[512,1536]{1,0:T(8,128)(2,1)}, u32[]{:S(2)}, u32[]{:S(2)}) %collective-permute-start.5) | collective-permute-done | bytes 1572896 | tf_op jit(solution)/shard_map/ppermute | solution.py:85
  74.3 2.8 %add_convert_fusion.3 = (bf16[512,1536]{1,0:T(8,128)(2,1)S(1)}, bf16[512,1536]{1,0:T(8,128)(2,1)S(1)}) fusion(f32[512,1536]{1,0:T(8,128)S(1)} %fusion.6, bf16[512,1536]{1,0:T(8,128)(2,1)} %collective-permute-done.5, bf16[512,1536]{1,0:T(8,128)(2,1)} %collective-permute-done.8), kind=kLoop, calls=%fused_computation.8 | loop fusion | flops 4718592 | bytes 9437184 | tf_op jit(solution)/shard_map/convert_element_type | solution.py:85
  77.1 1.8 %collective-permute-start.9 = (bf16[512,1536]{1,0:T(8,128)(2,1)S(1)}, bf16[512,1536]{1,0:T(8,128)(2,1)}, u32[]{:S(2)}, u32[]{:S(2)}) collective-permute-start(bf16[512,1536]{1,0:T(8,128)(2,1)S(1)} %get-tuple-element.18), channel_id=1, source_target_pairs={{2,1},{3,2},{6,5},{7,6},{10,9},{11,10},{14,13},{15,14},{18,17},{19... | collective-permute-start | bytes 4718600 | tf_op jit(solution)/shard_map/ppermute | solution.py:86
  78.9 5.1 %collective-permute-start.6 = (bf16[512,1536]{1,0:T(8,128)(2,1)S(1)}, bf16[512,1536]{1,0:T(8,128)(2,1)}, u32[]{:S(2)}, u32[]{:S(2)}) collective-permute-start(bf16[512,1536]{1,0:T(8,128)(2,1)S(1)} %get-tuple-element.17), channel_id=1, source_target_pairs={{0,1},{1,2},{4,5},{5,6},{8,9},{9,10},{12,13},{13,14},{16,17},{17,1... | collective-permute-start | bytes 4718600 | tf_op jit(solution)/shard_map/ppermute | solution.py:85
  84.0 4.1 %fusion.8 = f32[512,1536]{1,0:T(8,128)S(1)} fusion(bf16[512,1024]{1,0:T(8,128)(2,1)} %copy-done.1, bf16[1024,6144]{1,0:T(8,128)(2,1)} %param.9, s32[]{:T(128)S(6)} %select_n.60), kind=kOutput, calls=%fused_computation.13 | convolution fusion | flops 1610612736 | bytes 7340036 | tf_op jit(solution)/shard_map/dot_general | solution.py:40
  88.1 3.7 %fusion.10 = f32[512,1536]{1,0:T(8,128)S(1)} fusion(bf16[512,1024]{1,0:T(8,128)(2,1)S(1)} %copy-done.2, bf16[1024,6144]{1,0:T(8,128)(2,1)} %param.9, s32[]{:T(128)S(6)} %select_n.59), kind=kOutput, calls=%fused_computation.15 | convolution fusion | flops 1610612736 | bytes 7340036 | tf_op jit(solution)/shard_map/dot_general | solution.py:40
  91.8 3.1 %add_convert_fusion = bf16[512,1536]{1,0:T(8,128)(2,1)} fusion(f32[512,1536]{1,0:T(8,128)S(1)} %fusion.8, bf16[512,1536]{1,0:T(8,128)(2,1)} %collective-permute-done.9), kind=kLoop, calls=%fused_computation.5 | loop fusion | flops 2359296 | bytes 6291456 | tf_op jit(solution)/shard_map/convert_element_type | solution.py:86
  94.9 1.3 collective-permute-start.10
  96.2 16.7 %collective-permute-done.6 = bf16[512,1536]{1,0:T(8,128)(2,1)} collective-permute-done((bf16[512,1536]{1,0:T(8,128)(2,1)S(1)}, bf16[512,1536]{1,0:T(8,128)(2,1)}, u32[]{:S(2)}, u32[]{:S(2)}) %collective-permute-start.6) | collective-permute-done | bytes 1572896 | tf_op jit(solution)/shard_map/ppermute | solution.py:85
  112.9 2.0 %add_convert_fusion.2 = bf16[512,1536]{1,0:T(8,128)(2,1)S(1)} fusion(f32[512,1536]{1,0:T(8,128)S(1)} %fusion.10, bf16[512,1536]{1,0:T(8,128)(2,1)} %collective-permute-done.6), kind=kLoop, calls=%fused_computation.7 | loop fusion | flops 2359296 | bytes 6291456 | tf_op jit(solution)/shard_map/convert_element_type | solution.py:85
  114.9 9.4 %collective-permute-start.7 = (bf16[512,1536]{1,0:T(8,128)(2,1)S(1)}, bf16[512,1536]{1,0:T(8,128)(2,1)}, u32[]{:S(2)}, u32[]{:S(2)}) collective-permute-start(bf16[512,1536]{1,0:T(8,128)(2,1)S(1)} %add_convert_fusion.2), channel_id=1, source_target_pairs={{0,1},{1,2},{2,3},{4,5},{5,6},{6,7},{8,9},{9,10},{10,11},{12,13},{... | collective-permute-start | bytes 4718600 | tf_op jit(solution)/shard_map/ppermute | solution.py:85
  124.3 4.0 %fusion.12 = f32[512,1536]{1,0:T(8,128)S(1)} fusion(bf16[512,1024]{1,0:T(8,128)(2,1)} %copy-done.1, bf16[1024,6144]{1,0:T(8,128)(2,1)} %param.9, s32[]{:T(128)S(6)} %select_n.58), kind=kOutput, calls=%fused_computation.17 | convolution fusion | flops 1610612736 | bytes 7340036 | tf_op jit(solution)/shard_map/dot_general | solution.py:40
  128.3 21.0 %collective-permute-done.10 = bf16[512,1536]{1,0:T(8,128)(2,1)S(1)} collective-permute-done((bf16[512,1536]{1,0:T(8,128)(2,1)}, bf16[512,1536]{1,0:T(8,128)(2,1)S(1)}, u32[]{:S(2)}, u32[]{:S(2)}) %collective-permute-start.10) | collective-permute-done | bytes 1572896 | tf_op jit(solution)/shard_map/ppermute | solution.py:86
  149.3 3.0 %collective-permute-done.7 = bf16[512,1536]{1,0:T(8,128)(2,1)} collective-permute-done((bf16[512,1536]{1,0:T(8,128)(2,1)S(1)}, bf16[512,1536]{1,0:T(8,128)(2,1)}, u32[]{:S(2)}, u32[]{:S(2)}) %collective-permute-start.7) | collective-permute-done | bytes 1572896 | tf_op jit(solution)/shard_map/ppermute | solution.py:85
  152.3 3.2 %multiply_convert_fusion.2 = bf16[512,1536]{1,0:T(8,128)(2,1)} fusion(bf16[512,1536]{1,0:T(8,128)(2,1)S(1)} %collective-permute-done.10, f32[512,1536]{1,0:T(8,128)S(1)} %fusion.12, bf16[512,1536]{1,0:T(8,128)(2,1)} %collective-permute-done.7, f32[512]{0:T(512)S(1)} %add_rsqrt_fusion), kind=kLoop, calls=%fused_computation.4 | loop fusion | flops 4718592 | bytes 7866368 | tf_op jit(solution)/shard_map/convert_element_type | solution.py:127
  (21 shorter events, 2.5 us)
Async XLA Ops:
  0.0 2.5 %copy-start.3 = (bf16[512,1024]{1,0:T(8,128)(2,1)S(1)}, bf16[512,1024]{1,0:T(8,128)(2,1)}, u32[]{:S(2)}) copy-start(bf16[512,1024]{1,0:T(8,128)(2,1)} %param.7) | copy-start | bytes 3145732
  3.3 1.7 %collective-permute-start = (bf16[8,128,128]{2,1,0:T(8,128)(2,1)S(1)}, bf16[8,128,128]{2,1,0:T(8,128)(2,1)S(1)}, u32[]{:S(2)}, u32[]{:S(2)}) collective-permute-start(bf16[8,128,128]{2,1,0:T(8,128)(2,1)S(1)} %get-tuple-element.19), channel_id=1, source_target_pairs={{0,4},{4,0},{8,12},{12,8},{16,20},{20,16},{24,28},{28,24},{1,5},{5... | collective-permute-start | bytes 786440 | tf_op jit(solution)/shard_map/ppermute | solution.py:29
  5.1 9.5 %collective-permute-start.1 = (bf16[8,128,128]{2,1,0:T(8,128)(2,1)S(1)}, bf16[8,128,128]{2,1,0:T(8,128)(2,1)S(1)}, u32[]{:S(2)}, u32[]{:S(2)}) collective-permute-start(bf16[8,128,128]{2,1,0:T(8,128)(2,1)S(1)} %fusion.44), channel_id=1, source_target_pairs={{0,8},{4,12},{8,0},{12,4},{16,24},{20,28},{24,16},{28,20},{1,9},{5... | collective-permute-start | bytes 786440 | tf_op jit(solution)/shard_map/ppermute | solution.py:29
  14.7 7.9 %collective-permute-start.2 = (bf16[8,128,128]{2,1,0:T(8,128)(2,1)S(1)}, bf16[8,128,128]{2,1,0:T(8,128)(2,1)}, u32[]{:S(2)}, u32[]{:S(2)}) collective-permute-start(bf16[8,128,128]{2,1,0:T(8,128)(2,1)S(1)} %fusion.43), channel_id=1, source_target_pairs={{0,16},{4,20},{8,24},{12,28},{16,0},{20,4},{24,8},{28,12},{1,17},{... | collective-permute-start | bytes 786440 | tf_op jit(solution)/shard_map/ppermute | solution.py:29
  28.0 3.6 %copy-start = (bf16[512,1024]{1,0:T(8,128)(2,1)S(1)}, bf16[512,1024]{1,0:T(8,128)(2,1)}, u32[]{:S(2)}) copy-start(bf16[512,1024]{1,0:T(8,128)(2,1)} %param.8) | copy-start | bytes 3145732
  30.0 3.7 %collective-permute-start.3 = (f32[512]{0:T(512)S(1)}, f32[512]{0:T(512)S(1)}, u32[]{:S(2)}, u32[]{:S(2)}) collective-permute-start(f32[512]{0:T(512)S(1)} %get-tuple-element.21), channel_id=1, source_target_pairs={{0,1},{1,0},{2,3},{3,2},{4,5},{5,4},{6,7},{7,6},{8,9},{9,8},{10,11... | collective-permute-start | bytes 6152 | tf_op jit(solution)/shard_map/ppermute | solution.py:49
  32.2 4.0 %copy-start.1 = (bf16[512,1024]{1,0:T(8,128)(2,1)}, bf16[512,1024]{1,0:T(8,128)(2,1)S(1)}, u32[]{:S(2)}) copy-start(bf16[512,1024]{1,0:T(8,128)(2,1)S(1)} %multiply_convert_fusion.3) | copy-start | bytes 3145732
  33.6 6.2 %collective-permute-start.4 = (f32[512]{0:T(512)S(1)}, f32[512]{0:T(512)S(1)}, u32[]{:S(2)}, u32[]{:S(2)}) collective-permute-start(f32[512]{0:T(512)S(1)} %add.141), channel_id=1, source_target_pairs={{0,2},{1,3},{2,0},{3,1},{4,6},{5,7},{6,4},{7,5},{8,10},{9,11},{10,... | collective-permute-start | bytes 6152 | tf_op jit(solution)/shard_map/ppermute | solution.py:49
  39.9 34.4 %collective-permute-start.5 = (bf16[512,1536]{1,0:T(8,128)(2,1)S(1)}, bf16[512,1536]{1,0:T(8,128)(2,1)}, u32[]{:S(2)}, u32[]{:S(2)}) collective-permute-start(bf16[512,1536]{1,0:T(8,128)(2,1)S(1)} %fusion.4), channel_id=1, source_target_pairs={{0,1},{4,5},{8,9},{12,13},{16,17},{20,21},{24,25},{28,29}} | collective-permute-start | bytes 4718600 | tf_op jit(solution)/shard_map/ppermute | solution.py:85
  44.6 29.7 %collective-permute-start.8 = (bf16[512,1536]{1,0:T(8,128)(2,1)S(1)}, bf16[512,1536]{1,0:T(8,128)(2,1)}, u32[]{:S(2)}, u32[]{:S(2)}) collective-permute-start(bf16[512,1536]{1,0:T(8,128)(2,1)S(1)} %fusion.4), channel_id=1, source_target_pairs={{3,2},{7,6},{11,10},{15,14},{19,18},{23,22},{27,26},{31,30}} | collective-permute-start | bytes 4718600 | tf_op jit(solution)/shard_map/ppermute | solution.py:86
  77.1 14.7 %collective-permute-start.9 = (bf16[512,1536]{1,0:T(8,128)(2,1)S(1)}, bf16[512,1536]{1,0:T(8,128)(2,1)}, u32[]{:S(2)}, u32[]{:S(2)}) collective-permute-start(bf16[512,1536]{1,0:T(8,128)(2,1)S(1)} %get-tuple-element.18), channel_id=1, source_target_pairs={{2,1},{3,2},{6,5},{7,6},{10,9},{11,10},{14,13},{15,14},{18,17},{19... | collective-permute-start | bytes 4718600 | tf_op jit(solution)/shard_map/ppermute | solution.py:86
  78.9 34.0 %collective-permute-start.6 = (bf16[512,1536]{1,0:T(8,128)(2,1)S(1)}, bf16[512,1536]{1,0:T(8,128)(2,1)}, u32[]{:S(2)}, u32[]{:S(2)}) collective-permute-start(bf16[512,1536]{1,0:T(8,128)(2,1)S(1)} %get-tuple-element.17), channel_id=1, source_target_pairs={{0,1},{1,2},{4,5},{5,6},{8,9},{9,10},{12,13},{13,14},{16,17},{17,1... | collective-permute-start | bytes 4718600 | tf_op jit(solution)/shard_map/ppermute | solution.py:85
  84.0 4.1 %copy-start.2 = (bf16[512,1024]{1,0:T(8,128)(2,1)S(1)}, bf16[512,1024]{1,0:T(8,128)(2,1)}, u32[]{:S(2)}) copy-start(bf16[512,1024]{1,0:T(8,128)(2,1)} %copy-done.1) | copy-start | bytes 3145732
  94.9 54.4 %collective-permute-start.10 = (bf16[512,1536]{1,0:T(8,128)(2,1)}, bf16[512,1536]{1,0:T(8,128)(2,1)S(1)}, u32[]{:S(2)}, u32[]{:S(2)}) collective-permute-start(bf16[512,1536]{1,0:T(8,128)(2,1)} %add_convert_fusion), channel_id=1, source_target_pairs={{1,0},{2,1},{3,2},{5,4},{6,5},{7,6},{9,8},{10,9},{11,10},{13,12},{... | collective-permute-start | bytes 4718600 | tf_op jit(solution)/shard_map/ppermute | solution.py:86
  114.9 37.4 %collective-permute-start.7 = (bf16[512,1536]{1,0:T(8,128)(2,1)S(1)}, bf16[512,1536]{1,0:T(8,128)(2,1)}, u32[]{:S(2)}, u32[]{:S(2)}) collective-permute-start(bf16[512,1536]{1,0:T(8,128)(2,1)S(1)} %add_convert_fusion.2), channel_id=1, source_target_pairs={{0,1},{1,2},{2,3},{4,5},{5,6},{6,7},{8,9},{9,10},{10,11},{12,13},{... | collective-permute-start | bytes 4718600 | tf_op jit(solution)/shard_map/ppermute | solution.py:85

commit v9 on v8

--- a/solution.py
+++ b/solution.py
@@ -11,7 +11,7 @@
     return jax.nn.silu(raw_input.astype(jnp.float32)).astype(jnp.bfloat16)
 
 
-def exclusive_prefix(span_total, axis_name):
+def exclusive_prefix(span_total, axis_name, companion):
     count = lax.axis_size(axis_name)
     my_index = lax.axis_index(axis_name)
     if count & (count - 1):
@@ -20,11 +20,13 @@
         ).astype(jnp.float32)
         positions = jnp.arange(count, dtype=jnp.int32)
         weights = (positions < my_index).astype(jnp.float32)
-        return jnp.sum(shards * weights[:, None, None, None], axis=0)
+        return jnp.sum(shards * weights[:, None, None, None], axis=0), companion
     group_total = span_total
     prefix = jnp.zeros_like(span_total)
     bit = 1
     while bit < count:
+        if bit * 2 == count and bit > 1:
+            group_total, companion = lax.optimization_barrier((group_total, companion))
         pairs = [(i, i ^ bit) for i in range(count)]
         arrived = lax.ppermute(group_total.astype(jnp.bfloat16), axis_name, pairs)
         arrived = arrived.astype(jnp.float32)
@@ -32,7 +34,7 @@
         prefix = prefix + upper * arrived
         group_total = group_total + arrived
         bit *= 2
-    return prefix
+    return prefix, companion
 
 
 def shard_product(gated, out_weight, shard, width):
@@ -108,13 +110,13 @@
     )
     span_total = jnp.sum(block_states, axis=0)
     earlier_local = jnp.cumsum(block_states, axis=0) - block_states
-    prefix = exclusive_prefix(span_total, "seq")
     causal_mask = jnp.tril(jnp.ones((block_rows, block_rows), jnp.float32))
     scores = jnp.einsum("nthd,nshd->nhts", active_q, active_k, preferred_element_type=jnp.float32)
     scores = (scores * causal_mask).astype(jnp.bfloat16)
     within_block = jnp.einsum(
         "nhts,nshd->nthd", scores, active_v, preferred_element_type=jnp.float32
     )
+    prefix, within_block = exclusive_prefix(span_total, "seq", within_block)
     within_block, prefix = lax.optimization_barrier((within_block, prefix))
     before = (prefix[None] + earlier_local).astype(jnp.bfloat16)
     from_state = jnp.einsum("nthd,nhde->nthe", active_q, before, preferred_element_type=jnp.float32)

time: 156 us -> 155 us (level)
  no operation moved by 1% of the time
where the time goes in v9:
time: 155 us
  waiting for transfers between devices  73 us (47%)
  starting transfers between devices  33.6 us (22%)
  matrix products  29.2 us (19%)
  other arithmetic  15.6 us (10%)
  local copies, waits for them, and re-layouts  3.11 us (2%)
    ppermute x3, waiting for transfers between devices, line_reduce_scatter(): lax.ppermute(to_right.astype(jnp.bfloat16), axis_name, right_pairs)  43.4 us
    ppermute x3, waiting for transfers between devices, line_reduce_scatter(): lax.ppermute(to_left.astype(jnp.bfloat16), axis_name, left_pairs)  20.9 us
    dot_general x5, matrix products, shard_product(): return jnp.dot(gated, columns, preferred_element_type=jnp.float32)  19.4 us
    ppermute x3, starting transfers between devices, line_reduce_scatter(): lax.ppermute(to_right.astype(jnp.bfloat16), axis_name, right_pairs)  19.2 us
    ppermute x3, waiting for transfers between devices, exclusive_prefix(): arrived = lax.ppermute(group_total.astype(jnp.bfloat16), axis_name, pairs)  7.25 us
    dot_general x1, matrix products, body(): jnp.einsum('nhts,nshd->nthd', scores, active_v, preferred_element_type=jn...  5.43 us
    ppermute x3, starting transfers between devices, exclusive_prefix(): arrived = lax.ppermute(group_total.astype(jnp.bfloat16), axis_name, pairs)  5.3 us
    ppermute x3, starting transfers between devices, line_reduce_scatter(): lax.ppermute(to_left.astype(jnp.bfloat16), axis_name, left_pairs)  4.93 us
  transfers between devices with their start and end apart: 11, of which 8 were waited for; matrix products, arithmetic and copies ran while one was open for 20% of the time, Pallas kernels for 0%

profile of v9, /device:TPU:0, one launch (start us, length us, event | category | flops | bytes accessed | tf_op | source)
XLA Modules:
  0.0 154.6 jit_solution(4289470907032853268)
XLA Ops:
  0.0 1.9 %fusion.17 = bf16[512,1024]{1,0:T(8,128)(2,1)S(1)} fusion(bf16[512,1024]{1,0:T(8,128)(2,1)} %param.6), kind=kLoop, calls=%fused_computation.28 | loop fusion | flops 3145728 | bytes 2097152 | tf_op jit(solution)/shard_map/convert_element_type | solution.py:11
  2.5 0.6 fusion.21
  4.7 1.1 fusion.31
  5.9 2.9 %collective-permute-start.1 = (bf16[8,128,128]{2,1,0:T(8,128)(2,1)S(1)}, bf16[8,128,128]{2,1,0:T(8,128)(2,1)S(1)}, u32[]{:S(2)}, u32[]{:S(2)}) collective-permute-start(bf16[8,128,128]{2,1,0:T(8,128)(2,1)S(1)} %fusion.37), channel_id=1, source_target_pairs={{0,8},{4,12},{8,0},{12,4},{16,24},{20,28},{24,16},{28,20},{1,9},{5... | collective-permute-start | bytes 786440 | tf_op jit(solution)/shard_map/ppermute | solution.py:31
  8.8 5.4 %fusion.26 = f32[1,512,8,128]{1,3,2,0:T(8,128)} fusion(bf16[512,8,128]{0,2,1:T(8,128)(2,1)S(1)} %bitcast.38, f32[512,512]{1,0:T(8,128)} %fusion.31, bf16[512,8,128]{0,2,1:T(8,128)(2,1)S(1)} %bitcast.36, bf16[512,1024]{1,0:T(8,128)(2,1)} %param.5), kind=kOutput, calls=%fused_computation.40 | convolution fusion | flops 1081081856 | bytes 6291456 | tf_op jit(solution)/shard_map/nhts,nshd->nthd/dot_general | solution.py:116
  14.2 1.2 collective-permute-done.1
  15.5 1.8 %collective-permute-start.2 = (bf16[8,128,128]{2,1,0:T(8,128)(2,1)S(1)}, bf16[8,128,128]{2,1,0:T(8,128)(2,1)S(1)}, u32[]{:S(2)}, u32[]{:S(2)}) collective-permute-start(bf16[8,128,128]{2,1,0:T(8,128)(2,1)S(1)} %convert_add_fusion), channel_id=1, source_target_pairs={{0,16},{4,20},{8,24},{12,28},{16,0},{20,4},{24,8},{28,12},{1,17},{... | collective-permute-start | bytes 786440 | tf_op jit(solution)/shard_map/ppermute | solution.py:31
  17.3 6.0 %collective-permute-done.2 = bf16[8,128,128]{2,1,0:T(8,128)(2,1)S(1)} collective-permute-done((bf16[8,128,128]{2,1,0:T(8,128)(2,1)S(1)}, bf16[8,128,128]{2,1,0:T(8,128)(2,1)S(1)}, u32[]{:S(2)}, u32[]{:S(2)}) %collective-permute-start.2) | collective-permute-done | bytes 262176 | tf_op jit(solution)/shard_map/ppermute | solution.py:31
  23.5 3.9 %multiply_reduce_fusion = (f32[512]{0:T(512)S(1)}, f32[1,512,8,128]{1,3,2,0:T(8,128)}) fusion(f32[1,512,8,128]{1,3,2,0:T(8,128)} %fusion.26, f32[8,128,128]{2,1,0:T(8,128)S(1)} %fusion.36, f32[8,128,128]{2,1,0:T(8,128)S(1)} %get-tuple-element.24, bf16[512,1024]{1,0:T(8,128)(2,1)S(1)} %copy-done.4), kind=kOutput, calls=%fused_computation.38 | convolution fusion | flops 139329024 | bytes 6293504 | tf_op jit(solution)/shard_map/nthd,nhde->nthe/dot_general | solution.py:122
  27.4 2.0 %copy.11 = f32[512,1024]{1,0:T(8,128)S(1)} copy(f32[512,1024]{0,1:T(8,128)} %bitcast.39) | data formatting | bytes 4194304 | tf_op jit(solution)/shard_map/reshape | solution.py:123
  29.4 1.6 %collective-permute-start.3 = (f32[512]{0:T(512)S(1)}, f32[512]{0:T(512)S(1)}, u32[]{:S(2)}, u32[]{:S(2)}) collective-permute-start(f32[512]{0:T(512)S(1)} %get-tuple-element.25), channel_id=1, source_target_pairs={{0,1},{1,0},{2,3},{3,2},{4,5},{5,4},{6,7},{7,6},{8,9},{9,8},{10,11... | collective-permute-start | bytes 6152 | tf_op jit(solution)/shard_map/ppermute | solution.py:51
  31.6 1.5 collective-permute-done.3
  33.0 2.6 %collective-permute-start.4 = (f32[512]{0:T(512)S(1)}, f32[512]{0:T(512)S(1)}, u32[]{:S(2)}, u32[]{:S(2)}) collective-permute-start(f32[512]{0:T(512)S(1)} %add.141), channel_id=1, source_target_pairs={{0,2},{1,3},{2,0},{3,1},{4,6},{5,7},{6,4},{7,5},{8,10},{9,11},{10,... | collective-permute-start | bytes 6152 | tf_op jit(solution)/shard_map/ppermute | solution.py:51
  35.6 3.7 %fusion.4 = bf16[512,1536]{1,0:T(8,128)(2,1)S(1)} fusion(bf16[512,1024]{1,0:T(8,128)(2,1)S(1)} %multiply_convert_fusion.3, bf16[1024,6144]{1,0:T(8,128)(2,1)} %param.9, s32[]{:T(128)S(6)} %select_n.64), kind=kOutput, calls=%fused_computation.9 | convolution fusion | flops 1610612736 | bytes 5767172 | tf_op jit(solution)/shard_map/dot_general | solution.py:42
  39.3 4.7 %collective-permute-start.5 = (bf16[512,1536]{1,0:T(8,128)(2,1)S(1)}, bf16[512,1536]{1,0:T(8,128)(2,1)}, u32[]{:S(2)}, u32[]{:S(2)}) collective-permute-start(bf16[512,1536]{1,0:T(8,128)(2,1)S(1)} %fusion.4), channel_id=1, source_target_pairs={{0,1},{4,5},{8,9},{12,13},{16,17},{20,21},{24,25},{28,29}} | collective-permute-start | bytes 4718600 | tf_op jit(solution)/shard_map/ppermute | solution.py:87
  44.0 1.8 %collective-permute-start.8 = (bf16[512,1536]{1,0:T(8,128)(2,1)S(1)}, bf16[512,1536]{1,0:T(8,128)(2,1)}, u32[]{:S(2)}, u32[]{:S(2)}) collective-permute-start(bf16[512,1536]{1,0:T(8,128)(2,1)S(1)} %fusion.4), channel_id=1, source_target_pairs={{3,2},{7,6},{11,10},{15,14},{19,18},{23,22},{27,26},{31,30}} | collective-permute-start | bytes 4718600 | tf_op jit(solution)/shard_map/ppermute | solution.py:88
  45.8 4.0 %fusion.6 = f32[512,1536]{1,0:T(8,128)S(1)} fusion(bf16[512,1024]{1,0:T(8,128)(2,1)} %copy-done.2, bf16[1024,6144]{1,0:T(8,128)(2,1)} %param.9, s32[]{:T(128)S(6)} %select_n.62), kind=kOutput, calls=%fused_computation.11 | convolution fusion | flops 1610612736 | bytes 7340036 | tf_op jit(solution)/shard_map/dot_general | solution.py:42
  49.8 23.8 %collective-permute-done.5 = bf16[512,1536]{1,0:T(8,128)(2,1)} collective-permute-done((bf16[512,1536]{1,0:T(8,128)(2,1)S(1)}, bf16[512,1536]{1,0:T(8,128)(2,1)}, u32[]{:S(2)}, u32[]{:S(2)}) %collective-permute-start.5) | collective-permute-done | bytes 1572896 | tf_op jit(solution)/shard_map/ppermute | solution.py:87
  73.6 2.8 %add_convert_fusion.3 = (bf16[512,1536]{1,0:T(8,128)(2,1)S(1)}, bf16[512,1536]{1,0:T(8,128)(2,1)S(1)}) fusion(f32[512,1536]{1,0:T(8,128)S(1)} %fusion.6, bf16[512,1536]{1,0:T(8,128)(2,1)} %collective-permute-done.5, bf16[512,1536]{1,0:T(8,128)(2,1)} %collective-permute-done.8), kind=kLoop, calls=%fused_computation.8 | loop fusion | flops 4718592 | bytes 9437184 | tf_op jit(solution)/shard_map/convert_element_type | solution.py:87
  76.3 1.8 %collective-permute-start.9 = (bf16[512,1536]{1,0:T(8,128)(2,1)S(1)}, bf16[512,1536]{1,0:T(8,128)(2,1)}, u32[]{:S(2)}, u32[]{:S(2)}) collective-permute-start(bf16[512,1536]{1,0:T(8,128)(2,1)S(1)} %get-tuple-element.22), channel_id=1, source_target_pairs={{2,1},{3,2},{6,5},{7,6},{10,9},{11,10},{14,13},{15,14},{18,17},{19... | collective-permute-start | bytes 4718600 | tf_op jit(solution)/shard_map/ppermute | solution.py:88
  78.2 5.1 %collective-permute-start.6 = (bf16[512,1536]{1,0:T(8,128)(2,1)S(1)}, bf16[512,1536]{1,0:T(8,128)(2,1)}, u32[]{:S(2)}, u32[]{:S(2)}) collective-permute-start(bf16[512,1536]{1,0:T(8,128)(2,1)S(1)} %get-tuple-element.21), channel_id=1, source_target_pairs={{0,1},{1,2},{4,5},{5,6},{8,9},{9,10},{12,13},{13,14},{16,17},{17,1... | collective-permute-start | bytes 4718600 | tf_op jit(solution)/shard_map/ppermute | solution.py:87
  83.3 4.1 %fusion.8 = f32[512,1536]{1,0:T(8,128)S(1)} fusion(bf16[512,1024]{1,0:T(8,128)(2,1)} %copy-done.2, bf16[1024,6144]{1,0:T(8,128)(2,1)} %param.9, s32[]{:T(128)S(6)} %select_n.60), kind=kOutput, calls=%fused_computation.13 | convolution fusion | flops 1610612736 | bytes 7340036 | tf_op jit(solution)/shard_map/dot_general | solution.py:42
  87.4 3.7 %fusion.10 = f32[512,1536]{1,0:T(8,128)S(1)} fusion(bf16[512,1024]{1,0:T(8,128)(2,1)S(1)} %copy-done.3, bf16[1024,6144]{1,0:T(8,128)(2,1)} %param.9, s32[]{:T(128)S(6)} %select_n.59), kind=kOutput, calls=%fused_computation.15 | convolution fusion | flops 1610612736 | bytes 7340036 | tf_op jit(solution)/shard_map/dot_general | solution.py:42
  91.1 3.1 %add_convert_fusion = bf16[512,1536]{1,0:T(8,128)(2,1)} fusion(f32[512,1536]{1,0:T(8,128)S(1)} %fusion.8, bf16[512,1536]{1,0:T(8,128)(2,1)} %collective-permute-done.9), kind=kLoop, calls=%fused_computation.5 | loop fusion | flops 2359296 | bytes 6291456 | tf_op jit(solution)/shard_map/convert_element_type | solution.py:88
  94.2 1.3 collective-permute-start.10
  95.5 16.6 %collective-permute-done.6 = bf16[512,1536]{1,0:T(8,128)(2,1)} collective-permute-done((bf16[512,1536]{1,0:T(8,128)(2,1)S(1)}, bf16[512,1536]{1,0:T(8,128)(2,1)}, u32[]{:S(2)}, u32[]{:S(2)}) %collective-permute-start.6) | collective-permute-done | bytes 1572896 | tf_op jit(solution)/shard_map/ppermute | solution.py:87
  112.1 2.0 %add_convert_fusion.2 = bf16[512,1536]{1,0:T(8,128)(2,1)S(1)} fusion(f32[512,1536]{1,0:T(8,128)S(1)} %fusion.10, bf16[512,1536]{1,0:T(8,128)(2,1)} %collective-permute-done.6), kind=kLoop, calls=%fused_computation.7 | loop fusion | flops 2359296 | bytes 6291456 | tf_op jit(solution)/shard_map/convert_element_type | solution.py:87
  114.1 9.4 %collective-permute-start.7 = (bf16[512,1536]{1,0:T(8,128)(2,1)S(1)}, bf16[512,1536]{1,0:T(8,128)(2,1)}, u32[]{:S(2)}, u32[]{:S(2)}) collective-permute-start(bf16[512,1536]{1,0:T(8,128)(2,1)S(1)} %add_convert_fusion.2), channel_id=1, source_target_pairs={{0,1},{1,2},{2,3},{4,5},{5,6},{6,7},{8,9},{9,10},{10,11},{12,13},{... | collective-permute-start | bytes 4718600 | tf_op jit(solution)/shard_map/ppermute | solution.py:87
  123.5 4.0 %fusion.12 = f32[512,1536]{1,0:T(8,128)S(1)} fusion(bf16[512,1024]{1,0:T(8,128)(2,1)} %copy-done.2, bf16[1024,6144]{1,0:T(8,128)(2,1)} %param.9, s32[]{:T(128)S(6)} %select_n.58), kind=kOutput, calls=%fused_computation.17 | convolution fusion | flops 1610612736 | bytes 7340036 | tf_op jit(solution)/shard_map/dot_general | solution.py:42
  127.5 20.9 %collective-permute-done.10 = bf16[512,1536]{1,0:T(8,128)(2,1)S(1)} collective-permute-done((bf16[512,1536]{1,0:T(8,128)(2,1)}, bf16[512,1536]{1,0:T(8,128)(2,1)S(1)}, u32[]{:S(2)}, u32[]{:S(2)}) %collective-permute-start.10) | collective-permute-done | bytes 1572896 | tf_op jit(solution)/shard_map/ppermute | solution.py:88
  148.4 3.0 %collective-permute-done.7 = bf16[512,1536]{1,0:T(8,128)(2,1)} collective-permute-done((bf16[512,1536]{1,0:T(8,128)(2,1)S(1)}, bf16[512,1536]{1,0:T(8,128)(2,1)}, u32[]{:S(2)}, u32[]{:S(2)}) %collective-permute-start.7) | collective-permute-done | bytes 1572896 | tf_op jit(solution)/shard_map/ppermute | solution.py:87
  151.4 3.2 %multiply_convert_fusion.2 = bf16[512,1536]{1,0:T(8,128)(2,1)} fusion(bf16[512,1536]{1,0:T(8,128)(2,1)S(1)} %collective-permute-done.10, f32[512,1536]{1,0:T(8,128)S(1)} %fusion.12, bf16[512,1536]{1,0:T(8,128)(2,1)} %collective-permute-done.7, f32[512]{0:T(512)S(1)} %add_rsqrt_fusion), kind=kLoop, calls=%fused_computation.4 | loop fusion | flops 4718592 | bytes 7866368 | tf_op jit(solution)/shard_map/convert_element_type | solution.py:129
  (25 shorter events, 3.0 us)
Async XLA Ops:
  0.0 2.5 %copy-start = (bf16[512,1024]{1,0:T(8,128)(2,1)S(1)}, bf16[512,1024]{1,0:T(8,128)(2,1)}, u32[]{:S(2)}) copy-start(bf16[512,1024]{1,0:T(8,128)(2,1)} %param.7) | copy-start | bytes 3145732
  4.1 1.7 %collective-permute-start = (bf16[8,128,128]{2,1,0:T(8,128)(2,1)S(1)}, bf16[8,128,128]{2,1,0:T(8,128)(2,1)S(1)}, u32[]{:S(2)}, u32[]{:S(2)}) collective-permute-start(bf16[8,128,128]{2,1,0:T(8,128)(2,1)S(1)} %get-tuple-element.23), channel_id=1, source_target_pairs={{0,4},{4,0},{8,12},{12,8},{16,20},{20,16},{24,28},{28,24},{1,5},{5... | collective-permute-start | bytes 786440 | tf_op jit(solution)/shard_map/ppermute | solution.py:31
  5.9 9.5 %collective-permute-start.1 = (bf16[8,128,128]{2,1,0:T(8,128)(2,1)S(1)}, bf16[8,128,128]{2,1,0:T(8,128)(2,1)S(1)}, u32[]{:S(2)}, u32[]{:S(2)}) collective-permute-start(bf16[8,128,128]{2,1,0:T(8,128)(2,1)S(1)} %fusion.37), channel_id=1, source_target_pairs={{0,8},{4,12},{8,0},{12,4},{16,24},{20,28},{24,16},{28,20},{1,9},{5... | collective-permute-start | bytes 786440 | tf_op jit(solution)/shard_map/ppermute | solution.py:31
  14.2 9.3 %copy-start.4 = (bf16[512,1024]{1,0:T(8,128)(2,1)S(1)}, bf16[512,1024]{1,0:T(8,128)(2,1)}, u32[]{:S(2)}) copy-start(bf16[512,1024]{1,0:T(8,128)(2,1)} %param.5) | copy-start | bytes 3145732
  15.5 7.8 %collective-permute-start.2 = (bf16[8,128,128]{2,1,0:T(8,128)(2,1)S(1)}, bf16[8,128,128]{2,1,0:T(8,128)(2,1)S(1)}, u32[]{:S(2)}, u32[]{:S(2)}) collective-permute-start(bf16[8,128,128]{2,1,0:T(8,128)(2,1)S(1)} %convert_add_fusion), channel_id=1, source_target_pairs={{0,16},{4,20},{8,24},{12,28},{16,0},{20,4},{24,8},{28,12},{1,17},{... | collective-permute-start | bytes 786440 | tf_op jit(solution)/shard_map/ppermute | solution.py:31
  27.4 3.6 %copy-start.1 = (bf16[512,1024]{1,0:T(8,128)(2,1)S(1)}, bf16[512,1024]{1,0:T(8,128)(2,1)}, u32[]{:S(2)}) copy-start(bf16[512,1024]{1,0:T(8,128)(2,1)} %param.8) | copy-start | bytes 3145732
  29.4 3.7 %collective-permute-start.3 = (f32[512]{0:T(512)S(1)}, f32[512]{0:T(512)S(1)}, u32[]{:S(2)}, u32[]{:S(2)}) collective-permute-start(f32[512]{0:T(512)S(1)} %get-tuple-element.25), channel_id=1, source_target_pairs={{0,1},{1,0},{2,3},{3,2},{4,5},{5,4},{6,7},{7,6},{8,9},{9,8},{10,11... | collective-permute-start | bytes 6152 | tf_op jit(solution)/shard_map/ppermute | solution.py:51
  31.5 4.0 %copy-start.2 = (bf16[512,1024]{1,0:T(8,128)(2,1)}, bf16[512,1024]{1,0:T(8,128)(2,1)S(1)}, u32[]{:S(2)}) copy-start(bf16[512,1024]{1,0:T(8,128)(2,1)S(1)} %multiply_convert_fusion.3) | copy-start | bytes 3145732
  33.0 6.2 %collective-permute-start.4 = (f32[512]{0:T(512)S(1)}, f32[512]{0:T(512)S(1)}, u32[]{:S(2)}, u32[]{:S(2)}) collective-permute-start(f32[512]{0:T(512)S(1)} %add.141), channel_id=1, source_target_pairs={{0,2},{1,3},{2,0},{3,1},{4,6},{5,7},{6,4},{7,5},{8,10},{9,11},{10,... | collective-permute-start | bytes 6152 | tf_op jit(solution)/shard_map/ppermute | solution.py:51
  39.3 34.3 %collective-permute-start.5 = (bf16[512,1536]{1,0:T(8,128)(2,1)S(1)}, bf16[512,1536]{1,0:T(8,128)(2,1)}, u32[]{:S(2)}, u32[]{:S(2)}) collective-permute-start(bf16[512,1536]{1,0:T(8,128)(2,1)S(1)} %fusion.4), channel_id=1, source_target_pairs={{0,1},{4,5},{8,9},{12,13},{16,17},{20,21},{24,25},{28,29}} | collective-permute-start | bytes 4718600 | tf_op jit(solution)/shard_map/ppermute | solution.py:87
  44.0 29.6 %collective-permute-start.8 = (bf16[512,1536]{1,0:T(8,128)(2,1)S(1)}, bf16[512,1536]{1,0:T(8,128)(2,1)}, u32[]{:S(2)}, u32[]{:S(2)}) collective-permute-start(bf16[512,1536]{1,0:T(8,128)(2,1)S(1)} %fusion.4), channel_id=1, source_target_pairs={{3,2},{7,6},{11,10},{15,14},{19,18},{23,22},{27,26},{31,30}} | collective-permute-start | bytes 4718600 | tf_op jit(solution)/shard_map/ppermute | solution.py:88
  76.3 14.7 %collective-permute-start.9 = (bf16[512,1536]{1,0:T(8,128)(2,1)S(1)}, bf16[512,1536]{1,0:T(8,128)(2,1)}, u32[]{:S(2)}, u32[]{:S(2)}) collective-permute-start(bf16[512,1536]{1,0:T(8,128)(2,1)S(1)} %get-tuple-element.22), channel_id=1, source_target_pairs={{2,1},{3,2},{6,5},{7,6},{10,9},{11,10},{14,13},{15,14},{18,17},{19... | collective-permute-start | bytes 4718600 | tf_op jit(solution)/shard_map/ppermute | solution.py:88
  78.2 33.9 %collective-permute-start.6 = (bf16[512,1536]{1,0:T(8,128)(2,1)S(1)}, bf16[512,1536]{1,0:T(8,128)(2,1)}, u32[]{:S(2)}, u32[]{:S(2)}) collective-permute-start(bf16[512,1536]{1,0:T(8,128)(2,1)S(1)} %get-tuple-element.21), channel_id=1, source_target_pairs={{0,1},{1,2},{4,5},{5,6},{8,9},{9,10},{12,13},{13,14},{16,17},{17,1... | collective-permute-start | bytes 4718600 | tf_op jit(solution)/shard_map/ppermute | solution.py:87
  83.3 4.1 %copy-start.3 = (bf16[512,1024]{1,0:T(8,128)(2,1)S(1)}, bf16[512,1024]{1,0:T(8,128)(2,1)}, u32[]{:S(2)}) copy-start(bf16[512,1024]{1,0:T(8,128)(2,1)} %copy-done.2) | copy-start | bytes 3145732
  94.2 54.2 %collective-permute-start.10 = (bf16[512,1536]{1,0:T(8,128)(2,1)}, bf16[512,1536]{1,0:T(8,128)(2,1)S(1)}, u32[]{:S(2)}, u32[]{:S(2)}) collective-permute-start(bf16[512,1536]{1,0:T(8,128)(2,1)} %add_convert_fusion), channel_id=1, source_target_pairs={{1,0},{2,1},{3,2},{5,4},{6,5},{7,6},{9,8},{10,9},{11,10},{13,12},{... | collective-permute-start | bytes 4718600 | tf_op jit(solution)/shard_map/ppermute | solution.py:88
  114.1 37.3 %collective-permute-start.7 = (bf16[512,1536]{1,0:T(8,128)(2,1)S(1)}, bf16[512,1536]{1,0:T(8,128)(2,1)}, u32[]{:S(2)}, u32[]{:S(2)}) collective-permute-start(bf16[512,1536]{1,0:T(8,128)(2,1)S(1)} %add_convert_fusion.2), channel_id=1, source_target_pairs={{0,1},{1,2},{2,3},{4,5},{5,6},{6,7},{8,9},{9,10},{10,11},{12,13},{... | collective-permute-start | bytes 4718600 | tf_op jit(solution)/shard_map/ppermute | solution.py:87

commit v10 on v9

--- a/solution.py
+++ b/solution.py
@@ -2,6 +2,7 @@
 import jax.numpy as jnp
 from jax import lax
 from jax.sharding import PartitionSpec as P
+from jax.experimental import pallas as pl
 
 HEADS = 32
 HEAD_DIM = 128
@@ -95,6 +96,42 @@
     return own * scaling[:, None]
 
 
+def finish_kernel(query_ref, within_ref, gate_ref, state_ref, gated_ref, squares_ref):
+    head = pl.program_id(0)
+    attended = within_ref[...] + jnp.dot(
+        query_ref[...], state_ref[0], preferred_element_type=jnp.float32
+    )
+
+    @pl.when(head == 0)
+    def _():
+        squares_ref[...] = jnp.zeros_like(squares_ref)
+
+    squares_ref[...] += jnp.sum(attended * attended, axis=1, keepdims=True)
+    gate = jax.nn.sigmoid(gate_ref[...].astype(jnp.float32))
+    gated_ref[...] = (attended * gate).astype(jnp.bfloat16)
+
+
+def finish(active_q, within, gate_logits, state):
+    tokens, features = active_q.shape
+    heads = features // HEAD_DIM
+    column = pl.BlockSpec((tokens, HEAD_DIM), lambda h: (0, h))
+    return pl.pallas_call(
+        finish_kernel,
+        grid=(heads,),
+        in_specs=[
+            column,
+            column,
+            column,
+            pl.BlockSpec((1, HEAD_DIM, HEAD_DIM), lambda h: (h, 0, 0)),
+        ],
+        out_specs=[column, pl.BlockSpec((tokens, 1), lambda h: (0, 0))],
+        out_shape=[
+            jax.ShapeDtypeStruct((tokens, features), jnp.bfloat16),
+            jax.ShapeDtypeStruct((tokens, 1), jnp.float32),
+        ],
+    )(active_q, within, gate_logits, state)
+
+
 def body(queries, keys, values, gate_logits, out_weight):
     tokens_here = queries.shape[0]
     feature_count = queries.shape[1]
@@ -116,14 +153,26 @@
     within_block = jnp.einsum(
         "nhts,nshd->nthd", scores, active_v, preferred_element_type=jnp.float32
     )
-    prefix, within_block = exclusive_prefix(span_total, "seq", within_block)
+    within_rows = within_block.reshape(tokens_here, feature_count)
+    prefix, within_rows = exclusive_prefix(span_total, "seq", within_rows)
     within_block, prefix = lax.optimization_barrier((within_block, prefix))
     before = (prefix[None] + earlier_local).astype(jnp.bfloat16)
-    from_state = jnp.einsum("nthd,nhde->nthe", active_q, before, preferred_element_type=jnp.float32)
-    attended = (within_block + from_state).reshape(tokens_here, feature_count)
-    square_sums = jnp.sum(attended * attended, axis=-1)
-    gate = jax.nn.sigmoid(gate_logits.astype(jnp.float32))
-    gated = (attended * gate).astype(jnp.bfloat16)
+    if block_count == 1:
+        gated, square_sums = finish(
+            active_q.reshape(tokens_here, feature_count),
+            within_rows,
+            gate_logits,
+            before[0],
+        )
+        square_sums = square_sums[:, 0]
+    else:
+        from_state = jnp.einsum(
+            "nthd,nhde->nthe", active_q, before, preferred_element_type=jnp.float32
+        )
+        attended = within_rows + from_state.reshape(tokens_here, feature_count)
+        square_sums = jnp.sum(attended * attended, axis=-1)
+        gate = jax.nn.sigmoid(gate_logits.astype(jnp.float32))
+        gated = (attended * gate).astype(jnp.bfloat16)
     total_squares = butterfly_sum(square_sums, "head")
     reduced = line_reduce_scatter(gated, out_weight, "head", total_squares)
     return reduced.astype(jnp.bfloat16)

time: 155 us -> 163 us (1.052)
  Pallas kernels: 0 us -> 7.03 us
  matrix products: 29.2 us -> 25.4 us
  other arithmetic: 15.6 us -> 19.2 us
    pallas_call x0 -> x1, Pallas kernels: none -> 7.03 us  [finish(): pl.pallas_call(finish_kernel, grid=(heads,), in_specs=[column, column, co...]
    dot_general x1 -> x0, matrix products: 3.86 us -> none  [body(): jnp.einsum('nthd,nhde->nthe', active_q, before, preferred_element_type=jn...]
    ppermute x3, waiting for transfers between devices: 7.25 us -> 5.05 us  [exclusive_prefix(): arrived = lax.ppermute(group_total.astype(jnp.bfloat16), axis_name, pairs)]
    convert_element_type x2 -> x3, other arithmetic: 2.53 us -> 4.12 us  [activate(): return jax.nn.silu(raw_input.astype(jnp.float32)).astype(jnp.bfloat16)]
  transfers between devices with their start and end apart: 11 -> 11, of which waited for: 8 -> 7; matrix products, arithmetic and copies ran while one was open for 20% -> 22% of each run, Pallas kernels for 0% -> 0%
where the time goes in v10:
time: 163 us
  waiting for transfers between devices  73.4 us (45%)
  starting transfers between devices  33.3 us (20%)
  matrix products  25.4 us (16%)
  other arithmetic  19.2 us (12%)
  Pallas kernels  7.03 us (4%)
  local copies, waits for them, and re-layouts  4.09 us (3%)
    ppermute x3, waiting for transfers between devices, line_reduce_scatter(): lax.ppermute(to_right.astype(jnp.bfloat16), axis_name, right_pairs)  44.9 us
    ppermute x3, waiting for transfers between devices, line_reduce_scatter(): lax.ppermute(to_left.astype(jnp.bfloat16), axis_name, left_pairs)  21.5 us
    dot_general x5, matrix products, shard_product(): return jnp.dot(gated, columns, preferred_element_type=jnp.float32)  19.5 us
    ppermute x3, starting transfers between devices, line_reduce_scatter(): lax.ppermute(to_right.astype(jnp.bfloat16), axis_name, right_pairs)  19.2 us
    pallas_call x1, Pallas kernels, finish(): pl.pallas_call(finish_kernel, grid=(heads,), in_specs=[column, column, co...  7.03 us
    dot_general x1, matrix products, body(): jnp.einsum('nhts,nshd->nthd', scores, active_v, preferred_element_type=jn...  5.42 us
    ppermute x3, waiting for transfers between devices, exclusive_prefix(): arrived = lax.ppermute(group_total.astype(jnp.bfloat16), axis_name, pairs)  5.05 us
    ppermute x3, starting transfers between devices, exclusive_prefix(): arrived = lax.ppermute(group_total.astype(jnp.bfloat16), axis_name, pairs)  4.99 us
  transfers between devices with their start and end apart: 11, of which 7 were waited for; matrix products, arithmetic and copies ran while one was open for 22% of the time, Pallas kernels for 0%

profile of v10, /device:TPU:0, one launch (start us, length us, event | category | flops | bytes accessed | tf_op | source)
XLA Modules:
  0.0 162.5 jit_solution(318463546851073934)
XLA Ops:
  0.0 1.9 %fusion.21 = bf16[512,1024]{1,0:T(8,128)(2,1)S(1)} fusion(bf16[512,1024]{1,0:T(8,128)(2,1)} %param.6), kind=kLoop, calls=%fused_computation.32 | loop fusion | flops 3145728 | bytes 2097152 | tf_op jit(solution)/shard_map/convert_element_type | solution.py:12
  4.7 1.1 fusion.30
  6.6 2.9 %collective-permute-start.1 = (bf16[8,128,128]{2,1,0:T(8,128)(2,1)}, bf16[8,128,128]{2,1,0:T(8,128)(2,1)S(1)}, u32[]{:S(2)}, u32[]{:S(2)}) collective-permute-start(bf16[8,128,128]{2,1,0:T(8,128)(2,1)} %fusion.33), channel_id=1, source_target_pairs={{0,8},{4,12},{8,0},{12,4},{16,24},{20,28},{24,16},{28,20},{1,9},{5... | collective-permute-start | bytes 786440 | tf_op jit(solution)/shard_map/ppermute | solution.py:32
  9.4 5.4 %fusion = f32[8,128,512]{2,1,0:T(8,128)} fusion(bf16[512,8,128]{0,2,1:T(8,128)(2,1)S(1)} %bitcast.28, f32[512,512]{1,0:T(8,128)} %fusion.30, bf16[512,8,128]{0,2,1:T(8,128)(2,1)S(1)} %bitcast.26, bf16[512,1024]{1,0:T(8,128)(2,1)} %param.5), kind=kOutput, calls=%fused_computation.1 | convolution fusion | flops 1081081856 | bytes 6291456 | tf_op jit(solution)/shard_map/nhts,nshd->nthd/dot_general | solution.py:153
  14.9 3.0 %copy.16.within_ref = f32[512,1024]{1,0:T(8,128)} copy(f32[512,1024]{0,1:T(8,128)} %bitcast.29) | data formatting | bytes 4194304 | tf_op jit(solution)/shard_map/reshape | solution.py:156
  17.9 1.6 collective-permute-start.2
  19.5 1.6 fusion.17.query_ref
  21.1 5.0 %collective-permute-done.2 = bf16[8,128,128]{2,1,0:T(8,128)(2,1)S(1)} collective-permute-done((bf16[8,128,128]{2,1,0:T(8,128)(2,1)S(1)}, bf16[8,128,128]{2,1,0:T(8,128)(2,1)S(1)}, u32[]{:S(2)}, u32[]{:S(2)}) %collective-permute-start.2) | collective-permute-done | bytes 262176 | tf_op jit(solution)/shard_map/ppermute | solution.py:32
  27.0 7.0 %shard_map.55 = (bf16[512,1024]{1,0:T(8,128)(2,1)}, f32[512,1]{1,0:T(8,128)}) custom-call(bf16[512,1024]{1,0:T(8,128)(2,1)} %fusion.17.query_ref, f32[512,1024]{1,0:T(8,128)} %copy.16.within_ref, bf16[512,1024]{1,0:T(8,128)(2,1)} %gate_ref.1, bf16[8,128,128]{2,1,0:T(8,128)(2,1)} %add_convert_fusion.4.state_ref), custom_call_target="tpu_custom_call" | custom-call | tf_op jit(solution)/shard_map/pallas_call | solution.py:118
  34.0 1.1 reduce
  35.1 1.6 %collective-permute-start.3 = (f32[512]{0:T(512)S(1)}, f32[512]{0:T(512)S(1)}, u32[]{:S(2)}, u32[]{:S(2)}) collective-permute-start(f32[512]{0:T(512)S(1)} %reduce), channel_id=1, source_target_pairs={{0,1},{1,0},{2,3},{3,2},{4,5},{5,4},{6,7},{7,6},{8,9},{9,8},{10,11... | collective-permute-start | bytes 6152 | tf_op jit(solution)/shard_map/ppermute | solution.py:52
  36.8 2.0 %collective-permute-done.3 = f32[512]{0:T(512)S(1)} collective-permute-done((f32[512]{0:T(512)S(1)}, f32[512]{0:T(512)S(1)}, u32[]{:S(2)}, u32[]{:S(2)}) %collective-permute-start.3) | collective-permute-done | bytes 2080 | tf_op jit(solution)/shard_map/ppermute | solution.py:52
  38.8 2.6 %collective-permute-start.4 = (f32[512]{0:T(512)S(1)}, f32[512]{0:T(512)S(1)}, u32[]{:S(2)}, u32[]{:S(2)}) collective-permute-start(f32[512]{0:T(512)S(1)} %add.133), channel_id=1, source_target_pairs={{0,2},{1,3},{2,0},{3,1},{4,6},{5,7},{6,4},{7,5},{8,10},{9,11},{10,... | collective-permute-start | bytes 6152 | tf_op jit(solution)/shard_map/ppermute | solution.py:52
  41.4 4.1 %fusion.4 = bf16[512,1536]{1,0:T(8,128)(2,1)S(1)} fusion(bf16[512,1024]{1,0:T(8,128)(2,1)} %get-tuple-element.17, bf16[1024,6144]{1,0:T(8,128)(2,1)} %param.9, s32[]{:T(128)S(6)} %select_n.64), kind=kOutput, calls=%fused_computation.9 | convolution fusion | flops 1610612736 | bytes 5767172 | tf_op jit(solution)/shard_map/dot_general | solution.py:43
  45.5 4.7 %collective-permute-start.5 = (bf16[512,1536]{1,0:T(8,128)(2,1)S(1)}, bf16[512,1536]{1,0:T(8,128)(2,1)}, u32[]{:S(2)}, u32[]{:S(2)}) collective-permute-start(bf16[512,1536]{1,0:T(8,128)(2,1)S(1)} %fusion.4), channel_id=1, source_target_pairs={{0,1},{4,5},{8,9},{12,13},{16,17},{20,21},{24,25},{28,29}} | collective-permute-start | bytes 4718600 | tf_op jit(solution)/shard_map/ppermute | solution.py:88
  50.1 1.8 %collective-permute-start.8 = (bf16[512,1536]{1,0:T(8,128)(2,1)S(1)}, bf16[512,1536]{1,0:T(8,128)(2,1)}, u32[]{:S(2)}, u32[]{:S(2)}) collective-permute-start(bf16[512,1536]{1,0:T(8,128)(2,1)S(1)} %fusion.4), channel_id=1, source_target_pairs={{3,2},{7,6},{11,10},{15,14},{19,18},{23,22},{27,26},{31,30}} | collective-permute-start | bytes 4718600 | tf_op jit(solution)/shard_map/ppermute | solution.py:89
  51.9 3.7 %fusion.6 = f32[512,1536]{1,0:T(8,128)S(1)} fusion(bf16[512,1024]{1,0:T(8,128)(2,1)S(1)} %copy-done.2, bf16[1024,6144]{1,0:T(8,128)(2,1)} %param.9, s32[]{:T(128)S(6)} %select_n.62), kind=kOutput, calls=%fused_computation.11 | convolution fusion | flops 1610612736 | bytes 7340036 | tf_op jit(solution)/shard_map/dot_general | solution.py:43
  55.6 24.7 %collective-permute-done.5 = bf16[512,1536]{1,0:T(8,128)(2,1)} collective-permute-done((bf16[512,1536]{1,0:T(8,128)(2,1)S(1)}, bf16[512,1536]{1,0:T(8,128)(2,1)}, u32[]{:S(2)}, u32[]{:S(2)}) %collective-permute-start.5) | collective-permute-done | bytes 1572896 | tf_op jit(solution)/shard_map/ppermute | solution.py:88
  80.4 2.8 %add_convert_fusion.3 = (bf16[512,1536]{1,0:T(8,128)(2,1)S(1)}, bf16[512,1536]{1,0:T(8,128)(2,1)S(1)}) fusion(f32[512,1536]{1,0:T(8,128)S(1)} %fusion.6, bf16[512,1536]{1,0:T(8,128)(2,1)} %collective-permute-done.5, bf16[512,1536]{1,0:T(8,128)(2,1)} %collective-permute-done.8), kind=kLoop, calls=%fused_computation.8 | loop fusion | flops 4718592 | bytes 9437184 | tf_op jit(solution)/shard_map/convert_element_type | solution.py:88
  83.1 1.8 %collective-permute-start.9 = (bf16[512,1536]{1,0:T(8,128)(2,1)S(1)}, bf16[512,1536]{1,0:T(8,128)(2,1)}, u32[]{:S(2)}, u32[]{:S(2)}) collective-permute-start(bf16[512,1536]{1,0:T(8,128)(2,1)S(1)} %get-tuple-element.24), channel_id=1, source_target_pairs={{2,1},{3,2},{6,5},{7,6},{10,9},{11,10},{14,13},{15,14},{18,17},{19... | collective-permute-start | bytes 4718600 | tf_op jit(solution)/shard_map/ppermute | solution.py:89
  84.9 5.1 %collective-permute-start.6 = (bf16[512,1536]{1,0:T(8,128)(2,1)S(1)}, bf16[512,1536]{1,0:T(8,128)(2,1)}, u32[]{:S(2)}, u32[]{:S(2)}) collective-permute-start(bf16[512,1536]{1,0:T(8,128)(2,1)S(1)} %get-tuple-element.23), channel_id=1, source_target_pairs={{0,1},{1,2},{4,5},{5,6},{8,9},{9,10},{12,13},{13,14},{16,17},{17,1... | collective-permute-start | bytes 4718600 | tf_op jit(solution)/shard_map/ppermute | solution.py:88
  90.1 4.1 %fusion.8 = f32[512,1536]{1,0:T(8,128)S(1)} fusion(bf16[512,1024]{1,0:T(8,128)(2,1)} %get-tuple-element.17, bf16[1024,6144]{1,0:T(8,128)(2,1)} %param.9, s32[]{:T(128)S(6)} %select_n.60), kind=kOutput, calls=%fused_computation.13 | convolution fusion | flops 1610612736 | bytes 7340036 | tf_op jit(solution)/shard_map/dot_general | solution.py:43
  94.1 3.7 %fusion.10 = f32[512,1536]{1,0:T(8,128)S(1)} fusion(bf16[512,1024]{1,0:T(8,128)(2,1)S(1)} %copy-done.3, bf16[1024,6144]{1,0:T(8,128)(2,1)} %param.9, s32[]{:T(128)S(6)} %select_n.59), kind=kOutput, calls=%fused_computation.15 | convolution fusion | flops 1610612736 | bytes 7340036 | tf_op jit(solution)/shard_map/dot_general | solution.py:43
  97.8 3.1 %add_convert_fusion = bf16[512,1536]{1,0:T(8,128)(2,1)} fusion(f32[512,1536]{1,0:T(8,128)S(1)} %fusion.8, bf16[512,1536]{1,0:T(8,128)(2,1)} %collective-permute-done.9), kind=kLoop, calls=%fused_computation.5 | loop fusion | flops 2359296 | bytes 6291456 | tf_op jit(solution)/shard_map/convert_element_type | solution.py:89
  101.0 1.3 collective-permute-start.10
  102.3 17.2 %collective-permute-done.6 = bf16[512,1536]{1,0:T(8,128)(2,1)} collective-permute-done((bf16[512,1536]{1,0:T(8,128)(2,1)S(1)}, bf16[512,1536]{1,0:T(8,128)(2,1)}, u32[]{:S(2)}, u32[]{:S(2)}) %collective-permute-start.6) | collective-permute-done | bytes 1572896 | tf_op jit(solution)/shard_map/ppermute | solution.py:88
  119.4 2.0 %add_convert_fusion.2 = bf16[512,1536]{1,0:T(8,128)(2,1)S(1)} fusion(f32[512,1536]{1,0:T(8,128)S(1)} %fusion.10, bf16[512,1536]{1,0:T(8,128)(2,1)} %collective-permute-done.6), kind=kLoop, calls=%fused_computation.7 | loop fusion | flops 2359296 | bytes 6291456 | tf_op jit(solution)/shard_map/convert_element_type | solution.py:88
  121.4 9.4 %collective-permute-start.7 = (bf16[512,1536]{1,0:T(8,128)(2,1)S(1)}, bf16[512,1536]{1,0:T(8,128)(2,1)}, u32[]{:S(2)}, u32[]{:S(2)}) collective-permute-start(bf16[512,1536]{1,0:T(8,128)(2,1)S(1)} %add_convert_fusion.2), channel_id=1, source_target_pairs={{0,1},{1,2},{2,3},{4,5},{5,6},{6,7},{8,9},{9,10},{10,11},{12,13},{... | collective-permute-start | bytes 4718600 | tf_op jit(solution)/shard_map/ppermute | solution.py:88
  130.8 4.0 %fusion.12 = f32[512,1536]{1,0:T(8,128)S(1)} fusion(bf16[512,1024]{1,0:T(8,128)(2,1)} %get-tuple-element.17, bf16[1024,6144]{1,0:T(8,128)(2,1)} %param.9, s32[]{:T(128)S(6)} %select_n.58), kind=kOutput, calls=%fused_computation.17 | convolution fusion | flops 1610612736 | bytes 7340036 | tf_op jit(solution)/shard_map/dot_general | solution.py:43
  134.9 21.5 %collective-permute-done.10 = bf16[512,1536]{1,0:T(8,128)(2,1)S(1)} collective-permute-done((bf16[512,1536]{1,0:T(8,128)(2,1)}, bf16[512,1536]{1,0:T(8,128)(2,1)S(1)}, u32[]{:S(2)}, u32[]{:S(2)}) %collective-permute-start.10) | collective-permute-done | bytes 1572896 | tf_op jit(solution)/shard_map/ppermute | solution.py:89
  156.4 3.0 %collective-permute-done.7 = bf16[512,1536]{1,0:T(8,128)(2,1)} collective-permute-done((bf16[512,1536]{1,0:T(8,128)(2,1)S(1)}, bf16[512,1536]{1,0:T(8,128)(2,1)}, u32[]{:S(2)}, u32[]{:S(2)}) %collective-permute-start.7) | collective-permute-done | bytes 1572896 | tf_op jit(solution)/shard_map/ppermute | solution.py:88
  159.3 3.2 %multiply_convert_fusion.2 = bf16[512,1536]{1,0:T(8,128)(2,1)} fusion(bf16[512,1536]{1,0:T(8,128)(2,1)S(1)} %collective-permute-done.10, f32[512,1536]{1,0:T(8,128)S(1)} %fusion.12, bf16[512,1536]{1,0:T(8,128)(2,1)} %collective-permute-done.7, f32[512]{0:T(512)S(1)} %add_rsqrt_fusion), kind=kLoop, calls=%fused_computation.4 | loop fusion | flops 4718592 | bytes 7866368 | tf_op jit(solution)/shard_map/convert_element_type | solution.py:178
  (25 shorter events, 4.6 us)
Async XLA Ops:
  0.0 2.5 %copy-start = (bf16[512,1024]{1,0:T(8,128)(2,1)S(1)}, bf16[512,1024]{1,0:T(8,128)(2,1)}, u32[]{:S(2)}) copy-start(bf16[512,1024]{1,0:T(8,128)(2,1)} %param.7) | copy-start | bytes 3145732
  4.1 1.7 %collective-permute-start = (bf16[8,128,128]{2,1,0:T(8,128)(2,1)S(1)}, bf16[8,128,128]{2,1,0:T(8,128)(2,1)S(1)}, u32[]{:S(2)}, u32[]{:S(2)}) collective-permute-start(bf16[8,128,128]{2,1,0:T(8,128)(2,1)S(1)} %get-tuple-element.25), channel_id=1, source_target_pairs={{0,4},{4,0},{8,12},{12,8},{16,20},{20,16},{24,28},{28,24},{1,5},{5... | collective-permute-start | bytes 786440 | tf_op jit(solution)/shard_map/ppermute | solution.py:32
  6.6 11.3 %collective-permute-start.1 = (bf16[8,128,128]{2,1,0:T(8,128)(2,1)}, bf16[8,128,128]{2,1,0:T(8,128)(2,1)S(1)}, u32[]{:S(2)}, u32[]{:S(2)}) collective-permute-start(bf16[8,128,128]{2,1,0:T(8,128)(2,1)} %fusion.33), channel_id=1, source_target_pairs={{0,8},{4,12},{8,0},{12,4},{16,24},{20,28},{24,16},{28,20},{1,9},{5... | collective-permute-start | bytes 786440 | tf_op jit(solution)/shard_map/ppermute | solution.py:32
  14.8 4.7 %copy-start.1 = (bf16[512,1024]{1,0:T(8,128)(2,1)S(1)}, bf16[512,1024]{1,0:T(8,128)(2,1)}, u32[]{:S(2)}) copy-start(bf16[512,1024]{1,0:T(8,128)(2,1)} %param.5) | copy-start | bytes 3145732
  17.9 8.1 %collective-permute-start.2 = (bf16[8,128,128]{2,1,0:T(8,128)(2,1)S(1)}, bf16[8,128,128]{2,1,0:T(8,128)(2,1)S(1)}, u32[]{:S(2)}, u32[]{:S(2)}) collective-permute-start(bf16[8,128,128]{2,1,0:T(8,128)(2,1)S(1)} %convert_add_fusion), channel_id=1, source_target_pairs={{0,16},{4,20},{8,24},{12,28},{16,0},{20,4},{24,8},{28,12},{1,17},{... | collective-permute-start | bytes 786440 | tf_op jit(solution)/shard_map/ppermute | solution.py:32
  35.1 3.7 %collective-permute-start.3 = (f32[512]{0:T(512)S(1)}, f32[512]{0:T(512)S(1)}, u32[]{:S(2)}, u32[]{:S(2)}) collective-permute-start(f32[512]{0:T(512)S(1)} %reduce), channel_id=1, source_target_pairs={{0,1},{1,0},{2,3},{3,2},{4,5},{5,4},{6,7},{7,6},{8,9},{9,8},{10,11... | collective-permute-start | bytes 6152 | tf_op jit(solution)/shard_map/ppermute | solution.py:52
  38.8 6.7 %collective-permute-start.4 = (f32[512]{0:T(512)S(1)}, f32[512]{0:T(512)S(1)}, u32[]{:S(2)}, u32[]{:S(2)}) collective-permute-start(f32[512]{0:T(512)S(1)} %add.133), channel_id=1, source_target_pairs={{0,2},{1,3},{2,0},{3,1},{4,6},{5,7},{6,4},{7,5},{8,10},{9,11},{10,... | collective-permute-start | bytes 6152 | tf_op jit(solution)/shard_map/ppermute | solution.py:52
  41.4 10.6 %copy-start.2 = (bf16[512,1024]{1,0:T(8,128)(2,1)S(1)}, bf16[512,1024]{1,0:T(8,128)(2,1)}, u32[]{:S(2)}) copy-start(bf16[512,1024]{1,0:T(8,128)(2,1)} %get-tuple-element.17) | copy-start | bytes 3145732
  45.5 34.9 %collective-permute-start.5 = (bf16[512,1536]{1,0:T(8,128)(2,1)S(1)}, bf16[512,1536]{1,0:T(8,128)(2,1)}, u32[]{:S(2)}, u32[]{:S(2)}) collective-permute-start(bf16[512,1536]{1,0:T(8,128)(2,1)S(1)} %fusion.4), channel_id=1, source_target_pairs={{0,1},{4,5},{8,9},{12,13},{16,17},{20,21},{24,25},{28,29}} | collective-permute-start | bytes 4718600 | tf_op jit(solution)/shard_map/ppermute | solution.py:88
  50.1 30.2 %collective-permute-start.8 = (bf16[512,1536]{1,0:T(8,128)(2,1)S(1)}, bf16[512,1536]{1,0:T(8,128)(2,1)}, u32[]{:S(2)}, u32[]{:S(2)}) collective-permute-start(bf16[512,1536]{1,0:T(8,128)(2,1)S(1)} %fusion.4), channel_id=1, source_target_pairs={{3,2},{7,6},{11,10},{15,14},{19,18},{23,22},{27,26},{31,30}} | collective-permute-start | bytes 4718600 | tf_op jit(solution)/shard_map/ppermute | solution.py:89
  83.1 14.7 %collective-permute-start.9 = (bf16[512,1536]{1,0:T(8,128)(2,1)S(1)}, bf16[512,1536]{1,0:T(8,128)(2,1)}, u32[]{:S(2)}, u32[]{:S(2)}) collective-permute-start(bf16[512,1536]{1,0:T(8,128)(2,1)S(1)} %get-tuple-element.24), channel_id=1, source_target_pairs={{2,1},{3,2},{6,5},{7,6},{10,9},{11,10},{14,13},{15,14},{18,17},{19... | collective-permute-start | bytes 4718600 | tf_op jit(solution)/shard_map/ppermute | solution.py:89
  84.9 34.5 %collective-permute-start.6 = (bf16[512,1536]{1,0:T(8,128)(2,1)S(1)}, bf16[512,1536]{1,0:T(8,128)(2,1)}, u32[]{:S(2)}, u32[]{:S(2)}) collective-permute-start(bf16[512,1536]{1,0:T(8,128)(2,1)S(1)} %get-tuple-element.23), channel_id=1, source_target_pairs={{0,1},{1,2},{4,5},{5,6},{8,9},{9,10},{12,13},{13,14},{16,17},{17,1... | collective-permute-start | bytes 4718600 | tf_op jit(solution)/shard_map/ppermute | solution.py:88
  90.1 4.1 %copy-start.3 = (bf16[512,1024]{1,0:T(8,128)(2,1)S(1)}, bf16[512,1024]{1,0:T(8,128)(2,1)}, u32[]{:S(2)}) copy-start(bf16[512,1024]{1,0:T(8,128)(2,1)} %get-tuple-element.17) | copy-start | bytes 3145732
  101.0 55.4 %collective-permute-start.10 = (bf16[512,1536]{1,0:T(8,128)(2,1)}, bf16[512,1536]{1,0:T(8,128)(2,1)S(1)}, u32[]{:S(2)}, u32[]{:S(2)}) collective-permute-start(bf16[512,1536]{1,0:T(8,128)(2,1)} %add_convert_fusion), channel_id=1, source_target_pairs={{1,0},{2,1},{3,2},{5,4},{6,5},{7,6},{9,8},{10,9},{11,10},{13,12},{... | collective-permute-start | bytes 4718600 | tf_op jit(solution)/shard_map/ppermute | solution.py:89
  121.4 37.9 %collective-permute-start.7 = (bf16[512,1536]{1,0:T(8,128)(2,1)S(1)}, bf16[512,1536]{1,0:T(8,128)(2,1)}, u32[]{:S(2)}, u32[]{:S(2)}) collective-permute-start(bf16[512,1536]{1,0:T(8,128)(2,1)S(1)} %add_convert_fusion.2), channel_id=1, source_target_pairs={{0,1},{1,2},{2,3},{4,5},{5,6},{6,7},{8,9},{9,10},{10,11},{12,13},{... | collective-permute-start | bytes 4718600 | tf_op jit(solution)/shard_map/ppermute | solution.py:88

commit v11 on v10

--- a/solution.py
+++ b/solution.py
@@ -93,38 +93,43 @@
     scaling = lax.rsqrt(total_squares / (HEADS * HEAD_DIM) + 1e-06)
     if from_left is not None:
         own = own + from_left + from_right
-    return own * scaling[:, None]
+    return own * scaling
 
 
 def finish_kernel(query_ref, within_ref, gate_ref, state_ref, gated_ref, squares_ref):
-    head = pl.program_id(0)
-    attended = within_ref[...] + jnp.dot(
-        query_ref[...], state_ref[0], preferred_element_type=jnp.float32
-    )
+    step = pl.program_id(0)
 
-    @pl.when(head == 0)
+    @pl.when(step == 0)
     def _():
         squares_ref[...] = jnp.zeros_like(squares_ref)
 
-    squares_ref[...] += jnp.sum(attended * attended, axis=1, keepdims=True)
-    gate = jax.nn.sigmoid(gate_ref[...].astype(jnp.float32))
-    gated_ref[...] = (attended * gate).astype(jnp.bfloat16)
+    total = jnp.zeros(squares_ref.shape, jnp.float32)
+    for head in range(state_ref.shape[0]):
+        cols = slice(head * HEAD_DIM, (head + 1) * HEAD_DIM)
+        attended = within_ref[:, cols] + jnp.dot(
+            query_ref[:, cols], state_ref[head], preferred_element_type=jnp.float32
+        )
+        total = total + jnp.sum(attended * attended, axis=1, keepdims=True)
+        gate = jax.nn.sigmoid(gate_ref[:, cols].astype(jnp.float32))
+        gated_ref[:, cols] = (attended * gate).astype(jnp.bfloat16)
+    squares_ref[...] += total
 
 
 def finish(active_q, within, gate_logits, state):
     tokens, features = active_q.shape
     heads = features // HEAD_DIM
-    column = pl.BlockSpec((tokens, HEAD_DIM), lambda h: (0, h))
+    group = 4 if heads % 4 == 0 else 1
+    column = pl.BlockSpec((tokens, group * HEAD_DIM), lambda g: (0, g))
     return pl.pallas_call(
         finish_kernel,
-        grid=(heads,),
+        grid=(heads // group,),
         in_specs=[
             column,
             column,
             column,
-            pl.BlockSpec((1, HEAD_DIM, HEAD_DIM), lambda h: (h, 0, 0)),
+            pl.BlockSpec((group, HEAD_DIM, HEAD_DIM), lambda g: (g, 0, 0)),
         ],
-        out_specs=[column, pl.BlockSpec((tokens, 1), lambda h: (0, 0))],
+        out_specs=[column, pl.BlockSpec((tokens, 1), lambda g: (0, 0))],
         out_shape=[
             jax.ShapeDtypeStruct((tokens, features), jnp.bfloat16),
             jax.ShapeDtypeStruct((tokens, 1), jnp.float32),
@@ -164,13 +169,12 @@
             gate_logits,
             before[0],
         )
-        square_sums = square_sums[:, 0]
     else:
         from_state = jnp.einsum(
             "nthd,nhde->nthe", active_q, before, preferred_element_type=jnp.float32
         )
         attended = within_rows + from_state.reshape(tokens_here, feature_count)
-        square_sums = jnp.sum(attended * attended, axis=-1)
+        square_sums = jnp.sum(attended * attended, axis=-1, keepdims=True)
         gate = jax.nn.sigmoid(gate_logits.astype(jnp.float32))
         gated = (attended * gate).astype(jnp.bfloat16)
     total_squares = butterfly_sum(square_sums, "head")

time: 163 us -> 178 us (1.092)
  waiting for transfers between devices: 73.4 us -> 91.2 us
  Pallas kernels: 7.03 us -> 3.48 us
    ppermute x2, waiting for transfers between devices: 2.02 us -> 12.1 us  [butterfly_sum(): lax.ppermute(values, axis_name, [(i, i ^ bit) for i in range(count)])]
    ppermute x3, waiting for transfers between devices: 44.9 us -> 49.8 us  [line_reduce_scatter(): lax.ppermute(to_right.astype(jnp.bfloat16), axis_name, right_pairs)]
    pallas_call x1, Pallas kernels: 7.03 us -> 3.48 us  [finish(): pl.pallas_call(finish_kernel, grid=(heads // group,), in_specs=[column, c...]
    ppermute x3, waiting for transfers between devices: 21.5 us -> 24.4 us  [line_reduce_scatter(): lax.ppermute(to_left.astype(jnp.bfloat16), axis_name, left_pairs)]
  transfers between devices with their start and end apart: 11 -> 11, of which waited for: 7 -> 8; matrix products, arithmetic and copies ran while one was open for 22% -> 20% of each run, Pallas kernels for 0% -> 0%
where the time goes in v11:
time: 178 us
  waiting for transfers between devices  91.2 us (51%)
  starting transfers between devices  34.3 us (19%)
  matrix products  25.4 us (14%)
  other arithmetic  19.2 us (11%)
  local copies, waits for them, and re-layouts  4.09 us (2%)
  Pallas kernels  3.48 us (2%)
    ppermute x3, waiting for transfers between devices, line_reduce_scatter(): lax.ppermute(to_right.astype(jnp.bfloat16), axis_name, right_pairs)  49.8 us
    ppermute x3, waiting for transfers between devices, line_reduce_scatter(): lax.ppermute(to_left.astype(jnp.bfloat16), axis_name, left_pairs)  24.4 us
    ppermute x3, starting transfers between devices, line_reduce_scatter(): lax.ppermute(to_right.astype(jnp.bfloat16), axis_name, right_pairs)  20.2 us
    dot_general x5, matrix products, shard_product(): return jnp.dot(gated, columns, preferred_element_type=jnp.float32)  19.5 us
    ppermute x2, waiting for transfers between devices, butterfly_sum(): lax.ppermute(values, axis_name, [(i, i ^ bit) for i in range(count)])  12.1 us
    dot_general x1, matrix products, body(): jnp.einsum('nhts,nshd->nthd', scores, active_v, preferred_element_type=jn...  5.42 us
    ppermute x3, waiting for transfers between devices, exclusive_prefix(): arrived = lax.ppermute(group_total.astype(jnp.bfloat16), axis_name, pairs)  5.05 us
    ppermute x3, starting transfers between devices, exclusive_prefix(): arrived = lax.ppermute(group_total.astype(jnp.bfloat16), axis_name, pairs)  4.99 us
  transfers between devices with their start and end apart: 11, of which 8 were waited for; matrix products, arithmetic and copies ran while one was open for 20% of the time, Pallas kernels for 0%

profile of v11, /device:TPU:0, one launch (start us, length us, event | category | flops | bytes accessed | tf_op | source)
XLA Modules:
  0.0 177.8 jit_solution(548329889717369450)
XLA Ops:
  0.0 1.9 %fusion.21 = bf16[512,1024]{1,0:T(8,128)(2,1)S(1)} fusion(bf16[512,1024]{1,0:T(8,128)(2,1)} %param.6), kind=kLoop, calls=%fused_computation.32 | loop fusion | flops 3145728 | bytes 2097152 | tf_op jit(solution)/shard_map/convert_element_type | solution.py:12
  4.7 1.1 fusion.30
  6.6 2.9 %collective-permute-start.1 = (bf16[8,128,128]{2,1,0:T(8,128)(2,1)}, bf16[8,128,128]{2,1,0:T(8,128)(2,1)S(1)}, u32[]{:S(2)}, u32[]{:S(2)}) collective-permute-start(bf16[8,128,128]{2,1,0:T(8,128)(2,1)} %fusion.33), channel_id=1, source_target_pairs={{0,8},{4,12},{8,0},{12,4},{16,24},{20,28},{24,16},{28,20},{1,9},{5... | collective-permute-start | bytes 786440 | tf_op jit(solution)/shard_map/ppermute | solution.py:32
  9.4 5.4 %fusion = f32[8,128,512]{2,1,0:T(8,128)} fusion(bf16[512,8,128]{0,2,1:T(8,128)(2,1)S(1)} %bitcast.28, f32[512,512]{1,0:T(8,128)} %fusion.30, bf16[512,8,128]{0,2,1:T(8,128)(2,1)S(1)} %bitcast.26, bf16[512,1024]{1,0:T(8,128)(2,1)} %param.5), kind=kOutput, calls=%fused_computation.1 | convolution fusion | flops 1081081856 | bytes 6291456 | tf_op jit(solution)/shard_map/nhts,nshd->nthd/dot_general | solution.py:158
  14.9 3.0 %copy.16.within_ref = f32[512,1024]{1,0:T(8,128)} copy(f32[512,1024]{0,1:T(8,128)} %bitcast.29) | data formatting | bytes 4194304 | tf_op jit(solution)/shard_map/reshape | solution.py:161
  17.9 1.6 collective-permute-start.2
  19.5 1.6 fusion.17.query_ref
  21.1 5.0 %collective-permute-done.2 = bf16[8,128,128]{2,1,0:T(8,128)(2,1)S(1)} collective-permute-done((bf16[8,128,128]{2,1,0:T(8,128)(2,1)S(1)}, bf16[8,128,128]{2,1,0:T(8,128)(2,1)S(1)}, u32[]{:S(2)}, u32[]{:S(2)}) %collective-permute-start.2) | collective-permute-done | bytes 262176 | tf_op jit(solution)/shard_map/ppermute | solution.py:32
  27.0 3.5 %shard_map.55 = (bf16[512,1024]{1,0:T(8,128)(2,1)}, f32[512,1]{1,0:T(8,128)}) custom-call(bf16[512,1024]{1,0:T(8,128)(2,1)} %fusion.17.query_ref, f32[512,1024]{1,0:T(8,128)} %copy.16.within_ref, bf16[512,1024]{1,0:T(8,128)(2,1)} %gate_ref.1, bf16[8,128,128]{2,1,0:T(8,128)(2,1)} %add_convert_fusion.4.state_ref), custom_call_target="tpu_custom_call" | custom-call | tf_op jit(solution)/shard_map/pallas_call | solution.py:123
  30.5 1.6 collective-permute-start.3
  32.1 5.9 %collective-permute-done.3 = f32[512,1]{1,0:T(8,128)S(1)} collective-permute-done((f32[512,1]{1,0:T(8,128)}, f32[512,1]{1,0:T(8,128)S(1)}, u32[]{:S(2)}, u32[]{:S(2)}) %collective-permute-start.3) | collective-permute-done | bytes 2080 | tf_op jit(solution)/shard_map/ppermute | solution.py:52
  38.9 2.6 %collective-permute-start.4 = (f32[512,1]{1,0:T(8,128)S(1)}, f32[512,1]{1,0:T(8,128)S(1)}, u32[]{:S(2)}, u32[]{:S(2)}) collective-permute-start(f32[512,1]{1,0:T(8,128)S(1)} %add.133), channel_id=1, source_target_pairs={{0,2},{1,3},{2,0},{3,1},{4,6},{5,7},{6,4},{7,5},{8,10},{9,11},{10,... | collective-permute-start | bytes 6152 | tf_op jit(solution)/shard_map/ppermute | solution.py:52
  41.5 4.1 %fusion.4 = bf16[512,1536]{1,0:T(8,128)(2,1)S(1)} fusion(bf16[512,1024]{1,0:T(8,128)(2,1)} %get-tuple-element.17, bf16[1024,6144]{1,0:T(8,128)(2,1)} %param.9, s32[]{:T(128)S(6)} %select_n.64), kind=kOutput, calls=%fused_computation.9 | convolution fusion | flops 1610612736 | bytes 5767172 | tf_op jit(solution)/shard_map/dot_general | solution.py:43
  45.6 6.2 %collective-permute-done.4 = f32[512,1]{1,0:T(8,128)S(1)} collective-permute-done((f32[512,1]{1,0:T(8,128)S(1)}, f32[512,1]{1,0:T(8,128)S(1)}, u32[]{:S(2)}, u32[]{:S(2)}) %collective-permute-start.4) | collective-permute-done | bytes 2080 | tf_op jit(solution)/shard_map/ppermute | solution.py:52
  51.9 3.7 %collective-permute-start.5 = (bf16[512,1536]{1,0:T(8,128)(2,1)S(1)}, bf16[512,1536]{1,0:T(8,128)(2,1)}, u32[]{:S(2)}, u32[]{:S(2)}) collective-permute-start(bf16[512,1536]{1,0:T(8,128)(2,1)S(1)} %fusion.4), channel_id=1, source_target_pairs={{0,1},{4,5},{8,9},{12,13},{16,17},{20,21},{24,25},{28,29}} | collective-permute-start | bytes 4718600 | tf_op jit(solution)/shard_map/ppermute | solution.py:88
  55.6 1.8 %collective-permute-start.8 = (bf16[512,1536]{1,0:T(8,128)(2,1)S(1)}, bf16[512,1536]{1,0:T(8,128)(2,1)}, u32[]{:S(2)}, u32[]{:S(2)}) collective-permute-start(bf16[512,1536]{1,0:T(8,128)(2,1)S(1)} %fusion.4), channel_id=1, source_target_pairs={{3,2},{7,6},{11,10},{15,14},{19,18},{23,22},{27,26},{31,30}} | collective-permute-start | bytes 4718600 | tf_op jit(solution)/shard_map/ppermute | solution.py:89
  57.4 3.7 %fusion.6 = f32[512,1536]{1,0:T(8,128)S(1)} fusion(bf16[512,1024]{1,0:T(8,128)(2,1)S(1)} %copy-done.2, bf16[1024,6144]{1,0:T(8,128)(2,1)} %param.9, s32[]{:T(128)S(6)} %select_n.62), kind=kOutput, calls=%fused_computation.11 | convolution fusion | flops 1610612736 | bytes 7340036 | tf_op jit(solution)/shard_map/dot_general | solution.py:43
  61.1 27.2 %collective-permute-done.5 = bf16[512,1536]{1,0:T(8,128)(2,1)} collective-permute-done((bf16[512,1536]{1,0:T(8,128)(2,1)S(1)}, bf16[512,1536]{1,0:T(8,128)(2,1)}, u32[]{:S(2)}, u32[]{:S(2)}) %collective-permute-start.5) | collective-permute-done | bytes 1572896 | tf_op jit(solution)/shard_map/ppermute | solution.py:88
  88.3 2.8 %add_convert_fusion.3 = (bf16[512,1536]{1,0:T(8,128)(2,1)S(1)}, bf16[512,1536]{1,0:T(8,128)(2,1)S(1)}) fusion(f32[512,1536]{1,0:T(8,128)S(1)} %fusion.6, bf16[512,1536]{1,0:T(8,128)(2,1)} %collective-permute-done.5, bf16[512,1536]{1,0:T(8,128)(2,1)} %collective-permute-done.8), kind=kLoop, calls=%fused_computation.8 | loop fusion | flops 4718592 | bytes 9437184 | tf_op jit(solution)/shard_map/convert_element_type | solution.py:88
  91.0 1.8 %collective-permute-start.9 = (bf16[512,1536]{1,0:T(8,128)(2,1)S(1)}, bf16[512,1536]{1,0:T(8,128)(2,1)}, u32[]{:S(2)}, u32[]{:S(2)}) collective-permute-start(bf16[512,1536]{1,0:T(8,128)(2,1)S(1)} %get-tuple-element.24), channel_id=1, source_target_pairs={{2,1},{3,2},{6,5},{7,6},{10,9},{11,10},{14,13},{15,14},{18,17},{19... | collective-permute-start | bytes 4718600 | tf_op jit(solution)/shard_map/ppermute | solution.py:89
  92.9 5.1 %collective-permute-start.6 = (bf16[512,1536]{1,0:T(8,128)(2,1)S(1)}, bf16[512,1536]{1,0:T(8,128)(2,1)}, u32[]{:S(2)}, u32[]{:S(2)}) collective-permute-start(bf16[512,1536]{1,0:T(8,128)(2,1)S(1)} %get-tuple-element.23), channel_id=1, source_target_pairs={{0,1},{1,2},{4,5},{5,6},{8,9},{9,10},{12,13},{13,14},{16,17},{17,1... | collective-permute-start | bytes 4718600 | tf_op jit(solution)/shard_map/ppermute | solution.py:88
  98.0 4.1 %fusion.8 = f32[512,1536]{1,0:T(8,128)S(1)} fusion(bf16[512,1024]{1,0:T(8,128)(2,1)} %get-tuple-element.17, bf16[1024,6144]{1,0:T(8,128)(2,1)} %param.9, s32[]{:T(128)S(6)} %select_n.60), kind=kOutput, calls=%fused_computation.13 | convolution fusion | flops 1610612736 | bytes 7340036 | tf_op jit(solution)/shard_map/dot_general | solution.py:43
  102.1 3.7 %fusion.10 = f32[512,1536]{1,0:T(8,128)S(1)} fusion(bf16[512,1024]{1,0:T(8,128)(2,1)S(1)} %copy-done.3, bf16[1024,6144]{1,0:T(8,128)(2,1)} %param.9, s32[]{:T(128)S(6)} %select_n.59), kind=kOutput, calls=%fused_computation.15 | convolution fusion | flops 1610612736 | bytes 7340036 | tf_op jit(solution)/shard_map/dot_general | solution.py:43
  105.8 3.1 %add_convert_fusion = bf16[512,1536]{1,0:T(8,128)(2,1)} fusion(f32[512,1536]{1,0:T(8,128)S(1)} %fusion.8, bf16[512,1536]{1,0:T(8,128)(2,1)} %collective-permute-done.9), kind=kLoop, calls=%fused_computation.5 | loop fusion | flops 2359296 | bytes 6291456 | tf_op jit(solution)/shard_map/convert_element_type | solution.py:89
  108.9 1.3 collective-permute-start.10
  110.2 19.6 %collective-permute-done.6 = bf16[512,1536]{1,0:T(8,128)(2,1)} collective-permute-done((bf16[512,1536]{1,0:T(8,128)(2,1)S(1)}, bf16[512,1536]{1,0:T(8,128)(2,1)}, u32[]{:S(2)}, u32[]{:S(2)}) %collective-permute-start.6) | collective-permute-done | bytes 1572896 | tf_op jit(solution)/shard_map/ppermute | solution.py:88
  129.8 2.0 %add_convert_fusion.2 = bf16[512,1536]{1,0:T(8,128)(2,1)S(1)} fusion(f32[512,1536]{1,0:T(8,128)S(1)} %fusion.10, bf16[512,1536]{1,0:T(8,128)(2,1)} %collective-permute-done.6), kind=kLoop, calls=%fused_computation.7 | loop fusion | flops 2359296 | bytes 6291456 | tf_op jit(solution)/shard_map/convert_element_type | solution.py:88
  131.8 11.4 %collective-permute-start.7 = (bf16[512,1536]{1,0:T(8,128)(2,1)S(1)}, bf16[512,1536]{1,0:T(8,128)(2,1)}, u32[]{:S(2)}, u32[]{:S(2)}) collective-permute-start(bf16[512,1536]{1,0:T(8,128)(2,1)S(1)} %add_convert_fusion.2), channel_id=1, source_target_pairs={{0,1},{1,2},{2,3},{4,5},{5,6},{6,7},{8,9},{9,10},{10,11},{12,13},{... | collective-permute-start | bytes 4718600 | tf_op jit(solution)/shard_map/ppermute | solution.py:88
  143.2 4.0 %fusion.12 = f32[512,1536]{1,0:T(8,128)S(1)} fusion(bf16[512,1024]{1,0:T(8,128)(2,1)} %get-tuple-element.17, bf16[1024,6144]{1,0:T(8,128)(2,1)} %param.9, s32[]{:T(128)S(6)} %select_n.58), kind=kOutput, calls=%fused_computation.17 | convolution fusion | flops 1610612736 | bytes 7340036 | tf_op jit(solution)/shard_map/dot_general | solution.py:43
  147.3 24.4 %collective-permute-done.10 = bf16[512,1536]{1,0:T(8,128)(2,1)S(1)} collective-permute-done((bf16[512,1536]{1,0:T(8,128)(2,1)}, bf16[512,1536]{1,0:T(8,128)(2,1)S(1)}, u32[]{:S(2)}, u32[]{:S(2)}) %collective-permute-start.10) | collective-permute-done | bytes 1572896 | tf_op jit(solution)/shard_map/ppermute | solution.py:89
  171.7 3.0 %collective-permute-done.7 = bf16[512,1536]{1,0:T(8,128)(2,1)} collective-permute-done((bf16[512,1536]{1,0:T(8,128)(2,1)S(1)}, bf16[512,1536]{1,0:T(8,128)(2,1)}, u32[]{:S(2)}, u32[]{:S(2)}) %collective-permute-start.7) | collective-permute-done | bytes 1572896 | tf_op jit(solution)/shard_map/ppermute | solution.py:88
  174.7 3.2 %multiply_convert_fusion.2 = bf16[512,1536]{1,0:T(8,128)(2,1)} fusion(bf16[512,1536]{1,0:T(8,128)(2,1)S(1)} %collective-permute-done.10, f32[512,1536]{1,0:T(8,128)S(1)} %fusion.12, bf16[512,1536]{1,0:T(8,128)(2,1)} %collective-permute-done.7, f32[512]{0:T(512)S(1)} %rsqrt_reduce_fusion), kind=kLoop, calls=%fused_computation.4 | loop fusion | flops 4718592 | bytes 7866368 | tf_op jit(solution)/shard_map/convert_element_type | solution.py:182
  (24 shorter events, 5.7 us)
Async XLA Ops:
  0.0 2.5 %copy-start = (bf16[512,1024]{1,0:T(8,128)(2,1)S(1)}, bf16[512,1024]{1,0:T(8,128)(2,1)}, u32[]{:S(2)}) copy-start(bf16[512,1024]{1,0:T(8,128)(2,1)} %param.7) | copy-start | bytes 3145732
  4.1 1.7 collective-permute-start
  6.6 11.3 %collective-permute-start.1 = (bf16[8,128,128]{2,1,0:T(8,128)(2,1)}, bf16[8,128,128]{2,1,0:T(8,128)(2,1)S(1)}, u32[]{:S(2)}, u32[]{:S(2)}) collective-permute-start(bf16[8,128,128]{2,1,0:T(8,128)(2,1)} %fusion.33), channel_id=1, source_target_pairs={{0,8},{4,12},{8,0},{12,4},{16,24},{20,28},{24,16},{28,20},{1,9},{5... | collective-permute-start | bytes 786440 | tf_op jit(solution)/shard_map/ppermute | solution.py:32
  14.8 4.7 %copy-start.1 = (bf16[512,1024]{1,0:T(8,128)(2,1)S(1)}, bf16[512,1024]{1,0:T(8,128)(2,1)}, u32[]{:S(2)}) copy-start(bf16[512,1024]{1,0:T(8,128)(2,1)} %param.5) | copy-start | bytes 3145732
  17.9 8.1 %collective-permute-start.2 = (bf16[8,128,128]{2,1,0:T(8,128)(2,1)S(1)}, bf16[8,128,128]{2,1,0:T(8,128)(2,1)S(1)}, u32[]{:S(2)}, u32[]{:S(2)}) collective-permute-start(bf16[8,128,128]{2,1,0:T(8,128)(2,1)S(1)} %convert_add_fusion), channel_id=1, source_target_pairs={{0,16},{4,20},{8,24},{12,28},{16,0},{20,4},{24,8},{28,12},{1,17},{... | collective-permute-start | bytes 786440 | tf_op jit(solution)/shard_map/ppermute | solution.py:32
  30.5 7.4 %collective-permute-start.3 = (f32[512,1]{1,0:T(8,128)}, f32[512,1]{1,0:T(8,128)S(1)}, u32[]{:S(2)}, u32[]{:S(2)}) collective-permute-start(f32[512,1]{1,0:T(8,128)} %get-tuple-element.19), channel_id=1, source_target_pairs={{0,1},{1,0},{2,3},{3,2},{4,5},{5,4},{6,7},{7,6},{8,9},{9,8},{10,11... | collective-permute-start | bytes 6152 | tf_op jit(solution)/shard_map/ppermute | solution.py:52
  38.9 12.9 %collective-permute-start.4 = (f32[512,1]{1,0:T(8,128)S(1)}, f32[512,1]{1,0:T(8,128)S(1)}, u32[]{:S(2)}, u32[]{:S(2)}) collective-permute-start(f32[512,1]{1,0:T(8,128)S(1)} %add.133), channel_id=1, source_target_pairs={{0,2},{1,3},{2,0},{3,1},{4,6},{5,7},{6,4},{7,5},{8,10},{9,11},{10,... | collective-permute-start | bytes 6152 | tf_op jit(solution)/shard_map/ppermute | solution.py:52
  41.5 15.9 %copy-start.2 = (bf16[512,1024]{1,0:T(8,128)(2,1)S(1)}, bf16[512,1024]{1,0:T(8,128)(2,1)}, u32[]{:S(2)}) copy-start(bf16[512,1024]{1,0:T(8,128)(2,1)} %get-tuple-element.17) | copy-start | bytes 3145732
  51.9 36.4 %collective-permute-start.5 = (bf16[512,1536]{1,0:T(8,128)(2,1)S(1)}, bf16[512,1536]{1,0:T(8,128)(2,1)}, u32[]{:S(2)}, u32[]{:S(2)}) collective-permute-start(bf16[512,1536]{1,0:T(8,128)(2,1)S(1)} %fusion.4), channel_id=1, source_target_pairs={{0,1},{4,5},{8,9},{12,13},{16,17},{20,21},{24,25},{28,29}} | collective-permute-start | bytes 4718600 | tf_op jit(solution)/shard_map/ppermute | solution.py:88
  55.6 32.7 %collective-permute-start.8 = (bf16[512,1536]{1,0:T(8,128)(2,1)S(1)}, bf16[512,1536]{1,0:T(8,128)(2,1)}, u32[]{:S(2)}, u32[]{:S(2)}) collective-permute-start(bf16[512,1536]{1,0:T(8,128)(2,1)S(1)} %fusion.4), channel_id=1, source_target_pairs={{3,2},{7,6},{11,10},{15,14},{19,18},{23,22},{27,26},{31,30}} | collective-permute-start | bytes 4718600 | tf_op jit(solution)/shard_map/ppermute | solution.py:89
  91.0 14.7 %collective-permute-start.9 = (bf16[512,1536]{1,0:T(8,128)(2,1)S(1)}, bf16[512,1536]{1,0:T(8,128)(2,1)}, u32[]{:S(2)}, u32[]{:S(2)}) collective-permute-start(bf16[512,1536]{1,0:T(8,128)(2,1)S(1)} %get-tuple-element.24), channel_id=1, source_target_pairs={{2,1},{3,2},{6,5},{7,6},{10,9},{11,10},{14,13},{15,14},{18,17},{19... | collective-permute-start | bytes 4718600 | tf_op jit(solution)/shard_map/ppermute | solution.py:89
  92.9 36.9 %collective-permute-start.6 = (bf16[512,1536]{1,0:T(8,128)(2,1)S(1)}, bf16[512,1536]{1,0:T(8,128)(2,1)}, u32[]{:S(2)}, u32[]{:S(2)}) collective-permute-start(bf16[512,1536]{1,0:T(8,128)(2,1)S(1)} %get-tuple-element.23), channel_id=1, source_target_pairs={{0,1},{1,2},{4,5},{5,6},{8,9},{9,10},{12,13},{13,14},{16,17},{17,1... | collective-permute-start | bytes 4718600 | tf_op jit(solution)/shard_map/ppermute | solution.py:88
  98.0 4.1 %copy-start.3 = (bf16[512,1024]{1,0:T(8,128)(2,1)S(1)}, bf16[512,1024]{1,0:T(8,128)(2,1)}, u32[]{:S(2)}) copy-start(bf16[512,1024]{1,0:T(8,128)(2,1)} %get-tuple-element.17) | copy-start | bytes 3145732
  108.9 62.8 %collective-permute-start.10 = (bf16[512,1536]{1,0:T(8,128)(2,1)}, bf16[512,1536]{1,0:T(8,128)(2,1)S(1)}, u32[]{:S(2)}, u32[]{:S(2)}) collective-permute-start(bf16[512,1536]{1,0:T(8,128)(2,1)} %add_convert_fusion), channel_id=1, source_target_pairs={{1,0},{2,1},{3,2},{5,4},{6,5},{7,6},{9,8},{10,9},{11,10},{13,12},{... | collective-permute-start | bytes 4718600 | tf_op jit(solution)/shard_map/ppermute | solution.py:89
  131.8 42.9 %collective-permute-start.7 = (bf16[512,1536]{1,0:T(8,128)(2,1)S(1)}, bf16[512,1536]{1,0:T(8,128)(2,1)}, u32[]{:S(2)}, u32[]{:S(2)}) collective-permute-start(bf16[512,1536]{1,0:T(8,128)(2,1)S(1)} %add_convert_fusion.2), channel_id=1, source_target_pairs={{0,1},{1,2},{2,3},{4,5},{5,6},{6,7},{8,9},{9,10},{10,11},{12,13},{... | collective-permute-start | bytes 4718600 | tf_op jit(solution)/shard_map/ppermute | solution.py:88

commit v12 on v11

--- a/solution.py
+++ b/solution.py
@@ -93,7 +93,7 @@
     scaling = lax.rsqrt(total_squares / (HEADS * HEAD_DIM) + 1e-06)
     if from_left is not None:
         own = own + from_left + from_right
-    return own * scaling
+    return own * scaling[:, None]
 
 
 def finish_kernel(query_ref, within_ref, gate_ref, state_ref, gated_ref, squares_ref):
@@ -169,12 +169,13 @@
             gate_logits,
             before[0],
         )
+        square_sums = square_sums[:, 0]
     else:
         from_state = jnp.einsum(
             "nthd,nhde->nthe", active_q, before, preferred_element_type=jnp.float32
         )
         attended = within_rows + from_state.reshape(tokens_here, feature_count)
-        square_sums = jnp.sum(attended * attended, axis=-1, keepdims=True)
+        square_sums = jnp.sum(attended * attended, axis=-1)
         gate = jax.nn.sigmoid(gate_logits.astype(jnp.float32))
         gated = (attended * gate).astype(jnp.bfloat16)
     total_squares = butterfly_sum(square_sums, "head")

time: 178 us -> 159 us (0.89)
  waiting for transfers between devices: 91.2 us -> 73.4 us
    ppermute x2, waiting for transfers between devices: 12.1 us -> 2.02 us  [butterfly_sum(): lax.ppermute(values, axis_name, [(i, i ^ bit) for i in range(count)])]
    ppermute x3, waiting for transfers between devices: 49.8 us -> 44.9 us  [line_reduce_scatter(): lax.ppermute(to_right.astype(jnp.bfloat16), axis_name, right_pairs)]
    ppermute x3, waiting for transfers between devices: 24.4 us -> 21.5 us  [line_reduce_scatter(): lax.ppermute(to_left.astype(jnp.bfloat16), axis_name, left_pairs)]
  transfers between devices with their start and end apart: 11 -> 11, of which waited for: 8 -> 7; matrix products, arithmetic and copies ran while one was open for 20% -> 22% of each run, Pallas kernels for 0% -> 0%
where the time goes in v12:
time: 159 us
  waiting for transfers between devices  73.4 us (46%)
  starting transfers between devices  33.3 us (21%)
  matrix products  25.4 us (16%)
  other arithmetic  19.2 us (12%)
  local copies, waits for them, and re-layouts  4.09 us (3%)
  Pallas kernels  3.48 us (2%)
    ppermute x3, waiting for transfers between devices, line_reduce_scatter(): lax.ppermute(to_right.astype(jnp.bfloat16), axis_name, right_pairs)  44.9 us
    ppermute x3, waiting for transfers between devices, line_reduce_scatter(): lax.ppermute(to_left.astype(jnp.bfloat16), axis_name, left_pairs)  21.5 us
    dot_general x5, matrix products, shard_product(): return jnp.dot(gated, columns, preferred_element_type=jnp.float32)  19.5 us
    ppermute x3, starting transfers between devices, line_reduce_scatter(): lax.ppermute(to_right.astype(jnp.bfloat16), axis_name, right_pairs)  19.2 us
    dot_general x1, matrix products, body(): jnp.einsum('nhts,nshd->nthd', scores, active_v, preferred_element_type=jn...  5.42 us
    ppermute x3, waiting for transfers between devices, exclusive_prefix(): arrived = lax.ppermute(group_total.astype(jnp.bfloat16), axis_name, pairs)  5.05 us
    ppermute x3, starting transfers between devices, exclusive_prefix(): arrived = lax.ppermute(group_total.astype(jnp.bfloat16), axis_name, pairs)  4.99 us
    ppermute x3, starting transfers between devices, line_reduce_scatter(): lax.ppermute(to_left.astype(jnp.bfloat16), axis_name, left_pairs)  4.91 us
  transfers between devices with their start and end apart: 11, of which 7 were waited for; matrix products, arithmetic and copies ran while one was open for 22% of the time, Pallas kernels for 0%

profile of v12, /device:TPU:0, one launch (start us, length us, event | category | flops | bytes accessed | tf_op | source)
XLA Modules:
  0.0 159.0 jit_solution(9962081733580148295)
XLA Ops:
  0.0 1.9 %fusion.21 = bf16[512,1024]{1,0:T(8,128)(2,1)S(1)} fusion(bf16[512,1024]{1,0:T(8,128)(2,1)} %param.6), kind=kLoop, calls=%fused_computation.32 | loop fusion | flops 3145728 | bytes 2097152 | tf_op jit(solution)/shard_map/convert_element_type | solution.py:12
  4.7 1.1 fusion.30
  6.6 2.9 %collective-permute-start.1 = (bf16[8,128,128]{2,1,0:T(8,128)(2,1)}, bf16[8,128,128]{2,1,0:T(8,128)(2,1)S(1)}, u32[]{:S(2)}, u32[]{:S(2)}) collective-permute-start(bf16[8,128,128]{2,1,0:T(8,128)(2,1)} %fusion.33), channel_id=1, source_target_pairs={{0,8},{4,12},{8,0},{12,4},{16,24},{20,28},{24,16},{28,20},{1,9},{5... | collective-permute-start | bytes 786440 | tf_op jit(solution)/shard_map/ppermute | solution.py:32
  9.4 5.4 %fusion = f32[8,128,512]{2,1,0:T(8,128)} fusion(bf16[512,8,128]{0,2,1:T(8,128)(2,1)S(1)} %bitcast.28, f32[512,512]{1,0:T(8,128)} %fusion.30, bf16[512,8,128]{0,2,1:T(8,128)(2,1)S(1)} %bitcast.26, bf16[512,1024]{1,0:T(8,128)(2,1)} %param.5), kind=kOutput, calls=%fused_computation.1 | convolution fusion | flops 1081081856 | bytes 6291456 | tf_op jit(solution)/shard_map/nhts,nshd->nthd/dot_general | solution.py:158
  14.9 3.0 %copy.16.within_ref = f32[512,1024]{1,0:T(8,128)} copy(f32[512,1024]{0,1:T(8,128)} %bitcast.29) | data formatting | bytes 4194304 | tf_op jit(solution)/shard_map/reshape | solution.py:161
  17.9 1.6 collective-permute-start.2
  19.5 1.6 fusion.17.query_ref
  21.1 5.0 %collective-permute-done.2 = bf16[8,128,128]{2,1,0:T(8,128)(2,1)S(1)} collective-permute-done((bf16[8,128,128]{2,1,0:T(8,128)(2,1)S(1)}, bf16[8,128,128]{2,1,0:T(8,128)(2,1)S(1)}, u32[]{:S(2)}, u32[]{:S(2)}) %collective-permute-start.2) | collective-permute-done | bytes 262176 | tf_op jit(solution)/shard_map/ppermute | solution.py:32
  27.0 3.5 %shard_map.55 = (bf16[512,1024]{1,0:T(8,128)(2,1)}, f32[512,1]{1,0:T(8,128)}) custom-call(bf16[512,1024]{1,0:T(8,128)(2,1)} %fusion.17.query_ref, f32[512,1024]{1,0:T(8,128)} %copy.16.within_ref, bf16[512,1024]{1,0:T(8,128)(2,1)} %gate_ref.1, bf16[8,128,128]{2,1,0:T(8,128)(2,1)} %add_convert_fusion.4.state_ref), custom_call_target="tpu_custom_call" | custom-call | tf_op jit(solution)/shard_map/pallas_call | solution.py:123
  30.5 1.1 reduce
  31.6 1.6 %collective-permute-start.3 = (f32[512]{0:T(512)S(1)}, f32[512]{0:T(512)S(1)}, u32[]{:S(2)}, u32[]{:S(2)}) collective-permute-start(f32[512]{0:T(512)S(1)} %reduce), channel_id=1, source_target_pairs={{0,1},{1,0},{2,3},{3,2},{4,5},{5,4},{6,7},{7,6},{8,9},{9,8},{10,11... | collective-permute-start | bytes 6152 | tf_op jit(solution)/shard_map/ppermute | solution.py:52
  33.2 2.0 %collective-permute-done.3 = f32[512]{0:T(512)S(1)} collective-permute-done((f32[512]{0:T(512)S(1)}, f32[512]{0:T(512)S(1)}, u32[]{:S(2)}, u32[]{:S(2)}) %collective-permute-start.3) | collective-permute-done | bytes 2080 | tf_op jit(solution)/shard_map/ppermute | solution.py:52
  35.2 2.6 %collective-permute-start.4 = (f32[512]{0:T(512)S(1)}, f32[512]{0:T(512)S(1)}, u32[]{:S(2)}, u32[]{:S(2)}) collective-permute-start(f32[512]{0:T(512)S(1)} %add.133), channel_id=1, source_target_pairs={{0,2},{1,3},{2,0},{3,1},{4,6},{5,7},{6,4},{7,5},{8,10},{9,11},{10,... | collective-permute-start | bytes 6152 | tf_op jit(solution)/shard_map/ppermute | solution.py:52
  37.8 4.1 %fusion.4 = bf16[512,1536]{1,0:T(8,128)(2,1)S(1)} fusion(bf16[512,1024]{1,0:T(8,128)(2,1)} %get-tuple-element.17, bf16[1024,6144]{1,0:T(8,128)(2,1)} %param.9, s32[]{:T(128)S(6)} %select_n.64), kind=kOutput, calls=%fused_computation.9 | convolution fusion | flops 1610612736 | bytes 5767172 | tf_op jit(solution)/shard_map/dot_general | solution.py:43
  41.9 4.7 %collective-permute-start.5 = (bf16[512,1536]{1,0:T(8,128)(2,1)S(1)}, bf16[512,1536]{1,0:T(8,128)(2,1)}, u32[]{:S(2)}, u32[]{:S(2)}) collective-permute-start(bf16[512,1536]{1,0:T(8,128)(2,1)S(1)} %fusion.4), channel_id=1, source_target_pairs={{0,1},{4,5},{8,9},{12,13},{16,17},{20,21},{24,25},{28,29}} | collective-permute-start | bytes 4718600 | tf_op jit(solution)/shard_map/ppermute | solution.py:88
  46.6 1.8 %collective-permute-start.8 = (bf16[512,1536]{1,0:T(8,128)(2,1)S(1)}, bf16[512,1536]{1,0:T(8,128)(2,1)}, u32[]{:S(2)}, u32[]{:S(2)}) collective-permute-start(bf16[512,1536]{1,0:T(8,128)(2,1)S(1)} %fusion.4), channel_id=1, source_target_pairs={{3,2},{7,6},{11,10},{15,14},{19,18},{23,22},{27,26},{31,30}} | collective-permute-start | bytes 4718600 | tf_op jit(solution)/shard_map/ppermute | solution.py:89
  48.4 3.7 %fusion.6 = f32[512,1536]{1,0:T(8,128)S(1)} fusion(bf16[512,1024]{1,0:T(8,128)(2,1)S(1)} %copy-done.2, bf16[1024,6144]{1,0:T(8,128)(2,1)} %param.9, s32[]{:T(128)S(6)} %select_n.62), kind=kOutput, calls=%fused_computation.11 | convolution fusion | flops 1610612736 | bytes 7340036 | tf_op jit(solution)/shard_map/dot_general | solution.py:43
  52.1 24.7 %collective-permute-done.5 = bf16[512,1536]{1,0:T(8,128)(2,1)} collective-permute-done((bf16[512,1536]{1,0:T(8,128)(2,1)S(1)}, bf16[512,1536]{1,0:T(8,128)(2,1)}, u32[]{:S(2)}, u32[]{:S(2)}) %collective-permute-start.5) | collective-permute-done | bytes 1572896 | tf_op jit(solution)/shard_map/ppermute | solution.py:88
  76.8 2.8 %add_convert_fusion.3 = (bf16[512,1536]{1,0:T(8,128)(2,1)S(1)}, bf16[512,1536]{1,0:T(8,128)(2,1)S(1)}) fusion(f32[512,1536]{1,0:T(8,128)S(1)} %fusion.6, bf16[512,1536]{1,0:T(8,128)(2,1)} %collective-permute-done.5, bf16[512,1536]{1,0:T(8,128)(2,1)} %collective-permute-done.8), kind=kLoop, calls=%fused_computation.8 | loop fusion | flops 4718592 | bytes 9437184 | tf_op jit(solution)/shard_map/convert_element_type | solution.py:88
  79.6 1.8 %collective-permute-start.9 = (bf16[512,1536]{1,0:T(8,128)(2,1)S(1)}, bf16[512,1536]{1,0:T(8,128)(2,1)}, u32[]{:S(2)}, u32[]{:S(2)}) collective-permute-start(bf16[512,1536]{1,0:T(8,128)(2,1)S(1)} %get-tuple-element.24), channel_id=1, source_target_pairs={{2,1},{3,2},{6,5},{7,6},{10,9},{11,10},{14,13},{15,14},{18,17},{19... | collective-permute-start | bytes 4718600 | tf_op jit(solution)/shard_map/ppermute | solution.py:89
  81.4 5.1 %collective-permute-start.6 = (bf16[512,1536]{1,0:T(8,128)(2,1)S(1)}, bf16[512,1536]{1,0:T(8,128)(2,1)}, u32[]{:S(2)}, u32[]{:S(2)}) collective-permute-start(bf16[512,1536]{1,0:T(8,128)(2,1)S(1)} %get-tuple-element.23), channel_id=1, source_target_pairs={{0,1},{1,2},{4,5},{5,6},{8,9},{9,10},{12,13},{13,14},{16,17},{17,1... | collective-permute-start | bytes 4718600 | tf_op jit(solution)/shard_map/ppermute | solution.py:88
  86.5 4.1 %fusion.8 = f32[512,1536]{1,0:T(8,128)S(1)} fusion(bf16[512,1024]{1,0:T(8,128)(2,1)} %get-tuple-element.17, bf16[1024,6144]{1,0:T(8,128)(2,1)} %param.9, s32[]{:T(128)S(6)} %select_n.60), kind=kOutput, calls=%fused_computation.13 | convolution fusion | flops 1610612736 | bytes 7340036 | tf_op jit(solution)/shard_map/dot_general | solution.py:43
  90.6 3.7 %fusion.10 = f32[512,1536]{1,0:T(8,128)S(1)} fusion(bf16[512,1024]{1,0:T(8,128)(2,1)S(1)} %copy-done.3, bf16[1024,6144]{1,0:T(8,128)(2,1)} %param.9, s32[]{:T(128)S(6)} %select_n.59), kind=kOutput, calls=%fused_computation.15 | convolution fusion | flops 1610612736 | bytes 7340036 | tf_op jit(solution)/shard_map/dot_general | solution.py:43
  94.3 3.1 %add_convert_fusion = bf16[512,1536]{1,0:T(8,128)(2,1)} fusion(f32[512,1536]{1,0:T(8,128)S(1)} %fusion.8, bf16[512,1536]{1,0:T(8,128)(2,1)} %collective-permute-done.9), kind=kLoop, calls=%fused_computation.5 | loop fusion | flops 2359296 | bytes 6291456 | tf_op jit(solution)/shard_map/convert_element_type | solution.py:89
  97.4 1.3 collective-permute-start.10
  98.7 17.2 %collective-permute-done.6 = bf16[512,1536]{1,0:T(8,128)(2,1)} collective-permute-done((bf16[512,1536]{1,0:T(8,128)(2,1)S(1)}, bf16[512,1536]{1,0:T(8,128)(2,1)}, u32[]{:S(2)}, u32[]{:S(2)}) %collective-permute-start.6) | collective-permute-done | bytes 1572896 | tf_op jit(solution)/shard_map/ppermute | solution.py:88
  115.9 2.0 %add_convert_fusion.2 = bf16[512,1536]{1,0:T(8,128)(2,1)S(1)} fusion(f32[512,1536]{1,0:T(8,128)S(1)} %fusion.10, bf16[512,1536]{1,0:T(8,128)(2,1)} %collective-permute-done.6), kind=kLoop, calls=%fused_computation.7 | loop fusion | flops 2359296 | bytes 6291456 | tf_op jit(solution)/shard_map/convert_element_type | solution.py:88
  117.9 9.4 %collective-permute-start.7 = (bf16[512,1536]{1,0:T(8,128)(2,1)S(1)}, bf16[512,1536]{1,0:T(8,128)(2,1)}, u32[]{:S(2)}, u32[]{:S(2)}) collective-permute-start(bf16[512,1536]{1,0:T(8,128)(2,1)S(1)} %add_convert_fusion.2), channel_id=1, source_target_pairs={{0,1},{1,2},{2,3},{4,5},{5,6},{6,7},{8,9},{9,10},{10,11},{12,13},{... | collective-permute-start | bytes 4718600 | tf_op jit(solution)/shard_map/ppermute | solution.py:88
  127.3 4.0 %fusion.12 = f32[512,1536]{1,0:T(8,128)S(1)} fusion(bf16[512,1024]{1,0:T(8,128)(2,1)} %get-tuple-element.17, bf16[1024,6144]{1,0:T(8,128)(2,1)} %param.9, s32[]{:T(128)S(6)} %select_n.58), kind=kOutput, calls=%fused_computation.17 | convolution fusion | flops 1610612736 | bytes 7340036 | tf_op jit(solution)/shard_map/dot_general | solution.py:43
  131.3 21.5 %collective-permute-done.10 = bf16[512,1536]{1,0:T(8,128)(2,1)S(1)} collective-permute-done((bf16[512,1536]{1,0:T(8,128)(2,1)}, bf16[512,1536]{1,0:T(8,128)(2,1)S(1)}, u32[]{:S(2)}, u32[]{:S(2)}) %collective-permute-start.10) | collective-permute-done | bytes 1572896 | tf_op jit(solution)/shard_map/ppermute | solution.py:89
  152.8 3.0 %collective-permute-done.7 = bf16[512,1536]{1,0:T(8,128)(2,1)} collective-permute-done((bf16[512,1536]{1,0:T(8,128)(2,1)S(1)}, bf16[512,1536]{1,0:T(8,128)(2,1)}, u32[]{:S(2)}, u32[]{:S(2)}) %collective-permute-start.7) | collective-permute-done | bytes 1572896 | tf_op jit(solution)/shard_map/ppermute | solution.py:88
  155.8 3.2 %multiply_convert_fusion.2 = bf16[512,1536]{1,0:T(8,128)(2,1)} fusion(bf16[512,1536]{1,0:T(8,128)(2,1)S(1)} %collective-permute-done.10, f32[512,1536]{1,0:T(8,128)S(1)} %fusion.12, bf16[512,1536]{1,0:T(8,128)(2,1)} %collective-permute-done.7, f32[512]{0:T(512)S(1)} %add_rsqrt_fusion), kind=kLoop, calls=%fused_computation.4 | loop fusion | flops 4718592 | bytes 7866368 | tf_op jit(solution)/shard_map/convert_element_type | solution.py:183
  (25 shorter events, 4.6 us)
Async XLA Ops:
  0.0 2.5 %copy-start = (bf16[512,1024]{1,0:T(8,128)(2,1)S(1)}, bf16[512,1024]{1,0:T(8,128)(2,1)}, u32[]{:S(2)}) copy-start(bf16[512,1024]{1,0:T(8,128)(2,1)} %param.7) | copy-start | bytes 3145732
  4.1 1.7 %collective-permute-start = (bf16[8,128,128]{2,1,0:T(8,128)(2,1)S(1)}, bf16[8,128,128]{2,1,0:T(8,128)(2,1)S(1)}, u32[]{:S(2)}, u32[]{:S(2)}) collective-permute-start(bf16[8,128,128]{2,1,0:T(8,128)(2,1)S(1)} %get-tuple-element.25), channel_id=1, source_target_pairs={{0,4},{4,0},{8,12},{12,8},{16,20},{20,16},{24,28},{28,24},{1,5},{5... | collective-permute-start | bytes 786440 | tf_op jit(solution)/shard_map/ppermute | solution.py:32
  6.6 11.3 %collective-permute-start.1 = (bf16[8,128,128]{2,1,0:T(8,128)(2,1)}, bf16[8,128,128]{2,1,0:T(8,128)(2,1)S(1)}, u32[]{:S(2)}, u32[]{:S(2)}) collective-permute-start(bf16[8,128,128]{2,1,0:T(8,128)(2,1)} %fusion.33), channel_id=1, source_target_pairs={{0,8},{4,12},{8,0},{12,4},{16,24},{20,28},{24,16},{28,20},{1,9},{5... | collective-permute-start | bytes 786440 | tf_op jit(solution)/shard_map/ppermute | solution.py:32
  14.8 4.7 %copy-start.1 = (bf16[512,1024]{1,0:T(8,128)(2,1)S(1)}, bf16[512,1024]{1,0:T(8,128)(2,1)}, u32[]{:S(2)}) copy-start(bf16[512,1024]{1,0:T(8,128)(2,1)} %param.5) | copy-start | bytes 3145732
  17.9 8.1 %collective-permute-start.2 = (bf16[8,128,128]{2,1,0:T(8,128)(2,1)S(1)}, bf16[8,128,128]{2,1,0:T(8,128)(2,1)S(1)}, u32[]{:S(2)}, u32[]{:S(2)}) collective-permute-start(bf16[8,128,128]{2,1,0:T(8,128)(2,1)S(1)} %convert_add_fusion), channel_id=1, source_target_pairs={{0,16},{4,20},{8,24},{12,28},{16,0},{20,4},{24,8},{28,12},{1,17},{... | collective-permute-start | bytes 786440 | tf_op jit(solution)/shard_map/ppermute | solution.py:32
  31.6 3.7 %collective-permute-start.3 = (f32[512]{0:T(512)S(1)}, f32[512]{0:T(512)S(1)}, u32[]{:S(2)}, u32[]{:S(2)}) collective-permute-start(f32[512]{0:T(512)S(1)} %reduce), channel_id=1, source_target_pairs={{0,1},{1,0},{2,3},{3,2},{4,5},{5,4},{6,7},{7,6},{8,9},{9,8},{10,11... | collective-permute-start | bytes 6152 | tf_op jit(solution)/shard_map/ppermute | solution.py:52
  35.2 6.7 %collective-permute-start.4 = (f32[512]{0:T(512)S(1)}, f32[512]{0:T(512)S(1)}, u32[]{:S(2)}, u32[]{:S(2)}) collective-permute-start(f32[512]{0:T(512)S(1)} %add.133), channel_id=1, source_target_pairs={{0,2},{1,3},{2,0},{3,1},{4,6},{5,7},{6,4},{7,5},{8,10},{9,11},{10,... | collective-permute-start | bytes 6152 | tf_op jit(solution)/shard_map/ppermute | solution.py:52
  37.8 10.6 %copy-start.2 = (bf16[512,1024]{1,0:T(8,128)(2,1)S(1)}, bf16[512,1024]{1,0:T(8,128)(2,1)}, u32[]{:S(2)}) copy-start(bf16[512,1024]{1,0:T(8,128)(2,1)} %get-tuple-element.17) | copy-start | bytes 3145732
  41.9 34.9 %collective-permute-start.5 = (bf16[512,1536]{1,0:T(8,128)(2,1)S(1)}, bf16[512,1536]{1,0:T(8,128)(2,1)}, u32[]{:S(2)}, u32[]{:S(2)}) collective-permute-start(bf16[512,1536]{1,0:T(8,128)(2,1)S(1)} %fusion.4), channel_id=1, source_target_pairs={{0,1},{4,5},{8,9},{12,13},{16,17},{20,21},{24,25},{28,29}} | collective-permute-start | bytes 4718600 | tf_op jit(solution)/shard_map/ppermute | solution.py:88
  46.6 30.2 %collective-permute-start.8 = (bf16[512,1536]{1,0:T(8,128)(2,1)S(1)}, bf16[512,1536]{1,0:T(8,128)(2,1)}, u32[]{:S(2)}, u32[]{:S(2)}) collective-permute-start(bf16[512,1536]{1,0:T(8,128)(2,1)S(1)} %fusion.4), channel_id=1, source_target_pairs={{3,2},{7,6},{11,10},{15,14},{19,18},{23,22},{27,26},{31,30}} | collective-permute-start | bytes 4718600 | tf_op jit(solution)/shard_map/ppermute | solution.py:89
  79.6 14.7 %collective-permute-start.9 = (bf16[512,1536]{1,0:T(8,128)(2,1)S(1)}, bf16[512,1536]{1,0:T(8,128)(2,1)}, u32[]{:S(2)}, u32[]{:S(2)}) collective-permute-start(bf16[512,1536]{1,0:T(8,128)(2,1)S(1)} %get-tuple-element.24), channel_id=1, source_target_pairs={{2,1},{3,2},{6,5},{7,6},{10,9},{11,10},{14,13},{15,14},{18,17},{19... | collective-permute-start | bytes 4718600 | tf_op jit(solution)/shard_map/ppermute | solution.py:89
  81.4 34.5 %collective-permute-start.6 = (bf16[512,1536]{1,0:T(8,128)(2,1)S(1)}, bf16[512,1536]{1,0:T(8,128)(2,1)}, u32[]{:S(2)}, u32[]{:S(2)}) collective-permute-start(bf16[512,1536]{1,0:T(8,128)(2,1)S(1)} %get-tuple-element.23), channel_id=1, source_target_pairs={{0,1},{1,2},{4,5},{5,6},{8,9},{9,10},{12,13},{13,14},{16,17},{17,1... | collective-permute-start | bytes 4718600 | tf_op jit(solution)/shard_map/ppermute | solution.py:88
  86.5 4.1 %copy-start.3 = (bf16[512,1024]{1,0:T(8,128)(2,1)S(1)}, bf16[512,1024]{1,0:T(8,128)(2,1)}, u32[]{:S(2)}) copy-start(bf16[512,1024]{1,0:T(8,128)(2,1)} %get-tuple-element.17) | copy-start | bytes 3145732
  97.4 55.4 %collective-permute-start.10 = (bf16[512,1536]{1,0:T(8,128)(2,1)}, bf16[512,1536]{1,0:T(8,128)(2,1)S(1)}, u32[]{:S(2)}, u32[]{:S(2)}) collective-permute-start(bf16[512,1536]{1,0:T(8,128)(2,1)} %add_convert_fusion), channel_id=1, source_target_pairs={{1,0},{2,1},{3,2},{5,4},{6,5},{7,6},{9,8},{10,9},{11,10},{13,12},{... | collective-permute-start | bytes 4718600 | tf_op jit(solution)/shard_map/ppermute | solution.py:89
  117.9 37.9 %collective-permute-start.7 = (bf16[512,1536]{1,0:T(8,128)(2,1)S(1)}, bf16[512,1536]{1,0:T(8,128)(2,1)}, u32[]{:S(2)}, u32[]{:S(2)}) collective-permute-start(bf16[512,1536]{1,0:T(8,128)(2,1)S(1)} %add_convert_fusion.2), channel_id=1, source_target_pairs={{0,1},{1,2},{2,3},{4,5},{5,6},{6,7},{8,9},{9,10},{10,11},{12,13},{... | collective-permute-start | bytes 4718600 | tf_op jit(solution)/shard_map/ppermute | solution.py:88

commit v13 on v9

--- a/solution.py
+++ b/solution.py
@@ -64,31 +64,34 @@
         left_shard = jnp.clip(here - count + step, 0, count - 1)
         if 2 * step <= count:
             shard = jnp.where(here < step, right_shard, left_shard)
-            to_right = shard_product(gated, out_weight, shard, width)
+            product = shard_product(gated, out_weight, shard, width).astype(jnp.bfloat16)
             if step == 1:
-                to_right, total_squares = lax.optimization_barrier((to_right, total_squares))
+                product, total_squares = lax.optimization_barrier((product, total_squares))
             else:
-                to_right = lax.optimization_barrier(to_right)
+                product = lax.optimization_barrier(product)
+            to_right = product.astype(jnp.float32)
+            if from_left is not None:
+                to_right = to_right + from_left + from_right
+            to_right = to_right.astype(jnp.bfloat16)
             to_left = to_right
         else:
-            to_right = shard_product(gated, out_weight, right_shard, width)
-            to_left = shard_product(gated, out_weight, left_shard, width)
+            to_right = shard_product(gated, out_weight, right_shard, width).astype(jnp.bfloat16)
+            to_left = shard_product(gated, out_weight, left_shard, width).astype(jnp.bfloat16)
             if step == 1:
                 to_right, to_left, total_squares = lax.optimization_barrier(
                     (to_right, to_left, total_squares)
                 )
             else:
                 to_right, to_left = lax.optimization_barrier((to_right, to_left))
-        if from_left is not None:
-            to_right = to_right + from_left
-            to_left = to_left + from_right
+            if from_left is not None:
+                to_right = (to_right.astype(jnp.float32) + from_left).astype(jnp.bfloat16)
+                to_left = (to_left.astype(jnp.float32) + from_right).astype(jnp.bfloat16)
         right_pairs = [(i, i + 1) for i in range(step) if i + 1 < count]
         left_pairs = [(i, i - 1) for i in range(count - step, count) if i >= 1]
-        from_left = lax.ppermute(to_right.astype(jnp.bfloat16), axis_name, right_pairs)
-        from_right = lax.ppermute(to_left.astype(jnp.bfloat16), axis_name, left_pairs)
-        from_left = from_left.astype(jnp.float32)
-        from_right = from_right.astype(jnp.float32)
-    own = shard_product(gated, out_weight, here, width)
+        from_left = lax.ppermute(to_right, axis_name, right_pairs).astype(jnp.float32)
+        from_right = lax.ppermute(to_left, axis_name, left_pairs).astype(jnp.float32)
+    own = shard_product(gated, out_weight, here, width).astype(jnp.bfloat16)
+    own = own.astype(jnp.float32)
     scaling = lax.rsqrt(total_squares / (HEADS * HEAD_DIM) + 1e-06)
     if from_left is not None:
         own = own + from_left + from_right

time: 155 us -> 153 us (0.987)
  waiting for transfers between devices: 73 us -> 76.9 us
  starting transfers between devices: 33.6 us -> 30.4 us
  other arithmetic: 15.6 us -> 13 us
    ppermute x6, waiting for transfers between devices: 64.3 us -> 68.2 us  [the longest x3 44.5 us: line_reduce_scatter(): lax.ppermute(to_right, axis_name, right_pairs).astype(jnp.float32)]
    ppermute x6, starting transfers between devices: 24.1 us -> 20.9 us  [the longest x3 17.1 us: line_reduce_scatter(): lax.ppermute(to_right, axis_name, right_pairs).astype(jnp.float32)]
    convert_element_type x3, other arithmetic: 7.88 us -> 5.32 us  [the longest x1 2.94 us: line_reduce_scatter(): to_left = (to_left.astype(jnp.float32) + from_right).astype(jnp.bfloat16)]
where the time goes in v13:
time: 153 us
  waiting for transfers between devices  76.9 us (50%)
  starting transfers between devices  30.4 us (20%)
  matrix products  29.2 us (19%)
  other arithmetic  13 us (8%)
  local copies, waits for them, and re-layouts  3.12 us (2%)
    ppermute x3, waiting for transfers between devices, line_reduce_scatter(): lax.ppermute(to_right, axis_name, right_pairs).astype(jnp.float32)  44.5 us
    ppermute x3, waiting for transfers between devices, line_reduce_scatter(): lax.ppermute(to_left, axis_name, left_pairs).astype(jnp.float32)  23.7 us
    dot_general x5, matrix products, shard_product(): return jnp.dot(gated, columns, preferred_element_type=jnp.float32)  19.4 us
    ppermute x3, starting transfers between devices, line_reduce_scatter(): lax.ppermute(to_right, axis_name, right_pairs).astype(jnp.float32)  17.1 us
    ppermute x3, waiting for transfers between devices, exclusive_prefix(): arrived = lax.ppermute(group_total.astype(jnp.bfloat16), axis_name, pairs)  7.25 us
    dot_general x1, matrix products, body(): jnp.einsum('nhts,nshd->nthd', scores, active_v, preferred_element_type=jn...  5.44 us
    ppermute x3, starting transfers between devices, exclusive_prefix(): arrived = lax.ppermute(group_total.astype(jnp.bfloat16), axis_name, pairs)  5.3 us
    ppermute x2, starting transfers between devices, butterfly_sum(): lax.ppermute(values, axis_name, [(i, i ^ bit) for i in range(count)])  4.17 us
  transfers between devices with their start and end apart: 11, of which 8 were waited for; matrix products, arithmetic and copies ran while one was open for 20% of the time, Pallas kernels for 0%

profile of v13, /device:TPU:0, one launch (start us, length us, event | category | flops | bytes accessed | tf_op | source)
XLA Modules:
  0.0 152.8 jit_solution(13578256739760843456)
XLA Ops:
  0.0 1.9 %fusion.32 = bf16[512,1024]{1,0:T(8,128)(2,1)S(1)} fusion(bf16[512,1024]{1,0:T(8,128)(2,1)} %param.6), kind=kLoop, calls=%fused_computation.32 | loop fusion | flops 3145728 | bytes 2097152 | tf_op jit(solution)/shard_map/convert_element_type | solution.py:11
  2.5 0.6 fusion.36
  4.1 0.6 collective-permute-start
  4.7 1.1 fusion.46
  5.9 2.9 %collective-permute-start.1 = (bf16[8,128,128]{2,1,0:T(8,128)(2,1)S(1)}, bf16[8,128,128]{2,1,0:T(8,128)(2,1)S(1)}, u32[]{:S(2)}, u32[]{:S(2)}) collective-permute-start(bf16[8,128,128]{2,1,0:T(8,128)(2,1)S(1)} %fusion.52), channel_id=1, source_target_pairs={{0,8},{4,12},{8,0},{12,4},{16,24},{20,28},{24,16},{28,20},{1,9},{5... | collective-permute-start | bytes 786440 | tf_op jit(solution)/shard_map/ppermute | solution.py:31
  8.8 5.4 %fusion.41 = f32[1,512,8,128]{1,3,2,0:T(8,128)} fusion(bf16[512,8,128]{0,2,1:T(8,128)(2,1)S(1)} %bitcast.38, f32[512,512]{1,0:T(8,128)} %fusion.46, bf16[512,8,128]{0,2,1:T(8,128)(2,1)S(1)} %bitcast.36, bf16[512,1024]{1,0:T(8,128)(2,1)} %param.5), kind=kOutput, calls=%fused_computation.44 | convolution fusion | flops 1081081856 | bytes 6291456 | tf_op jit(solution)/shard_map/nhts,nshd->nthd/dot_general | solution.py:119
  14.2 1.2 collective-permute-done.1
  15.5 1.8 %collective-permute-start.2 = (bf16[8,128,128]{2,1,0:T(8,128)(2,1)S(1)}, bf16[8,128,128]{2,1,0:T(8,128)(2,1)S(1)}, u32[]{:S(2)}, u32[]{:S(2)}) collective-permute-start(bf16[8,128,128]{2,1,0:T(8,128)(2,1)S(1)} %convert_add_fusion), channel_id=1, source_target_pairs={{0,16},{4,20},{8,24},{12,28},{16,0},{20,4},{24,8},{28,12},{1,17},{... | collective-permute-start | bytes 786440 | tf_op jit(solution)/shard_map/ppermute | solution.py:31
  17.3 6.0 %collective-permute-done.2 = bf16[8,128,128]{2,1,0:T(8,128)(2,1)S(1)} collective-permute-done((bf16[8,128,128]{2,1,0:T(8,128)(2,1)S(1)}, bf16[8,128,128]{2,1,0:T(8,128)(2,1)S(1)}, u32[]{:S(2)}, u32[]{:S(2)}) %collective-permute-start.2) | collective-permute-done | bytes 262176 | tf_op jit(solution)/shard_map/ppermute | solution.py:31
  23.5 3.9 %multiply_reduce_fusion = (f32[512]{0:T(512)S(1)}, f32[1,512,8,128]{1,3,2,0:T(8,128)}) fusion(f32[1,512,8,128]{1,3,2,0:T(8,128)} %fusion.41, f32[8,128,128]{2,1,0:T(8,128)S(1)} %fusion.51, f32[8,128,128]{2,1,0:T(8,128)S(1)} %get-tuple-element.22, bf16[512,1024]{1,0:T(8,128)(2,1)S(1)} %copy-done.4), kind=kOutput, calls=%fused_computation.42 | convolution fusion | flops 139329024 | bytes 6293504 | tf_op jit(solution)/shard_map/nthd,nhde->nthe/dot_general | solution.py:125
  27.4 2.0 %copy.11 = f32[512,1024]{1,0:T(8,128)S(1)} copy(f32[512,1024]{0,1:T(8,128)} %bitcast.39) | data formatting | bytes 4194304 | tf_op jit(solution)/shard_map/reshape | solution.py:126
  29.4 1.6 %collective-permute-start.3 = (f32[512]{0:T(512)S(1)}, f32[512]{0:T(512)S(1)}, u32[]{:S(2)}, u32[]{:S(2)}) collective-permute-start(f32[512]{0:T(512)S(1)} %get-tuple-element.23), channel_id=1, source_target_pairs={{0,1},{1,0},{2,3},{3,2},{4,5},{5,4},{6,7},{7,6},{8,9},{9,8},{10,11... | collective-permute-start | bytes 6152 | tf_op jit(solution)/shard_map/ppermute | solution.py:51
  31.6 1.5 collective-permute-done.3
  33.0 2.6 %collective-permute-start.4 = (f32[512]{0:T(512)S(1)}, f32[512]{0:T(512)S(1)}, u32[]{:S(2)}, u32[]{:S(2)}) collective-permute-start(f32[512]{0:T(512)S(1)} %add.141), channel_id=1, source_target_pairs={{0,2},{1,3},{2,0},{3,1},{4,6},{5,7},{6,4},{7,5},{8,10},{9,11},{10,... | collective-permute-start | bytes 6152 | tf_op jit(solution)/shard_map/ppermute | solution.py:51
  35.6 3.7 %fusion.26 = bf16[512,1536]{1,0:T(8,128)(2,1)S(1)} fusion(bf16[512,1024]{1,0:T(8,128)(2,1)S(1)} %multiply_convert_fusion.3, bf16[1024,6144]{1,0:T(8,128)(2,1)} %param.9, s32[]{:T(128)S(6)} %select_n.64), kind=kOutput, calls=%fused_computation.22 | convolution fusion | flops 1611399168 | bytes 5767172 | tf_op jit(solution)/shard_map/dot_general | solution.py:42
  39.3 0.8 collective-permute-start.6
  40.1 4.7 %collective-permute-start.5 = (bf16[512,1536]{1,0:T(8,128)(2,1)S(1)}, bf16[512,1536]{1,0:T(8,128)(2,1)}, u32[]{:S(2)}, u32[]{:S(2)}) collective-permute-start(bf16[512,1536]{1,0:T(8,128)(2,1)S(1)} %fusion.26), channel_id=1, source_target_pairs={{0,1},{4,5},{8,9},{12,13},{16,17},{20,21},{24,25},{28,29}} | collective-permute-start | bytes 4718600 | tf_op jit(solution)/shard_map/ppermute | solution.py:91
  44.7 4.0 %fusion.23 = bf16[512,1536]{1,0:T(8,128)(2,1)S(1)} fusion(bf16[512,1024]{1,0:T(8,128)(2,1)} %copy-done.2, bf16[1024,6144]{1,0:T(8,128)(2,1)} %param.9, s32[]{:T(128)S(6)} %select_n.62), kind=kOutput, calls=%fused_computation.21 | convolution fusion | flops 1611399168 | bytes 5767172 | tf_op jit(solution)/shard_map/dot_general | solution.py:42
  48.7 25.6 %collective-permute-done.5 = bf16[512,1536]{1,0:T(8,128)(2,1)} collective-permute-done((bf16[512,1536]{1,0:T(8,128)(2,1)S(1)}, bf16[512,1536]{1,0:T(8,128)(2,1)}, u32[]{:S(2)}, u32[]{:S(2)}) %collective-permute-start.5) | collective-permute-done | bytes 1572896 | tf_op jit(solution)/shard_map/ppermute | solution.py:91
  74.4 2.0 %add_convert_fusion.2 = bf16[512,1536]{1,0:T(8,128)(2,1)S(1)} fusion(bf16[512,1536]{1,0:T(8,128)(2,1)S(1)} %collective-permute-done.6, bf16[512,1536]{1,0:T(8,128)(2,1)} %collective-permute-done.5, bf16[512,1536]{1,0:T(8,128)(2,1)S(1)} %fusion.23), kind=kLoop, calls=%fused_computation.7 | loop fusion | flops 4718592 | bytes 6291456 | tf_op jit(solution)/shard_map/convert_element_type | solution.py:75
  76.4 1.8 %collective-permute-start.9 = (bf16[512,1536]{1,0:T(8,128)(2,1)S(1)}, bf16[512,1536]{1,0:T(8,128)(2,1)}, u32[]{:S(2)}, u32[]{:S(2)}) collective-permute-start(bf16[512,1536]{1,0:T(8,128)(2,1)S(1)} %add_convert_fusion.2), channel_id=1, source_target_pairs={{2,1},{3,2},{6,5},{7,6},{10,9},{11,10},{14,13},{15,14},{18,17},{19... | collective-permute-start | bytes 4718600 | tf_op jit(solution)/shard_map/ppermute | solution.py:92
  78.2 4.2 %collective-permute-start.7 = (bf16[512,1536]{1,0:T(8,128)(2,1)S(1)}, bf16[512,1536]{1,0:T(8,128)(2,1)S(1)}, u32[]{:S(2)}, u32[]{:S(2)}) collective-permute-start(bf16[512,1536]{1,0:T(8,128)(2,1)S(1)} %add_convert_fusion.2), channel_id=1, source_target_pairs={{0,1},{1,2},{4,5},{5,6},{8,9},{9,10},{12,13},{13,14},{16,17},{17,1... | collective-permute-start | bytes 4718600 | tf_op jit(solution)/shard_map/ppermute | solution.py:91
  82.5 4.1 %fusion.17 = bf16[512,1536]{1,0:T(8,128)(2,1)S(1)} fusion(bf16[512,1024]{1,0:T(8,128)(2,1)} %copy-done.2, bf16[1024,6144]{1,0:T(8,128)(2,1)} %param.9, s32[]{:T(128)S(6)} %select_n.59), kind=kOutput, calls=%fused_computation.19 | convolution fusion | flops 1611399168 | bytes 5767172 | tf_op jit(solution)/shard_map/dot_general | solution.py:42
  86.6 3.7 %fusion.20 = bf16[512,1536]{1,0:T(8,128)(2,1)S(1)} fusion(bf16[512,1024]{1,0:T(8,128)(2,1)S(1)} %copy-done.3, bf16[1024,6144]{1,0:T(8,128)(2,1)} %param.9, s32[]{:T(128)S(6)} %select_n.60), kind=kOutput, calls=%fused_computation.20 | convolution fusion | flops 1611399168 | bytes 5767172 | tf_op jit(solution)/shard_map/dot_general | solution.py:42
  90.3 2.9 %add_convert_fusion = bf16[512,1536]{1,0:T(8,128)(2,1)} fusion(bf16[512,1536]{1,0:T(8,128)(2,1)} %collective-permute-done.9, bf16[512,1536]{1,0:T(8,128)(2,1)S(1)} %fusion.20), kind=kLoop, calls=%fused_computation.5 | loop fusion | flops 3145728 | bytes 4718592 | tf_op jit(solution)/shard_map/convert_element_type | solution.py:88
  93.2 1.3 collective-permute-start.10
  94.5 17.6 %collective-permute-done.7 = bf16[512,1536]{1,0:T(8,128)(2,1)S(1)} collective-permute-done((bf16[512,1536]{1,0:T(8,128)(2,1)S(1)}, bf16[512,1536]{1,0:T(8,128)(2,1)S(1)}, u32[]{:S(2)}, u32[]{:S(2)}) %collective-permute-start.7) | collective-permute-done | bytes 1572896 | tf_op jit(solution)/shard_map/ppermute | solution.py:91
  112.5 8.2 %collective-permute-start.8 = (bf16[512,1536]{1,0:T(8,128)(2,1)S(1)}, bf16[512,1536]{1,0:T(8,128)(2,1)S(1)}, u32[]{:S(2)}, u32[]{:S(2)}) collective-permute-start(bf16[512,1536]{1,0:T(8,128)(2,1)S(1)} %add_convert_fusion.1), channel_id=1, source_target_pairs={{0,1},{1,2},{2,3},{4,5},{5,6},{6,7},{8,9},{9,10},{10,11},{12,13},{... | collective-permute-start | bytes 4718600 | tf_op jit(solution)/shard_map/ppermute | solution.py:91
  120.7 4.0 %fusion.14 = bf16[512,1536]{1,0:T(8,128)(2,1)S(1)} fusion(bf16[512,1024]{1,0:T(8,128)(2,1)} %copy-done.2, bf16[1024,6144]{1,0:T(8,128)(2,1)} %param.9, s32[]{:T(128)S(6)} %select_n.58), kind=kOutput, calls=%fused_computation.18 | convolution fusion | flops 1611399168 | bytes 5767172 | tf_op jit(solution)/shard_map/dot_general | solution.py:42
  124.7 23.7 %collective-permute-done.10 = bf16[512,1536]{1,0:T(8,128)(2,1)} collective-permute-done((bf16[512,1536]{1,0:T(8,128)(2,1)}, bf16[512,1536]{1,0:T(8,128)(2,1)}, u32[]{:S(2)}, u32[]{:S(2)}) %collective-permute-start.10) | collective-permute-done | bytes 1572896 | tf_op jit(solution)/shard_map/ppermute | solution.py:92
  148.4 1.3 collective-permute-done.8
  149.6 3.2 %multiply_convert_fusion.2 = bf16[512,1536]{1,0:T(8,128)(2,1)} fusion(bf16[512,1536]{1,0:T(8,128)(2,1)} %collective-permute-done.10, bf16[512,1536]{1,0:T(8,128)(2,1)S(1)} %collective-permute-done.8, bf16[512,1536]{1,0:T(8,128)(2,1)S(1)} %fusion.14, f32[512]{0:T(512)S(1)} %add_rsqrt_fusion), kind=kLoop, calls=%fused_computation.4 | loop fusion | flops 5505024 | bytes 6293504 | tf_op jit(solution)/shard_map/convert_element_type | solution.py:132
  (25 shorter events, 2.9 us)
Async XLA Ops:
  0.0 2.5 %copy-start = (bf16[512,1024]{1,0:T(8,128)(2,1)S(1)}, bf16[512,1024]{1,0:T(8,128)(2,1)}, u32[]{:S(2)}) copy-start(bf16[512,1024]{1,0:T(8,128)(2,1)} %param.7) | copy-start | bytes 3145732
  4.1 1.7 %collective-permute-start = (bf16[8,128,128]{2,1,0:T(8,128)(2,1)S(1)}, bf16[8,128,128]{2,1,0:T(8,128)(2,1)S(1)}, u32[]{:S(2)}, u32[]{:S(2)}) collective-permute-start(bf16[8,128,128]{2,1,0:T(8,128)(2,1)S(1)} %get-tuple-element.21), channel_id=1, source_target_pairs={{0,4},{4,0},{8,12},{12,8},{16,20},{20,16},{24,28},{28,24},{1,5},{5... | collective-permute-start | bytes 786440 | tf_op jit(solution)/shard_map/ppermute | solution.py:31
  5.9 9.5 %collective-permute-start.1 = (bf16[8,128,128]{2,1,0:T(8,128)(2,1)S(1)}, bf16[8,128,128]{2,1,0:T(8,128)(2,1)S(1)}, u32[]{:S(2)}, u32[]{:S(2)}) collective-permute-start(bf16[8,128,128]{2,1,0:T(8,128)(2,1)S(1)} %fusion.52), channel_id=1, source_target_pairs={{0,8},{4,12},{8,0},{12,4},{16,24},{20,28},{24,16},{28,20},{1,9},{5... | collective-permute-start | bytes 786440 | tf_op jit(solution)/shard_map/ppermute | solution.py:31
  14.2 9.2 %copy-start.4 = (bf16[512,1024]{1,0:T(8,128)(2,1)S(1)}, bf16[512,1024]{1,0:T(8,128)(2,1)}, u32[]{:S(2)}) copy-start(bf16[512,1024]{1,0:T(8,128)(2,1)} %param.5) | copy-start | bytes 3145732
  15.5 7.8 %collective-permute-start.2 = (bf16[8,128,128]{2,1,0:T(8,128)(2,1)S(1)}, bf16[8,128,128]{2,1,0:T(8,128)(2,1)S(1)}, u32[]{:S(2)}, u32[]{:S(2)}) collective-permute-start(bf16[8,128,128]{2,1,0:T(8,128)(2,1)S(1)} %convert_add_fusion), channel_id=1, source_target_pairs={{0,16},{4,20},{8,24},{12,28},{16,0},{20,4},{24,8},{28,12},{1,17},{... | collective-permute-start | bytes 786440 | tf_op jit(solution)/shard_map/ppermute | solution.py:31
  27.4 3.6 %copy-start.1 = (bf16[512,1024]{1,0:T(8,128)(2,1)S(1)}, bf16[512,1024]{1,0:T(8,128)(2,1)}, u32[]{:S(2)}) copy-start(bf16[512,1024]{1,0:T(8,128)(2,1)} %param.8) | copy-start | bytes 3145732
  29.4 3.7 %collective-permute-start.3 = (f32[512]{0:T(512)S(1)}, f32[512]{0:T(512)S(1)}, u32[]{:S(2)}, u32[]{:S(2)}) collective-permute-start(f32[512]{0:T(512)S(1)} %get-tuple-element.23), channel_id=1, source_target_pairs={{0,1},{1,0},{2,3},{3,2},{4,5},{5,4},{6,7},{7,6},{8,9},{9,8},{10,11... | collective-permute-start | bytes 6152 | tf_op jit(solution)/shard_map/ppermute | solution.py:51
  31.6 7.7 %copy-start.2 = (bf16[512,1024]{1,0:T(8,128)(2,1)}, bf16[512,1024]{1,0:T(8,128)(2,1)S(1)}, u32[]{:S(2)}) copy-start(bf16[512,1024]{1,0:T(8,128)(2,1)S(1)} %multiply_convert_fusion.3) | copy-start | bytes 3145732
  33.0 6.2 %collective-permute-start.4 = (f32[512]{0:T(512)S(1)}, f32[512]{0:T(512)S(1)}, u32[]{:S(2)}, u32[]{:S(2)}) collective-permute-start(f32[512]{0:T(512)S(1)} %add.141), channel_id=1, source_target_pairs={{0,2},{1,3},{2,0},{3,1},{4,6},{5,7},{6,4},{7,5},{8,10},{9,11},{10,... | collective-permute-start | bytes 6152 | tf_op jit(solution)/shard_map/ppermute | solution.py:51
  39.3 9.4 %collective-permute-start.6 = (bf16[512,1536]{1,0:T(8,128)(2,1)S(1)}, bf16[512,1536]{1,0:T(8,128)(2,1)S(1)}, u32[]{:S(2)}, u32[]{:S(2)}) collective-permute-start(bf16[512,1536]{1,0:T(8,128)(2,1)S(1)} %fusion.26), channel_id=1, source_target_pairs={{3,2},{7,6},{11,10},{15,14},{19,18},{23,22},{27,26},{31,30}} | collective-permute-start | bytes 4718600 | tf_op jit(solution)/shard_map/ppermute | solution.py:92
  40.1 34.3 %collective-permute-start.5 = (bf16[512,1536]{1,0:T(8,128)(2,1)S(1)}, bf16[512,1536]{1,0:T(8,128)(2,1)}, u32[]{:S(2)}, u32[]{:S(2)}) collective-permute-start(bf16[512,1536]{1,0:T(8,128)(2,1)S(1)} %fusion.26), channel_id=1, source_target_pairs={{0,1},{4,5},{8,9},{12,13},{16,17},{20,21},{24,25},{28,29}} | collective-permute-start | bytes 4718600 | tf_op jit(solution)/shard_map/ppermute | solution.py:91
  76.4 13.9 %collective-permute-start.9 = (bf16[512,1536]{1,0:T(8,128)(2,1)S(1)}, bf16[512,1536]{1,0:T(8,128)(2,1)}, u32[]{:S(2)}, u32[]{:S(2)}) collective-permute-start(bf16[512,1536]{1,0:T(8,128)(2,1)S(1)} %add_convert_fusion.2), channel_id=1, source_target_pairs={{2,1},{3,2},{6,5},{7,6},{10,9},{11,10},{14,13},{15,14},{18,17},{19... | collective-permute-start | bytes 4718600 | tf_op jit(solution)/shard_map/ppermute | solution.py:92
  78.2 33.9 %collective-permute-start.7 = (bf16[512,1536]{1,0:T(8,128)(2,1)S(1)}, bf16[512,1536]{1,0:T(8,128)(2,1)S(1)}, u32[]{:S(2)}, u32[]{:S(2)}) collective-permute-start(bf16[512,1536]{1,0:T(8,128)(2,1)S(1)} %add_convert_fusion.2), channel_id=1, source_target_pairs={{0,1},{1,2},{4,5},{5,6},{8,9},{9,10},{12,13},{13,14},{16,17},{17,1... | collective-permute-start | bytes 4718600 | tf_op jit(solution)/shard_map/ppermute | solution.py:91
  82.5 4.1 %copy-start.3 = (bf16[512,1024]{1,0:T(8,128)(2,1)S(1)}, bf16[512,1024]{1,0:T(8,128)(2,1)}, u32[]{:S(2)}) copy-start(bf16[512,1024]{1,0:T(8,128)(2,1)} %copy-done.2) | copy-start | bytes 3145732
  93.2 55.2 %collective-permute-start.10 = (bf16[512,1536]{1,0:T(8,128)(2,1)}, bf16[512,1536]{1,0:T(8,128)(2,1)}, u32[]{:S(2)}, u32[]{:S(2)}) collective-permute-start(bf16[512,1536]{1,0:T(8,128)(2,1)} %add_convert_fusion), channel_id=1, source_target_pairs={{1,0},{2,1},{3,2},{5,4},{6,5},{7,6},{9,8},{10,9},{11,10},{13,12},{... | collective-permute-start | bytes 4718600 | tf_op jit(solution)/shard_map/ppermute | solution.py:92
  112.5 37.1 %collective-permute-start.8 = (bf16[512,1536]{1,0:T(8,128)(2,1)S(1)}, bf16[512,1536]{1,0:T(8,128)(2,1)S(1)}, u32[]{:S(2)}, u32[]{:S(2)}) collective-permute-start(bf16[512,1536]{1,0:T(8,128)(2,1)S(1)} %add_convert_fusion.1), channel_id=1, source_target_pairs={{0,1},{1,2},{2,3},{4,5},{5,6},{6,7},{8,9},{9,10},{10,11},{12,13},{... | collective-permute-start | bytes 4718600 | tf_op jit(solution)/shard_map/ppermute | solution.py:91

commit v14 on v13

--- a/solution.py
+++ b/solution.py
@@ -24,6 +24,16 @@
     group_total = span_total
     prefix = jnp.zeros_like(span_total)
     bit = 1
+    if count % 4 == 0 and count > 4:
+        sent = span_total.astype(jnp.bfloat16)
+        low = my_index % 4
+        for partner in range(1, 4):
+            pairs = [(i, i ^ partner) for i in range(count)]
+            arrived = lax.ppermute(sent, axis_name, pairs).astype(jnp.float32)
+            earlier = ((low ^ partner) < low).astype(jnp.float32)
+            prefix = prefix + earlier * arrived
+            group_total = group_total + arrived
+        bit = 4
     while bit < count:
         if bit * 2 == count and bit > 1:
             group_total, companion = lax.optimization_barrier((group_total, companion))

time: 153 us -> 163 us (1.065)
  waiting for transfers between devices: 76.9 us -> 83.8 us
    ppermute x0 -> x3, waiting for transfers between devices: none -> 5.49 us  [exclusive_prefix(): arrived = lax.ppermute(sent, axis_name, pairs).astype(jnp.float32)]
    ppermute x0 -> x3, starting transfers between devices: none -> 3.09 us  [exclusive_prefix(): arrived = lax.ppermute(sent, axis_name, pairs).astype(jnp.float32)]
    ppermute x3 -> x1, starting transfers between devices: 5.3 us -> 2.4 us  [exclusive_prefix(): arrived = lax.ppermute(group_total.astype(jnp.bfloat16), axis_name, pairs)]
    ppermute x3 -> x1, waiting for transfers between devices: 7.25 us -> 6.54 us  [exclusive_prefix(): arrived = lax.ppermute(group_total.astype(jnp.bfloat16), axis_name, pairs)]
  transfers between devices with their start and end apart: 11 -> 12, of which waited for: 8 -> 7; matrix products, arithmetic and copies ran while one was open for 20% -> 18% of each run, Pallas kernels for 0% -> 0%
where the time goes in v14:
time: 163 us; the launch traced here: 162 us
  waiting for transfers between devices  83.8 us (51%)
  starting transfers between devices  31.1 us (19%)
  matrix products  29.9 us (18%)
  other arithmetic  14.2 us (9%)
  local copies, waits for them, and re-layouts  3.11 us (2%)
    ppermute x3, waiting for transfers between devices, line_reduce_scatter(): lax.ppermute(to_right, axis_name, right_pairs).astype(jnp.float32)  46.1 us
    ppermute x3, waiting for transfers between devices, line_reduce_scatter(): lax.ppermute(to_left, axis_name, left_pairs).astype(jnp.float32)  24.5 us
    dot_general x5, matrix products, shard_product(): return jnp.dot(gated, columns, preferred_element_type=jnp.float32)  19.4 us
    ppermute x3, starting transfers between devices, line_reduce_scatter(): lax.ppermute(to_right, axis_name, right_pairs).astype(jnp.float32)  17.1 us
    ppermute x1, waiting for transfers between devices, exclusive_prefix(): arrived = lax.ppermute(group_total.astype(jnp.bfloat16), axis_name, pairs)  6.54 us
    ppermute x3, waiting for transfers between devices, exclusive_prefix(): arrived = lax.ppermute(sent, axis_name, pairs).astype(jnp.float32)  5.49 us
    dot_general x1, matrix products, body(): jnp.einsum('nhts,nshd->nthd', scores, active_v, preferred_element_type=jn...  5.44 us
    ppermute x2, starting transfers between devices, butterfly_sum(): lax.ppermute(values, axis_name, [(i, i ^ bit) for i in range(count)])  4.67 us
  transfers between devices with their start and end apart: 12, of which 7 were waited for; matrix products, arithmetic and copies ran while one was open for 18% of the time, Pallas kernels for 0%

profile of v14, /device:TPU:0, one launch (start us, length us, event | category | flops | bytes accessed | tf_op | source)
XLA Modules:
  0.0 162.3 jit_solution(16758459054574393327)
XLA Ops:
  0.0 1.8 %fusion.32 = bf16[512,1024]{1,0:T(8,128)(2,1)S(1)} fusion(bf16[512,1024]{1,0:T(8,128)(2,1)} %param.6), kind=kLoop, calls=%fused_computation.32 | loop fusion | flops 3145728 | bytes 2097152 | tf_op jit(solution)/shard_map/convert_element_type | solution.py:11
  2.4 1.8 %fusion.36 = bf16[512,1024]{1,0:T(8,128)(2,1)S(1)} fusion(bf16[512,1024]{1,0:T(8,128)(2,1)} %param.7), kind=kLoop, calls=%fused_computation.36 | loop fusion | flops 3145728 | bytes 2097152 | tf_op jit(solution)/shard_map/convert_element_type | solution.py:11
  4.8 1.1 fusion.58
  5.9 2.4 %collective-permute-start.2 = (bf16[8,128,128]{2,1,0:T(8,128)(2,1)}, bf16[8,128,128]{2,1,0:T(8,128)(2,1)S(1)}, u32[]{:S(2)}, u32[]{:S(2)}) collective-permute-start(bf16[8,128,128]{2,1,0:T(8,128)(2,1)} %get-tuple-element.21), channel_id=1, source_target_pairs={{0,12},{4,8},{8,4},{12,0},{16,28},{20,24},{24,20},{28,16},{1,13},{... | collective-permute-start | bytes 786440 | tf_op jit(solution)/shard_map/ppermute | solution.py:32
  9.0 1.1 fusion.46
  10.1 5.4 %fusion.41 = f32[1,512,8,128]{1,3,2,0:T(8,128)} fusion(bf16[512,8,128]{0,2,1:T(8,128)(2,1)S(1)} %bitcast.38, f32[512,512]{1,0:T(8,128)} %fusion.46, bf16[512,8,128]{0,2,1:T(8,128)(2,1)S(1)} %bitcast.36, bf16[512,1024]{1,0:T(8,128)(2,1)} %param.5), kind=kOutput, calls=%fused_computation.44 | convolution fusion | flops 1081081856 | bytes 6291456 | tf_op jit(solution)/shard_map/nhts,nshd->nthd/dot_general | solution.py:129
  15.5 5.5 %collective-permute-done.1 = bf16[8,128,128]{2,1,0:T(8,128)(2,1)S(1)} collective-permute-done((bf16[8,128,128]{2,1,0:T(8,128)(2,1)}, bf16[8,128,128]{2,1,0:T(8,128)(2,1)S(1)}, u32[]{:S(2)}, u32[]{:S(2)}) %collective-permute-start.1) | collective-permute-done | bytes 262176 | tf_op jit(solution)/shard_map/ppermute | solution.py:32
  21.2 2.4 %collective-permute-start.3 = (bf16[8,128,128]{2,1,0:T(8,128)(2,1)S(1)}, bf16[8,128,128]{2,1,0:T(8,128)(2,1)S(1)}, u32[]{:S(2)}, u32[]{:S(2)}) collective-permute-start(bf16[8,128,128]{2,1,0:T(8,128)(2,1)S(1)} %convert_add_fusion), channel_id=1, source_target_pairs={{0,16},{4,20},{8,24},{12,28},{16,0},{20,4},{24,8},{28,12},{1,17},{... | collective-permute-start | bytes 786440 | tf_op jit(solution)/shard_map/ppermute | solution.py:41
  23.6 6.5 %collective-permute-done.3 = bf16[8,128,128]{2,1,0:T(8,128)(2,1)S(1)} collective-permute-done((bf16[8,128,128]{2,1,0:T(8,128)(2,1)S(1)}, bf16[8,128,128]{2,1,0:T(8,128)(2,1)S(1)}, u32[]{:S(2)}, u32[]{:S(2)}) %collective-permute-start.3) | collective-permute-done | bytes 262176 | tf_op jit(solution)/shard_map/ppermute | solution.py:41
  30.3 3.9 %multiply_reduce_fusion = (f32[512]{0:T(512)S(1)}, f32[1,512,8,128]{1,3,2,0:T(8,128)}) fusion(f32[1,512,8,128]{1,3,2,0:T(8,128)} %fusion.41, f32[8,128,128]{2,1,0:T(8,128)S(1)} %fusion.52, f32[8,128,128]{2,1,0:T(8,128)S(1)} %get-tuple-element.22, bf16[512,1024]{1,0:T(8,128)(2,1)S(1)} %copy-done.3), kind=kOutput, calls=%fused_computation.42 | convolution fusion | flops 139329024 | bytes 6293504 | tf_op jit(solution)/shard_map/nthd,nhde->nthe/dot_general | solution.py:135
  34.2 2.0 %copy.11 = f32[512,1024]{1,0:T(8,128)S(1)} copy(f32[512,1024]{0,1:T(8,128)} %bitcast.39) | data formatting | bytes 4194304 | tf_op jit(solution)/shard_map/reshape | solution.py:136
  36.2 1.9 %collective-permute-start.4 = (f32[512]{0:T(512)S(1)}, f32[512]{0:T(512)S(1)}, u32[]{:S(2)}, u32[]{:S(2)}) collective-permute-start(f32[512]{0:T(512)S(1)} %get-tuple-element.23), channel_id=1, source_target_pairs={{0,1},{1,0},{2,3},{3,2},{4,5},{5,4},{6,7},{7,6},{8,9},{9,8},{10,11... | collective-permute-start | bytes 6152 | tf_op jit(solution)/shard_map/ppermute | solution.py:61
  38.6 1.2 collective-permute-done.4
  39.8 2.8 %collective-permute-start.5 = (f32[512]{0:T(512)S(1)}, f32[512]{0:T(512)S(1)}, u32[]{:S(2)}, u32[]{:S(2)}) collective-permute-start(f32[512]{0:T(512)S(1)} %add.143), channel_id=1, source_target_pairs={{0,2},{1,3},{2,0},{3,1},{4,6},{5,7},{6,4},{7,5},{8,10},{9,11},{10,... | collective-permute-start | bytes 6152 | tf_op jit(solution)/shard_map/ppermute | solution.py:61
  42.7 3.7 %fusion.26 = bf16[512,1536]{1,0:T(8,128)(2,1)S(1)} fusion(bf16[512,1024]{1,0:T(8,128)(2,1)S(1)} %multiply_convert_fusion.3, bf16[1024,6144]{1,0:T(8,128)(2,1)} %param.9, s32[]{:T(128)S(6)} %select_n.54), kind=kOutput, calls=%fused_computation.22 | convolution fusion | flops 1611399168 | bytes 5767172 | tf_op jit(solution)/shard_map/dot_general | solution.py:52
  46.4 0.8 collective-permute-start.7
  47.1 4.7 %collective-permute-start.6 = (bf16[512,1536]{1,0:T(8,128)(2,1)S(1)}, bf16[512,1536]{1,0:T(8,128)(2,1)}, u32[]{:S(2)}, u32[]{:S(2)}) collective-permute-start(bf16[512,1536]{1,0:T(8,128)(2,1)S(1)} %fusion.26), channel_id=1, source_target_pairs={{0,1},{4,5},{8,9},{12,13},{16,17},{20,21},{24,25},{28,29}} | collective-permute-start | bytes 4718600 | tf_op jit(solution)/shard_map/ppermute | solution.py:101
  51.8 4.0 %fusion.23 = bf16[512,1536]{1,0:T(8,128)(2,1)S(1)} fusion(bf16[512,1024]{1,0:T(8,128)(2,1)} %copy-done.1, bf16[1024,6144]{1,0:T(8,128)(2,1)} %param.9, s32[]{:T(128)S(6)} %select_n.52), kind=kOutput, calls=%fused_computation.21 | convolution fusion | flops 1611399168 | bytes 5767172 | tf_op jit(solution)/shard_map/dot_general | solution.py:52
  55.8 26.4 %collective-permute-done.6 = bf16[512,1536]{1,0:T(8,128)(2,1)} collective-permute-done((bf16[512,1536]{1,0:T(8,128)(2,1)S(1)}, bf16[512,1536]{1,0:T(8,128)(2,1)}, u32[]{:S(2)}, u32[]{:S(2)}) %collective-permute-start.6) | collective-permute-done | bytes 1572896 | tf_op jit(solution)/shard_map/ppermute | solution.py:101
  82.2 2.0 %add_convert_fusion.2 = bf16[512,1536]{1,0:T(8,128)(2,1)S(1)} fusion(bf16[512,1536]{1,0:T(8,128)(2,1)S(1)} %collective-permute-done.7, bf16[512,1536]{1,0:T(8,128)(2,1)} %collective-permute-done.6, bf16[512,1536]{1,0:T(8,128)(2,1)S(1)} %fusion.23), kind=kLoop, calls=%fused_computation.7 | loop fusion | flops 4718592 | bytes 6291456 | tf_op jit(solution)/shard_map/convert_element_type | solution.py:85
  84.2 1.8 %collective-permute-start.10 = (bf16[512,1536]{1,0:T(8,128)(2,1)S(1)}, bf16[512,1536]{1,0:T(8,128)(2,1)}, u32[]{:S(2)}, u32[]{:S(2)}) collective-permute-start(bf16[512,1536]{1,0:T(8,128)(2,1)S(1)} %add_convert_fusion.2), channel_id=1, source_target_pairs={{2,1},{3,2},{6,5},{7,6},{10,9},{11,10},{14,13},{15,14},{18,17},{19... | collective-permute-start | bytes 4718600 | tf_op jit(solution)/shard_map/ppermute | solution.py:102
  86.1 4.2 %collective-permute-start.8 = (bf16[512,1536]{1,0:T(8,128)(2,1)S(1)}, bf16[512,1536]{1,0:T(8,128)(2,1)S(1)}, u32[]{:S(2)}, u32[]{:S(2)}) collective-permute-start(bf16[512,1536]{1,0:T(8,128)(2,1)S(1)} %add_convert_fusion.2), channel_id=1, source_target_pairs={{0,1},{1,2},{4,5},{5,6},{8,9},{9,10},{12,13},{13,14},{16,17},{17,1... | collective-permute-start | bytes 4718600 | tf_op jit(solution)/shard_map/ppermute | solution.py:101
  90.3 4.1 %fusion.17 = bf16[512,1536]{1,0:T(8,128)(2,1)S(1)} fusion(bf16[512,1024]{1,0:T(8,128)(2,1)} %copy-done.1, bf16[1024,6144]{1,0:T(8,128)(2,1)} %param.9, s32[]{:T(128)S(6)} %select_n.49), kind=kOutput, calls=%fused_computation.19 | convolution fusion | flops 1611399168 | bytes 5767172 | tf_op jit(solution)/shard_map/dot_general | solution.py:52
  94.4 3.7 %fusion.20 = bf16[512,1536]{1,0:T(8,128)(2,1)S(1)} fusion(bf16[512,1024]{1,0:T(8,128)(2,1)S(1)} %copy-done.2, bf16[1024,6144]{1,0:T(8,128)(2,1)} %param.9, s32[]{:T(128)S(6)} %select_n.50), kind=kOutput, calls=%fused_computation.20 | convolution fusion | flops 1611399168 | bytes 5767172 | tf_op jit(solution)/shard_map/dot_general | solution.py:52
  98.1 2.9 %add_convert_fusion = bf16[512,1536]{1,0:T(8,128)(2,1)} fusion(bf16[512,1536]{1,0:T(8,128)(2,1)} %collective-permute-done.10, bf16[512,1536]{1,0:T(8,128)(2,1)S(1)} %fusion.20), kind=kLoop, calls=%fused_computation.5 | loop fusion | flops 3145728 | bytes 4718592 | tf_op jit(solution)/shard_map/convert_element_type | solution.py:98
  101.1 1.3 collective-permute-start.11
  102.4 18.4 %collective-permute-done.8 = bf16[512,1536]{1,0:T(8,128)(2,1)S(1)} collective-permute-done((bf16[512,1536]{1,0:T(8,128)(2,1)S(1)}, bf16[512,1536]{1,0:T(8,128)(2,1)S(1)}, u32[]{:S(2)}, u32[]{:S(2)}) %collective-permute-start.8) | collective-permute-done | bytes 1572896 | tf_op jit(solution)/shard_map/ppermute | solution.py:101
  121.1 8.2 %collective-permute-start.9 = (bf16[512,1536]{1,0:T(8,128)(2,1)S(1)}, bf16[512,1536]{1,0:T(8,128)(2,1)S(1)}, u32[]{:S(2)}, u32[]{:S(2)}) collective-permute-start(bf16[512,1536]{1,0:T(8,128)(2,1)S(1)} %add_convert_fusion.1), channel_id=1, source_target_pairs={{0,1},{1,2},{2,3},{4,5},{5,6},{6,7},{8,9},{9,10},{10,11},{12,13},{... | collective-permute-start | bytes 4718600 | tf_op jit(solution)/shard_map/ppermute | solution.py:101
  129.3 4.0 %fusion.14 = bf16[512,1536]{1,0:T(8,128)(2,1)S(1)} fusion(bf16[512,1024]{1,0:T(8,128)(2,1)} %copy-done.1, bf16[1024,6144]{1,0:T(8,128)(2,1)} %param.9, s32[]{:T(128)S(6)} %select_n.48), kind=kOutput, calls=%fused_computation.18 | convolution fusion | flops 1611399168 | bytes 5767172 | tf_op jit(solution)/shard_map/dot_general | solution.py:52
  133.3 24.5 %collective-permute-done.11 = bf16[512,1536]{1,0:T(8,128)(2,1)} collective-permute-done((bf16[512,1536]{1,0:T(8,128)(2,1)}, bf16[512,1536]{1,0:T(8,128)(2,1)}, u32[]{:S(2)}, u32[]{:S(2)}) %collective-permute-start.11) | collective-permute-done | bytes 1572896 | tf_op jit(solution)/shard_map/ppermute | solution.py:102
  157.8 1.3 collective-permute-done.9
  159.1 3.2 %multiply_convert_fusion.2 = bf16[512,1536]{1,0:T(8,128)(2,1)} fusion(bf16[512,1536]{1,0:T(8,128)(2,1)} %collective-permute-done.11, bf16[512,1536]{1,0:T(8,128)(2,1)S(1)} %collective-permute-done.9, bf16[512,1536]{1,0:T(8,128)(2,1)S(1)} %fusion.14, f32[512]{0:T(512)S(1)} %add_rsqrt_fusion), kind=kLoop, calls=%fused_computation.4 | loop fusion | flops 5505024 | bytes 6293504 | tf_op jit(solution)/shard_map/convert_element_type | solution.py:142
  (24 shorter events, 3.1 us)
Async XLA Ops:
  5.9 9.6 %collective-permute-start.2 = (bf16[8,128,128]{2,1,0:T(8,128)(2,1)}, bf16[8,128,128]{2,1,0:T(8,128)(2,1)S(1)}, u32[]{:S(2)}, u32[]{:S(2)}) collective-permute-start(bf16[8,128,128]{2,1,0:T(8,128)(2,1)} %get-tuple-element.21), channel_id=1, source_target_pairs={{0,12},{4,8},{8,4},{12,0},{16,28},{20,24},{24,20},{28,16},{1,13},{... | collective-permute-start | bytes 786440 | tf_op jit(solution)/shard_map/ppermute | solution.py:32
  8.3 12.7 %collective-permute-start.1 = (bf16[8,128,128]{2,1,0:T(8,128)(2,1)}, bf16[8,128,128]{2,1,0:T(8,128)(2,1)S(1)}, u32[]{:S(2)}, u32[]{:S(2)}) collective-permute-start(bf16[8,128,128]{2,1,0:T(8,128)(2,1)} %get-tuple-element.21), channel_id=1, source_target_pairs={{0,8},{4,12},{8,0},{12,4},{16,24},{20,28},{24,16},{28,20},{1,9},{5... | collective-permute-start | bytes 786440 | tf_op jit(solution)/shard_map/ppermute | solution.py:32
  8.9 12.1 %collective-permute-start = (bf16[8,128,128]{2,1,0:T(8,128)(2,1)}, bf16[8,128,128]{2,1,0:T(8,128)(2,1)S(1)}, u32[]{:S(2)}, u32[]{:S(2)}) collective-permute-start(bf16[8,128,128]{2,1,0:T(8,128)(2,1)} %get-tuple-element.21), channel_id=1, source_target_pairs={{0,4},{4,0},{8,12},{12,8},{16,20},{20,16},{24,28},{28,24},{1,5},{5... | collective-permute-start | bytes 786440 | tf_op jit(solution)/shard_map/ppermute | solution.py:32
  15.5 14.8 %copy-start.3 = (bf16[512,1024]{1,0:T(8,128)(2,1)S(1)}, bf16[512,1024]{1,0:T(8,128)(2,1)}, u32[]{:S(2)}) copy-start(bf16[512,1024]{1,0:T(8,128)(2,1)} %param.5) | copy-start | bytes 3145732
  21.2 8.9 %collective-permute-start.3 = (bf16[8,128,128]{2,1,0:T(8,128)(2,1)S(1)}, bf16[8,128,128]{2,1,0:T(8,128)(2,1)S(1)}, u32[]{:S(2)}, u32[]{:S(2)}) collective-permute-start(bf16[8,128,128]{2,1,0:T(8,128)(2,1)S(1)} %convert_add_fusion), channel_id=1, source_target_pairs={{0,16},{4,20},{8,24},{12,28},{16,0},{20,4},{24,8},{28,12},{1,17},{... | collective-permute-start | bytes 786440 | tf_op jit(solution)/shard_map/ppermute | solution.py:41
  34.2 3.9 %copy-start = (bf16[512,1024]{1,0:T(8,128)(2,1)S(1)}, bf16[512,1024]{1,0:T(8,128)(2,1)}, u32[]{:S(2)}) copy-start(bf16[512,1024]{1,0:T(8,128)(2,1)} %param.8) | copy-start | bytes 3145732
  36.2 3.7 %collective-permute-start.4 = (f32[512]{0:T(512)S(1)}, f32[512]{0:T(512)S(1)}, u32[]{:S(2)}, u32[]{:S(2)}) collective-permute-start(f32[512]{0:T(512)S(1)} %get-tuple-element.23), channel_id=1, source_target_pairs={{0,1},{1,0},{2,3},{3,2},{4,5},{5,4},{6,7},{7,6},{8,9},{9,8},{10,11... | collective-permute-start | bytes 6152 | tf_op jit(solution)/shard_map/ppermute | solution.py:61
  38.6 7.7 %copy-start.1 = (bf16[512,1024]{1,0:T(8,128)(2,1)}, bf16[512,1024]{1,0:T(8,128)(2,1)S(1)}, u32[]{:S(2)}) copy-start(bf16[512,1024]{1,0:T(8,128)(2,1)S(1)} %multiply_convert_fusion.3) | copy-start | bytes 3145732
  39.8 6.5 %collective-permute-start.5 = (f32[512]{0:T(512)S(1)}, f32[512]{0:T(512)S(1)}, u32[]{:S(2)}, u32[]{:S(2)}) collective-permute-start(f32[512]{0:T(512)S(1)} %add.143), channel_id=1, source_target_pairs={{0,2},{1,3},{2,0},{3,1},{4,6},{5,7},{6,4},{7,5},{8,10},{9,11},{10,... | collective-permute-start | bytes 6152 | tf_op jit(solution)/shard_map/ppermute | solution.py:61
  46.4 9.4 %collective-permute-start.7 = (bf16[512,1536]{1,0:T(8,128)(2,1)S(1)}, bf16[512,1536]{1,0:T(8,128)(2,1)S(1)}, u32[]{:S(2)}, u32[]{:S(2)}) collective-permute-start(bf16[512,1536]{1,0:T(8,128)(2,1)S(1)} %fusion.26), channel_id=1, source_target_pairs={{3,2},{7,6},{11,10},{15,14},{19,18},{23,22},{27,26},{31,30}} | collective-permute-start | bytes 4718600 | tf_op jit(solution)/shard_map/ppermute | solution.py:102
  47.1 35.1 %collective-permute-start.6 = (bf16[512,1536]{1,0:T(8,128)(2,1)S(1)}, bf16[512,1536]{1,0:T(8,128)(2,1)}, u32[]{:S(2)}, u32[]{:S(2)}) collective-permute-start(bf16[512,1536]{1,0:T(8,128)(2,1)S(1)} %fusion.26), channel_id=1, source_target_pairs={{0,1},{4,5},{8,9},{12,13},{16,17},{20,21},{24,25},{28,29}} | collective-permute-start | bytes 4718600 | tf_op jit(solution)/shard_map/ppermute | solution.py:101
  84.2 13.9 %collective-permute-start.10 = (bf16[512,1536]{1,0:T(8,128)(2,1)S(1)}, bf16[512,1536]{1,0:T(8,128)(2,1)}, u32[]{:S(2)}, u32[]{:S(2)}) collective-permute-start(bf16[512,1536]{1,0:T(8,128)(2,1)S(1)} %add_convert_fusion.2), channel_id=1, source_target_pairs={{2,1},{3,2},{6,5},{7,6},{10,9},{11,10},{14,13},{15,14},{18,17},{19... | collective-permute-start | bytes 4718600 | tf_op jit(solution)/shard_map/ppermute | solution.py:102
  86.1 34.7 %collective-permute-start.8 = (bf16[512,1536]{1,0:T(8,128)(2,1)S(1)}, bf16[512,1536]{1,0:T(8,128)(2,1)S(1)}, u32[]{:S(2)}, u32[]{:S(2)}) collective-permute-start(bf16[512,1536]{1,0:T(8,128)(2,1)S(1)} %add_convert_fusion.2), channel_id=1, source_target_pairs={{0,1},{1,2},{4,5},{5,6},{8,9},{9,10},{12,13},{13,14},{16,17},{17,1... | collective-permute-start | bytes 4718600 | tf_op jit(solution)/shard_map/ppermute | solution.py:101
  90.3 4.1 %copy-start.2 = (bf16[512,1024]{1,0:T(8,128)(2,1)S(1)}, bf16[512,1024]{1,0:T(8,128)(2,1)}, u32[]{:S(2)}) copy-start(bf16[512,1024]{1,0:T(8,128)(2,1)} %copy-done.1) | copy-start | bytes 3145732
  101.1 56.7 %collective-permute-start.11 = (bf16[512,1536]{1,0:T(8,128)(2,1)}, bf16[512,1536]{1,0:T(8,128)(2,1)}, u32[]{:S(2)}, u32[]{:S(2)}) collective-permute-start(bf16[512,1536]{1,0:T(8,128)(2,1)} %add_convert_fusion), channel_id=1, source_target_pairs={{1,0},{2,1},{3,2},{5,4},{6,5},{7,6},{9,8},{10,9},{11,10},{13,12},{... | collective-permute-start | bytes 4718600 | tf_op jit(solution)/shard_map/ppermute | solution.py:102
  121.1 37.9 %collective-permute-start.9 = (bf16[512,1536]{1,0:T(8,128)(2,1)S(1)}, bf16[512,1536]{1,0:T(8,128)(2,1)S(1)}, u32[]{:S(2)}, u32[]{:S(2)}) collective-permute-start(bf16[512,1536]{1,0:T(8,128)(2,1)S(1)} %add_convert_fusion.1), channel_id=1, source_target_pairs={{0,1},{1,2},{2,3},{4,5},{5,6},{6,7},{8,9},{9,10},{10,11},{12,13},{... | collective-permute-start | bytes 4718600 | tf_op jit(solution)/shard_map/ppermute | solution.py:101

commit v15 on v13

--- a/solution.py
+++ b/solution.py
@@ -119,11 +119,24 @@
     within_block = jnp.einsum(
         "nhts,nshd->nthd", scores, active_v, preferred_element_type=jnp.float32
     )
-    prefix, within_block = exclusive_prefix(span_total, "seq", within_block)
+    within_rows = within_block.reshape(tokens_here, feature_count)
+    prefix, within_rows = exclusive_prefix(span_total, "seq", within_rows)
     within_block, prefix = lax.optimization_barrier((within_block, prefix))
     before = (prefix[None] + earlier_local).astype(jnp.bfloat16)
-    from_state = jnp.einsum("nthd,nhde->nthe", active_q, before, preferred_element_type=jnp.float32)
-    attended = (within_block + from_state).reshape(tokens_here, feature_count)
+    if block_count == 1:
+        identity = jnp.eye(heads_here, dtype=jnp.bfloat16)
+        diagonal = jnp.einsum("hde,hg->hdge", before[0], identity).reshape(
+            feature_count, feature_count
+        )
+        from_state = jnp.dot(
+            active_q.reshape(tokens_here, feature_count), diagonal,
+            preferred_element_type=jnp.float32,
+        )
+    else:
+        from_state = jnp.einsum(
+            "nthd,nhde->nthe", active_q, before, preferred_element_type=jnp.float32
+        ).reshape(tokens_here, feature_count)
+    attended = within_rows + from_state
     square_sums = jnp.sum(attended * attended, axis=-1)
     gate = jax.nn.sigmoid(gate_logits.astype(jnp.float32))
     gated = (attended * gate).astype(jnp.bfloat16)

time: 153 us -> 153 us (level)
    reshape x2 -> x1, local copies, waits for them, and re-layouts: 2.55 us -> 0.54 us  [the longest x1 2.01 us: body(): attended = (within_block + from_state).reshape(tokens_here, feature_count)]
    optimization_barrier x0 -> x1, local copies, waits for them, and re-layouts: none -> 1.92 us  [exclusive_prefix(): group_total, companion = lax.optimization_barrier((group_total, companion))]
    ppermute x3, waiting for transfers between devices: 7.25 us -> 5.42 us  [exclusive_prefix(): arrived = lax.ppermute(group_total.astype(jnp.bfloat16), axis_name, pairs)]
  transfers between devices with their start and end apart: 11 -> 11, of which waited for: 8 -> 8; matrix products, arithmetic and copies ran while one was open for 20% -> 21% of each run, Pallas kernels for 0% -> 0%
where the time goes in v15:
time: 153 us
  waiting for transfers between devices  75.6 us (49%)
  starting transfers between devices  30.3 us (20%)
  matrix products  28.3 us (18%)
  other arithmetic  13.8 us (9%)
  local copies, waits for them, and re-layouts  4.15 us (3%)
    ppermute x3, waiting for transfers between devices, line_reduce_scatter(): lax.ppermute(to_right, axis_name, right_pairs).astype(jnp.float32)  44.5 us
    ppermute x3, waiting for transfers between devices, line_reduce_scatter(): lax.ppermute(to_left, axis_name, left_pairs).astype(jnp.float32)  23.7 us
    dot_general x5, matrix products, shard_product(): return jnp.dot(gated, columns, preferred_element_type=jnp.float32)  19.8 us
    ppermute x3, starting transfers between devices, line_reduce_scatter(): lax.ppermute(to_right, axis_name, right_pairs).astype(jnp.float32)  17.1 us
    dot_general x1, matrix products, body(): jnp.einsum('nhts,nshd->nthd', scores, active_v, preferred_element_type=jn...  5.44 us
    ppermute x3, waiting for transfers between devices, exclusive_prefix(): arrived = lax.ppermute(group_total.astype(jnp.bfloat16), axis_name, pairs)  5.42 us
    ppermute x3, starting transfers between devices, exclusive_prefix(): arrived = lax.ppermute(group_total.astype(jnp.bfloat16), axis_name, pairs)  5.3 us
    ppermute x2, starting transfers between devices, butterfly_sum(): lax.ppermute(values, axis_name, [(i, i ^ bit) for i in range(count)])  4.11 us
  transfers between devices with their start and end apart: 11, of which 8 were waited for; matrix products, arithmetic and copies ran while one was open for 21% of the time, Pallas kernels for 0%

profile of v15, /device:TPU:0, one launch (start us, length us, event | category | flops | bytes accessed | tf_op | source)
XLA Modules:
  0.0 152.5 jit_solution(4081901246100919651)
XLA Ops:
  0.0 1.9 %fusion.32 = bf16[512,1024]{1,0:T(8,128)(2,1)S(1)} fusion(bf16[512,1024]{1,0:T(8,128)(2,1)} %param.6), kind=kLoop, calls=%fused_computation.32 | loop fusion | flops 3145728 | bytes 2097152 | tf_op jit(solution)/shard_map/convert_element_type | solution.py:11
  4.7 1.1 fusion.51
  5.9 2.9 %collective-permute-start.1 = (bf16[8,128,128]{2,1,0:T(8,128)(2,1)S(1)}, bf16[8,128,128]{2,1,0:T(8,128)(2,1)S(1)}, u32[]{:S(2)}, u32[]{:S(2)}) collective-permute-start(bf16[8,128,128]{2,1,0:T(8,128)(2,1)S(1)} %fusion.54), channel_id=1, source_target_pairs={{0,8},{4,12},{8,0},{12,4},{16,24},{20,28},{24,16},{28,20},{1,9},{5... | collective-permute-start | bytes 786440 | tf_op jit(solution)/shard_map/ppermute | solution.py:31
  8.8 5.4 %fusion = f32[8,128,512]{2,1,0:T(8,128)} fusion(bf16[512,8,128]{0,2,1:T(8,128)(2,1)S(1)} %bitcast.38, f32[512,512]{1,0:T(8,128)} %fusion.51, bf16[512,8,128]{0,2,1:T(8,128)(2,1)S(1)} %bitcast.36, bf16[512,1024]{1,0:T(8,128)(2,1)} %param.5), kind=kOutput, calls=%fused_computation.1 | convolution fusion | flops 1081081856 | bytes 6291456 | tf_op jit(solution)/shard_map/nhts,nshd->nthd/dot_general | solution.py:119
  14.2 1.2 collective-permute-done.1
  15.5 1.8 %collective-permute-start.2 = (bf16[8,128,128]{2,1,0:T(8,128)(2,1)S(1)}, bf16[8,128,128]{2,1,0:T(8,128)(2,1)}, u32[]{:S(2)}, u32[]{:S(2)}) collective-permute-start(bf16[8,128,128]{2,1,0:T(8,128)(2,1)S(1)} %convert_add_fusion), channel_id=1, source_target_pairs={{0,16},{4,20},{8,24},{12,28},{16,0},{20,4},{24,8},{28,12},{1,17},{... | collective-permute-start | bytes 786440 | tf_op jit(solution)/shard_map/ppermute | solution.py:31
  17.3 1.9 %copy.13 = f32[512,1024]{1,0:T(8,128)S(1)} copy(f32[512,1024]{0,1:T(8,128)} %bitcast.39) | data formatting | bytes 4194304 | tf_op jit(solution)/shard_map/optimization_barrier | solution.py:29
  19.3 4.2 %collective-permute-done.2 = bf16[8,128,128]{2,1,0:T(8,128)(2,1)} collective-permute-done((bf16[8,128,128]{2,1,0:T(8,128)(2,1)S(1)}, bf16[8,128,128]{2,1,0:T(8,128)(2,1)}, u32[]{:S(2)}, u32[]{:S(2)}) %collective-permute-start.2) | collective-permute-done | bytes 262176 | tf_op jit(solution)/shard_map/ppermute | solution.py:31
  23.4 1.1 fusion.53
  25.0 0.8 copy-done.1
  26.1 2.7 %multiply_reduce_fusion = (f32[512]{0:T(512)S(1)}, bf16[512,1024]{1,0:T(8,128)(2,1)}) fusion(bf16[512,1024]{1,0:T(8,128)(2,1)S(1)} %copy-done.1, f32[512,1024]{1,0:T(8,128)S(1)} %copy.13, bf16[128,8,8,128]{3,2,1,0:T(8,128)(2,1)S(1)} %bitcast.40, bf16[512,1024]{1,0:T(8,128)(2,1)S(1)} %copy-done.2), kind=kOutput, calls=%fused_computation.44 | convolution fusion | flops 1081605632 | bytes 7342080 | tf_op jit(solution)/shard_map/dot_general | solution.py:131
  28.8 1.6 %collective-permute-start.3 = (f32[512]{0:T(512)S(1)}, f32[512]{0:T(512)S(1)}, u32[]{:S(2)}, u32[]{:S(2)}) collective-permute-start(f32[512]{0:T(512)S(1)} %get-tuple-element.19), channel_id=1, source_target_pairs={{0,1},{1,0},{2,3},{3,2},{4,5},{5,4},{6,7},{7,6},{8,9},{9,8},{10,11... | collective-permute-start | bytes 6152 | tf_op jit(solution)/shard_map/ppermute | solution.py:51
  30.3 2.0 %collective-permute-done.3 = f32[512]{0:T(512)S(1)} collective-permute-done((f32[512]{0:T(512)S(1)}, f32[512]{0:T(512)S(1)}, u32[]{:S(2)}, u32[]{:S(2)}) %collective-permute-start.3) | collective-permute-done | bytes 2080 | tf_op jit(solution)/shard_map/ppermute | solution.py:51
  32.4 2.6 %collective-permute-start.4 = (f32[512]{0:T(512)S(1)}, f32[512]{0:T(512)S(1)}, u32[]{:S(2)}, u32[]{:S(2)}) collective-permute-start(f32[512]{0:T(512)S(1)} %add.141), channel_id=1, source_target_pairs={{0,2},{1,3},{2,0},{3,1},{4,6},{5,7},{6,4},{7,5},{8,10},{9,11},{10,... | collective-permute-start | bytes 6152 | tf_op jit(solution)/shard_map/ppermute | solution.py:51
  34.9 4.0 %fusion.26 = bf16[512,1536]{1,0:T(8,128)(2,1)S(1)} fusion(bf16[512,1024]{1,0:T(8,128)(2,1)} %get-tuple-element.20, bf16[1024,6144]{1,0:T(8,128)(2,1)} %param.9, s32[]{:T(128)S(6)} %select_n.64), kind=kOutput, calls=%fused_computation.22 | convolution fusion | flops 1611399168 | bytes 5767172 | tf_op jit(solution)/shard_map/dot_general | solution.py:42
  39.0 0.8 collective-permute-start.6
  39.7 4.7 %collective-permute-start.5 = (bf16[512,1536]{1,0:T(8,128)(2,1)S(1)}, bf16[512,1536]{1,0:T(8,128)(2,1)}, u32[]{:S(2)}, u32[]{:S(2)}) collective-permute-start(bf16[512,1536]{1,0:T(8,128)(2,1)S(1)} %fusion.26), channel_id=1, source_target_pairs={{0,1},{4,5},{8,9},{12,13},{16,17},{20,21},{24,25},{28,29}} | collective-permute-start | bytes 4718600 | tf_op jit(solution)/shard_map/ppermute | solution.py:91
  44.4 4.0 %fusion.23 = bf16[512,1536]{1,0:T(8,128)(2,1)S(1)} fusion(bf16[512,1024]{1,0:T(8,128)(2,1)} %get-tuple-element.20, bf16[1024,6144]{1,0:T(8,128)(2,1)} %param.9, s32[]{:T(128)S(6)} %select_n.62), kind=kOutput, calls=%fused_computation.21 | convolution fusion | flops 1611399168 | bytes 5767172 | tf_op jit(solution)/shard_map/dot_general | solution.py:42
  48.4 25.6 %collective-permute-done.5 = bf16[512,1536]{1,0:T(8,128)(2,1)} collective-permute-done((bf16[512,1536]{1,0:T(8,128)(2,1)S(1)}, bf16[512,1536]{1,0:T(8,128)(2,1)}, u32[]{:S(2)}, u32[]{:S(2)}) %collective-permute-start.5) | collective-permute-done | bytes 1572896 | tf_op jit(solution)/shard_map/ppermute | solution.py:91
  74.0 2.0 %add_convert_fusion.2 = bf16[512,1536]{1,0:T(8,128)(2,1)S(1)} fusion(bf16[512,1536]{1,0:T(8,128)(2,1)S(1)} %collective-permute-done.6, bf16[512,1536]{1,0:T(8,128)(2,1)} %collective-permute-done.5, bf16[512,1536]{1,0:T(8,128)(2,1)S(1)} %fusion.23), kind=kLoop, calls=%fused_computation.7 | loop fusion | flops 4718592 | bytes 6291456 | tf_op jit(solution)/shard_map/convert_element_type | solution.py:75
  76.0 1.8 %collective-permute-start.9 = (bf16[512,1536]{1,0:T(8,128)(2,1)S(1)}, bf16[512,1536]{1,0:T(8,128)(2,1)}, u32[]{:S(2)}, u32[]{:S(2)}) collective-permute-start(bf16[512,1536]{1,0:T(8,128)(2,1)S(1)} %add_convert_fusion.2), channel_id=1, source_target_pairs={{2,1},{3,2},{6,5},{7,6},{10,9},{11,10},{14,13},{15,14},{18,17},{19... | collective-permute-start | bytes 4718600 | tf_op jit(solution)/shard_map/ppermute | solution.py:92
  77.9 4.2 %collective-permute-start.7 = (bf16[512,1536]{1,0:T(8,128)(2,1)S(1)}, bf16[512,1536]{1,0:T(8,128)(2,1)S(1)}, u32[]{:S(2)}, u32[]{:S(2)}) collective-permute-start(bf16[512,1536]{1,0:T(8,128)(2,1)S(1)} %add_convert_fusion.2), channel_id=1, source_target_pairs={{0,1},{1,2},{4,5},{5,6},{8,9},{9,10},{12,13},{13,14},{16,17},{17,1... | collective-permute-start | bytes 4718600 | tf_op jit(solution)/shard_map/ppermute | solution.py:91
  82.1 4.1 %fusion.17 = bf16[512,1536]{1,0:T(8,128)(2,1)S(1)} fusion(bf16[512,1024]{1,0:T(8,128)(2,1)} %get-tuple-element.20, bf16[1024,6144]{1,0:T(8,128)(2,1)} %param.9, s32[]{:T(128)S(6)} %select_n.59), kind=kOutput, calls=%fused_computation.19 | convolution fusion | flops 1611399168 | bytes 5767172 | tf_op jit(solution)/shard_map/dot_general | solution.py:42
  86.2 3.7 %fusion.20 = bf16[512,1536]{1,0:T(8,128)(2,1)S(1)} fusion(bf16[512,1024]{1,0:T(8,128)(2,1)S(1)} %copy-done.3, bf16[1024,6144]{1,0:T(8,128)(2,1)} %param.9, s32[]{:T(128)S(6)} %select_n.60), kind=kOutput, calls=%fused_computation.20 | convolution fusion | flops 1611399168 | bytes 5767172 | tf_op jit(solution)/shard_map/dot_general | solution.py:42
  89.9 2.9 %add_convert_fusion = bf16[512,1536]{1,0:T(8,128)(2,1)} fusion(bf16[512,1536]{1,0:T(8,128)(2,1)} %collective-permute-done.9, bf16[512,1536]{1,0:T(8,128)(2,1)S(1)} %fusion.20), kind=kLoop, calls=%fused_computation.5 | loop fusion | flops 3145728 | bytes 4718592 | tf_op jit(solution)/shard_map/convert_element_type | solution.py:88
  92.9 1.3 collective-permute-start.10
  94.2 17.6 %collective-permute-done.7 = bf16[512,1536]{1,0:T(8,128)(2,1)S(1)} collective-permute-done((bf16[512,1536]{1,0:T(8,128)(2,1)S(1)}, bf16[512,1536]{1,0:T(8,128)(2,1)S(1)}, u32[]{:S(2)}, u32[]{:S(2)}) %collective-permute-start.7) | collective-permute-done | bytes 1572896 | tf_op jit(solution)/shard_map/ppermute | solution.py:91
  112.2 8.2 %collective-permute-start.8 = (bf16[512,1536]{1,0:T(8,128)(2,1)S(1)}, bf16[512,1536]{1,0:T(8,128)(2,1)S(1)}, u32[]{:S(2)}, u32[]{:S(2)}) collective-permute-start(bf16[512,1536]{1,0:T(8,128)(2,1)S(1)} %add_convert_fusion.1), channel_id=1, source_target_pairs={{0,1},{1,2},{2,3},{4,5},{5,6},{6,7},{8,9},{9,10},{10,11},{12,13},{... | collective-permute-start | bytes 4718600 | tf_op jit(solution)/shard_map/ppermute | solution.py:91
  120.3 4.0 %fusion.14 = bf16[512,1536]{1,0:T(8,128)(2,1)S(1)} fusion(bf16[512,1024]{1,0:T(8,128)(2,1)} %get-tuple-element.20, bf16[1024,6144]{1,0:T(8,128)(2,1)} %param.9, s32[]{:T(128)S(6)} %select_n.58), kind=kOutput, calls=%fused_computation.18 | convolution fusion | flops 1611399168 | bytes 5767172 | tf_op jit(solution)/shard_map/dot_general | solution.py:42
  124.3 23.7 %collective-permute-done.10 = bf16[512,1536]{1,0:T(8,128)(2,1)} collective-permute-done((bf16[512,1536]{1,0:T(8,128)(2,1)}, bf16[512,1536]{1,0:T(8,128)(2,1)}, u32[]{:S(2)}, u32[]{:S(2)}) %collective-permute-start.10) | collective-permute-done | bytes 1572896 | tf_op jit(solution)/shard_map/ppermute | solution.py:92
  148.0 1.3 collective-permute-done.8
  149.3 3.2 %multiply_convert_fusion.2 = bf16[512,1536]{1,0:T(8,128)(2,1)} fusion(bf16[512,1536]{1,0:T(8,128)(2,1)} %collective-permute-done.10, bf16[512,1536]{1,0:T(8,128)(2,1)S(1)} %collective-permute-done.8, bf16[512,1536]{1,0:T(8,128)(2,1)S(1)} %fusion.14, f32[512]{0:T(512)S(1)} %add_rsqrt_fusion), kind=kLoop, calls=%fused_computation.4 | loop fusion | flops 5505024 | bytes 6293504 | tf_op jit(solution)/shard_map/convert_element_type | solution.py:145
  (25 shorter events, 4.0 us)
Async XLA Ops:
  0.0 2.5 %copy-start = (bf16[512,1024]{1,0:T(8,128)(2,1)S(1)}, bf16[512,1024]{1,0:T(8,128)(2,1)}, u32[]{:S(2)}) copy-start(bf16[512,1024]{1,0:T(8,128)(2,1)} %param.7) | copy-start | bytes 3145732
  4.1 1.7 %collective-permute-start = (bf16[8,128,128]{2,1,0:T(8,128)(2,1)S(1)}, bf16[8,128,128]{2,1,0:T(8,128)(2,1)S(1)}, u32[]{:S(2)}, u32[]{:S(2)}) collective-permute-start(bf16[8,128,128]{2,1,0:T(8,128)(2,1)S(1)} %get-tuple-element.21), channel_id=1, source_target_pairs={{0,4},{4,0},{8,12},{12,8},{16,20},{20,16},{24,28},{28,24},{1,5},{5... | collective-permute-start | bytes 786440 | tf_op jit(solution)/shard_map/ppermute | solution.py:31
  5.9 9.5 %collective-permute-start.1 = (bf16[8,128,128]{2,1,0:T(8,128)(2,1)S(1)}, bf16[8,128,128]{2,1,0:T(8,128)(2,1)S(1)}, u32[]{:S(2)}, u32[]{:S(2)}) collective-permute-start(bf16[8,128,128]{2,1,0:T(8,128)(2,1)S(1)} %fusion.54), channel_id=1, source_target_pairs={{0,8},{4,12},{8,0},{12,4},{16,24},{20,28},{24,16},{28,20},{1,9},{5... | collective-permute-start | bytes 786440 | tf_op jit(solution)/shard_map/ppermute | solution.py:31
  15.5 7.9 %collective-permute-start.2 = (bf16[8,128,128]{2,1,0:T(8,128)(2,1)S(1)}, bf16[8,128,128]{2,1,0:T(8,128)(2,1)}, u32[]{:S(2)}, u32[]{:S(2)}) collective-permute-start(bf16[8,128,128]{2,1,0:T(8,128)(2,1)S(1)} %convert_add_fusion), channel_id=1, source_target_pairs={{0,16},{4,20},{8,24},{12,28},{16,0},{20,4},{24,8},{28,12},{1,17},{... | collective-permute-start | bytes 786440 | tf_op jit(solution)/shard_map/ppermute | solution.py:31
  24.5 1.2 copy-start.1
  24.6 1.5 %copy-start.2 = (bf16[512,1024]{1,0:T(8,128)(2,1)S(1)}, bf16[512,1024]{1,0:T(8,128)(2,1)}, u32[]{:S(2)}) copy-start(bf16[512,1024]{1,0:T(8,128)(2,1)} %param.5) | copy-start | bytes 3145732
  28.8 3.6 %collective-permute-start.3 = (f32[512]{0:T(512)S(1)}, f32[512]{0:T(512)S(1)}, u32[]{:S(2)}, u32[]{:S(2)}) collective-permute-start(f32[512]{0:T(512)S(1)} %get-tuple-element.19), channel_id=1, source_target_pairs={{0,1},{1,0},{2,3},{3,2},{4,5},{5,4},{6,7},{7,6},{8,9},{9,8},{10,11... | collective-permute-start | bytes 6152 | tf_op jit(solution)/shard_map/ppermute | solution.py:51
  32.4 6.6 %collective-permute-start.4 = (f32[512]{0:T(512)S(1)}, f32[512]{0:T(512)S(1)}, u32[]{:S(2)}, u32[]{:S(2)}) collective-permute-start(f32[512]{0:T(512)S(1)} %add.141), channel_id=1, source_target_pairs={{0,2},{1,3},{2,0},{3,1},{4,6},{5,7},{6,4},{7,5},{8,10},{9,11},{10,... | collective-permute-start | bytes 6152 | tf_op jit(solution)/shard_map/ppermute | solution.py:51
  39.0 9.4 %collective-permute-start.6 = (bf16[512,1536]{1,0:T(8,128)(2,1)S(1)}, bf16[512,1536]{1,0:T(8,128)(2,1)S(1)}, u32[]{:S(2)}, u32[]{:S(2)}) collective-permute-start(bf16[512,1536]{1,0:T(8,128)(2,1)S(1)} %fusion.26), channel_id=1, source_target_pairs={{3,2},{7,6},{11,10},{15,14},{19,18},{23,22},{27,26},{31,30}} | collective-permute-start | bytes 4718600 | tf_op jit(solution)/shard_map/ppermute | solution.py:92
  39.7 34.3 %collective-permute-start.5 = (bf16[512,1536]{1,0:T(8,128)(2,1)S(1)}, bf16[512,1536]{1,0:T(8,128)(2,1)}, u32[]{:S(2)}, u32[]{:S(2)}) collective-permute-start(bf16[512,1536]{1,0:T(8,128)(2,1)S(1)} %fusion.26), channel_id=1, source_target_pairs={{0,1},{4,5},{8,9},{12,13},{16,17},{20,21},{24,25},{28,29}} | collective-permute-start | bytes 4718600 | tf_op jit(solution)/shard_map/ppermute | solution.py:91
  76.0 13.9 %collective-permute-start.9 = (bf16[512,1536]{1,0:T(8,128)(2,1)S(1)}, bf16[512,1536]{1,0:T(8,128)(2,1)}, u32[]{:S(2)}, u32[]{:S(2)}) collective-permute-start(bf16[512,1536]{1,0:T(8,128)(2,1)S(1)} %add_convert_fusion.2), channel_id=1, source_target_pairs={{2,1},{3,2},{6,5},{7,6},{10,9},{11,10},{14,13},{15,14},{18,17},{19... | collective-permute-start | bytes 4718600 | tf_op jit(solution)/shard_map/ppermute | solution.py:92
  77.9 33.9 %collective-permute-start.7 = (bf16[512,1536]{1,0:T(8,128)(2,1)S(1)}, bf16[512,1536]{1,0:T(8,128)(2,1)S(1)}, u32[]{:S(2)}, u32[]{:S(2)}) collective-permute-start(bf16[512,1536]{1,0:T(8,128)(2,1)S(1)} %add_convert_fusion.2), channel_id=1, source_target_pairs={{0,1},{1,2},{4,5},{5,6},{8,9},{9,10},{12,13},{13,14},{16,17},{17,1... | collective-permute-start | bytes 4718600 | tf_op jit(solution)/shard_map/ppermute | solution.py:91
  82.1 4.1 %copy-start.3 = (bf16[512,1024]{1,0:T(8,128)(2,1)S(1)}, bf16[512,1024]{1,0:T(8,128)(2,1)}, u32[]{:S(2)}) copy-start(bf16[512,1024]{1,0:T(8,128)(2,1)} %get-tuple-element.20) | copy-start | bytes 3145732
  92.9 55.2 %collective-permute-start.10 = (bf16[512,1536]{1,0:T(8,128)(2,1)}, bf16[512,1536]{1,0:T(8,128)(2,1)}, u32[]{:S(2)}, u32[]{:S(2)}) collective-permute-start(bf16[512,1536]{1,0:T(8,128)(2,1)} %add_convert_fusion), channel_id=1, source_target_pairs={{1,0},{2,1},{3,2},{5,4},{6,5},{7,6},{9,8},{10,9},{11,10},{13,12},{... | collective-permute-start | bytes 4718600 | tf_op jit(solution)/shard_map/ppermute | solution.py:92
  112.2 37.1 %collective-permute-start.8 = (bf16[512,1536]{1,0:T(8,128)(2,1)S(1)}, bf16[512,1536]{1,0:T(8,128)(2,1)S(1)}, u32[]{:S(2)}, u32[]{:S(2)}) collective-permute-start(bf16[512,1536]{1,0:T(8,128)(2,1)S(1)} %add_convert_fusion.1), channel_id=1, source_target_pairs={{0,1},{1,2},{2,3},{4,5},{5,6},{6,7},{8,9},{9,10},{10,11},{12,13},{... | collective-permute-start | bytes 4718600 | tf_op jit(solution)/shard_map/ppermute | solution.py:91

commit v16 on v15

--- a/solution.py
+++ b/solution.py
@@ -53,13 +53,27 @@
     return values
 
 
-def line_reduce_scatter(gated, out_weight, axis_name, total_squares):
+def line_reduce_scatter(gated, out_weight, axis_name, square_sums):
     count = lax.axis_size(axis_name)
     here = lax.axis_index(axis_name)
     width = out_weight.shape[1] // count
     from_left = None
     from_right = None
+    power_of_two = not count & (count - 1)
+    if power_of_two:
+        total_squares = square_sums + lax.ppermute(
+            square_sums, axis_name, [(i, i ^ 1) for i in range(count)]
+        )
+    else:
+        total_squares = lax.psum(square_sums, axis_name)
     for step in range(1, count):
+        if power_of_two and step == 2:
+            bit = 2
+            while bit < count:
+                total_squares = total_squares + lax.ppermute(
+                    total_squares, axis_name, [(i, i ^ bit) for i in range(count)]
+                )
+                bit *= 2
         right_shard = jnp.clip(here + count - step, 0, count - 1)
         left_shard = jnp.clip(here - count + step, 0, count - 1)
         if 2 * step <= count:
@@ -73,6 +87,8 @@
             if from_left is not None:
                 to_right = to_right + from_left + from_right
             to_right = to_right.astype(jnp.bfloat16)
+            if step == 2:
+                to_right, total_squares = lax.optimization_barrier((to_right, total_squares))
             to_left = to_right
         else:
             to_right = shard_product(gated, out_weight, right_shard, width).astype(jnp.bfloat16)
@@ -140,8 +156,7 @@
     square_sums = jnp.sum(attended * attended, axis=-1)
     gate = jax.nn.sigmoid(gate_logits.astype(jnp.float32))
     gated = (attended * gate).astype(jnp.bfloat16)
-    total_squares = butterfly_sum(square_sums, "head")
-    reduced = line_reduce_scatter(gated, out_weight, "head", total_squares)
+    reduced = line_reduce_scatter(gated, out_weight, "head", square_sums)
     return reduced.astype(jnp.bfloat16)
 
 

time: 153 us -> 152 us (level)
    ppermute x3, waiting for transfers between devices: 44.5 us -> 19.7 us  [line_reduce_scatter(): lax.ppermute(to_right, axis_name, right_pairs).astype(jnp.float32)]
    ppermute x2, waiting for transfers between devices: 2.03 us -> 26 us  [the longest x1 26 us: line_reduce_scatter(): lax.ppermute(total_squares, axis_name, [(i, i ^ bit) for i in range(count)])]
  transfers between devices with their start and end apart: 11 -> 11, of which waited for: 8 -> 7; matrix products, arithmetic and copies ran while one was open for 21% -> 21% of each run, Pallas kernels for 0% -> 0%
where the time goes in v16:
time: 152 us; the launch traced here: 151 us
  waiting for transfers between devices  75.7 us (50%)
  starting transfers between devices  29 us (19%)
  matrix products  28.3 us (19%)
  other arithmetic  13.8 us (9%)
  local copies, waits for them, and re-layouts  4.16 us (3%)
    ppermute x1, waiting for transfers between devices, line_reduce_scatter(): lax.ppermute(total_squares, axis_name, [(i, i ^ bit) for i in range(count)])  26 us
    ppermute x3, waiting for transfers between devices, line_reduce_scatter(): lax.ppermute(to_left, axis_name, left_pairs).astype(jnp.float32)  24.5 us
    dot_general x5, matrix products, shard_product(): return jnp.dot(gated, columns, preferred_element_type=jnp.float32)  20.6 us
    ppermute x3, waiting for transfers between devices, line_reduce_scatter(): lax.ppermute(to_right, axis_name, right_pairs).astype(jnp.float32)  19.7 us
    ppermute x3, starting transfers between devices, line_reduce_scatter(): lax.ppermute(to_right, axis_name, right_pairs).astype(jnp.float32)  16.8 us
    dot_general x1, matrix products, body(): jnp.einsum('nhts,nshd->nthd', scores, active_v, preferred_element_type=jn...  5.44 us
    ppermute x3, waiting for transfers between devices, exclusive_prefix(): arrived = lax.ppermute(group_total.astype(jnp.bfloat16), axis_name, pairs)  5.42 us
    ppermute x3, starting transfers between devices, exclusive_prefix(): arrived = lax.ppermute(group_total.astype(jnp.bfloat16), axis_name, pairs)  5.3 us
  transfers between devices with their start and end apart: 11, of which 7 were waited for; matrix products, arithmetic and copies ran while one was open for 21% of the time, Pallas kernels for 0%

profile of v16, /device:TPU:0, one launch (start us, length us, event | category | flops | bytes accessed | tf_op | source)
XLA Modules:
  0.0 151.2 jit_solution(7530505917703200680)
XLA Ops:
  0.0 1.9 %fusion.32 = bf16[512,1024]{1,0:T(8,128)(2,1)S(1)} fusion(bf16[512,1024]{1,0:T(8,128)(2,1)} %param.6), kind=kLoop, calls=%fused_computation.32 | loop fusion | flops 3145728 | bytes 2097152 | tf_op jit(solution)/shard_map/convert_element_type | solution.py:11
  2.5 0.6 fusion.36
  4.7 1.1 fusion.51
  5.9 2.9 %collective-permute-start.1 = (bf16[8,128,128]{2,1,0:T(8,128)(2,1)S(1)}, bf16[8,128,128]{2,1,0:T(8,128)(2,1)S(1)}, u32[]{:S(2)}, u32[]{:S(2)}) collective-permute-start(bf16[8,128,128]{2,1,0:T(8,128)(2,1)S(1)} %fusion.54), channel_id=1, source_target_pairs={{0,8},{4,12},{8,0},{12,4},{16,24},{20,28},{24,16},{28,20},{1,9},{5... | collective-permute-start | bytes 786440 | tf_op jit(solution)/shard_map/ppermute | solution.py:31
  8.8 5.4 %fusion = f32[8,128,512]{2,1,0:T(8,128)} fusion(bf16[512,8,128]{0,2,1:T(8,128)(2,1)S(1)} %bitcast.38, f32[512,512]{1,0:T(8,128)} %fusion.51, bf16[512,8,128]{0,2,1:T(8,128)(2,1)S(1)} %bitcast.36, bf16[512,1024]{1,0:T(8,128)(2,1)} %param.5), kind=kOutput, calls=%fused_computation.1 | convolution fusion | flops 1081081856 | bytes 6291456 | tf_op jit(solution)/shard_map/nhts,nshd->nthd/dot_general | solution.py:135
  14.2 1.2 collective-permute-done.1
  15.5 1.8 %collective-permute-start.2 = (bf16[8,128,128]{2,1,0:T(8,128)(2,1)S(1)}, bf16[8,128,128]{2,1,0:T(8,128)(2,1)}, u32[]{:S(2)}, u32[]{:S(2)}) collective-permute-start(bf16[8,128,128]{2,1,0:T(8,128)(2,1)S(1)} %convert_add_fusion), channel_id=1, source_target_pairs={{0,16},{4,20},{8,24},{12,28},{16,0},{20,4},{24,8},{28,12},{1,17},{... | collective-permute-start | bytes 786440 | tf_op jit(solution)/shard_map/ppermute | solution.py:31
  17.3 1.9 %copy.13 = f32[512,1024]{1,0:T(8,128)S(1)} copy(f32[512,1024]{0,1:T(8,128)} %bitcast.39) | data formatting | bytes 4194304 | tf_op jit(solution)/shard_map/optimization_barrier | solution.py:29
  19.3 4.2 %collective-permute-done.2 = bf16[8,128,128]{2,1,0:T(8,128)(2,1)} collective-permute-done((bf16[8,128,128]{2,1,0:T(8,128)(2,1)S(1)}, bf16[8,128,128]{2,1,0:T(8,128)(2,1)}, u32[]{:S(2)}, u32[]{:S(2)}) %collective-permute-start.2) | collective-permute-done | bytes 262176 | tf_op jit(solution)/shard_map/ppermute | solution.py:31
  23.4 1.1 fusion.53
  25.0 0.8 copy-done.1
  26.1 1.8 %multiply_reduce_fusion = (f32[512]{0:T(512)S(1)}, bf16[512,1024]{1,0:T(8,128)(2,1)S(1)}) fusion(bf16[512,1024]{1,0:T(8,128)(2,1)S(1)} %copy-done.1, f32[512,1024]{1,0:T(8,128)S(1)} %copy.13, bf16[128,8,8,128]{3,2,1,0:T(8,128)(2,1)S(1)} %bitcast.40, bf16[512,1024]{1,0:T(8,128)(2,1)S(1)} %copy-done.2), kind=kOutput, calls=%fused_computation.44 | convolution fusion | flops 1081605632 | bytes 7342080 | tf_op jit(solution)/shard_map/dot_general | solution.py:147
  27.9 1.6 %collective-permute-start.3 = (f32[512]{0:T(512)S(1)}, f32[512]{0:T(512)S(1)}, u32[]{:S(2)}, u32[]{:S(2)}) collective-permute-start(f32[512]{0:T(512)S(1)} %get-tuple-element.23), channel_id=1, source_target_pairs={{0,1},{1,0},{2,3},{3,2},{4,5},{5,4},{6,7},{7,6},{8,9},{9,8},{10,11... | collective-permute-start | bytes 6152 | tf_op jit(solution)/shard_map/ppermute | solution.py:64
  29.5 4.8 %fusion.26 = bf16[512,1536]{1,0:T(8,128)(2,1)} fusion(bf16[512,1024]{1,0:T(8,128)(2,1)S(1)} %get-tuple-element.24, bf16[1024,6144]{1,0:T(8,128)(2,1)} %param.9, s32[]{:T(128)S(6)} %select_n.64), kind=kOutput, calls=%fused_computation.22 | convolution fusion | flops 1611399168 | bytes 5767172 | tf_op jit(solution)/shard_map/dot_general | solution.py:42
  34.4 0.8 collective-permute-start.5
  35.1 3.6 %collective-permute-start.4 = (bf16[512,1536]{1,0:T(8,128)(2,1)}, bf16[512,1536]{1,0:T(8,128)(2,1)}, u32[]{:S(2)}, u32[]{:S(2)}) collective-permute-start(bf16[512,1536]{1,0:T(8,128)(2,1)} %fusion.26), channel_id=1, source_target_pairs={{0,1},{4,5},{8,9},{12,13},{16,17},{20,21},{24,25},{28,29}} | collective-permute-start | bytes 4718600 | tf_op jit(solution)/shard_map/ppermute | solution.py:107
  38.7 1.4 collective-permute-start.6
  40.1 4.0 %fusion.23 = bf16[512,1536]{1,0:T(8,128)(2,1)S(1)} fusion(bf16[512,1024]{1,0:T(8,128)(2,1)} %copy-done.3, bf16[1024,6144]{1,0:T(8,128)(2,1)} %param.9, s32[]{:T(128)S(6)} %select_n.62), kind=kOutput, calls=%fused_computation.21 | convolution fusion | flops 1611399168 | bytes 5767172 | tf_op jit(solution)/shard_map/dot_general | solution.py:42
  44.1 26.0 %collective-permute-done.6 = f32[512]{0:T(512)S(1)} collective-permute-done((f32[512]{0:T(512)S(1)}, f32[512]{0:T(512)S(1)}, u32[]{:S(2)}, u32[]{:S(2)}) %collective-permute-start.6) | collective-permute-done | bytes 2080 | tf_op jit(solution)/shard_map/ppermute | solution.py:73
  70.1 2.0 %add_convert_fusion.2 = bf16[512,1536]{1,0:T(8,128)(2,1)S(1)} fusion(bf16[512,1536]{1,0:T(8,128)(2,1)S(1)} %collective-permute-done.5, bf16[512,1536]{1,0:T(8,128)(2,1)} %collective-permute-done.4, bf16[512,1536]{1,0:T(8,128)(2,1)S(1)} %fusion.23), kind=kLoop, calls=%fused_computation.7 | loop fusion | flops 4718592 | bytes 6291456 | tf_op jit(solution)/shard_map/convert_element_type | solution.py:89
  72.1 1.8 %collective-permute-start.9 = (bf16[512,1536]{1,0:T(8,128)(2,1)S(1)}, bf16[512,1536]{1,0:T(8,128)(2,1)}, u32[]{:S(2)}, u32[]{:S(2)}) collective-permute-start(bf16[512,1536]{1,0:T(8,128)(2,1)S(1)} %add_convert_fusion.2), channel_id=1, source_target_pairs={{2,1},{3,2},{6,5},{7,6},{10,9},{11,10},{14,13},{15,14},{18,17},{19... | collective-permute-start | bytes 4718600 | tf_op jit(solution)/shard_map/ppermute | solution.py:108
  73.9 5.1 %collective-permute-start.7 = (bf16[512,1536]{1,0:T(8,128)(2,1)S(1)}, bf16[512,1536]{1,0:T(8,128)(2,1)S(1)}, u32[]{:S(2)}, u32[]{:S(2)}) collective-permute-start(bf16[512,1536]{1,0:T(8,128)(2,1)S(1)} %add_convert_fusion.2), channel_id=1, source_target_pairs={{0,1},{1,2},{4,5},{5,6},{8,9},{9,10},{12,13},{13,14},{16,17},{17,1... | collective-permute-start | bytes 4718600 | tf_op jit(solution)/shard_map/ppermute | solution.py:107
  79.1 4.1 %fusion.17 = bf16[512,1536]{1,0:T(8,128)(2,1)S(1)} fusion(bf16[512,1024]{1,0:T(8,128)(2,1)} %copy-done.3, bf16[1024,6144]{1,0:T(8,128)(2,1)} %param.9, s32[]{:T(128)S(6)} %select_n.59), kind=kOutput, calls=%fused_computation.19 | convolution fusion | flops 1611399168 | bytes 5767172 | tf_op jit(solution)/shard_map/dot_general | solution.py:42
  83.2 3.7 %fusion.20 = bf16[512,1536]{1,0:T(8,128)(2,1)S(1)} fusion(bf16[512,1024]{1,0:T(8,128)(2,1)S(1)} %copy-done.4, bf16[1024,6144]{1,0:T(8,128)(2,1)} %param.9, s32[]{:T(128)S(6)} %select_n.60), kind=kOutput, calls=%fused_computation.20 | convolution fusion | flops 1611399168 | bytes 5767172 | tf_op jit(solution)/shard_map/dot_general | solution.py:42
  86.9 2.9 %add_convert_fusion = bf16[512,1536]{1,0:T(8,128)(2,1)} fusion(bf16[512,1536]{1,0:T(8,128)(2,1)} %collective-permute-done.9, bf16[512,1536]{1,0:T(8,128)(2,1)S(1)} %fusion.20), kind=kLoop, calls=%fused_computation.5 | loop fusion | flops 3145728 | bytes 4718592 | tf_op jit(solution)/shard_map/convert_element_type | solution.py:104
  89.8 1.3 collective-permute-start.10
  91.1 18.5 %collective-permute-done.7 = bf16[512,1536]{1,0:T(8,128)(2,1)S(1)} collective-permute-done((bf16[512,1536]{1,0:T(8,128)(2,1)S(1)}, bf16[512,1536]{1,0:T(8,128)(2,1)S(1)}, u32[]{:S(2)}, u32[]{:S(2)}) %collective-permute-start.7) | collective-permute-done | bytes 1572896 | tf_op jit(solution)/shard_map/ppermute | solution.py:107
  109.9 8.2 %collective-permute-start.8 = (bf16[512,1536]{1,0:T(8,128)(2,1)S(1)}, bf16[512,1536]{1,0:T(8,128)(2,1)S(1)}, u32[]{:S(2)}, u32[]{:S(2)}) collective-permute-start(bf16[512,1536]{1,0:T(8,128)(2,1)S(1)} %add_convert_fusion.1), channel_id=1, source_target_pairs={{0,1},{1,2},{2,3},{4,5},{5,6},{6,7},{8,9},{9,10},{10,11},{12,13},{... | collective-permute-start | bytes 4718600 | tf_op jit(solution)/shard_map/ppermute | solution.py:107
  118.1 4.0 %fusion.14 = bf16[512,1536]{1,0:T(8,128)(2,1)S(1)} fusion(bf16[512,1024]{1,0:T(8,128)(2,1)} %copy-done.3, bf16[1024,6144]{1,0:T(8,128)(2,1)} %param.9, s32[]{:T(128)S(6)} %select_n.58), kind=kOutput, calls=%fused_computation.18 | convolution fusion | flops 1611399168 | bytes 5767172 | tf_op jit(solution)/shard_map/dot_general | solution.py:42
  122.1 24.5 %collective-permute-done.10 = bf16[512,1536]{1,0:T(8,128)(2,1)} collective-permute-done((bf16[512,1536]{1,0:T(8,128)(2,1)}, bf16[512,1536]{1,0:T(8,128)(2,1)}, u32[]{:S(2)}, u32[]{:S(2)}) %collective-permute-start.10) | collective-permute-done | bytes 1572896 | tf_op jit(solution)/shard_map/ppermute | solution.py:108
  146.7 1.3 collective-permute-done.8
  147.9 3.2 %multiply_convert_fusion.2 = bf16[512,1536]{1,0:T(8,128)(2,1)} fusion(bf16[512,1536]{1,0:T(8,128)(2,1)} %collective-permute-done.10, bf16[512,1536]{1,0:T(8,128)(2,1)S(1)} %collective-permute-done.8, bf16[512,1536]{1,0:T(8,128)(2,1)S(1)} %fusion.14, f32[512]{0:T(512)S(1)} %add_rsqrt_fusion), kind=kLoop, calls=%fused_computation.4 | loop fusion | flops 5505024 | bytes 6293504 | tf_op jit(solution)/shard_map/convert_element_type | solution.py:160
  (27 shorter events, 3.4 us)
Async XLA Ops:
  0.0 2.5 %copy-start = (bf16[512,1024]{1,0:T(8,128)(2,1)S(1)}, bf16[512,1024]{1,0:T(8,128)(2,1)}, u32[]{:S(2)}) copy-start(bf16[512,1024]{1,0:T(8,128)(2,1)} %param.7) | copy-start | bytes 3145732
  4.1 1.7 %collective-permute-start = (bf16[8,128,128]{2,1,0:T(8,128)(2,1)S(1)}, bf16[8,128,128]{2,1,0:T(8,128)(2,1)S(1)}, u32[]{:S(2)}, u32[]{:S(2)}) collective-permute-start(bf16[8,128,128]{2,1,0:T(8,128)(2,1)S(1)} %get-tuple-element.25), channel_id=1, source_target_pairs={{0,4},{4,0},{8,12},{12,8},{16,20},{20,16},{24,28},{28,24},{1,5},{5... | collective-permute-start | bytes 786440 | tf_op jit(solution)/shard_map/ppermute | solution.py:31
  5.9 9.5 %collective-permute-start.1 = (bf16[8,128,128]{2,1,0:T(8,128)(2,1)S(1)}, bf16[8,128,128]{2,1,0:T(8,128)(2,1)S(1)}, u32[]{:S(2)}, u32[]{:S(2)}) collective-permute-start(bf16[8,128,128]{2,1,0:T(8,128)(2,1)S(1)} %fusion.54), channel_id=1, source_target_pairs={{0,8},{4,12},{8,0},{12,4},{16,24},{20,28},{24,16},{28,20},{1,9},{5... | collective-permute-start | bytes 786440 | tf_op jit(solution)/shard_map/ppermute | solution.py:31
  15.5 7.9 %collective-permute-start.2 = (bf16[8,128,128]{2,1,0:T(8,128)(2,1)S(1)}, bf16[8,128,128]{2,1,0:T(8,128)(2,1)}, u32[]{:S(2)}, u32[]{:S(2)}) collective-permute-start(bf16[8,128,128]{2,1,0:T(8,128)(2,1)S(1)} %convert_add_fusion), channel_id=1, source_target_pairs={{0,16},{4,20},{8,24},{12,28},{16,0},{20,4},{24,8},{28,12},{1,17},{... | collective-permute-start | bytes 786440 | tf_op jit(solution)/shard_map/ppermute | solution.py:31
  24.5 1.2 copy-start.1
  24.6 1.5 %copy-start.2 = (bf16[512,1024]{1,0:T(8,128)(2,1)S(1)}, bf16[512,1024]{1,0:T(8,128)(2,1)}, u32[]{:S(2)}) copy-start(bf16[512,1024]{1,0:T(8,128)(2,1)} %param.5) | copy-start | bytes 3145732
  27.9 6.5 %copy-start.3 = (bf16[512,1024]{1,0:T(8,128)(2,1)}, bf16[512,1024]{1,0:T(8,128)(2,1)S(1)}, u32[]{:S(2)}) copy-start(bf16[512,1024]{1,0:T(8,128)(2,1)S(1)} %get-tuple-element.24) | copy-start | bytes 3145732
  27.9 6.4 %collective-permute-start.3 = (f32[512]{0:T(512)S(1)}, f32[512]{0:T(512)S(1)}, u32[]{:S(2)}, u32[]{:S(2)}) collective-permute-start(f32[512]{0:T(512)S(1)} %get-tuple-element.23), channel_id=1, source_target_pairs={{0,1},{1,0},{2,3},{3,2},{4,5},{5,4},{6,7},{7,6},{8,9},{9,8},{10,11... | collective-permute-start | bytes 6152 | tf_op jit(solution)/shard_map/ppermute | solution.py:64
  34.4 35.7 %collective-permute-start.5 = (bf16[512,1536]{1,0:T(8,128)(2,1)}, bf16[512,1536]{1,0:T(8,128)(2,1)S(1)}, u32[]{:S(2)}, u32[]{:S(2)}) collective-permute-start(bf16[512,1536]{1,0:T(8,128)(2,1)} %fusion.26), channel_id=1, source_target_pairs={{3,2},{7,6},{11,10},{15,14},{19,18},{23,22},{27,26},{31,30}} | collective-permute-start | bytes 4718600 | tf_op jit(solution)/shard_map/ppermute | solution.py:108
  35.1 35.0 %collective-permute-start.4 = (bf16[512,1536]{1,0:T(8,128)(2,1)}, bf16[512,1536]{1,0:T(8,128)(2,1)}, u32[]{:S(2)}, u32[]{:S(2)}) collective-permute-start(bf16[512,1536]{1,0:T(8,128)(2,1)} %fusion.26), channel_id=1, source_target_pairs={{0,1},{4,5},{8,9},{12,13},{16,17},{20,21},{24,25},{28,29}} | collective-permute-start | bytes 4718600 | tf_op jit(solution)/shard_map/ppermute | solution.py:107
  38.7 31.4 %collective-permute-start.6 = (f32[512]{0:T(512)S(1)}, f32[512]{0:T(512)S(1)}, u32[]{:S(2)}, u32[]{:S(2)}) collective-permute-start(f32[512]{0:T(512)S(1)} %add.141), channel_id=1, source_target_pairs={{0,2},{1,3},{2,0},{3,1},{4,6},{5,7},{6,4},{7,5},{8,10},{9,11},{10,... | collective-permute-start | bytes 6152 | tf_op jit(solution)/shard_map/ppermute | solution.py:73
  72.1 14.8 %collective-permute-start.9 = (bf16[512,1536]{1,0:T(8,128)(2,1)S(1)}, bf16[512,1536]{1,0:T(8,128)(2,1)}, u32[]{:S(2)}, u32[]{:S(2)}) collective-permute-start(bf16[512,1536]{1,0:T(8,128)(2,1)S(1)} %add_convert_fusion.2), channel_id=1, source_target_pairs={{2,1},{3,2},{6,5},{7,6},{10,9},{11,10},{14,13},{15,14},{18,17},{19... | collective-permute-start | bytes 4718600 | tf_op jit(solution)/shard_map/ppermute | solution.py:108
  73.9 35.6 %collective-permute-start.7 = (bf16[512,1536]{1,0:T(8,128)(2,1)S(1)}, bf16[512,1536]{1,0:T(8,128)(2,1)S(1)}, u32[]{:S(2)}, u32[]{:S(2)}) collective-permute-start(bf16[512,1536]{1,0:T(8,128)(2,1)S(1)} %add_convert_fusion.2), channel_id=1, source_target_pairs={{0,1},{1,2},{4,5},{5,6},{8,9},{9,10},{12,13},{13,14},{16,17},{17,1... | collective-permute-start | bytes 4718600 | tf_op jit(solution)/shard_map/ppermute | solution.py:107
  79.1 4.1 %copy-start.4 = (bf16[512,1024]{1,0:T(8,128)(2,1)S(1)}, bf16[512,1024]{1,0:T(8,128)(2,1)}, u32[]{:S(2)}) copy-start(bf16[512,1024]{1,0:T(8,128)(2,1)} %copy-done.3) | copy-start | bytes 3145732
  89.8 56.9 %collective-permute-start.10 = (bf16[512,1536]{1,0:T(8,128)(2,1)}, bf16[512,1536]{1,0:T(8,128)(2,1)}, u32[]{:S(2)}, u32[]{:S(2)}) collective-permute-start(bf16[512,1536]{1,0:T(8,128)(2,1)} %add_convert_fusion), channel_id=1, source_target_pairs={{1,0},{2,1},{3,2},{5,4},{6,5},{7,6},{9,8},{10,9},{11,10},{13,12},{... | collective-permute-start | bytes 4718600 | tf_op jit(solution)/shard_map/ppermute | solution.py:108
  109.9 38.0 %collective-permute-start.8 = (bf16[512,1536]{1,0:T(8,128)(2,1)S(1)}, bf16[512,1536]{1,0:T(8,128)(2,1)S(1)}, u32[]{:S(2)}, u32[]{:S(2)}) collective-permute-start(bf16[512,1536]{1,0:T(8,128)(2,1)S(1)} %add_convert_fusion.1), channel_id=1, source_target_pairs={{0,1},{1,2},{2,3},{4,5},{5,6},{6,7},{8,9},{9,10},{10,11},{12,13},{... | collective-permute-start | bytes 4718600 | tf_op jit(solution)/shard_map/ppermute | solution.py:107

commit v17 on v16

--- a/solution.py
+++ b/solution.py
@@ -104,8 +104,12 @@
                 to_left = (to_left.astype(jnp.float32) + from_right).astype(jnp.bfloat16)
         right_pairs = [(i, i + 1) for i in range(step) if i + 1 < count]
         left_pairs = [(i, i - 1) for i in range(count - step, count) if i >= 1]
-        from_left = lax.ppermute(to_right, axis_name, right_pairs).astype(jnp.float32)
-        from_right = lax.ppermute(to_left, axis_name, left_pairs).astype(jnp.float32)
+        from_left = sum(
+            lax.ppermute(to_right, axis_name, [pair]).astype(jnp.float32) for pair in right_pairs
+        )
+        from_right = sum(
+            lax.ppermute(to_left, axis_name, [pair]).astype(jnp.float32) for pair in left_pairs
+        )
     own = shard_product(gated, out_weight, here, width).astype(jnp.bfloat16)
     own = own.astype(jnp.float32)
     scaling = lax.rsqrt(total_squares / (HEADS * HEAD_DIM) + 1e-06)

time: 152 us -> 188 us (1.24)
  the two profiles are of different devices: /device:TPU:0 before, /device:TPU:18 now
where the time goes in v17:
time: 188 us
  waiting for transfers between devices  107 us (57%)
  starting transfers between devices  30.9 us (16%)
  matrix products  28.4 us (15%)
  other arithmetic  16.4 us (9%)
  local copies, waits for them, and re-layouts  5.3 us (3%)
    ppermute x6, waiting for transfers between devices, line_reduce_scatter(): lax.ppermute(to_left, axis_name, [pair]).astype(jnp.float32)  36.5 us
    ppermute x6, waiting for transfers between devices, line_reduce_scatter(): lax.ppermute(to_right, axis_name, [pair]).astype(jnp.float32)  36.3 us
    ppermute x1, waiting for transfers between devices, line_reduce_scatter(): lax.ppermute(total_squares, axis_name, [(i, i ^ bit) for i in range(count)])  26.9 us
    dot_general x5, matrix products, shard_product(): return jnp.dot(gated, columns, preferred_element_type=jnp.float32)  20.7 us
    ppermute x6, starting transfers between devices, line_reduce_scatter(): lax.ppermute(to_left, axis_name, [pair]).astype(jnp.float32)  14.8 us
    ppermute x6, starting transfers between devices, line_reduce_scatter(): lax.ppermute(to_right, axis_name, [pair]).astype(jnp.float32)  9.6 us
    ppermute x3, waiting for transfers between devices, exclusive_prefix(): arrived = lax.ppermute(group_total.astype(jnp.bfloat16), axis_name, pairs)  6.95 us
    convert_element_type x1, other arithmetic, body(): return reduced.astype(jnp.bfloat16)  6.04 us
  transfers between devices with their start and end apart: 17, of which 11 were waited for; matrix products, arithmetic and copies ran while one was open for 17% of the time, Pallas kernels for 0%

profile of v17, /device:TPU:18, one launch (start us, length us, event | category | flops | bytes accessed | tf_op | source)
XLA Modules:
  0.0 187.8 jit_solution(13545869476908256271)
XLA Ops:
  0.0 1.9 %fusion.32 = bf16[512,1024]{1,0:T(8,128)(2,1)S(1)} fusion(bf16[512,1024]{1,0:T(8,128)(2,1)} %param.6), kind=kLoop, calls=%fused_computation.32 | loop fusion | flops 3145728 | bytes 2097152 | tf_op jit(solution)/shard_map/convert_element_type | solution.py:11
  6.4 5.4 %fusion = f32[8,128,512]{2,1,0:T(8,128)} fusion(bf16[512,8,128]{0,2,1:T(8,128)(2,1)S(1)} %bitcast.38, f32[512,512]{1,0:T(8,128)} %fusion.51, bf16[512,8,128]{0,2,1:T(8,128)(2,1)S(1)} %bitcast.36, bf16[512,1024]{1,0:T(8,128)(2,1)} %param.5), kind=kOutput, calls=%fused_computation.1 | convolution fusion | flops 1081081856 | bytes 6291456 | tf_op jit(solution)/shard_map/nhts,nshd->nthd/dot_general | solution.py:139
  11.8 2.4 %collective-permute-done.1 = bf16[8,128,128]{2,1,0:T(8,128)(2,1)S(1)} collective-permute-done((bf16[8,128,128]{2,1,0:T(8,128)(2,1)S(1)}, bf16[8,128,128]{2,1,0:T(8,128)(2,1)S(1)}, u32[]{:S(2)}, u32[]{:S(2)}) %collective-permute-start.1) | collective-permute-done | bytes 262176 | tf_op jit(solution)/shard_map/ppermute | solution.py:31
  14.3 1.6 collective-permute-start.2
  15.9 1.9 %copy.13 = f32[512,1024]{1,0:T(8,128)S(1)} copy(f32[512,1024]{0,1:T(8,128)} %bitcast.39) | data formatting | bytes 4194304 | tf_op jit(solution)/shard_map/optimization_barrier | solution.py:29
  17.8 4.1 %collective-permute-done.2 = bf16[8,128,128]{2,1,0:T(8,128)(2,1)} collective-permute-done((bf16[8,128,128]{2,1,0:T(8,128)(2,1)S(1)}, bf16[8,128,128]{2,1,0:T(8,128)(2,1)}, u32[]{:S(2)}, u32[]{:S(2)}) %collective-permute-start.2) | collective-permute-done | bytes 262176 | tf_op jit(solution)/shard_map/ppermute | solution.py:31
  24.6 1.8 multiply_reduce_fusion
  26.4 1.6 collective-permute-start.3
  28.0 4.8 %fusion.26 = bf16[512,1536]{1,0:T(8,128)(2,1)} fusion(bf16[512,1024]{1,0:T(8,128)(2,1)S(1)} %get-tuple-element.24, bf16[1024,6144]{1,0:T(8,128)(2,1)} %param.9, s32[]{:T(128)S(6)} %select_n.64), kind=kOutput, calls=%fused_computation.22 | convolution fusion | flops 1611399168 | bytes 5767172 | tf_op jit(solution)/shard_map/dot_general | solution.py:42
  35.0 2.5 %collective-permute-start.6 = (f32[512]{0:T(512)S(1)}, f32[512]{0:T(512)S(1)}, u32[]{:S(2)}, u32[]{:S(2)}) collective-permute-start(f32[512]{0:T(512)S(1)} %add.159), channel_id=1, source_target_pairs={{0,2},{1,3},{2,0},{3,1},{4,6},{5,7},{6,4},{7,5},{8,10},{9,11},{10,... | collective-permute-start | bytes 6152 | tf_op jit(solution)/shard_map/ppermute | solution.py:73
  37.5 4.0 %fusion.23 = bf16[512,1536]{1,0:T(8,128)(2,1)S(1)} fusion(bf16[512,1024]{1,0:T(8,128)(2,1)} %copy-done.5, bf16[1024,6144]{1,0:T(8,128)(2,1)} %param.9, s32[]{:T(128)S(6)} %select_n.62), kind=kOutput, calls=%fused_computation.21 | convolution fusion | flops 1611399168 | bytes 5767172 | tf_op jit(solution)/shard_map/dot_general | solution.py:42
  41.5 26.9 %collective-permute-done.6 = f32[512]{0:T(512)S(1)} collective-permute-done((f32[512]{0:T(512)S(1)}, f32[512]{0:T(512)S(1)}, u32[]{:S(2)}, u32[]{:S(2)}) %collective-permute-start.6) | collective-permute-done | bytes 2080 | tf_op jit(solution)/shard_map/ppermute | solution.py:73
  68.4 2.0 %collective-permute-done.5 = bf16[512,1536]{1,0:T(8,128)(2,1)} collective-permute-done((bf16[512,1536]{1,0:T(8,128)(2,1)}, bf16[512,1536]{1,0:T(8,128)(2,1)}, u32[]{:S(2)}, u32[]{:S(2)}) %collective-permute-start.5) | collective-permute-done | bytes 1572896 | tf_op jit(solution)/shard_map/ppermute | solution.py:111
  70.3 2.0 %add_convert_fusion.2 = bf16[512,1536]{1,0:T(8,128)(2,1)S(1)} fusion(bf16[512,1536]{1,0:T(8,128)(2,1)} %collective-permute-done.5, bf16[512,1536]{1,0:T(8,128)(2,1)S(1)} %collective-permute-done.4, bf16[512,1536]{1,0:T(8,128)(2,1)S(1)} %fusion.23), kind=kLoop, calls=%fused_computation.7 | loop fusion | flops 4718592 | bytes 6291456 | tf_op jit(solution)/shard_map/convert_element_type | solution.py:89
  72.3 1.8 collective-permute-start.7
  74.1 1.5 collective-permute-start.8
  75.6 4.1 %fusion.17 = bf16[512,1536]{1,0:T(8,128)(2,1)S(1)} fusion(bf16[512,1024]{1,0:T(8,128)(2,1)} %copy-done.5, bf16[1024,6144]{1,0:T(8,128)(2,1)} %param.9, s32[]{:T(128)S(6)} %select_n.59), kind=kOutput, calls=%fused_computation.19 | convolution fusion | flops 1611399168 | bytes 5767172 | tf_op jit(solution)/shard_map/dot_general | solution.py:42
  79.7 3.7 %fusion.20 = bf16[512,1536]{1,0:T(8,128)(2,1)S(1)} fusion(bf16[512,1024]{1,0:T(8,128)(2,1)S(1)} %copy-done.6, bf16[1024,6144]{1,0:T(8,128)(2,1)} %param.9, s32[]{:T(128)S(6)} %select_n.60), kind=kOutput, calls=%fused_computation.20 | convolution fusion | flops 1611399168 | bytes 5767172 | tf_op jit(solution)/shard_map/dot_general | solution.py:42
  83.4 5.6 %collective-permute-start.12 = (bf16[512,1536]{1,0:T(8,128)(2,1)S(1)}, bf16[512,1536]{1,0:T(8,128)(2,1)S(1)}, u32[]{:S(2)}, u32[]{:S(2)}) collective-permute-start(bf16[512,1536]{1,0:T(8,128)(2,1)S(1)} %add_convert_fusion.2), channel_id=1, source_target_pairs={{2,1},{6,5},{10,9},{14,13},{18,17},{22,21},{26,25},{30,29}} | collective-permute-start | bytes 4718600 | tf_op jit(solution)/shard_map/ppermute | solution.py:111
  90.3 19.4 %collective-permute-done.8 = bf16[512,1536]{1,0:T(8,128)(2,1)} collective-permute-done((bf16[512,1536]{1,0:T(8,128)(2,1)S(1)}, bf16[512,1536]{1,0:T(8,128)(2,1)}, u32[]{:S(2)}, u32[]{:S(2)}) %collective-permute-start.8) | collective-permute-done | bytes 1572896 | tf_op jit(solution)/shard_map/ppermute | solution.py:108
  109.7 2.5 %add_convert_fusion.1 = bf16[512,1536]{1,0:T(8,128)(2,1)S(1)} fusion(bf16[512,1536]{1,0:T(8,128)(2,1)} %collective-permute-done.8, bf16[512,1536]{1,0:T(8,128)(2,1)} %collective-permute-done.7, bf16[512,1536]{1,0:T(8,128)(2,1)S(1)} %fusion.17), kind=kLoop, calls=%fused_computation.6 | loop fusion | flops 4718592 | bytes 6291456 | tf_op jit(solution)/shard_map/convert_element_type | solution.py:103
  113.5 2.5 %collective-permute-start.11 = (bf16[512,1536]{1,0:T(8,128)(2,1)S(1)}, bf16[512,1536]{1,0:T(8,128)(2,1)}, u32[]{:S(2)}, u32[]{:S(2)}) collective-permute-start(bf16[512,1536]{1,0:T(8,128)(2,1)S(1)} %add_convert_fusion.1), channel_id=1, source_target_pairs={{2,3},{6,7},{10,11},{14,15},{18,19},{22,23},{26,27},{30,31}} | collective-permute-start | bytes 4718600 | tf_op jit(solution)/shard_map/ppermute | solution.py:108
  116.0 1.8 collective-permute-start.9
  117.8 1.9 %collective-permute-done.12 = bf16[512,1536]{1,0:T(8,128)(2,1)S(1)} collective-permute-done((bf16[512,1536]{1,0:T(8,128)(2,1)S(1)}, bf16[512,1536]{1,0:T(8,128)(2,1)S(1)}, u32[]{:S(2)}, u32[]{:S(2)}) %collective-permute-start.12) | collective-permute-done | bytes 1572896 | tf_op jit(solution)/shard_map/ppermute | solution.py:111
  119.7 4.2 %collective-permute-done.13 = bf16[512,1536]{1,0:T(8,128)(2,1)S(1)} collective-permute-done((bf16[512,1536]{1,0:T(8,128)(2,1)S(1)}, bf16[512,1536]{1,0:T(8,128)(2,1)S(1)}, u32[]{:S(2)}, u32[]{:S(2)}) %collective-permute-start.13) | collective-permute-done | bytes 1572896 | tf_op jit(solution)/shard_map/ppermute | solution.py:111
  124.6 1.8 collective-permute-start.14
  126.4 3.5 %collective-permute-start.15 = (bf16[512,1536]{1,0:T(8,128)(2,1)S(1)}, bf16[512,1536]{1,0:T(8,128)(2,1)}, u32[]{:S(2)}, u32[]{:S(2)}) collective-permute-start(bf16[512,1536]{1,0:T(8,128)(2,1)S(1)} %add_convert_fusion), channel_id=1, source_target_pairs={{2,1},{6,5},{10,9},{14,13},{18,17},{22,21},{26,25},{30,29}} | collective-permute-start | bytes 4718600 | tf_op jit(solution)/shard_map/ppermute | solution.py:111
  129.9 16.9 %collective-permute-done.10 = bf16[512,1536]{1,0:T(8,128)(2,1)S(1)} collective-permute-done((bf16[512,1536]{1,0:T(8,128)(2,1)S(1)}, bf16[512,1536]{1,0:T(8,128)(2,1)S(1)}, u32[]{:S(2)}, u32[]{:S(2)}) %collective-permute-start.10) | collective-permute-done | bytes 1572896 | tf_op jit(solution)/shard_map/ppermute | solution.py:108
  149.2 4.1 %fusion.14 = bf16[512,1536]{1,0:T(8,128)(2,1)S(1)} fusion(bf16[512,1024]{1,0:T(8,128)(2,1)} %copy-done.5, bf16[1024,6144]{1,0:T(8,128)(2,1)} %param.9, s32[]{:T(128)S(6)} %select_n.58), kind=kOutput, calls=%fused_computation.18 | convolution fusion | flops 1611399168 | bytes 5767172 | tf_op jit(solution)/shard_map/dot_general | solution.py:42
  153.4 4.7 %collective-permute-done.15 = bf16[512,1536]{1,0:T(8,128)(2,1)} collective-permute-done((bf16[512,1536]{1,0:T(8,128)(2,1)S(1)}, bf16[512,1536]{1,0:T(8,128)(2,1)}, u32[]{:S(2)}, u32[]{:S(2)}) %collective-permute-start.15) | collective-permute-done | bytes 1572896 | tf_op jit(solution)/shard_map/ppermute | solution.py:111
  158.1 23.7 %collective-permute-done.16 = bf16[512,1536]{1,0:T(8,128)(2,1)} collective-permute-done((bf16[512,1536]{1,0:T(8,128)(2,1)S(1)}, bf16[512,1536]{1,0:T(8,128)(2,1)}, u32[]{:S(2)}, u32[]{:S(2)}) %collective-permute-start.16) | collective-permute-done | bytes 1572896 | tf_op jit(solution)/shard_map/ppermute | solution.py:111
  181.8 6.0 %multiply_convert_fusion.2 = bf16[512,1536]{1,0:T(8,128)(2,1)} fusion(bf16[512,1536]{1,0:T(8,128)(2,1)} %collective-permute-done.16, bf16[512,1536]{1,0:T(8,128)(2,1)} %collective-permute-done.15, bf16[512,1536]{1,0:T(8,128)(2,1)} %collective-permute-done.14, bf16[512,1536]{1,0:T(8,128)(2,1)} %collective-permute-done.11, bf16[512,1536]{1,0:T(8,128)(2,1)S(1)} %copy-done.1, ...), kind=kLoop, calls=%fused_computation.4 | loop fusion | flops 11796480 | bytes 12584960 | tf_op jit(solution)/shard_map/convert_element_type | solution.py:164
  (43 shorter events, 14.8 us)
Async XLA Ops:
  0.0 2.5 %copy-start.2 = (bf16[512,1024]{1,0:T(8,128)(2,1)S(1)}, bf16[512,1024]{1,0:T(8,128)(2,1)}, u32[]{:S(2)}) copy-start(bf16[512,1024]{1,0:T(8,128)(2,1)} %param.7) | copy-start | bytes 3145732
  4.1 1.6 collective-permute-start
  5.8 8.4 %collective-permute-start.1 = (bf16[8,128,128]{2,1,0:T(8,128)(2,1)S(1)}, bf16[8,128,128]{2,1,0:T(8,128)(2,1)S(1)}, u32[]{:S(2)}, u32[]{:S(2)}) collective-permute-start(bf16[8,128,128]{2,1,0:T(8,128)(2,1)S(1)} %fusion.54), channel_id=1, source_target_pairs={{0,8},{4,12},{8,0},{12,4},{16,24},{20,28},{24,16},{28,20},{1,9},{5... | collective-permute-start | bytes 786440 | tf_op jit(solution)/shard_map/ppermute | solution.py:31
  14.3 7.7 %collective-permute-start.2 = (bf16[8,128,128]{2,1,0:T(8,128)(2,1)S(1)}, bf16[8,128,128]{2,1,0:T(8,128)(2,1)}, u32[]{:S(2)}, u32[]{:S(2)}) collective-permute-start(bf16[8,128,128]{2,1,0:T(8,128)(2,1)S(1)} %convert_add_fusion), channel_id=1, source_target_pairs={{0,16},{4,20},{8,24},{12,28},{16,0},{20,4},{24,8},{28,12},{1,17},{... | collective-permute-start | bytes 786440 | tf_op jit(solution)/shard_map/ppermute | solution.py:31
  23.0 1.2 copy-start.3
  23.0 1.5 copy-start.4
  26.4 6.5 %copy-start.5 = (bf16[512,1024]{1,0:T(8,128)(2,1)}, bf16[512,1024]{1,0:T(8,128)(2,1)S(1)}, u32[]{:S(2)}) copy-start(bf16[512,1024]{1,0:T(8,128)(2,1)S(1)} %get-tuple-element.24) | copy-start | bytes 3145732
  26.4 6.5 %collective-permute-start.3 = (f32[512]{0:T(512)S(1)}, f32[512]{0:T(512)S(1)}, u32[]{:S(2)}, u32[]{:S(2)}) collective-permute-start(f32[512]{0:T(512)S(1)} %get-tuple-element.23), channel_id=1, source_target_pairs={{0,1},{1,0},{2,3},{3,2},{4,5},{5,4},{6,7},{7,6},{8,9},{9,8},{10,11... | collective-permute-start | bytes 6152 | tf_op jit(solution)/shard_map/ppermute | solution.py:64
  32.9 35.5 %collective-permute-start.4 = (bf16[512,1536]{1,0:T(8,128)(2,1)}, bf16[512,1536]{1,0:T(8,128)(2,1)S(1)}, u32[]{:S(2)}, u32[]{:S(2)}) collective-permute-start(bf16[512,1536]{1,0:T(8,128)(2,1)} %fusion.26), channel_id=1, source_target_pairs={{0,1},{4,5},{8,9},{12,13},{16,17},{20,21},{24,25},{28,29}} | collective-permute-start | bytes 4718600 | tf_op jit(solution)/shard_map/ppermute | solution.py:108
  33.6 36.7 %collective-permute-start.5 = (bf16[512,1536]{1,0:T(8,128)(2,1)}, bf16[512,1536]{1,0:T(8,128)(2,1)}, u32[]{:S(2)}, u32[]{:S(2)}) collective-permute-start(bf16[512,1536]{1,0:T(8,128)(2,1)} %fusion.26), channel_id=1, source_target_pairs={{3,2},{7,6},{11,10},{15,14},{19,18},{23,22},{27,26},{31,30}} | collective-permute-start | bytes 4718600 | tf_op jit(solution)/shard_map/ppermute | solution.py:111
  35.0 33.4 %collective-permute-start.6 = (f32[512]{0:T(512)S(1)}, f32[512]{0:T(512)S(1)}, u32[]{:S(2)}, u32[]{:S(2)}) collective-permute-start(f32[512]{0:T(512)S(1)} %add.159), channel_id=1, source_target_pairs={{0,2},{1,3},{2,0},{3,1},{4,6},{5,7},{6,4},{7,5},{8,10},{9,11},{10,... | collective-permute-start | bytes 6152 | tf_op jit(solution)/shard_map/ppermute | solution.py:73
  72.3 18.0 %collective-permute-start.7 = (bf16[512,1536]{1,0:T(8,128)(2,1)S(1)}, bf16[512,1536]{1,0:T(8,128)(2,1)}, u32[]{:S(2)}, u32[]{:S(2)}) collective-permute-start(bf16[512,1536]{1,0:T(8,128)(2,1)S(1)} %add_convert_fusion.2), channel_id=1, source_target_pairs={{0,1},{4,5},{8,9},{12,13},{16,17},{20,21},{24,25},{28,29}} | collective-permute-start | bytes 4718600 | tf_op jit(solution)/shard_map/ppermute | solution.py:108
  74.1 35.6 %collective-permute-start.8 = (bf16[512,1536]{1,0:T(8,128)(2,1)S(1)}, bf16[512,1536]{1,0:T(8,128)(2,1)}, u32[]{:S(2)}, u32[]{:S(2)}) collective-permute-start(bf16[512,1536]{1,0:T(8,128)(2,1)S(1)} %add_convert_fusion.2), channel_id=1, source_target_pairs={{1,2},{5,6},{9,10},{13,14},{17,18},{21,22},{25,26},{29,30}} | collective-permute-start | bytes 4718600 | tf_op jit(solution)/shard_map/ppermute | solution.py:108
  75.6 4.1 %copy-start.6 = (bf16[512,1024]{1,0:T(8,128)(2,1)S(1)}, bf16[512,1024]{1,0:T(8,128)(2,1)}, u32[]{:S(2)}) copy-start(bf16[512,1024]{1,0:T(8,128)(2,1)} %copy-done.5) | copy-start | bytes 3145732
  83.4 36.3 %collective-permute-start.12 = (bf16[512,1536]{1,0:T(8,128)(2,1)S(1)}, bf16[512,1536]{1,0:T(8,128)(2,1)S(1)}, u32[]{:S(2)}, u32[]{:S(2)}) collective-permute-start(bf16[512,1536]{1,0:T(8,128)(2,1)S(1)} %add_convert_fusion.2), channel_id=1, source_target_pairs={{2,1},{6,5},{10,9},{14,13},{18,17},{22,21},{26,25},{30,29}} | collective-permute-start | bytes 4718600 | tf_op jit(solution)/shard_map/ppermute | solution.py:111
  89.0 34.9 %collective-permute-start.13 = (bf16[512,1536]{1,0:T(8,128)(2,1)S(1)}, bf16[512,1536]{1,0:T(8,128)(2,1)S(1)}, u32[]{:S(2)}, u32[]{:S(2)}) collective-permute-start(bf16[512,1536]{1,0:T(8,128)(2,1)S(1)} %add_convert_fusion.2), channel_id=1, source_target_pairs={{3,2},{7,6},{11,10},{15,14},{19,18},{23,22},{27,26},{31,30}} | collective-permute-start | bytes 4718600 | tf_op jit(solution)/shard_map/ppermute | solution.py:111
  112.2 34.6 %collective-permute-start.10 = (bf16[512,1536]{1,0:T(8,128)(2,1)S(1)}, bf16[512,1536]{1,0:T(8,128)(2,1)S(1)}, u32[]{:S(2)}, u32[]{:S(2)}) collective-permute-start(bf16[512,1536]{1,0:T(8,128)(2,1)S(1)} %add_convert_fusion.1), channel_id=1, source_target_pairs={{1,2},{5,6},{9,10},{13,14},{17,18},{21,22},{25,26},{29,30}} | collective-permute-start | bytes 4718600 | tf_op jit(solution)/shard_map/ppermute | solution.py:108
  113.5 39.9 %collective-permute-start.11 = (bf16[512,1536]{1,0:T(8,128)(2,1)S(1)}, bf16[512,1536]{1,0:T(8,128)(2,1)}, u32[]{:S(2)}, u32[]{:S(2)}) collective-permute-start(bf16[512,1536]{1,0:T(8,128)(2,1)S(1)} %add_convert_fusion.1), channel_id=1, source_target_pairs={{2,3},{6,7},{10,11},{14,15},{18,19},{22,23},{26,27},{30,31}} | collective-permute-start | bytes 4718600 | tf_op jit(solution)/shard_map/ppermute | solution.py:108
  116.0 37.4 %collective-permute-start.9 = (bf16[512,1536]{1,0:T(8,128)(2,1)S(1)}, bf16[512,1536]{1,0:T(8,128)(2,1)}, u32[]{:S(2)}, u32[]{:S(2)}) collective-permute-start(bf16[512,1536]{1,0:T(8,128)(2,1)S(1)} %add_convert_fusion.1), channel_id=1, source_target_pairs={{0,1},{4,5},{8,9},{12,13},{16,17},{20,21},{24,25},{28,29}} | collective-permute-start | bytes 4718600 | tf_op jit(solution)/shard_map/ppermute | solution.py:108
  124.6 28.8 %collective-permute-start.14 = (bf16[512,1536]{1,0:T(8,128)(2,1)S(1)}, bf16[512,1536]{1,0:T(8,128)(2,1)}, u32[]{:S(2)}, u32[]{:S(2)}) collective-permute-start(bf16[512,1536]{1,0:T(8,128)(2,1)S(1)} %add_convert_fusion), channel_id=1, source_target_pairs={{1,0},{5,4},{9,8},{13,12},{17,16},{21,20},{25,24},{29,28}} | collective-permute-start | bytes 4718600 | tf_op jit(solution)/shard_map/ppermute | solution.py:111
  126.4 31.7 %collective-permute-start.15 = (bf16[512,1536]{1,0:T(8,128)(2,1)S(1)}, bf16[512,1536]{1,0:T(8,128)(2,1)}, u32[]{:S(2)}, u32[]{:S(2)}) collective-permute-start(bf16[512,1536]{1,0:T(8,128)(2,1)S(1)} %add_convert_fusion), channel_id=1, source_target_pairs={{2,1},{6,5},{10,9},{14,13},{18,17},{22,21},{26,25},{30,29}} | collective-permute-start | bytes 4718600 | tf_op jit(solution)/shard_map/ppermute | solution.py:111
  146.8 1.1 copy-start
  147.9 33.8 %collective-permute-start.16 = (bf16[512,1536]{1,0:T(8,128)(2,1)S(1)}, bf16[512,1536]{1,0:T(8,128)(2,1)}, u32[]{:S(2)}, u32[]{:S(2)}) collective-permute-start(bf16[512,1536]{1,0:T(8,128)(2,1)S(1)} %add_convert_fusion), channel_id=1, source_target_pairs={{3,2},{7,6},{11,10},{15,14},{19,18},{23,22},{27,26},{31,30}} | collective-permute-start | bytes 4718600 | tf_op jit(solution)/shard_map/ppermute | solution.py:111
  149.2 32.6 %copy-start.1 = (bf16[512,1536]{1,0:T(8,128)(2,1)S(1)}, bf16[512,1536]{1,0:T(8,128)(2,1)}, u32[]{:S(2)}) copy-start(bf16[512,1536]{1,0:T(8,128)(2,1)} %copy-done) | copy-start | bytes 4718596

commit v18 on v15

--- a/solution.py
+++ b/solution.py
@@ -53,45 +53,51 @@
     return values
 
 
-def line_reduce_scatter(gated, out_weight, axis_name, total_squares):
+def line_reduce_scatter(gated, out_weight, axis_name, square_sums):
     count = lax.axis_size(axis_name)
     here = lax.axis_index(axis_name)
     width = out_weight.shape[1] // count
+    tokens = gated.shape[0]
+    extra = 8 * (-(-tokens // (8 * width)))
+
+    def packed(main, squares):
+        flat = jnp.zeros((extra * width,), jnp.float32).at[:tokens].set(squares)
+        rows = flat.reshape(extra, width).astype(jnp.bfloat16)
+        return jnp.concatenate([main.astype(jnp.bfloat16), rows], axis=0)
+
+    def unpacked(block):
+        block = block.astype(jnp.float32)
+        return block[:tokens], block[tokens:].reshape(-1)[:tokens]
+
     from_left = None
     from_right = None
+    left_squares = jnp.zeros_like(square_sums)
+    right_squares = jnp.zeros_like(square_sums)
     for step in range(1, count):
         right_shard = jnp.clip(here + count - step, 0, count - 1)
         left_shard = jnp.clip(here - count + step, 0, count - 1)
         if 2 * step <= count:
             shard = jnp.where(here < step, right_shard, left_shard)
             product = shard_product(gated, out_weight, shard, width).astype(jnp.bfloat16)
-            if step == 1:
-                product, total_squares = lax.optimization_barrier((product, total_squares))
-            else:
-                product = lax.optimization_barrier(product)
-            to_right = product.astype(jnp.float32)
+            product = lax.optimization_barrier(product)
+            main = product.astype(jnp.float32)
             if from_left is not None:
-                to_right = to_right + from_left + from_right
-            to_right = to_right.astype(jnp.bfloat16)
+                main = main + from_left + from_right
+            to_right = packed(main, square_sums + left_squares + right_squares)
             to_left = to_right
         else:
-            to_right = shard_product(gated, out_weight, right_shard, width).astype(jnp.bfloat16)
-            to_left = shard_product(gated, out_weight, left_shard, width).astype(jnp.bfloat16)
-            if step == 1:
-                to_right, to_left, total_squares = lax.optimization_barrier(
-                    (to_right, to_left, total_squares)
-                )
-            else:
-                to_right, to_left = lax.optimization_barrier((to_right, to_left))
-            if from_left is not None:
-                to_right = (to_right.astype(jnp.float32) + from_left).astype(jnp.bfloat16)
-                to_left = (to_left.astype(jnp.float32) + from_right).astype(jnp.bfloat16)
+            product_r = shard_product(gated, out_weight, right_shard, width).astype(jnp.bfloat16)
+            product_l = shard_product(gated, out_weight, left_shard, width).astype(jnp.bfloat16)
+            product_r, product_l = lax.optimization_barrier((product_r, product_l))
+            to_right = packed(product_r.astype(jnp.float32) + from_left, square_sums + left_squares)
+            to_left = packed(product_l.astype(jnp.float32) + from_right, square_sums + right_squares)
         right_pairs = [(i, i + 1) for i in range(step) if i + 1 < count]
         left_pairs = [(i, i - 1) for i in range(count - step, count) if i >= 1]
-        from_left = lax.ppermute(to_right, axis_name, right_pairs).astype(jnp.float32)
-        from_right = lax.ppermute(to_left, axis_name, left_pairs).astype(jnp.float32)
+        from_left, left_squares = unpacked(lax.ppermute(to_right, axis_name, right_pairs))
+        from_right, right_squares = unpacked(lax.ppermute(to_left, axis_name, left_pairs))
     own = shard_product(gated, out_weight, here, width).astype(jnp.bfloat16)
     own = own.astype(jnp.float32)
+    total_squares = square_sums + left_squares + right_squares
     scaling = lax.rsqrt(total_squares / (HEADS * HEAD_DIM) + 1e-06)
     if from_left is not None:
         own = own + from_left + from_right
@@ -140,8 +146,7 @@
     square_sums = jnp.sum(attended * attended, axis=-1)
     gate = jax.nn.sigmoid(gate_logits.astype(jnp.float32))
     gated = (attended * gate).astype(jnp.bfloat16)
-    total_squares = butterfly_sum(square_sums, "head")
-    reduced = line_reduce_scatter(gated, out_weight, "head", total_squares)
+    reduced = line_reduce_scatter(gated, out_weight, "head", square_sums)
     return reduced.astype(jnp.bfloat16)
 
 

time: 153 us -> 165 us (1.078)
  waiting for transfers between devices: 75.6 us -> 85.2 us
  starting transfers between devices: 30.3 us -> 23.6 us
  matrix products: 28.3 us -> 32.7 us
  local copies, waits for them, and re-layouts: 4.15 us -> 8.27 us
    ppermute x8 -> x6, waiting for transfers between devices: 70.2 us -> 79.8 us  [the longest x3 53.3 us: line_reduce_scatter(): lax.ppermute(to_right, axis_name, right_pairs)]
    ppermute x8 -> x6, starting transfers between devices: 25 us -> 18.3 us  [the longest x3 15.4 us: line_reduce_scatter(): lax.ppermute(to_right, axis_name, right_pairs)]
    concatenate x0 -> x4, other arithmetic: none -> 5.07 us  [packed(): return jnp.concatenate([main.astype(jnp.bfloat16), rows], axis=0)]
    convert_element_type x4 -> x9, other arithmetic: 8.53 us -> 4.22 us  [the longest x6 2.43 us: unpacked(): block = block.astype(jnp.float32)]
    dot_general x5, matrix products: 19.8 us -> 24.1 us  [shard_product(): return jnp.dot(gated, columns, preferred_element_type=jnp.float32)]
    unnamed x8 -> x16, local copies, waits for them, and re-layouts: 1.14 us -> 4.93 us
  transfers between devices with their start and end apart: 11 -> 9, of which waited for: 8 -> 7; matrix products, arithmetic and copies ran while one was open for 21% -> 16% of each run, Pallas kernels for 0% -> 0%
where the time goes in v18:
time: 165 us
  waiting for transfers between devices  85.2 us (52%)
  matrix products  32.7 us (20%)
  starting transfers between devices  23.6 us (14%)
  other arithmetic  14.6 us (9%)
  local copies, waits for them, and re-layouts  8.27 us (5%)
    ppermute x3, waiting for transfers between devices, line_reduce_scatter(): lax.ppermute(to_right, axis_name, right_pairs)  53.3 us
    ppermute x3, waiting for transfers between devices, line_reduce_scatter(): lax.ppermute(to_left, axis_name, left_pairs)  26.5 us
    dot_general x5, matrix products, shard_product(): return jnp.dot(gated, columns, preferred_element_type=jnp.float32)  24.1 us
    ppermute x3, starting transfers between devices, line_reduce_scatter(): lax.ppermute(to_right, axis_name, right_pairs)  15.4 us
    dot_general x1, matrix products, body(): jnp.einsum('nhts,nshd->nthd', scores, active_v, preferred_element_type=jn...  5.44 us
    ppermute x3, waiting for transfers between devices, exclusive_prefix(): arrived = lax.ppermute(group_total.astype(jnp.bfloat16), axis_name, pairs)  5.42 us
    ppermute x3, starting transfers between devices, exclusive_prefix(): arrived = lax.ppermute(group_total.astype(jnp.bfloat16), axis_name, pairs)  5.3 us
    concatenate x4, other arithmetic, packed(): return jnp.concatenate([main.astype(jnp.bfloat16), rows], axis=0)  5.07 us
  transfers between devices with their start and end apart: 9, of which 7 were waited for; matrix products, arithmetic and copies ran while one was open for 16% of the time, Pallas kernels for 0%

profile of v18, /device:TPU:0, one launch (start us, length us, event | category | flops | bytes accessed | tf_op | source)
XLA Modules:
  0.0 164.8 jit_solution(5842023592642307116)
XLA Ops:
  0.0 1.9 %fusion.39 = bf16[512,1024]{1,0:T(8,128)(2,1)S(1)} fusion(bf16[512,1024]{1,0:T(8,128)(2,1)} %param.14), kind=kLoop, calls=%fused_computation.39 | loop fusion | flops 3145728 | bytes 2097152 | tf_op jit(solution)/shard_map/convert_element_type | solution.py:11
  4.7 1.1 fusion.58
  5.9 2.9 %collective-permute-start.1 = (bf16[8,128,128]{2,1,0:T(8,128)(2,1)S(1)}, bf16[8,128,128]{2,1,0:T(8,128)(2,1)S(1)}, u32[]{:S(2)}, u32[]{:S(2)}) collective-permute-start(bf16[8,128,128]{2,1,0:T(8,128)(2,1)S(1)} %fusion.61), channel_id=1, source_target_pairs={{0,8},{4,12},{8,0},{12,4},{16,24},{20,28},{24,16},{28,20},{1,9},{5... | collective-permute-start | bytes 786440 | tf_op jit(solution)/shard_map/ppermute | solution.py:31
  8.8 5.4 %fusion = f32[8,128,512]{2,1,0:T(8,128)} fusion(bf16[512,8,128]{0,2,1:T(8,128)(2,1)S(1)} %bitcast.38, f32[512,512]{1,0:T(8,128)} %fusion.58, bf16[512,8,128]{0,2,1:T(8,128)(2,1)S(1)} %bitcast.36, bf16[512,1024]{1,0:T(8,128)(2,1)} %param.13), kind=kOutput, calls=%fused_computation.1 | convolution fusion | flops 1081081856 | bytes 6291456 | tf_op jit(solution)/shard_map/nhts,nshd->nthd/dot_general | solution.py:125
  14.2 1.2 collective-permute-done.1
  15.5 1.8 %collective-permute-start.2 = (bf16[8,128,128]{2,1,0:T(8,128)(2,1)S(1)}, bf16[8,128,128]{2,1,0:T(8,128)(2,1)}, u32[]{:S(2)}, u32[]{:S(2)}) collective-permute-start(bf16[8,128,128]{2,1,0:T(8,128)(2,1)S(1)} %convert_add_fusion), channel_id=1, source_target_pairs={{0,16},{4,20},{8,24},{12,28},{16,0},{20,4},{24,8},{28,12},{1,17},{... | collective-permute-start | bytes 786440 | tf_op jit(solution)/shard_map/ppermute | solution.py:31
  17.3 1.9 %copy.13 = f32[512,1024]{1,0:T(8,128)S(1)} copy(f32[512,1024]{0,1:T(8,128)} %bitcast.39) | data formatting | bytes 4194304 | tf_op jit(solution)/shard_map/optimization_barrier | solution.py:29
  19.3 4.2 %collective-permute-done.2 = bf16[8,128,128]{2,1,0:T(8,128)(2,1)} collective-permute-done((bf16[8,128,128]{2,1,0:T(8,128)(2,1)S(1)}, bf16[8,128,128]{2,1,0:T(8,128)(2,1)}, u32[]{:S(2)}, u32[]{:S(2)}) %collective-permute-start.2) | collective-permute-done | bytes 262176 | tf_op jit(solution)/shard_map/ppermute | solution.py:31
  23.4 1.1 fusion.60
  26.1 2.7 %multiply_convert_fusion.2 = (bf16[512,1024]{1,0:T(8,128)(2,1)}, f32[512]{0:T(512)S(1)}) fusion(bf16[512,1024]{1,0:T(8,128)(2,1)S(1)} %copy-done.4, f32[512,1024]{1,0:T(8,128)S(1)} %copy.13, bf16[128,8,8,128]{3,2,1,0:T(8,128)(2,1)S(1)} %bitcast.40, bf16[512,1024]{1,0:T(8,128)(2,1)S(1)} %copy-done.5), kind=kOutput, calls=%fused_computation.52 | convolution fusion | flops 1081605632 | bytes 7342080 | tf_op jit(solution)/shard_map/dot_general | solution.py:137
  28.9 4.0 %fusion.31 = bf16[512,1536]{1,0:T(8,128)(2,1)S(1)} fusion(bf16[512,1024]{1,0:T(8,128)(2,1)} %get-tuple-element.63, bf16[1024,6144]{1,0:T(8,128)(2,1)} %param.17, s32[]{:T(128)S(6)} %select_n.64), kind=kOutput, calls=%fused_computation.29 | convolution fusion | flops 1611399168 | bytes 5767172 | tf_op jit(solution)/shard_map/dot_general | solution.py:42
  32.9 1.3 pad_maximum_fusion
  34.9 3.5 %collective-permute-start.3 = (bf16[520,1536]{1,0:T(8,128)(2,1)}, bf16[520,1536]{1,0:T(8,128)(2,1)S(1)}, u32[]{:S(2)}, u32[]{:S(2)}) collective-permute-start(bf16[520,1536]{1,0:T(8,128)(2,1)} %pad_maximum_fusion), channel_id=1, source_target_pairs={{0,1},{4,5},{8,9},{12,13},{16,17},{20,21},{24,25},{28,29}} | collective-permute-start | bytes 4792328 | tf_op jit(solution)/shard_map/ppermute | solution.py:96
  38.5 5.2 %fusion.28 = bf16[512,1536]{1,0:T(8,128)(2,1)} fusion(bf16[512,1024]{1,0:T(8,128)(2,1)} %get-tuple-element.63, bf16[1024,6144]{1,0:T(8,128)(2,1)} %param.17, s32[]{:T(128)S(6)} %select_n.62), kind=kOutput, calls=%fused_computation.28 | convolution fusion | flops 1611399168 | bytes 5767172 | tf_op jit(solution)/shard_map/dot_general | solution.py:42
  43.7 27.8 %collective-permute-done.3 = bf16[520,1536]{1,0:T(8,128)(2,1)S(1)} collective-permute-done((bf16[520,1536]{1,0:T(8,128)(2,1)}, bf16[520,1536]{1,0:T(8,128)(2,1)S(1)}, u32[]{:S(2)}, u32[]{:S(2)}) %collective-permute-start.3) | collective-permute-done | bytes 1597472 | tf_op jit(solution)/shard_map/ppermute | solution.py:96
  72.4 1.0 copy-done
  73.4 0.9 fusion.8
  74.3 1.3 pad_maximum_fusion.1
  75.5 4.4 %collective-permute-start.5 = (bf16[520,1536]{1,0:T(8,128)(2,1)}, bf16[520,1536]{1,0:T(8,128)(2,1)S(1)}, u32[]{:S(2)}, u32[]{:S(2)}) collective-permute-start(bf16[520,1536]{1,0:T(8,128)(2,1)} %pad_maximum_fusion.1), channel_id=1, source_target_pairs={{0,1},{1,2},{4,5},{5,6},{8,9},{9,10},{12,13},{13,14},{16,17},{17,1... | collective-permute-start | bytes 4792328 | tf_op jit(solution)/shard_map/ppermute | solution.py:96
  79.9 0.9 collective-permute-start.7
  80.9 5.2 %fusion.22 = bf16[512,1536]{1,0:T(8,128)(2,1)} fusion(bf16[512,1024]{1,0:T(8,128)(2,1)} %get-tuple-element.63, bf16[1024,6144]{1,0:T(8,128)(2,1)} %param.17, s32[]{:T(128)S(6)} %select_n.59), kind=kOutput, calls=%fused_computation.26 | convolution fusion | flops 1611399168 | bytes 5767172 | tf_op jit(solution)/shard_map/dot_general | solution.py:42
  86.1 4.8 %fusion.25 = bf16[512,1536]{1,0:T(8,128)(2,1)} fusion(bf16[512,1024]{1,0:T(8,128)(2,1)S(1)} %copy-done.6, bf16[1024,6144]{1,0:T(8,128)(2,1)} %param.17, s32[]{:T(128)S(6)} %select_n.60), kind=kOutput, calls=%fused_computation.27 | convolution fusion | flops 1611399168 | bytes 5767172 | tf_op jit(solution)/shard_map/dot_general | solution.py:42
  90.9 21.1 %collective-permute-done.5 = bf16[520,1536]{1,0:T(8,128)(2,1)S(1)} collective-permute-done((bf16[520,1536]{1,0:T(8,128)(2,1)}, bf16[520,1536]{1,0:T(8,128)(2,1)S(1)}, u32[]{:S(2)}, u32[]{:S(2)}) %collective-permute-start.5) | collective-permute-done | bytes 1597472 | tf_op jit(solution)/shard_map/ppermute | solution.py:96
  112.6 1.0 copy-done.2
  114.0 1.3 pad_maximum_fusion.3
  115.3 1.3 collective-permute-start.8
  117.1 1.0 copy-done.1
  118.6 1.3 pad_maximum_fusion.2
  119.8 7.4 %collective-permute-start.6 = (bf16[520,1536]{1,0:T(8,128)(2,1)}, bf16[520,1536]{1,0:T(8,128)(2,1)S(1)}, u32[]{:S(2)}, u32[]{:S(2)}) collective-permute-start(bf16[520,1536]{1,0:T(8,128)(2,1)} %pad_maximum_fusion.2), channel_id=1, source_target_pairs={{0,1},{1,2},{2,3},{4,5},{5,6},{6,7},{8,9},{9,10},{10,11},{12,13},{... | collective-permute-start | bytes 4792328 | tf_op jit(solution)/shard_map/ppermute | solution.py:96
  127.3 26.5 %collective-permute-done.8 = bf16[520,1536]{1,0:T(8,128)(2,1)S(1)} collective-permute-done((bf16[520,1536]{1,0:T(8,128)(2,1)}, bf16[520,1536]{1,0:T(8,128)(2,1)S(1)}, u32[]{:S(2)}, u32[]{:S(2)}) %collective-permute-start.8) | collective-permute-done | bytes 1597472 | tf_op jit(solution)/shard_map/ppermute | solution.py:97
  153.8 4.5 %collective-permute-done.6 = bf16[520,1536]{1,0:T(8,128)(2,1)S(1)} collective-permute-done((bf16[520,1536]{1,0:T(8,128)(2,1)}, bf16[520,1536]{1,0:T(8,128)(2,1)S(1)}, u32[]{:S(2)}, u32[]{:S(2)}) %collective-permute-start.6) | collective-permute-done | bytes 1597472 | tf_op jit(solution)/shard_map/ppermute | solution.py:96
  159.9 4.8 %fusion.5 = bf16[512,1536]{1,0:T(8,128)(2,1)} fusion(f32[520,1536]{1,0:T(8,128)S(1)} %convert_element_type.175, f32[520,1536]{1,0:T(8,128)S(1)} %convert_element_type.170, bf16[512,1024]{1,0:T(8,128)(2,1)S(1)} %copy-done.7, bf16[1024,6144]{1,0:T(8,128)(2,1)} %param.17, s32[]{:T(128)S(6)} %select_n.58, f32[512]{0:T(512)S(1)} %fusion.65), kind=kOutput, calls=%fused_computation.6 | convolution fusion | flops 1615331328 | bytes 12060676 | tf_op jit(solution)/shard_map/dot_general | solution.py:42
  (59 shorter events, 9.7 us)
Async XLA Ops:
  0.0 2.5 %copy-start.3 = (bf16[512,1024]{1,0:T(8,128)(2,1)S(1)}, bf16[512,1024]{1,0:T(8,128)(2,1)}, u32[]{:S(2)}) copy-start(bf16[512,1024]{1,0:T(8,128)(2,1)} %param.15) | copy-start | bytes 3145732
  4.1 1.7 %collective-permute-start = (bf16[8,128,128]{2,1,0:T(8,128)(2,1)S(1)}, bf16[8,128,128]{2,1,0:T(8,128)(2,1)S(1)}, u32[]{:S(2)}, u32[]{:S(2)}) collective-permute-start(bf16[8,128,128]{2,1,0:T(8,128)(2,1)S(1)} %get-tuple-element.67), channel_id=1, source_target_pairs={{0,4},{4,0},{8,12},{12,8},{16,20},{20,16},{24,28},{28,24},{1,5},{5... | collective-permute-start | bytes 786440 | tf_op jit(solution)/shard_map/ppermute | solution.py:31
  5.9 9.5 %collective-permute-start.1 = (bf16[8,128,128]{2,1,0:T(8,128)(2,1)S(1)}, bf16[8,128,128]{2,1,0:T(8,128)(2,1)S(1)}, u32[]{:S(2)}, u32[]{:S(2)}) collective-permute-start(bf16[8,128,128]{2,1,0:T(8,128)(2,1)S(1)} %fusion.61), channel_id=1, source_target_pairs={{0,8},{4,12},{8,0},{12,4},{16,24},{20,28},{24,16},{28,20},{1,9},{5... | collective-permute-start | bytes 786440 | tf_op jit(solution)/shard_map/ppermute | solution.py:31
  15.5 7.9 %collective-permute-start.2 = (bf16[8,128,128]{2,1,0:T(8,128)(2,1)S(1)}, bf16[8,128,128]{2,1,0:T(8,128)(2,1)}, u32[]{:S(2)}, u32[]{:S(2)}) collective-permute-start(bf16[8,128,128]{2,1,0:T(8,128)(2,1)S(1)} %convert_add_fusion), channel_id=1, source_target_pairs={{0,16},{4,20},{8,24},{12,28},{16,0},{20,4},{24,8},{28,12},{1,17},{... | collective-permute-start | bytes 786440 | tf_op jit(solution)/shard_map/ppermute | solution.py:31
  24.5 1.2 copy-start.4
  24.6 1.5 copy-start.5
  34.2 9.5 %collective-permute-start.4 = (bf16[520,1536]{1,0:T(8,128)(2,1)}, bf16[520,1536]{1,0:T(8,128)(2,1)S(1)}, u32[]{:S(2)}, u32[]{:S(2)}) collective-permute-start(bf16[520,1536]{1,0:T(8,128)(2,1)} %pad_maximum_fusion), channel_id=1, source_target_pairs={{3,2},{7,6},{11,10},{15,14},{19,18},{23,22},{27,26},{31,30}} | collective-permute-start | bytes 4792328 | tf_op jit(solution)/shard_map/ppermute | solution.py:97
  34.9 36.5 %collective-permute-start.3 = (bf16[520,1536]{1,0:T(8,128)(2,1)}, bf16[520,1536]{1,0:T(8,128)(2,1)S(1)}, u32[]{:S(2)}, u32[]{:S(2)}) collective-permute-start(bf16[520,1536]{1,0:T(8,128)(2,1)} %pad_maximum_fusion), channel_id=1, source_target_pairs={{0,1},{4,5},{8,9},{12,13},{16,17},{20,21},{24,25},{28,29}} | collective-permute-start | bytes 4792328 | tf_op jit(solution)/shard_map/ppermute | solution.py:96
  72.0 1.4 copy-start
  75.5 36.5 %collective-permute-start.5 = (bf16[520,1536]{1,0:T(8,128)(2,1)}, bf16[520,1536]{1,0:T(8,128)(2,1)S(1)}, u32[]{:S(2)}, u32[]{:S(2)}) collective-permute-start(bf16[520,1536]{1,0:T(8,128)(2,1)} %pad_maximum_fusion.1), channel_id=1, source_target_pairs={{0,1},{1,2},{4,5},{5,6},{8,9},{9,10},{12,13},{13,14},{16,17},{17,1... | collective-permute-start | bytes 4792328 | tf_op jit(solution)/shard_map/ppermute | solution.py:96
  79.9 32.1 %collective-permute-start.7 = (bf16[520,1536]{1,0:T(8,128)(2,1)}, bf16[520,1536]{1,0:T(8,128)(2,1)S(1)}, u32[]{:S(2)}, u32[]{:S(2)}) collective-permute-start(bf16[520,1536]{1,0:T(8,128)(2,1)} %pad_maximum_fusion.1), channel_id=1, source_target_pairs={{2,1},{3,2},{6,5},{7,6},{10,9},{11,10},{14,13},{15,14},{18,17},{19... | collective-permute-start | bytes 4792328 | tf_op jit(solution)/shard_map/ppermute | solution.py:97
  80.9 5.3 %copy-start.6 = (bf16[512,1024]{1,0:T(8,128)(2,1)S(1)}, bf16[512,1024]{1,0:T(8,128)(2,1)}, u32[]{:S(2)}) copy-start(bf16[512,1024]{1,0:T(8,128)(2,1)} %get-tuple-element.63) | copy-start | bytes 3145732
  112.2 1.4 copy-start.2
  115.3 38.4 %collective-permute-start.8 = (bf16[520,1536]{1,0:T(8,128)(2,1)}, bf16[520,1536]{1,0:T(8,128)(2,1)S(1)}, u32[]{:S(2)}, u32[]{:S(2)}) collective-permute-start(bf16[520,1536]{1,0:T(8,128)(2,1)} %pad_maximum_fusion.3), channel_id=1, source_target_pairs={{1,0},{2,1},{3,2},{5,4},{6,5},{7,6},{9,8},{10,9},{11,10},{13,12},{... | collective-permute-start | bytes 4792328 | tf_op jit(solution)/shard_map/ppermute | solution.py:97
  116.7 1.4 copy-start.1
  119.8 38.4 %collective-permute-start.6 = (bf16[520,1536]{1,0:T(8,128)(2,1)}, bf16[520,1536]{1,0:T(8,128)(2,1)S(1)}, u32[]{:S(2)}, u32[]{:S(2)}) collective-permute-start(bf16[520,1536]{1,0:T(8,128)(2,1)} %pad_maximum_fusion.2), channel_id=1, source_target_pairs={{0,1},{1,2},{2,3},{4,5},{5,6},{6,7},{8,9},{9,10},{10,11},{12,13},{... | collective-permute-start | bytes 4792328 | tf_op jit(solution)/shard_map/ppermute | solution.py:96
  158.7 1.2 copy-start.7

commit v19 on v16

--- a/solution.py
+++ b/solution.py
@@ -137,7 +137,6 @@
     )
     within_rows = within_block.reshape(tokens_here, feature_count)
     prefix, within_rows = exclusive_prefix(span_total, "seq", within_rows)
-    within_block, prefix = lax.optimization_barrier((within_block, prefix))
     before = (prefix[None] + earlier_local).astype(jnp.bfloat16)
     if block_count == 1:
         identity = jnp.eye(heads_here, dtype=jnp.bfloat16)

time: 152 us -> 151 us (level)
  transfers between devices with their start and end apart: 11 -> 11, of which waited for: 7 -> 7; matrix products, arithmetic and copies ran while one was open for 21% -> 22% of each run, Pallas kernels for 0% -> 0%
where the time goes in v19:
time: 151 us; the launch traced here: 150 us
  waiting for transfers between devices  75.7 us (50%)
  starting transfers between devices  29 us (19%)
  matrix products  28.3 us (19%)
  other arithmetic  13.8 us (9%)
  local copies, waits for them, and re-layouts  3.03 us (2%)
    ppermute x1, waiting for transfers between devices, line_reduce_scatter(): lax.ppermute(total_squares, axis_name, [(i, i ^ bit) for i in range(count)])  26 us
    ppermute x3, waiting for transfers between devices, line_reduce_scatter(): lax.ppermute(to_left, axis_name, left_pairs).astype(jnp.float32)  24.6 us
    dot_general x5, matrix products, shard_product(): return jnp.dot(gated, columns, preferred_element_type=jnp.float32)  20.6 us
    ppermute x3, waiting for transfers between devices, line_reduce_scatter(): lax.ppermute(to_right, axis_name, right_pairs).astype(jnp.float32)  19.7 us
    ppermute x3, starting transfers between devices, line_reduce_scatter(): lax.ppermute(to_right, axis_name, right_pairs).astype(jnp.float32)  16.8 us
    dot_general x1, matrix products, body(): jnp.einsum('nhts,nshd->nthd', scores, active_v, preferred_element_type=jn...  5.44 us
    ppermute x3, waiting for transfers between devices, exclusive_prefix(): arrived = lax.ppermute(group_total.astype(jnp.bfloat16), axis_name, pairs)  5.4 us
    ppermute x3, starting transfers between devices, exclusive_prefix(): arrived = lax.ppermute(group_total.astype(jnp.bfloat16), axis_name, pairs)  5.3 us
  transfers between devices with their start and end apart: 11, of which 7 were waited for; matrix products, arithmetic and copies ran while one was open for 22% of the time, Pallas kernels for 0%

profile of v19, /device:TPU:0, one launch (start us, length us, event | category | flops | bytes accessed | tf_op | source)
XLA Modules:
  0.0 150.0 jit_solution(7449202616632217669)
XLA Ops:
  0.0 1.9 %fusion.32 = bf16[512,1024]{1,0:T(8,128)(2,1)S(1)} fusion(bf16[512,1024]{1,0:T(8,128)(2,1)} %param.6), kind=kLoop, calls=%fused_computation.32 | loop fusion | flops 3145728 | bytes 2097152 | tf_op jit(solution)/shard_map/convert_element_type | solution.py:11
  2.5 0.6 fusion.36
  4.1 0.6 collective-permute-start
  4.7 1.1 fusion.51
  5.9 2.9 %collective-permute-start.1 = (bf16[8,128,128]{2,1,0:T(8,128)(2,1)S(1)}, bf16[8,128,128]{2,1,0:T(8,128)(2,1)S(1)}, u32[]{:S(2)}, u32[]{:S(2)}) collective-permute-start(bf16[8,128,128]{2,1,0:T(8,128)(2,1)S(1)} %fusion.56), channel_id=1, source_target_pairs={{0,8},{4,12},{8,0},{12,4},{16,24},{20,28},{24,16},{28,20},{1,9},{5... | collective-permute-start | bytes 786440 | tf_op jit(solution)/shard_map/ppermute | solution.py:31
  8.8 5.4 %fusion = f32[8,128,512]{2,1,0:T(8,128)} fusion(bf16[512,8,128]{0,2,1:T(8,128)(2,1)S(1)} %bitcast.38, f32[512,512]{1,0:T(8,128)} %fusion.51, bf16[512,8,128]{0,2,1:T(8,128)(2,1)S(1)} %bitcast.36, bf16[512,1024]{1,0:T(8,128)(2,1)} %param.5), kind=kOutput, calls=%fused_computation.1 | convolution fusion | flops 1081081856 | bytes 6291456 | tf_op jit(solution)/shard_map/nhts,nshd->nthd/dot_general | solution.py:135
  14.2 1.2 collective-permute-done.1
  15.5 1.8 %collective-permute-start.2 = (bf16[8,128,128]{2,1,0:T(8,128)(2,1)S(1)}, bf16[8,128,128]{2,1,0:T(8,128)(2,1)}, u32[]{:S(2)}, u32[]{:S(2)}) collective-permute-start(bf16[8,128,128]{2,1,0:T(8,128)(2,1)S(1)} %convert_add_fusion), channel_id=1, source_target_pairs={{0,16},{4,20},{8,24},{12,28},{16,0},{20,4},{24,8},{28,12},{1,17},{... | collective-permute-start | bytes 786440 | tf_op jit(solution)/shard_map/ppermute | solution.py:31
  17.3 1.9 %copy.13 = f32[512,1024]{1,0:T(8,128)S(1)} copy(f32[512,1024]{0,1:T(8,128)} %bitcast.39) | data formatting | bytes 4194304 | tf_op jit(solution)/shard_map/optimization_barrier | solution.py:29
  19.3 4.2 %collective-permute-done.2 = bf16[8,128,128]{2,1,0:T(8,128)(2,1)} collective-permute-done((bf16[8,128,128]{2,1,0:T(8,128)(2,1)S(1)}, bf16[8,128,128]{2,1,0:T(8,128)(2,1)}, u32[]{:S(2)}, u32[]{:S(2)}) %collective-permute-start.2) | collective-permute-done | bytes 262176 | tf_op jit(solution)/shard_map/ppermute | solution.py:31
  23.4 1.1 fusion.55
  24.9 1.8 %multiply_reduce_fusion = (f32[512]{0:T(512)S(1)}, bf16[512,1024]{1,0:T(8,128)(2,1)S(1)}) fusion(bf16[512,1024]{1,0:T(8,128)(2,1)S(1)} %copy-done.1, f32[512,1024]{1,0:T(8,128)S(1)} %copy.13, bf16[128,8,8,128]{3,2,1,0:T(8,128)(2,1)S(1)} %bitcast.40, bf16[512,1024]{1,0:T(8,128)(2,1)S(1)} %copy-done.2), kind=kOutput, calls=%fused_computation.44 | convolution fusion | flops 1081605632 | bytes 7342080 | tf_op jit(solution)/shard_map/dot_general | solution.py:146
  26.7 1.6 %collective-permute-start.3 = (f32[512]{0:T(512)S(1)}, f32[512]{0:T(512)S(1)}, u32[]{:S(2)}, u32[]{:S(2)}) collective-permute-start(f32[512]{0:T(512)S(1)} %get-tuple-element.21), channel_id=1, source_target_pairs={{0,1},{1,0},{2,3},{3,2},{4,5},{5,4},{6,7},{7,6},{8,9},{9,8},{10,11... | collective-permute-start | bytes 6152 | tf_op jit(solution)/shard_map/ppermute | solution.py:64
  28.3 4.8 %fusion.26 = bf16[512,1536]{1,0:T(8,128)(2,1)} fusion(bf16[512,1024]{1,0:T(8,128)(2,1)S(1)} %get-tuple-element.22, bf16[1024,6144]{1,0:T(8,128)(2,1)} %param.9, s32[]{:T(128)S(6)} %select_n.64), kind=kOutput, calls=%fused_computation.22 | convolution fusion | flops 1611399168 | bytes 5767172 | tf_op jit(solution)/shard_map/dot_general | solution.py:42
  33.2 0.8 collective-permute-start.5
  34.0 3.6 %collective-permute-start.4 = (bf16[512,1536]{1,0:T(8,128)(2,1)}, bf16[512,1536]{1,0:T(8,128)(2,1)}, u32[]{:S(2)}, u32[]{:S(2)}) collective-permute-start(bf16[512,1536]{1,0:T(8,128)(2,1)} %fusion.26), channel_id=1, source_target_pairs={{0,1},{4,5},{8,9},{12,13},{16,17},{20,21},{24,25},{28,29}} | collective-permute-start | bytes 4718600 | tf_op jit(solution)/shard_map/ppermute | solution.py:107
  37.5 1.4 collective-permute-start.6
  38.9 4.0 %fusion.23 = bf16[512,1536]{1,0:T(8,128)(2,1)S(1)} fusion(bf16[512,1024]{1,0:T(8,128)(2,1)} %copy-done.3, bf16[1024,6144]{1,0:T(8,128)(2,1)} %param.9, s32[]{:T(128)S(6)} %select_n.62), kind=kOutput, calls=%fused_computation.21 | convolution fusion | flops 1611399168 | bytes 5767172 | tf_op jit(solution)/shard_map/dot_general | solution.py:42
  42.9 26.0 %collective-permute-done.6 = f32[512]{0:T(512)S(1)} collective-permute-done((f32[512]{0:T(512)S(1)}, f32[512]{0:T(512)S(1)}, u32[]{:S(2)}, u32[]{:S(2)}) %collective-permute-start.6) | collective-permute-done | bytes 2080 | tf_op jit(solution)/shard_map/ppermute | solution.py:73
  68.9 2.0 %add_convert_fusion.2 = bf16[512,1536]{1,0:T(8,128)(2,1)S(1)} fusion(bf16[512,1536]{1,0:T(8,128)(2,1)S(1)} %collective-permute-done.5, bf16[512,1536]{1,0:T(8,128)(2,1)} %collective-permute-done.4, bf16[512,1536]{1,0:T(8,128)(2,1)S(1)} %fusion.23), kind=kLoop, calls=%fused_computation.7 | loop fusion | flops 4718592 | bytes 6291456 | tf_op jit(solution)/shard_map/convert_element_type | solution.py:89
  70.9 1.8 %collective-permute-start.9 = (bf16[512,1536]{1,0:T(8,128)(2,1)S(1)}, bf16[512,1536]{1,0:T(8,128)(2,1)}, u32[]{:S(2)}, u32[]{:S(2)}) collective-permute-start(bf16[512,1536]{1,0:T(8,128)(2,1)S(1)} %add_convert_fusion.2), channel_id=1, source_target_pairs={{2,1},{3,2},{6,5},{7,6},{10,9},{11,10},{14,13},{15,14},{18,17},{19... | collective-permute-start | bytes 4718600 | tf_op jit(solution)/shard_map/ppermute | solution.py:108
  72.8 5.1 %collective-permute-start.7 = (bf16[512,1536]{1,0:T(8,128)(2,1)S(1)}, bf16[512,1536]{1,0:T(8,128)(2,1)S(1)}, u32[]{:S(2)}, u32[]{:S(2)}) collective-permute-start(bf16[512,1536]{1,0:T(8,128)(2,1)S(1)} %add_convert_fusion.2), channel_id=1, source_target_pairs={{0,1},{1,2},{4,5},{5,6},{8,9},{9,10},{12,13},{13,14},{16,17},{17,1... | collective-permute-start | bytes 4718600 | tf_op jit(solution)/shard_map/ppermute | solution.py:107
  77.9 4.1 %fusion.17 = bf16[512,1536]{1,0:T(8,128)(2,1)S(1)} fusion(bf16[512,1024]{1,0:T(8,128)(2,1)} %copy-done.3, bf16[1024,6144]{1,0:T(8,128)(2,1)} %param.9, s32[]{:T(128)S(6)} %select_n.59), kind=kOutput, calls=%fused_computation.19 | convolution fusion | flops 1611399168 | bytes 5767172 | tf_op jit(solution)/shard_map/dot_general | solution.py:42
  82.0 3.7 %fusion.20 = bf16[512,1536]{1,0:T(8,128)(2,1)S(1)} fusion(bf16[512,1024]{1,0:T(8,128)(2,1)S(1)} %copy-done.4, bf16[1024,6144]{1,0:T(8,128)(2,1)} %param.9, s32[]{:T(128)S(6)} %select_n.60), kind=kOutput, calls=%fused_computation.20 | convolution fusion | flops 1611399168 | bytes 5767172 | tf_op jit(solution)/shard_map/dot_general | solution.py:42
  85.7 2.9 %add_convert_fusion = bf16[512,1536]{1,0:T(8,128)(2,1)} fusion(bf16[512,1536]{1,0:T(8,128)(2,1)} %collective-permute-done.9, bf16[512,1536]{1,0:T(8,128)(2,1)S(1)} %fusion.20), kind=kLoop, calls=%fused_computation.5 | loop fusion | flops 3145728 | bytes 4718592 | tf_op jit(solution)/shard_map/convert_element_type | solution.py:104
  88.6 1.3 collective-permute-start.10
  89.9 18.5 %collective-permute-done.7 = bf16[512,1536]{1,0:T(8,128)(2,1)S(1)} collective-permute-done((bf16[512,1536]{1,0:T(8,128)(2,1)S(1)}, bf16[512,1536]{1,0:T(8,128)(2,1)S(1)}, u32[]{:S(2)}, u32[]{:S(2)}) %collective-permute-start.7) | collective-permute-done | bytes 1572896 | tf_op jit(solution)/shard_map/ppermute | solution.py:107
  108.8 8.2 %collective-permute-start.8 = (bf16[512,1536]{1,0:T(8,128)(2,1)S(1)}, bf16[512,1536]{1,0:T(8,128)(2,1)S(1)}, u32[]{:S(2)}, u32[]{:S(2)}) collective-permute-start(bf16[512,1536]{1,0:T(8,128)(2,1)S(1)} %add_convert_fusion.1), channel_id=1, source_target_pairs={{0,1},{1,2},{2,3},{4,5},{5,6},{6,7},{8,9},{9,10},{10,11},{12,13},{... | collective-permute-start | bytes 4718600 | tf_op jit(solution)/shard_map/ppermute | solution.py:107
  117.0 4.0 %fusion.14 = bf16[512,1536]{1,0:T(8,128)(2,1)S(1)} fusion(bf16[512,1024]{1,0:T(8,128)(2,1)} %copy-done.3, bf16[1024,6144]{1,0:T(8,128)(2,1)} %param.9, s32[]{:T(128)S(6)} %select_n.58), kind=kOutput, calls=%fused_computation.18 | convolution fusion | flops 1611399168 | bytes 5767172 | tf_op jit(solution)/shard_map/dot_general | solution.py:42
  121.0 24.6 %collective-permute-done.10 = bf16[512,1536]{1,0:T(8,128)(2,1)} collective-permute-done((bf16[512,1536]{1,0:T(8,128)(2,1)}, bf16[512,1536]{1,0:T(8,128)(2,1)}, u32[]{:S(2)}, u32[]{:S(2)}) %collective-permute-start.10) | collective-permute-done | bytes 1572896 | tf_op jit(solution)/shard_map/ppermute | solution.py:108
  145.5 1.3 collective-permute-done.8
  146.8 3.2 %multiply_convert_fusion.2 = bf16[512,1536]{1,0:T(8,128)(2,1)} fusion(bf16[512,1536]{1,0:T(8,128)(2,1)} %collective-permute-done.10, bf16[512,1536]{1,0:T(8,128)(2,1)S(1)} %collective-permute-done.8, bf16[512,1536]{1,0:T(8,128)(2,1)S(1)} %fusion.14, f32[512]{0:T(512)S(1)} %add_rsqrt_fusion), kind=kLoop, calls=%fused_computation.4 | loop fusion | flops 5505024 | bytes 6293504 | tf_op jit(solution)/shard_map/convert_element_type | solution.py:159
  (26 shorter events, 2.5 us)
Async XLA Ops:
  0.0 2.5 %copy-start = (bf16[512,1024]{1,0:T(8,128)(2,1)S(1)}, bf16[512,1024]{1,0:T(8,128)(2,1)}, u32[]{:S(2)}) copy-start(bf16[512,1024]{1,0:T(8,128)(2,1)} %param.7) | copy-start | bytes 3145732
  4.1 1.7 %collective-permute-start = (bf16[8,128,128]{2,1,0:T(8,128)(2,1)S(1)}, bf16[8,128,128]{2,1,0:T(8,128)(2,1)S(1)}, u32[]{:S(2)}, u32[]{:S(2)}) collective-permute-start(bf16[8,128,128]{2,1,0:T(8,128)(2,1)S(1)} %get-tuple-element.23), channel_id=1, source_target_pairs={{0,4},{4,0},{8,12},{12,8},{16,20},{20,16},{24,28},{28,24},{1,5},{5... | collective-permute-start | bytes 786440 | tf_op jit(solution)/shard_map/ppermute | solution.py:31
  5.9 9.5 %collective-permute-start.1 = (bf16[8,128,128]{2,1,0:T(8,128)(2,1)S(1)}, bf16[8,128,128]{2,1,0:T(8,128)(2,1)S(1)}, u32[]{:S(2)}, u32[]{:S(2)}) collective-permute-start(bf16[8,128,128]{2,1,0:T(8,128)(2,1)S(1)} %fusion.56), channel_id=1, source_target_pairs={{0,8},{4,12},{8,0},{12,4},{16,24},{20,28},{24,16},{28,20},{1,9},{5... | collective-permute-start | bytes 786440 | tf_op jit(solution)/shard_map/ppermute | solution.py:31
  15.5 7.9 %collective-permute-start.2 = (bf16[8,128,128]{2,1,0:T(8,128)(2,1)S(1)}, bf16[8,128,128]{2,1,0:T(8,128)(2,1)}, u32[]{:S(2)}, u32[]{:S(2)}) collective-permute-start(bf16[8,128,128]{2,1,0:T(8,128)(2,1)S(1)} %convert_add_fusion), channel_id=1, source_target_pairs={{0,16},{4,20},{8,24},{12,28},{16,0},{20,4},{24,8},{28,12},{1,17},{... | collective-permute-start | bytes 786440 | tf_op jit(solution)/shard_map/ppermute | solution.py:31
  19.3 5.6 %copy-start.1 = (bf16[512,1024]{1,0:T(8,128)(2,1)S(1)}, bf16[512,1024]{1,0:T(8,128)(2,1)}, u32[]{:S(2)}) copy-start(bf16[512,1024]{1,0:T(8,128)(2,1)} %param.8) | copy-start | bytes 3145732
  19.3 5.6 %copy-start.2 = (bf16[512,1024]{1,0:T(8,128)(2,1)S(1)}, bf16[512,1024]{1,0:T(8,128)(2,1)}, u32[]{:S(2)}) copy-start(bf16[512,1024]{1,0:T(8,128)(2,1)} %param.5) | copy-start | bytes 3145732
  26.7 6.5 %copy-start.3 = (bf16[512,1024]{1,0:T(8,128)(2,1)}, bf16[512,1024]{1,0:T(8,128)(2,1)S(1)}, u32[]{:S(2)}) copy-start(bf16[512,1024]{1,0:T(8,128)(2,1)S(1)} %get-tuple-element.22) | copy-start | bytes 3145732
  26.7 6.4 %collective-permute-start.3 = (f32[512]{0:T(512)S(1)}, f32[512]{0:T(512)S(1)}, u32[]{:S(2)}, u32[]{:S(2)}) collective-permute-start(f32[512]{0:T(512)S(1)} %get-tuple-element.21), channel_id=1, source_target_pairs={{0,1},{1,0},{2,3},{3,2},{4,5},{5,4},{6,7},{7,6},{8,9},{9,8},{10,11... | collective-permute-start | bytes 6152 | tf_op jit(solution)/shard_map/ppermute | solution.py:64
  33.2 35.7 %collective-permute-start.5 = (bf16[512,1536]{1,0:T(8,128)(2,1)}, bf16[512,1536]{1,0:T(8,128)(2,1)S(1)}, u32[]{:S(2)}, u32[]{:S(2)}) collective-permute-start(bf16[512,1536]{1,0:T(8,128)(2,1)} %fusion.26), channel_id=1, source_target_pairs={{3,2},{7,6},{11,10},{15,14},{19,18},{23,22},{27,26},{31,30}} | collective-permute-start | bytes 4718600 | tf_op jit(solution)/shard_map/ppermute | solution.py:108
  34.0 35.0 %collective-permute-start.4 = (bf16[512,1536]{1,0:T(8,128)(2,1)}, bf16[512,1536]{1,0:T(8,128)(2,1)}, u32[]{:S(2)}, u32[]{:S(2)}) collective-permute-start(bf16[512,1536]{1,0:T(8,128)(2,1)} %fusion.26), channel_id=1, source_target_pairs={{0,1},{4,5},{8,9},{12,13},{16,17},{20,21},{24,25},{28,29}} | collective-permute-start | bytes 4718600 | tf_op jit(solution)/shard_map/ppermute | solution.py:107
  37.5 31.4 %collective-permute-start.6 = (f32[512]{0:T(512)S(1)}, f32[512]{0:T(512)S(1)}, u32[]{:S(2)}, u32[]{:S(2)}) collective-permute-start(f32[512]{0:T(512)S(1)} %add.141), channel_id=1, source_target_pairs={{0,2},{1,3},{2,0},{3,1},{4,6},{5,7},{6,4},{7,5},{8,10},{9,11},{10,... | collective-permute-start | bytes 6152 | tf_op jit(solution)/shard_map/ppermute | solution.py:73
  70.9 14.8 %collective-permute-start.9 = (bf16[512,1536]{1,0:T(8,128)(2,1)S(1)}, bf16[512,1536]{1,0:T(8,128)(2,1)}, u32[]{:S(2)}, u32[]{:S(2)}) collective-permute-start(bf16[512,1536]{1,0:T(8,128)(2,1)S(1)} %add_convert_fusion.2), channel_id=1, source_target_pairs={{2,1},{3,2},{6,5},{7,6},{10,9},{11,10},{14,13},{15,14},{18,17},{19... | collective-permute-start | bytes 4718600 | tf_op jit(solution)/shard_map/ppermute | solution.py:108
  72.8 35.6 %collective-permute-start.7 = (bf16[512,1536]{1,0:T(8,128)(2,1)S(1)}, bf16[512,1536]{1,0:T(8,128)(2,1)S(1)}, u32[]{:S(2)}, u32[]{:S(2)}) collective-permute-start(bf16[512,1536]{1,0:T(8,128)(2,1)S(1)} %add_convert_fusion.2), channel_id=1, source_target_pairs={{0,1},{1,2},{4,5},{5,6},{8,9},{9,10},{12,13},{13,14},{16,17},{17,1... | collective-permute-start | bytes 4718600 | tf_op jit(solution)/shard_map/ppermute | solution.py:107
  77.9 4.1 %copy-start.4 = (bf16[512,1024]{1,0:T(8,128)(2,1)S(1)}, bf16[512,1024]{1,0:T(8,128)(2,1)}, u32[]{:S(2)}) copy-start(bf16[512,1024]{1,0:T(8,128)(2,1)} %copy-done.3) | copy-start | bytes 3145732
  88.6 56.9 %collective-permute-start.10 = (bf16[512,1536]{1,0:T(8,128)(2,1)}, bf16[512,1536]{1,0:T(8,128)(2,1)}, u32[]{:S(2)}, u32[]{:S(2)}) collective-permute-start(bf16[512,1536]{1,0:T(8,128)(2,1)} %add_convert_fusion), channel_id=1, source_target_pairs={{1,0},{2,1},{3,2},{5,4},{6,5},{7,6},{9,8},{10,9},{11,10},{13,12},{... | collective-permute-start | bytes 4718600 | tf_op jit(solution)/shard_map/ppermute | solution.py:108
  108.8 38.0 %collective-permute-start.8 = (bf16[512,1536]{1,0:T(8,128)(2,1)S(1)}, bf16[512,1536]{1,0:T(8,128)(2,1)S(1)}, u32[]{:S(2)}, u32[]{:S(2)}) collective-permute-start(bf16[512,1536]{1,0:T(8,128)(2,1)S(1)} %add_convert_fusion.1), channel_id=1, source_target_pairs={{0,1},{1,2},{2,3},{4,5},{5,6},{6,7},{8,9},{9,10},{10,11},{12,13},{... | collective-permute-start | bytes 4718600 | tf_op jit(solution)/shard_map/ppermute | solution.py:107
